TPU v7x, 32 devices: a whole 2x2x4 slice. The times are simulated.
32 devices in a mesh: wide: 8 (over z, y), narrow: 4 (over x, core).
Axes of the slice: x: 2, y: 2, z: 4, core: 2. Of those that a mesh axis runs over, the one named last changes fastest.
Arguments:
- spectra: bfloat16 [512, 2, 8192], P('wide'), may hold values from -6 to 6
- band_gain: float32 [8192], replicated, may hold values from 0.1 to 1.9
- owners: int32 [2], replicated, may hold values from 0 to 7
- pair_near: int32 [8, 2, 512], P('wide', None, 'narrow'), may hold values from 0 to 63
- pair_far: int32 [8, 2, 512], P('wide', None, 'narrow'), may hold values from 0 to 63
- stack_bins: int32 [8, 2, 512], P('wide', None, 'narrow'), may hold values from 0 to 255, as said below
Outputs:
- stacked: float32 [4, 64, 1024], P('narrow', 'wide')
Inputs may be any that keep to these rules, and one draw needn't show every extreme that they name: `stack_bins`: bins n * 64 to (n + 1) * 64 - 1 belong to narrow index n. Of the 256 rows of one device (steps together), at most 128 have bins of one narrow index; in every draw some narrow index gets exactly 128 rows from each device of its group.
All inputs are finite; a program needn't handle non-finite values.
Results may differ from a plain program's by a relative error of at most 0.0036.
Values may be sent and summed in bfloat16 or wider, within the bound.
No kernel may reach another device: no remote copies, remote signals or barrier semaphores. Data moves between devices by JAX's collectives and lax.ppermute only.
A program may use at most 128 MiB of HBM per device.

v0:
```python
import jax
import jax.numpy as jnp
from jax import lax
from jax.sharding import PartitionSpec as P

F = 8192
LAGS = 1024
STEPS = 2
PAIRS = 128
GW = 8


def broadcast(value, axis, root):
    mine = lax.axis_index(axis) == root
    return lax.psum(jnp.where(mine, value, jnp.zeros_like(value)), axis)


def trig_pair(freq_values, lag_values, freqs):
    turns = freq_values[:, None] * lag_values[None, :] % (2 * freqs)
    phase = turns.astype(jnp.float32) * (jnp.pi / freqs)
    return (jnp.cos(phase), jnp.sin(phase))


def lag_table(freqs, lag_count):
    unit_size = 64
    lag_values = jnp.arange(lag_count, dtype=jnp.int32) - lag_count // 2
    coarse_freq = jnp.arange(freqs // unit_size, dtype=jnp.int32) * unit_size
    fine_freq = jnp.arange(unit_size, dtype=jnp.int32)
    coarse_cos, coarse_sin = trig_pair(coarse_freq, lag_values, freqs)
    fine_cos, fine_sin = trig_pair(fine_freq, lag_values, freqs)
    cosine = (
        coarse_cos[:, None, :] * fine_cos[None, :, :]
        - coarse_sin[:, None, :] * fine_sin[None, :, :]
    )
    sine = (
        coarse_sin[:, None, :] * fine_cos[None, :, :]
        + coarse_cos[:, None, :] * fine_sin[None, :, :]
    )
    cosine = cosine.reshape(freqs, lag_count).astype(jnp.bfloat16)
    minus_sine = (-sine).reshape(freqs, lag_count).astype(jnp.bfloat16)
    return jnp.concatenate([cosine, minus_sine], axis=0)


def select_rows(block, indices):
    block_rows = block.shape[0]
    flat_block = block.reshape(block_rows, -1)
    picker = (indices[:, None] == jnp.arange(block_rows, dtype=jnp.int32)[None, :]).astype(
        jnp.bfloat16
    )
    chosen = jnp.dot(picker, flat_block, preferred_element_type=jnp.bfloat16)
    return chosen.reshape(indices.shape[0], 2, -1)


def cross_rows(near_rows, far_rows, band_gain):
    near_real = near_rows[:, 0].astype(jnp.float32)
    near_imag = near_rows[:, 1].astype(jnp.float32)
    far_real = far_rows[:, 0].astype(jnp.float32)
    far_imag = far_rows[:, 1].astype(jnp.float32)
    real_part = (near_real * far_real + near_imag * far_imag) * band_gain
    imag_part = (near_imag * far_real - near_real * far_imag) * band_gain
    return jnp.concatenate([real_part, imag_part], axis=1).astype(jnp.bfloat16)


def local(spectra, band_gain, owners, pair_near, pair_far, stack_bins):
    lag_matrix = lag_table(F, LAGS)
    inv_root = 1.0 / F**0.5
    narrow_count = lax.axis_size("narrow")
    bins_each = GW * lax.axis_size("wide")
    pieces = []
    for step_index in range(STEPS):
        root_index = owners[step_index]
        part_rows = spectra.shape[0] // narrow_count
        own_part = lax.dynamic_slice_in_dim(
            spectra, lax.axis_index("narrow") * part_rows, part_rows, 0
        )
        sent_part = broadcast(own_part, "wide", root_index)
        far_block = lax.all_gather(sent_part, "narrow", axis=0, tiled=True)
        near_rows = select_rows(spectra, pair_near[0, step_index])
        far_rows = select_rows(far_block, pair_far[0, step_index])
        cross_part = cross_rows(near_rows, far_rows, band_gain)
        pieces.append(
            jnp.dot(cross_part, lag_matrix, preferred_element_type=jnp.float32) * inv_root
        )
    lagged = jnp.concatenate(pieces, axis=0)
    bin_ids = stack_bins[0].reshape(-1)
    owner_ids = bin_ids // bins_each
    within = bin_ids % bins_each
    capacity = STEPS * PAIRS // 2
    owner_hits = (owner_ids[:, None] == jnp.arange(narrow_count, dtype=jnp.int32)[None, :]).astype(
        jnp.int32
    )
    ranks = jnp.sum((jnp.cumsum(owner_hits, axis=0) - 1) * owner_hits, axis=1)
    target = owner_ids * capacity + ranks
    outgoing = jnp.zeros((narrow_count * capacity, LAGS), jnp.float32).at[target].set(lagged)
    outgoing = outgoing.reshape(narrow_count, capacity, LAGS)
    slot_bins = jnp.full((narrow_count * capacity,), bins_each, jnp.int32).at[target].set(within)
    slot_bins = slot_bins.reshape(narrow_count, capacity)
    arrived, arrived_bins = (
        lax.all_to_all(outgoing, "narrow", split_axis=0, concat_axis=0, tiled=True),
        lax.all_to_all(slot_bins, "narrow", split_axis=0, concat_axis=0, tiled=True),
    )
    owner_stack = jax.ops.segment_sum(
        arrived.reshape(-1, LAGS), arrived_bins.reshape(-1), num_segments=bins_each + 1
    )[:bins_each]
    stacked = lax.psum_scatter(owner_stack, "wide", scatter_dimension=0, tiled=True)
    stack_scale = (GW / (STEPS * PAIRS)) ** 0.5
    return (stacked * stack_scale)[None]


def solution(mesh):
    in_specs = (
        P("wide", None, None),
        P(),
        P(),
        P("wide", None, "narrow"),
        P("wide", None, "narrow"),
        P("wide", None, "narrow"),
    )
    out_specs = P("narrow", "wide", None)
    return jax.shard_map(local, mesh=mesh, in_specs=in_specs, out_specs=out_specs, check_vma=False)
```

profile of v0, /device:TPU:0, one launch (start us, length us, event | category | flops | bytes accessed | tf_op | source)
XLA Modules:
  0.0 284.0 jit_solution(11070871599337607712)
XLA Ops:
  6.5 1.5 fusion.80
  9.4 2.8 broadcast_select_fusion.1
  12.2 81.1 %all-reduce.3.cloned.1.call-done = (bf16[16,2,8192]{2,1,0:T(2,128)(2,1)}, bf16[16,2,8192]{2,1,0:T(2,128)(2,1)}) async-done(((bf16[16,2,8192]{2,1,0:T(2,128)(2,1)}, bf16[16,2,8192]{2,1,0:T(2,128)(2,1)}), (bf16[16,2,8192]{2,1,0:T(2,128)(2,1)}, bf16[16,2,8192]{2,1,0:T(2,128)(2,1)})) %all-reduce.3.cloned.1.call-update) | async-done | bytes 1048592 | tf_op jit(solution)/shard_map/psum | solution.py:15
  93.3 0.7 and_select_fusion.2
  94.0 1.2 reduce-window.6
  95.3 0.1 slice.68
  95.3 0.1 copy.15
  95.5 0.1 copy.16
  95.6 0.7 and_select_fusion.1
  96.3 0.1 add_bitcast_fusion
  96.4 0.7 compare_select_fusion
  97.1 2.0 scatter_custom_fusion
  99.0 3.2 %all-to-all-start = ((s32[4,1,128]{2,1,0:T(1,128)}), s32[4,1,128]{2,1,0:T(1,128)S(1)}, u32[]{:S(2)}, u32[]{:S(2)}) async-start(s32[4,1,128]{2,1,0:T(1,128)} %bitcast.7), calls=%async_computation | async-start | bytes 4096 | tf_op jit(solution)/shard_map/all_to_all | solution.py:100
  102.3 0.8 slice_bitcast_fusion.2
  103.1 1.7 fusion.61
  104.8 2.1 fusion.56
  107.0 0.0 reduce-scatter.2.cloned.1.call-start
  107.0 5.1 %fusion.30 = bf16[128,2,8192]{2,0,1:T(8,128)(2,1)} fusion(s32[128]{0:T(128)S(1)} %get-tuple-element.22, bf16[8,8,2,8192]{3,2,1,0:T(2,128)(2,1)S(1)} %bitcast.141), kind=kOutput, calls=%fused_computation.44 | convolution fusion | flops 268443648 | bytes 6291968 | tf_op jit(solution)/shard_map/dot_general | solution.py:50
  112.2 5.3 %fusion.32 = bf16[128,2,8192]{2,0,1:T(8,128)(2,1)} fusion(s32[128]{0:T(128)S(1)} %get-tuple-element.21, bf16[8,8,2,8192]{3,2,1,0:T(2,128)(2,1)S(1)} %bitcast.142), kind=kOutput, calls=%fused_computation.46 | convolution fusion | flops 268443648 | bytes 6291968 | tf_op jit(solution)/shard_map/dot_general | solution.py:50
  117.5 14.9 %subtract_convert_fusion = (bf16[128,64,1024]{2,1,0:T(8,128)(2,1)}, bf16[128,64,1024]{2,1,0:T(8,128)(2,1)}) fusion(f32[64,1024]{1,0:T(8,128)S(1)} %copy-done.2, f32[128,1024]{1,0:T(8,128)S(1)} %get-tuple-element.18, f32[64,1024]{1,0:T(8,128)S(1)} %get-tuple-element.19, f32[128,1024]{1,0:T(8,128)S(1)} %get-tuple-element.17), kind=kLoop, calls=%fused_computation.5 | loop fusion | flops 75497472 | bytes 35127296 | tf_op jit(solution)/shard_map/convert_element_type | solution.py:39
  132.3 6.7 %fusion.24 = bf16[128,2,8192]{2,0,1:T(8,128)(2,1)} fusion(s32[128]{0:T(128)S(1)} %get-tuple-element.24, bf16[8,8,2,8192]{3,2,1,0:T(2,128)(2,1)} %bitcast.144), kind=kOutput, calls=%fused_computation.38 | convolution fusion | flops 268443648 | bytes 6291968 | tf_op jit(solution)/shard_map/dot_general | solution.py:50
  139.0 2.3 all-gather.3.cloned.1.call-done
  141.4 4.9 %fusion.27 = bf16[128,2,8192]{2,0,1:T(8,128)(2,1)S(1)} fusion(s32[128]{0:T(128)S(1)} %get-tuple-element.23, bf16[8,8,2,8192]{3,2,1,0:T(2,128)(2,1)} %bitcast.145), kind=kOutput, calls=%fused_computation.41 | convolution fusion | flops 268443648 | bytes 6291968 | tf_op jit(solution)/shard_map/dot_general | solution.py:50
  146.3 6.0 %fusion.5 = (bf16[128,8192]{1,0:T(8,128)(2,1)S(1)}, bf16[128,8192]{1,0:T(8,128)(2,1)S(1)}, bf16[128,8192]{1,0:T(8,128)(2,1)S(1)}, bf16[128,8192]{1,0:T(8,128)(2,1)S(1)}) fusion(f32[8192]{0:T(1024)S(1)} %copy-done.3, bf16[128,2,8192]{2,0,1:T(8,128)(2,1)S(1)} %fusion.27, bf16[128,2,8192]{2,0,1:T(8,128)(2,1)} %fusion.32, bf16[128,2,8192]{2,0,1:T(8,128)(2,1)} %fusion.24, ...), kind=kLoop, calls=%fused_computation.19 | loop fusion | flops 29360128 | bytes 25198592 | tf_op jit(solution)/shard_map/convert.2
  152.4 12.3 %fusion.41 = f32[128,1024]{1,0:T(8,128)S(1)} fusion(bf16[8192,1024]{1,0:T(8,128)(2,1)} %bitcast.139, bf16[8192,1024]{1,0:T(8,128)(2,1)} %bitcast.137, bf16[128,8192]{1,0:T(8,128)(2,1)S(1)} %get-tuple-element.8, bf16[128,8192]{1,0:T(8,128)(2,1)S(1)} %get-tuple-element.7), kind=kOutput, calls=%fused_computation.62 | convolution fusion | flops 4370595840 | bytes 38273024 | tf_op jit(solution)/shard_map/dot_general | solution.py:82
  164.7 12.3 %fusion.44 = f32[128,1024]{1,0:T(8,128)S(1)} fusion(bf16[8192,1024]{1,0:T(8,128)(2,1)} %bitcast.140, bf16[8192,1024]{1,0:T(8,128)(2,1)} %bitcast.138, bf16[128,8192]{1,0:T(8,128)(2,1)S(1)} %get-tuple-element.15, bf16[128,8192]{1,0:T(8,128)(2,1)S(1)} %get-tuple-element.16), kind=kOutput, calls=%fused_computation.63 | convolution fusion | flops 4370595840 | bytes 38273024 | tf_op jit(solution)/shard_map/dot_general | solution.py:82
  176.9 2.2 scatter_custom_fusion.1
  179.2 28.9 %all_to_all.14 = f32[4,128,1024]{2,1,0:T(8,128)} all-to-all(f32[4,128,1024]{2,1,0:T(8,128)S(1)} %bitcast.143), channel_id=1, replica_groups=mesh['wide'=8,'narrow'=4] {'narrow'}, dimensions={0} | all-to-all | bytes 4194304 | tf_op jit(solution)/shard_map/all_to_all | solution.py:99
  208.1 5.8 %scatter_custom_fusion.2 = f32[65,1024]{1,0:T(8,128)S(1)} fusion(s32[512]{0:T(512)S(1)} %bitcast.150, f32[512,1024]{1,0:T(8,128)} %bitcast.146, f32[]{:T(128)} %constant.70.clone.1), kind=kCustom, calls=%fused_computation.78 | custom fusion | flops 524288 | bytes 266752 | tf_op jit(solution)/shard_map/scatter-add | solution.py:102
  213.9 0.7 slice.77
  214.6 61.4 %reduce-scatter.2.cloned.1.call-done = f32[8,1024]{1,0:T(8,128)} async-done(((f32[64,1024]{1,0:T(8,128)}), f32[8,1024]{1,0:T(8,128)}) %reduce-scatter.2.cloned.1.call-update) | async-done | bytes 32784 | tf_op jit(solution)/shard_map/reduce_scatter | solution.py:105
  276.0 1.4 multiply_bitcast_fusion
  (26 shorter events, 0.3 us)
Async XLA Ops:
  6.5 100.5 %copy-start.1 = (bf16[64,2,8192]{2,1,0:T(2,128)(2,1)S(1)}, bf16[64,2,8192]{2,1,0:T(2,128)(2,1)}, u32[]{:S(2)}) copy-start(bf16[64,2,8192]{2,1,0:T(2,128)(2,1)} %param.6) | copy-start | bytes 6291460
  6.5 100.5 %copy-start.4 = (s32[1,2,128]{2,1,0:T(2,128)S(1)}, s32[1,2,128]{2,1,0:T(2,128)}, u32[]{:S(2)}) copy-start(s32[1,2,128]{2,1,0:T(2,128)} %param.9) | copy-start | bytes 3076
  6.5 86.8 %all-reduce.3.cloned.1.call-start = ((), (), s32[]{:S(2)}) async-start(), calls=%async_computation.6 | async-start | bytes 2097152 | tf_op jit(solution)/shard_map/psum | solution.py:15
  12.2 120.1 %all-gather.5.cloned.1.call-start = ((), (), s32[]{:S(2)}) async-start(), calls=%async_computation.4 | async-start | bytes 2621440 | tf_op jit(solution)/shard_map/all_gather | solution.py:77
  99.0 80.1 %all-to-all-start = ((s32[4,1,128]{2,1,0:T(1,128)}), s32[4,1,128]{2,1,0:T(1,128)S(1)}, u32[]{:S(2)}, u32[]{:S(2)}) async-start(s32[4,1,128]{2,1,0:T(1,128)} %bitcast.7), calls=%async_computation | async-start | bytes 4096 | tf_op jit(solution)/shard_map/all_to_all | solution.py:100
  102.3 39.1 %all-gather.3.cloned.1.call-start = ((), (), s32[]{:S(2)}) async-start(), calls=%async_computation.3 | async-start | bytes 2621440 | tf_op jit(solution)/shard_map/all_gather | solution.py:77
  107.0 169.1 %reduce-scatter.2.cloned.1.call-start = ((), (), s32[]{:S(2)}) async-start(), calls=%async_computation.5 | async-start | bytes 294912 | tf_op jit(solution)/shard_map/reduce_scatter | solution.py:105
  112.2 5.3 %copy-start.2 = (f32[64,1024]{1,0:T(8,128)S(1)}, f32[64,1024]{1,0:T(8,128)}, u32[]{:S(2)}) copy-start(f32[64,1024]{1,0:T(8,128)} %get-tuple-element.20) | copy-start | bytes 786436
  139.0 7.3 %copy-start.3 = (f32[8192]{0:T(1024)S(1)}, f32[8192]{0:T(1024)}, u32[]{:S(2)}) copy-start(f32[8192]{0:T(1024)} %param.7) | copy-start | bytes 98308
  141.4 4.9 %copy-start = (bf16[128,2,8192]{2,0,1:T(8,128)(2,1)S(1)}, bf16[128,2,8192]{2,0,1:T(8,128)(2,1)}, u32[]{:S(2)}) copy-start(bf16[128,2,8192]{2,0,1:T(8,128)(2,1)} %fusion.30) | copy-start | bytes 12582916
Sparse Core Ops, SparseCore 0:
  12.3 80.9 all-reduce.2
  95.0 22.1 all-gather.4
  118.8 22.5 all-gather.2
  214.8 61.2 reduce-scatter.1
where the time goes:
time: 284 us
  waiting for transfers between devices  145 us (51%)
  matrix products  46.6 us (16%)
  other arithmetic  40.4 us (14%)
  blocking collectives  28.9 us (10%)
  between operations  14.6 us (5%)
  local copies, waits for them, and re-layouts  5.21 us (2%)
  starting transfers between devices  3.35 us (1%)
    psum x1, waiting for transfers between devices, broadcast(): return lax.psum(jnp.where(mine, value, jnp.zeros_like(value)), axis)  81.1 us
    reduce_scatter x1, waiting for transfers between devices, local(): lax.psum_scatter(owner_stack, 'wide', scatter_dimension=0, tiled=True)  61.4 us
    all_to_all x1, blocking collectives, local(): lax.all_to_all(outgoing, 'narrow', split_axis=0, concat_axis=0, tiled=True)  28.9 us
    dot_general x2, matrix products, local(): jnp.dot(cross_part, lag_matrix, preferred_element_type=jnp.float32)  24.5 us
    dot_general x4, matrix products, select_rows(): chosen = jnp.dot(picker, flat_block, preferred_element_type=jnp.bfloat16)  22 us
    convert_element_type x1, other arithmetic, lag_table(): cosine = cosine.reshape(freqs, lag_count).astype(jnp.bfloat16)  14.9 us
    another operation x3, other arithmetic  7.31 us
    scatter-add x1, other arithmetic, local(): jax.ops.segment_sum(arrived.reshape(-1, LAGS), arrived_bins.reshape(-1),...  5.77 us
  transfers between devices with their start and end apart: 5, of which 3 were waited for; matrix products, arithmetic and copies ran while one was open for 28% of the time, Pallas kernels for 0%

commit v1 on v0

v1 whole, which is shorter than its diff:
```python
import jax
import jax.numpy as jnp
from jax import lax
from jax.sharding import PartitionSpec as P

LAGS = 1024
GW = 8


def trig_pair(freq_values, lag_values, freqs):
    turns = freq_values[:, None] * lag_values[None, :] % (2 * freqs)
    phase = turns.astype(jnp.float32) * (jnp.pi / freqs)
    return (jnp.cos(phase), jnp.sin(phase))


def lag_rows(first_freq, row_count, freqs, lag_count):
    unit_size = 64
    lag_values = jnp.arange(lag_count, dtype=jnp.int32) - lag_count // 2
    coarse_freq = first_freq + jnp.arange(row_count // unit_size, dtype=jnp.int32) * unit_size
    fine_freq = jnp.arange(unit_size, dtype=jnp.int32)
    coarse_cos, coarse_sin = trig_pair(coarse_freq, lag_values, freqs)
    fine_cos, fine_sin = trig_pair(fine_freq, lag_values, freqs)
    cosine = (
        coarse_cos[:, None, :] * fine_cos[None, :, :]
        - coarse_sin[:, None, :] * fine_sin[None, :, :]
    )
    sine = (
        coarse_sin[:, None, :] * fine_cos[None, :, :]
        + coarse_cos[:, None, :] * fine_sin[None, :, :]
    )
    cosine = cosine.reshape(row_count, lag_count).astype(jnp.bfloat16)
    minus_sine = (-sine).reshape(row_count, lag_count).astype(jnp.bfloat16)
    return jnp.concatenate([cosine, minus_sine], axis=0)


def select_rows(block, indices):
    block_rows = block.shape[0]
    flat_block = block.reshape(block_rows, -1)
    picker = (indices[:, None] == jnp.arange(block_rows, dtype=jnp.int32)[None, :]).astype(
        jnp.bfloat16
    )
    chosen = jnp.dot(picker, flat_block, preferred_element_type=jnp.bfloat16)
    return chosen.reshape(indices.shape[0], 2, -1)


def cross_rows(near_rows, far_rows, band_gain):
    near_real = near_rows[:, 0].astype(jnp.float32)
    near_imag = near_rows[:, 1].astype(jnp.float32)
    far_real = far_rows[:, 0].astype(jnp.float32)
    far_imag = far_rows[:, 1].astype(jnp.float32)
    real_part = (near_real * far_real + near_imag * far_imag) * band_gain
    imag_part = (near_imag * far_real - near_real * far_imag) * band_gain
    return jnp.concatenate([real_part, imag_part], axis=1).astype(jnp.bfloat16)


def local(spectra, band_gain, owners, pair_near, pair_far, stack_bins):
    narrow_count = lax.axis_size("narrow")
    wide_count = lax.axis_size("wide")
    narrow_index = lax.axis_index("narrow")
    block_rows, _, freqs = spectra.shape
    steps = owners.shape[0]
    share = freqs // narrow_count
    piece = share // wide_count
    total_bins = narrow_count * wide_count * GW
    first_freq = narrow_index * share

    near = lax.dynamic_slice_in_dim(spectra, first_freq, share, axis=2)
    gain = lax.dynamic_slice_in_dim(band_gain, first_freq, share, axis=0)

    with jax.named_scope("owner_share_exchange"):
        outgoing = near.reshape(block_rows, 2, wide_count, piece).transpose(2, 0, 1, 3)
        arrived = lax.all_to_all(outgoing, "wide", split_axis=0, concat_axis=0, tiled=True)
        chosen = jnp.stack(
            [lax.dynamic_index_in_dim(arrived, owners[s], 0, keepdims=False) for s in range(steps)]
        )
        gathered = lax.all_gather(chosen, "wide", axis=0, tiled=False)

    near_ids = lax.all_gather(pair_near[0], "narrow", axis=1, tiled=True)
    far_ids = lax.all_gather(pair_far[0], "narrow", axis=1, tiled=True)
    bin_ids = lax.all_gather(stack_bins[0], "narrow", axis=1, tiled=True).reshape(-1)

    with jax.named_scope("cross_spectra"):
        pieces = []
        for s in range(steps):
            far = gathered[:, s].transpose(1, 2, 0, 3).reshape(block_rows, 2, share)
            near_rows = select_rows(near, near_ids[s])
            far_rows = select_rows(far, far_ids[s])
            pieces.append(cross_rows(near_rows, far_rows, gain))
        cross_part = jnp.concatenate(pieces, axis=0)

    with jax.named_scope("lag_product"):
        lag_matrix = lag_rows(first_freq, share, freqs, LAGS)
        lagged = jnp.dot(cross_part, lag_matrix, preferred_element_type=jnp.float32)

    with jax.named_scope("bin_sums"):
        bin_hits = (
            jnp.arange(total_bins, dtype=jnp.int32)[:, None] == bin_ids[None, :]
        ).astype(jnp.float32)
        binned = jnp.dot(bin_hits, lagged, precision=lax.Precision.HIGHEST)
        binned = binned.reshape(narrow_count * wide_count, GW, LAGS)
        owned = lax.all_to_all(
            binned, ("narrow", "wide"), split_axis=0, concat_axis=0, tiled=True
        )
        stacked = jnp.sum(owned, axis=0)

    inv_root = 1.0 / freqs**0.5
    stack_scale = (GW / (steps * pair_near.shape[2])) ** 0.5
    return (stacked * (inv_root * stack_scale))[None]


def solution(mesh):
    in_specs = (
        P("wide", None, None),
        P(),
        P(),
        P("wide", None, "narrow"),
        P("wide", None, "narrow"),
        P("wide", None, "narrow"),
    )
    out_specs = P("narrow", "wide", None)
    return jax.shard_map(local, mesh=mesh, in_specs=in_specs, out_specs=out_specs, check_vma=False)
```

time: 284 us -> 147 us (0.52)
  waiting for transfers between devices: 145 us -> 23.4 us
  other arithmetic: 40.4 us -> 16 us
  blocking collectives: 28.9 us -> 45.9 us
  matrix products: 46.6 us -> 30.3 us
  starting transfers between devices: 3.35 us -> 7.32 us
    psum x1 -> x0, waiting for transfers between devices: 81.1 us -> none  [broadcast(): return lax.psum(jnp.where(mine, value, jnp.zeros_like(value)), axis)]
    reduce_scatter x1 -> x0, waiting for transfers between devices: 61.4 us -> none  [local(): lax.psum_scatter(owner_stack, 'wide', scatter_dimension=0, tiled=True)]
    all_gather x2 -> x1, waiting for transfers between devices: 2.34 us -> 23.3 us  [local(): gathered = lax.all_gather(chosen, 'wide', axis=0, tiled=False)]
    all_gather x0 -> x3, blocking collectives: none -> 15.2 us  [the longest x1 5.07 us: local(): far_ids = lax.all_gather(pair_far[0], 'narrow', axis=1, tiled=True)]
    dot_general x4, matrix products: 22 us -> 9.1 us  [select_rows(): chosen = jnp.dot(picker, flat_block, preferred_element_type=jnp.bfloat16)]
    convert_element_type x2 -> x1, other arithmetic: 14.9 us -> 5.03 us  [lag_rows(): cosine = cosine.reshape(row_count, lag_count).astype(jnp.bfloat16)]
    scatter-add x1 -> x0, other arithmetic: 5.77 us -> none  [local(): jax.ops.segment_sum(arrived.reshape(-1, LAGS), arrived_bins.reshape(-1),...]
    select_n x4 -> x0, other arithmetic: 4.89 us -> none  [the longest x1 2.82 us: broadcast(): return lax.psum(jnp.where(mine, value, jnp.zeros_like(value)), axis)]
  transfers between devices with their start and end apart: 5 -> 2, of which waited for: 3 -> 2; matrix products, arithmetic and copies ran while one was open for 28% -> 9% of each run, Pallas kernels for 0% -> 0%
where the time goes in v1:
time: 147 us
  blocking collectives  45.9 us (31%)
  matrix products  30.3 us (21%)
  waiting for transfers between devices  23.4 us (16%)
  between operations  17.1 us (12%)
  other arithmetic  16 us (11%)
  starting transfers between devices  7.32 us (5%)
  local copies, waits for them, and re-layouts  7.01 us (5%)
    all_to_all x1, blocking collectives, local(): lax.all_to_all(binned, ('narrow', 'wide'), split_axis=0, concat_axis=0, t...  30.7 us
    all_gather x1, waiting for transfers between devices, local(): gathered = lax.all_gather(chosen, 'wide', axis=0, tiled=False)  23.3 us
    dot_general x1, matrix products, local(): lagged = jnp.dot(cross_part, lag_matrix, preferred_element_type=jnp.float32)  16.6 us
    dot_general x4, matrix products, select_rows(): chosen = jnp.dot(picker, flat_block, preferred_element_type=jnp.bfloat16)  9.1 us
    another operation x1, other arithmetic  7.98 us
    all_to_all x1, starting transfers between devices, local(): lax.all_to_all(outgoing, 'wide', split_axis=0, concat_axis=0, tiled=True)  7.28 us
    all_gather x1, blocking collectives, local(): far_ids = lax.all_gather(pair_far[0], 'narrow', axis=1, tiled=True)  5.07 us
    all_gather x1, blocking collectives, local(): lax.all_gather(stack_bins[0], 'narrow', axis=1, tiled=True).reshape(-1)  5.07 us
  transfers between devices with their start and end apart: 2, of which 2 were waited for; matrix products, arithmetic and copies ran while one was open for 9% of the time, Pallas kernels for 0%

profile of v1, /device:TPU:0, one launch (start us, length us, event | category | flops | bytes accessed | tf_op | source)
XLA Modules:
  0.0 147.1 jit_solution(3719754967302724662)
XLA Ops:
  6.6 1.6 %copy-done = bf16[64,2,8192]{2,1,0:T(2,128)(2,1)S(1)} copy-done((bf16[64,2,8192]{2,1,0:T(2,128)(2,1)S(1)}, bf16[64,2,8192]{2,1,0:T(2,128)(2,1)}, u32[]{:S(2)}) %copy-start) | copy-done | bytes 2097176
  8.1 0.5 constant_dynamic-slice_fusion.2
  8.6 0.3 reshape.222
  9.0 1.0 copy.22
  9.9 7.3 %all-to-all-start = ((bf16[8,64,2,256]{3,1,2,0:T(8,128)(2,1)}), bf16[8,64,2,256]{3,1,2,0:T(8,128)(2,1)S(1)}, u32[]{:S(2)}, u32[]{:S(2)}) async-start(bf16[8,64,2,256]{3,1,2,0:T(8,128)(2,1)} %copy.22), calls=%async_computation | async-start | bytes 1048576 | tf_op jit(solution)/shard_map/owner_share_exchange/all_to_all | solution.py:72
  17.2 0.0 all-gather.6.cloned.1.call-start
  17.2 0.6 fusion.68
  21.4 5.1 %all-gather.2 = s32[1,2,512]{2,1,0:T(2,128)S(1)} all-gather(s32[1,2,128]{2,1,0:T(2,128)S(1)} %copy-done.4), channel_id=4, replica_groups=mesh['wide'=8,'narrow'=4] {'narrow'}, dimensions={2}, use_global_device_ids=true | all-gather | bytes 5120 | tf_op jit(solution)/shard_map/all_gather | solution.py:79
  26.4 5.1 %all-gather.1 = s32[1,2,512]{2,1,0:T(2,128)S(1)} all-gather(s32[1,2,128]{2,1,0:T(2,128)S(1)} %copy-done.5), channel_id=3, replica_groups=mesh['wide'=8,'narrow'=4] {'narrow'}, dimensions={2}, use_global_device_ids=true | all-gather | bytes 5120 | tf_op jit(solution)/shard_map/all_gather | solution.py:78
  31.5 0.2 all-to-all-done
  31.7 0.7 pad_maximum_fusion
  32.4 5.1 %all-gather = s32[1,2,512]{2,1,0:T(2,128)S(1)} all-gather(s32[1,2,128]{2,1,0:T(2,128)S(1)} %copy-done.6), channel_id=2, replica_groups=mesh['wide'=8,'narrow'=4] {'narrow'}, dimensions={2}, use_global_device_ids=true | all-gather | bytes 5120 | tf_op jit(solution)/shard_map/all_gather | solution.py:80
  37.5 0.6 fusion.60
  38.1 1.0 fusion.50
  39.1 3.2 %fusion.33 = bf16[512,2,2048]{2,0,1:T(8,128)(2,1)} fusion(s32[512]{0:T(512)S(1)} %bitcast.110, bf16[8,8,2,2048]{3,2,1,0:T(2,128)(2,1)S(1)} %bitcast.95), kind=kOutput, calls=%fused_computation.45 | convolution fusion | flops 268468224 | bytes 4720640 | tf_op jit(solution)/shard_map/cross_spectra/dot_general | solution.py:42
  42.4 3.3 %fusion.35 = bf16[512,2,2048]{2,0,1:T(8,128)(2,1)} fusion(s32[512]{0:T(512)S(1)} %bitcast.109, bf16[8,8,2,2048]{3,2,1,0:T(2,128)(2,1)S(1)} %bitcast.96), kind=kOutput, calls=%fused_computation.47 | convolution fusion | flops 268468224 | bytes 4720640 | tf_op jit(solution)/shard_map/cross_spectra/dot_general | solution.py:42
  45.6 5.0 %subtract_convert_fusion = (bf16[32,64,1024]{2,1,0:T(8,128)(2,1)}, bf16[32,64,1024]{2,1,0:T(8,128)(2,1)}) fusion(f32[64,1024]{1,0:T(8,128)S(1)} %get-tuple-element.20, f32[32,1024]{1,0:T(8,128)S(1)} %get-tuple-element.18, f32[64,1024]{1,0:T(8,128)S(1)} %get-tuple-element.19, f32[32,1024]{1,0:T(8,128)S(1)} %get-tuple-element.17), kind=kLoop, calls=%fused_computation.12 | loop fusion | flops 18874368 | bytes 9175040 | tf_op jit(solution)/shard_map/lag_product/convert_element_type | solution.py:31
  50.7 23.3 %all-gather.6.cloned.1.call-done = bf16[16,64,2,256]{3,1,2,0:T(8,128)(2,1)} async-done(((bf16[2,64,2,256]{3,1,2,0:T(8,128)(2,1)}), bf16[16,64,2,256]{3,1,2,0:T(8,128)(2,1)}) %all-gather.6.cloned.1.call-update) | async-done | bytes 1048592 | tf_op jit(solution)/shard_map/owner_share_exchange/all_gather | solution.py:76
  73.9 1.3 slice_bitcast_fusion.1
  75.2 0.3 copy.26
  75.5 0.2 copy.36
  75.7 0.3 copy.23
  76.0 0.2 copy.35
  76.2 1.3 fusion.27
  77.5 1.3 fusion.30
  78.8 0.8 copy-done.2
  79.6 8.0 %fusion.14 = (bf16[512,2048]{1,0:T(8,128)(2,1)}, bf16[512,2048]{1,0:T(8,128)(2,1)}, bf16[512,2048]{1,0:T(8,128)(2,1)}, bf16[512,2048]{1,0:T(8,128)(2,1)}) fusion(f32[2048]{0:T(1024)S(1)} %dynamic-slice-done, bf16[512,2,2048]{2,0,1:T(8,128)(2,1)S(1)} %fusion.30, bf16[512,2,2048]{2,0,1:T(8,128)(2,1)S(1)} %copy-done.2, bf16[512,2,2048]{2,0,1:T(8,128)(2,1)S(1)} %fusion.27, ...), kind=kLoop, calls=%fused_computation.24 | loop fusion | flops 29360128 | bytes 25174016 | tf_op jit(solution)/shard_map/convert.2
  87.6 16.6 %fusion = f32[1024,1024]{1,0:T(8,128)} fusion(bf16[512,2048]{1,0:T(8,128)(2,1)} %get-tuple-element.15, bf16[512,2048]{1,0:T(8,128)(2,1)} %get-tuple-element.16, bf16[512,2048]{1,0:T(8,128)(2,1)} %get-tuple-element.6, bf16[512,2048]{1,0:T(8,128)(2,1)} %get-tuple-element.5, bf16[2048,1024]{1,0:T(8,128)(2,1)} %bitcast.98, bf16[2048,1024]{1,0:T(8,128)(2,1)} %bitcast.97), kind=kOutput, calls=%fused_computation | convolution fusion | flops 8640266240 | bytes 20971520 | tf_op jit(solution)/shard_map/lag_product/dot_general | solution.py:93
  104.3 4.6 %convolution_bitcast_fusion = f32[32,8,1024]{2,1,0:T(8,128)S(1)} fusion(f32[1024,1024]{1,0:T(8,128)} %fusion, s32[1024]{0:T(1024)S(1)} %bitcast.106), kind=kOutput, calls=%fused_computation.37 | convolution fusion | flops 3221487616 | bytes 5246976 | tf_op jit(solution)/shard_map/bin_sums/dot_general | solution.py:99
  108.8 30.7 %all_to_all.10 = f32[32,8,1024]{2,1,0:T(8,128)S(1)} all-to-all(f32[32,8,1024]{2,1,0:T(8,128)S(1)} %convolution_bitcast_fusion), channel_id=1, replica_groups=mesh['wide'=8,'narrow'=4] {'narrow','wide'}, dimensions={0} | all-to-all | bytes 2097152 | tf_op jit(solution)/shard_map/bin_sums/all_to_all | solution.py:101
  139.6 0.1 reduce_sum.9
  139.6 0.6 multiply_bitcast_fusion
  (21 shorter events, 0.1 us)
Async XLA Ops:
  6.5 1.6 %copy-start = (bf16[64,2,8192]{2,1,0:T(2,128)(2,1)S(1)}, bf16[64,2,8192]{2,1,0:T(2,128)(2,1)}, u32[]{:S(2)}) copy-start(bf16[64,2,8192]{2,1,0:T(2,128)(2,1)} %param.6) | copy-start | bytes 6291460
  6.5 10.7 %copy-start.3 = (s32[2]{0:T(128)S(1)}, s32[2]{0:T(128)}, u32[]{:S(2)}) copy-start(s32[2]{0:T(128)} %param.8) | copy-start | bytes 28
  6.5 14.8 %copy-start.4 = (s32[1,2,128]{2,1,0:T(2,128)S(1)}, s32[1,2,128]{2,1,0:T(2,128)}, u32[]{:S(2)}) copy-start(s32[1,2,128]{2,1,0:T(2,128)} %param.10) | copy-start | bytes 3076
  6.5 19.9 %copy-start.5 = (s32[1,2,128]{2,1,0:T(2,128)S(1)}, s32[1,2,128]{2,1,0:T(2,128)}, u32[]{:S(2)}) copy-start(s32[1,2,128]{2,1,0:T(2,128)} %param.9) | copy-start | bytes 3076
  6.5 25.9 %copy-start.6 = (s32[1,2,128]{2,1,0:T(2,128)S(1)}, s32[1,2,128]{2,1,0:T(2,128)}, u32[]{:S(2)}) copy-start(s32[1,2,128]{2,1,0:T(2,128)} %param.11) | copy-start | bytes 3076
  9.9 21.8 %all-to-all-start = ((bf16[8,64,2,256]{3,1,2,0:T(8,128)(2,1)}), bf16[8,64,2,256]{3,1,2,0:T(8,128)(2,1)S(1)}, u32[]{:S(2)}, u32[]{:S(2)}) async-start(bf16[8,64,2,256]{3,1,2,0:T(8,128)(2,1)} %copy.22), calls=%async_computation | async-start | bytes 1048576 | tf_op jit(solution)/shard_map/owner_share_exchange/all_to_all | solution.py:72
  17.2 56.7 %all-gather.6.cloned.1.call-start = ((), (), s32[]{:S(2)}) async-start(), calls=%async_computation.2 | async-start | bytes 1179648 | tf_op jit(solution)/shard_map/owner_share_exchange/all_gather | solution.py:76
  76.2 2.6 %copy-start.1 = (bf16[512,2,2048]{2,0,1:T(8,128)(2,1)S(1)}, bf16[512,2,2048]{2,0,1:T(8,128)(2,1)}, u32[]{:S(2)}) copy-start(bf16[512,2,2048]{2,0,1:T(8,128)(2,1)} %fusion.33) | copy-start | bytes 12582916
  76.2 3.5 %copy-start.2 = (bf16[512,2,2048]{2,0,1:T(8,128)(2,1)S(1)}, bf16[512,2,2048]{2,0,1:T(8,128)(2,1)}, u32[]{:S(2)}) copy-start(bf16[512,2,2048]{2,0,1:T(8,128)(2,1)} %fusion.35) | copy-start | bytes 12582916
  76.2 3.5 %dynamic-slice-start = ((f32[8192]{0:T(1024)}, s32[]{:T(128)}), f32[2048]{0:T(1024)S(1)}, s32[]{:S(2)}) async-start(f32[8192]{0:T(1024)} %param.7, s32[]{:T(128)} %select_n.44), calls=%async_computation.3 | async-start | bytes 16896 | tf_op jit(solution)/shard_map/dynamic_slice | solution.py:68
Sparse Core Ops, SparseCore 0:
  32.5 41.3 all-gather.5

commit v2 on v1

--- a/solution.py
+++ b/solution.py
@@ -73,11 +73,13 @@
         chosen = jnp.stack(
             [lax.dynamic_index_in_dim(arrived, owners[s], 0, keepdims=False) for s in range(steps)]
         )
-        gathered = lax.all_gather(chosen, "wide", axis=0, tiled=False)
+        copies = jnp.broadcast_to(chosen[None], (wide_count,) + chosen.shape)
+        gathered = lax.all_to_all(copies, "wide", split_axis=0, concat_axis=0, tiled=True)
 
-    near_ids = lax.all_gather(pair_near[0], "narrow", axis=1, tiled=True)
-    far_ids = lax.all_gather(pair_far[0], "narrow", axis=1, tiled=True)
-    bin_ids = lax.all_gather(stack_bins[0], "narrow", axis=1, tiled=True).reshape(-1)
+    ids = jnp.stack([pair_near[0], pair_far[0], stack_bins[0]])
+    ids = lax.all_gather(ids, "narrow", axis=2, tiled=True)
+    near_ids, far_ids = ids[0], ids[1]
+    bin_ids = ids[2].reshape(-1)
 
     with jax.named_scope("cross_spectra"):
         pieces = []
@@ -97,10 +99,10 @@
             jnp.arange(total_bins, dtype=jnp.int32)[:, None] == bin_ids[None, :]
         ).astype(jnp.float32)
         binned = jnp.dot(bin_hits, lagged, precision=lax.Precision.HIGHEST)
-        binned = binned.reshape(narrow_count * wide_count, GW, LAGS)
-        owned = lax.all_to_all(
-            binned, ("narrow", "wide"), split_axis=0, concat_axis=0, tiled=True
-        )
+        binned = binned.reshape(narrow_count, wide_count * GW, LAGS)
+        owned = lax.all_to_all(binned, "narrow", split_axis=0, concat_axis=0, tiled=True)
+        owned = jnp.sum(owned, axis=0).reshape(wide_count, GW, LAGS)
+        owned = lax.all_to_all(owned, "wide", split_axis=0, concat_axis=0, tiled=True)
         stacked = jnp.sum(owned, axis=0)
 
     inv_root = 1.0 / freqs**0.5

time: 147 us -> 123 us (0.84)
  between operations: 17.1 us -> 3.77 us
  blocking collectives: 45.9 us -> 33.8 us
  waiting for transfers between devices: 23.4 us -> 17.5 us
  starting transfers between devices: 7.32 us -> 11.7 us
  local copies, waits for them, and re-layouts: 7.01 us -> 10.2 us
    all_gather x1 -> x0, waiting for transfers between devices: 23.3 us -> none  [local(): gathered = lax.all_gather(chosen, 'wide', axis=0, tiled=False)]
    all_to_all x0 -> x1, waiting for transfers between devices: none -> 12.3 us  [local(): lax.all_to_all(copies, 'wide', split_axis=0, concat_axis=0, tiled=True)]
    all_gather x3 -> x1, blocking collectives: 15.2 us -> 5.1 us  [local(): ids = lax.all_gather(ids, 'narrow', axis=2, tiled=True)]
    all_to_all x1, waiting for transfers between devices: 0.16 us -> 5.2 us  [local(): lax.all_to_all(outgoing, 'wide', split_axis=0, concat_axis=0, tiled=True)]
    all_to_all x0 -> x1, starting transfers between devices: none -> 4.43 us  [local(): lax.all_to_all(copies, 'wide', split_axis=0, concat_axis=0, tiled=True)]
    all_to_all x1 -> x2, blocking collectives: 30.7 us -> 28.7 us  [the longest x1 17 us: local(): lax.all_to_all(binned, 'narrow', split_axis=0, concat_axis=0, tiled=True)]
    broadcast_in_dim x0 -> x1, local copies, waits for them, and re-layouts: none -> 1.81 us  [local(): copies = jnp.broadcast_to(chosen[None], (wide_count,) + chosen.shape)]
    another operation x1 -> x2, other arithmetic: 7.98 us -> 7.99 us
  transfers between devices with their start and end apart: 2 -> 2, of which waited for: 2 -> 2; matrix products, arithmetic and copies ran while one was open for 9% -> 11% of each run, Pallas kernels for 0% -> 0%
where the time goes in v2:
time: 123 us
  blocking collectives  33.8 us (27%)
  matrix products  30.2 us (25%)
  waiting for transfers between devices  17.5 us (14%)
  other arithmetic  15.4 us (13%)
  starting transfers between devices  11.7 us (10%)
  local copies, waits for them, and re-layouts  10.2 us (8%)
  between operations  3.77 us (3%)
    all_to_all x1, blocking collectives, local(): lax.all_to_all(binned, 'narrow', split_axis=0, concat_axis=0, tiled=True)  17 us
    dot_general x1, matrix products, local(): lagged = jnp.dot(cross_part, lag_matrix, preferred_element_type=jnp.float32)  16.6 us
    all_to_all x1, waiting for transfers between devices, local(): lax.all_to_all(copies, 'wide', split_axis=0, concat_axis=0, tiled=True)  12.3 us
    all_to_all x1, blocking collectives, local(): lax.all_to_all(owned, 'wide', split_axis=0, concat_axis=0, tiled=True)  11.7 us
    dot_general x4, matrix products, select_rows(): chosen = jnp.dot(picker, flat_block, preferred_element_type=jnp.bfloat16)  9.08 us
    another operation x1, other arithmetic  7.99 us
    all_to_all x1, starting transfers between devices, local(): lax.all_to_all(outgoing, 'wide', split_axis=0, concat_axis=0, tiled=True)  7.28 us
    all_to_all x1, waiting for transfers between devices, local(): lax.all_to_all(outgoing, 'wide', split_axis=0, concat_axis=0, tiled=True)  5.2 us
  transfers between devices with their start and end apart: 2, of which 2 were waited for; matrix products, arithmetic and copies ran while one was open for 11% of the time, Pallas kernels for 0%

profile of v2, /device:TPU:0, one launch (start us, length us, event | category | flops | bytes accessed | tf_op | source)
XLA Modules:
  0.0 122.6 jit_solution(15095738777813372428)
XLA Ops:
  0.0 1.6 %copy-done = bf16[64,2,8192]{2,1,0:T(2,128)(2,1)S(1)} copy-done((bf16[64,2,8192]{2,1,0:T(2,128)(2,1)S(1)}, bf16[64,2,8192]{2,1,0:T(2,128)(2,1)}, u32[]{:S(2)}) %copy-start) | copy-done | bytes 2097176
  1.6 0.5 constant_dynamic-slice_fusion.2
  2.1 0.3 reshape.222
  2.4 0.9 copy.24
  3.4 7.3 %all-to-all-start = ((bf16[8,64,2,256]{3,1,2,0:T(8,128)(2,1)}), bf16[8,64,2,256]{3,1,2,0:T(8,128)(2,1)S(1)}, u32[]{:S(2)}, u32[]{:S(2)}) async-start(bf16[8,64,2,256]{3,1,2,0:T(8,128)(2,1)} %copy.24), calls=%async_computation | async-start | bytes 1048576 | tf_op jit(solution)/shard_map/owner_share_exchange/all_to_all | solution.py:72
  10.7 0.6 fusion.68
  14.8 5.1 %all_gather.3 = s32[3,2,512]{2,1,0:T(2,128)S(1)} all-gather(s32[3,2,128]{2,1,0:T(2,128)S(1)} %pad_add_fusion), channel_id=1, replica_groups=mesh['wide'=8,'narrow'=4] {'narrow'}, dimensions={2}, use_global_device_ids=true | all-gather | bytes 15360 | tf_op jit(solution)/shard_map/all_gather | solution.py:80
  19.9 5.2 %all-to-all-done = bf16[8,64,2,256]{3,1,2,0:T(8,128)(2,1)S(1)} async-done(((bf16[8,64,2,256]{3,1,2,0:T(8,128)(2,1)}), bf16[8,64,2,256]{3,1,2,0:T(8,128)(2,1)S(1)}, u32[]{:S(2)}, u32[]{:S(2)}) %all-to-all-start) | async-done | bytes 524320 | tf_op jit(solution)/shard_map/owner_share_exchange/all_to_all | solution.py:72
  25.2 0.1 copy.25
  25.3 1.8 %broadcast_in_dim.2 = bf16[8,2,64,2,256]{4,3,2,1,0:T(2,128)(2,1)} broadcast(bf16[2,64,2,256]{3,2,1,0:T(2,128)(2,1)S(1)} %copy.25), dimensions={1,2,3,4} | broadcast | bytes 1179648 | tf_op jit(solution)/shard_map/owner_share_exchange/broadcast_in_dim | solution.py:76
  27.1 4.4 %all-to-all-start.1 = ((bf16[8,2,64,2,256]{4,3,2,1,0:T(2,128)(2,1)}), bf16[8,2,64,2,256]{4,3,2,1,0:T(2,128)(2,1)}, u32[]{:S(2)}, u32[]{:S(2)}) async-start(bf16[8,2,64,2,256]{4,3,2,1,0:T(2,128)(2,1)} %broadcast_in_dim.2), calls=%async_computation.1 | async-start | bytes 2097152 | tf_op jit(solution)/shard_map/owner_share_exchange/all_to_all | solution.py:77
  31.6 0.6 fusion.61
  32.2 1.0 fusion.51
  33.2 3.2 %fusion.34 = bf16[512,2,2048]{2,0,1:T(8,128)(2,1)} fusion(s32[512]{0:T(512)S(1)} %bitcast.110, bf16[8,8,2,2048]{3,2,1,0:T(2,128)(2,1)S(1)} %bitcast.95), kind=kOutput, calls=%fused_computation.45 | convolution fusion | flops 268468224 | bytes 4720640 | tf_op jit(solution)/shard_map/cross_spectra/dot_general | solution.py:42
  36.5 3.3 %fusion.36 = bf16[512,2,2048]{2,0,1:T(8,128)(2,1)} fusion(s32[512]{0:T(512)S(1)} %bitcast.109, bf16[8,8,2,2048]{3,2,1,0:T(2,128)(2,1)S(1)} %bitcast.96), kind=kOutput, calls=%fused_computation.47 | convolution fusion | flops 268468224 | bytes 4720640 | tf_op jit(solution)/shard_map/cross_spectra/dot_general | solution.py:42
  39.7 5.0 %subtract_convert_fusion = (bf16[32,64,1024]{2,1,0:T(8,128)(2,1)}, bf16[32,64,1024]{2,1,0:T(8,128)(2,1)}) fusion(f32[64,1024]{1,0:T(8,128)S(1)} %get-tuple-element.24, f32[32,1024]{1,0:T(8,128)S(1)} %get-tuple-element.22, f32[64,1024]{1,0:T(8,128)S(1)} %get-tuple-element.23, f32[32,1024]{1,0:T(8,128)S(1)} %get-tuple-element.21), kind=kLoop, calls=%fused_computation.12 | loop fusion | flops 18874368 | bytes 9175040 | tf_op jit(solution)/shard_map/lag_product/convert_element_type | solution.py:31
  44.7 12.3 %all-to-all-done.1 = bf16[8,2,64,2,256]{4,3,2,1,0:T(2,128)(2,1)} async-done(((bf16[8,2,64,2,256]{4,3,2,1,0:T(2,128)(2,1)}), bf16[8,2,64,2,256]{4,3,2,1,0:T(2,128)(2,1)}, u32[]{:S(2)}, u32[]{:S(2)}) %all-to-all-start.1) | async-done | bytes 1048608 | tf_op jit(solution)/shard_map/owner_share_exchange/all_to_all | solution.py:77
  57.0 2.0 %slice_bitcast_fusion.1 = (bf16[64,2,8,256]{3,1,0,2:T(2,128)(2,1)S(1)}, bf16[64,2,8,256]{3,1,0,2:T(2,128)(2,1)S(1)}) fusion(bf16[8,2,64,2,256]{4,3,2,1,0:T(2,128)(2,1)} %all-to-all-done.1), kind=kLoop, calls=%fused_computation.50 | loop fusion | bytes 2097152 | tf_op jit(solution)/shard_map/cross_spectra/transpose | solution.py:87
  59.0 0.6 copy.29
  59.6 0.2 copy.39
  59.8 0.6 copy.26
  60.3 0.2 copy.38
  60.6 1.3 %fusion.28 = bf16[512,2,2048]{2,0,1:T(8,128)(2,1)S(1)} fusion(bf16[8,2,8,2048]{3,2,1,0:T(8,128)(2,1)S(1)} %bitcast.100, s32[512]{0:T(512)S(1)} %bitcast.108), kind=kOutput, calls=%fused_computation.39 | convolution fusion | flops 268468224 | bytes 4720640 | tf_op jit(solution)/shard_map/cross_spectra/dot_general | solution.py:42
  61.9 1.3 %fusion.31 = bf16[512,2,2048]{2,0,1:T(8,128)(2,1)S(1)} fusion(bf16[8,2,8,2048]{3,2,1,0:T(8,128)(2,1)S(1)} %bitcast.101, s32[512]{0:T(512)S(1)} %bitcast.107), kind=kOutput, calls=%fused_computation.42 | convolution fusion | flops 268468224 | bytes 4720640 | tf_op jit(solution)/shard_map/cross_spectra/dot_general | solution.py:42
  63.2 0.8 copy-done.2
  64.0 8.0 %fusion.14 = (bf16[512,2048]{1,0:T(8,128)(2,1)}, bf16[512,2048]{1,0:T(8,128)(2,1)}, bf16[512,2048]{1,0:T(8,128)(2,1)}, bf16[512,2048]{1,0:T(8,128)(2,1)}) fusion(f32[2048]{0:T(1024)S(1)} %dynamic-slice-done, bf16[512,2,2048]{2,0,1:T(8,128)(2,1)S(1)} %fusion.31, bf16[512,2,2048]{2,0,1:T(8,128)(2,1)S(1)} %copy-done.2, bf16[512,2,2048]{2,0,1:T(8,128)(2,1)S(1)} %fusion.28, ...), kind=kLoop, calls=%fused_computation.24 | loop fusion | flops 29360128 | bytes 25174016 | tf_op jit(solution)/shard_map/convert.2
  72.0 16.6 %fusion = f32[1024,1024]{1,0:T(8,128)} fusion(bf16[512,2048]{1,0:T(8,128)(2,1)} %get-tuple-element.19, bf16[512,2048]{1,0:T(8,128)(2,1)} %get-tuple-element.20, bf16[512,2048]{1,0:T(8,128)(2,1)} %get-tuple-element.6, bf16[512,2048]{1,0:T(8,128)(2,1)} %get-tuple-element.5, bf16[2048,1024]{1,0:T(8,128)(2,1)} %bitcast.98, bf16[2048,1024]{1,0:T(8,128)(2,1)} %bitcast.97), kind=kOutput, calls=%fused_computation | convolution fusion | flops 8640266240 | bytes 20971520 | tf_op jit(solution)/shard_map/lag_product/dot_general | solution.py:95
  88.6 4.5 %fusion.27 = f32[256,1024]{1,0:T(8,128)S(1)} fusion(f32[1024,1024]{1,0:T(8,128)} %fusion, s32[1024]{0:T(1024)S(1)} %bitcast.106), kind=kOutput, calls=%fused_computation.38 | convolution fusion | flops 3221487616 | bytes 5246976 | tf_op jit(solution)/shard_map/bin_sums/dot_general | solution.py:101
  93.2 17.0 %all_to_all.20 = f32[4,64,1024]{2,1,0:T(8,128)S(1)} all-to-all(f32[4,64,1024]{2,1,0:T(8,128)S(1)} %bitcast.99), channel_id=1, replica_groups=mesh['wide'=8,'narrow'=4] {'narrow'}, dimensions={0} | all-to-all | bytes 2097152 | tf_op jit(solution)/shard_map/bin_sums/all_to_all | solution.py:103
  110.2 0.1 reduce_sum.18
  110.3 11.7 %all_to_all.21 = f32[8,8,1024]{2,1,0:T(8,128)S(1)} all-to-all(f32[8,8,1024]{2,1,0:T(8,128)S(1)} %bitcast.105), channel_id=1, replica_groups=mesh['wide'=8,'narrow'=4] {'wide'}, dimensions={0} | all-to-all | bytes 524288 | tf_op jit(solution)/shard_map/bin_sums/all_to_all | solution.py:105
  122.0 0.6 multiply_bitcast_fusion
  (23 shorter events, 0.1 us)
Async XLA Ops:
  0.0 1.6 %copy-start = (bf16[64,2,8192]{2,1,0:T(2,128)(2,1)S(1)}, bf16[64,2,8192]{2,1,0:T(2,128)(2,1)}, u32[]{:S(2)}) copy-start(bf16[64,2,8192]{2,1,0:T(2,128)(2,1)} %param.6) | copy-start | bytes 6291460
  0.0 10.7 %copy-start.3 = (s32[2]{0:T(128)S(1)}, s32[2]{0:T(128)}, u32[]{:S(2)}) copy-start(s32[2]{0:T(128)} %param.8) | copy-start | bytes 28
  0.0 14.8 %copy-start.5 = (s32[1,2,128]{2,1,0:T(2,128)S(1)}, s32[1,2,128]{2,1,0:T(2,128)}, u32[]{:S(2)}) copy-start(s32[1,2,128]{2,1,0:T(2,128)} %param.10) | copy-start | bytes 3076
  0.0 14.8 %copy-start.4 = (s32[1,2,128]{2,1,0:T(2,128)S(1)}, s32[1,2,128]{2,1,0:T(2,128)}, u32[]{:S(2)}) copy-start(s32[1,2,128]{2,1,0:T(2,128)} %param.11) | copy-start | bytes 3076
  0.0 14.8 %copy-start.6 = (s32[1,2,128]{2,1,0:T(2,128)S(1)}, s32[1,2,128]{2,1,0:T(2,128)}, u32[]{:S(2)}) copy-start(s32[1,2,128]{2,1,0:T(2,128)} %param.9) | copy-start | bytes 3076
  3.4 21.8 %all-to-all-start = ((bf16[8,64,2,256]{3,1,2,0:T(8,128)(2,1)}), bf16[8,64,2,256]{3,1,2,0:T(8,128)(2,1)S(1)}, u32[]{:S(2)}, u32[]{:S(2)}) async-start(bf16[8,64,2,256]{3,1,2,0:T(8,128)(2,1)} %copy.24), calls=%async_computation | async-start | bytes 1048576 | tf_op jit(solution)/shard_map/owner_share_exchange/all_to_all | solution.py:72
  27.1 29.9 %all-to-all-start.1 = ((bf16[8,2,64,2,256]{4,3,2,1,0:T(2,128)(2,1)}), bf16[8,2,64,2,256]{4,3,2,1,0:T(2,128)(2,1)}, u32[]{:S(2)}, u32[]{:S(2)}) async-start(bf16[8,2,64,2,256]{4,3,2,1,0:T(2,128)(2,1)} %broadcast_in_dim.2), calls=%async_computation.1 | async-start | bytes 2097152 | tf_op jit(solution)/shard_map/owner_share_exchange/all_to_all | solution.py:77
  60.5 2.6 %copy-start.1 = (bf16[512,2,2048]{2,0,1:T(8,128)(2,1)S(1)}, bf16[512,2,2048]{2,0,1:T(8,128)(2,1)}, u32[]{:S(2)}) copy-start(bf16[512,2,2048]{2,0,1:T(8,128)(2,1)} %fusion.34) | copy-start | bytes 12582916
  60.5 3.5 %copy-start.2 = (bf16[512,2,2048]{2,0,1:T(8,128)(2,1)S(1)}, bf16[512,2,2048]{2,0,1:T(8,128)(2,1)}, u32[]{:S(2)}) copy-start(bf16[512,2,2048]{2,0,1:T(8,128)(2,1)} %fusion.36) | copy-start | bytes 12582916
  60.6 3.5 %dynamic-slice-start = ((f32[8192]{0:T(1024)}, s32[]{:T(128)}), f32[2048]{0:T(1024)S(1)}, s32[]{:S(2)}) async-start(f32[8192]{0:T(1024)} %param.7, s32[]{:T(128)} %select_n.44), calls=%async_computation.4 | async-start | bytes 16896 | tf_op jit(solution)/shard_map/dynamic_slice | solution.py:68

commit v3 on v2

--- a/solution.py
+++ b/solution.py
@@ -13,9 +13,9 @@
     return (jnp.cos(phase), jnp.sin(phase))
 
 
-def lag_rows(first_freq, row_count, freqs, lag_count):
+def lag_halves(first_freq, row_count, freqs, lag_count):
     unit_size = 64
-    lag_values = jnp.arange(lag_count, dtype=jnp.int32) - lag_count // 2
+    lag_values = jnp.arange(lag_count // 2, dtype=jnp.int32) + 1
     coarse_freq = first_freq + jnp.arange(row_count // unit_size, dtype=jnp.int32) * unit_size
     fine_freq = jnp.arange(unit_size, dtype=jnp.int32)
     coarse_cos, coarse_sin = trig_pair(coarse_freq, lag_values, freqs)
@@ -28,9 +28,9 @@
         coarse_sin[:, None, :] * fine_cos[None, :, :]
         + coarse_cos[:, None, :] * fine_sin[None, :, :]
     )
-    cosine = cosine.reshape(row_count, lag_count).astype(jnp.bfloat16)
-    minus_sine = (-sine).reshape(row_count, lag_count).astype(jnp.bfloat16)
-    return jnp.concatenate([cosine, minus_sine], axis=0)
+    cosine = cosine.reshape(row_count, lag_count // 2).astype(jnp.bfloat16)
+    sine = sine.reshape(row_count, lag_count // 2).astype(jnp.bfloat16)
+    return cosine, sine
 
 
 def select_rows(block, indices):
@@ -90,15 +90,27 @@
             pieces.append(cross_rows(near_rows, far_rows, gain))
         cross_part = jnp.concatenate(pieces, axis=0)
 
-    with jax.named_scope("lag_product"):
-        lag_matrix = lag_rows(first_freq, share, freqs, LAGS)
-        lagged = jnp.dot(cross_part, lag_matrix, preferred_element_type=jnp.float32)
-
     with jax.named_scope("bin_sums"):
         bin_hits = (
             jnp.arange(total_bins, dtype=jnp.int32)[:, None] == bin_ids[None, :]
-        ).astype(jnp.float32)
-        binned = jnp.dot(bin_hits, lagged, precision=lax.Precision.HIGHEST)
+        ).astype(jnp.bfloat16)
+        bin_cross = jnp.dot(bin_hits, cross_part, preferred_element_type=jnp.float32)
+        high = lax.reduce_precision(bin_cross, exponent_bits=8, mantissa_bits=7)
+        low = bin_cross - high
+        split = jnp.concatenate([high, low], axis=0).astype(jnp.bfloat16)
+
+    with jax.named_scope("lag_product"):
+        cosine, sine = lag_halves(first_freq, share, freqs, LAGS)
+        even = jnp.dot(split[:, :share], cosine, preferred_element_type=jnp.float32)
+        odd = jnp.dot(split[:, share:], sine, preferred_element_type=jnp.float32)
+        even = even[:total_bins] + even[total_bins:]
+        odd = odd[:total_bins] + odd[total_bins:]
+        zero_lag = jnp.sum(bin_cross[:, :share], axis=1, keepdims=True)
+        binned = jnp.concatenate(
+            [jnp.flip(even + odd, axis=1), zero_lag, (even - odd)[:, : LAGS // 2 - 1]], axis=1
+        )
+
+    with jax.named_scope("bin_exchange"):
         binned = binned.reshape(narrow_count, wide_count * GW, LAGS)
         owned = lax.all_to_all(binned, "narrow", split_axis=0, concat_axis=0, tiled=True)
         owned = jnp.sum(owned, axis=0).reshape(wide_count, GW, LAGS)

time: 123 us -> 145 us (1.18)
  matrix products: 30.2 us -> 45.8 us
  local copies, waits for them, and re-layouts: 10.2 us -> 15.8 us
  waiting for transfers between devices: 17.5 us -> 19.9 us
  other arithmetic: 15.4 us -> 13.8 us
    dot_general x2 -> x3, matrix products: 21.2 us -> 36.7 us  [the longest x1 34.2 us: local(): jnp.dot(bin_hits, cross_part, preferred_element_type=jnp.float32)]
    rev x0 -> x1, local copies, waits for them, and re-layouts: none -> 5.07 us  [local(): jnp.flip(even + odd, axis=1)]
    another operation x1, other arithmetic: 7.99 us -> 4.71 us
    all_to_all x1, waiting for transfers between devices: 12.3 us -> 14.7 us  [local(): lax.all_to_all(copies, 'wide', split_axis=0, concat_axis=0, tiled=True)]
    reduce_sum x0 -> x1, other arithmetic: none -> 1.77 us  [local(): zero_lag = jnp.sum(bin_cross[:, :share], axis=1, keepdims=True)]
    convert_element_type x1, other arithmetic: 5 us -> 3.31 us  [lag_halves(): sine = sine.reshape(row_count, lag_count // 2).astype(jnp.bfloat16)]
    unnamed x18 -> x22, local copies, waits for them, and re-layouts: 2.78 us -> 3.12 us
  transfers between devices with their start and end apart: 2 -> 2, of which waited for: 2 -> 2; matrix products, arithmetic and copies ran while one was open for 11% -> 8% of each run, Pallas kernels for 0% -> 0%
where the time goes in v3:
time: 145 us
  matrix products  45.8 us (32%)
  blocking collectives  33.9 us (23%)
  waiting for transfers between devices  19.9 us (14%)
  local copies, waits for them, and re-layouts  15.8 us (11%)
  other arithmetic  13.8 us (10%)
  starting transfers between devices  11.7 us (8%)
  between operations  3.82 us (3%)
    dot_general x1, matrix products, local(): jnp.dot(bin_hits, cross_part, preferred_element_type=jnp.float32)  34.2 us
    all_to_all x1, blocking collectives, local(): lax.all_to_all(binned, 'narrow', split_axis=0, concat_axis=0, tiled=True)  17 us
    all_to_all x1, waiting for transfers between devices, local(): lax.all_to_all(copies, 'wide', split_axis=0, concat_axis=0, tiled=True)  14.7 us
    all_to_all x1, blocking collectives, local(): lax.all_to_all(owned, 'wide', split_axis=0, concat_axis=0, tiled=True)  11.7 us
    dot_general x4, matrix products, select_rows(): chosen = jnp.dot(picker, flat_block, preferred_element_type=jnp.bfloat16)  9.15 us
    all_to_all x1, starting transfers between devices, local(): lax.all_to_all(outgoing, 'wide', split_axis=0, concat_axis=0, tiled=True)  7.28 us
    all_to_all x1, waiting for transfers between devices, local(): lax.all_to_all(outgoing, 'wide', split_axis=0, concat_axis=0, tiled=True)  5.17 us
    all_gather x1, blocking collectives, local(): ids = lax.all_gather(ids, 'narrow', axis=2, tiled=True)  5.1 us
  transfers between devices with their start and end apart: 2, of which 2 were waited for; matrix products, arithmetic and copies ran while one was open for 8% of the time, Pallas kernels for 0%

profile of v3, /device:TPU:0, one launch (start us, length us, event | category | flops | bytes accessed | tf_op | source)
XLA Modules:
  0.0 144.6 jit_solution(16932796197117702237)
XLA Ops:
  0.0 1.6 %copy-done = bf16[64,2,8192]{2,1,0:T(2,128)(2,1)S(1)} copy-done((bf16[64,2,8192]{2,1,0:T(2,128)(2,1)S(1)}, bf16[64,2,8192]{2,1,0:T(2,128)(2,1)}, u32[]{:S(2)}) %copy-start) | copy-done | bytes 2097176
  1.6 0.5 constant_dynamic-slice_fusion.2
  2.4 1.0 copy.26
  3.4 7.3 %all-to-all-start = ((bf16[8,64,2,256]{3,1,2,0:T(8,128)(2,1)}), bf16[8,64,2,256]{3,1,2,0:T(8,128)(2,1)S(1)}, u32[]{:S(2)}, u32[]{:S(2)}) async-start(bf16[8,64,2,256]{3,1,2,0:T(8,128)(2,1)} %copy.26), calls=%async_computation | async-start | bytes 1048576 | tf_op jit(solution)/shard_map/owner_share_exchange/all_to_all | solution.py:72
  10.7 0.6 fusion.73
  14.9 5.1 %all_gather.3 = s32[3,2,512]{2,1,0:T(2,128)S(1)} all-gather(s32[3,2,128]{2,1,0:T(2,128)S(1)} %pad_add_fusion), channel_id=1, replica_groups=mesh['wide'=8,'narrow'=4] {'narrow'}, dimensions={2}, use_global_device_ids=true | all-gather | bytes 15360 | tf_op jit(solution)/shard_map/all_gather | solution.py:80
  20.0 5.2 %all-to-all-done = bf16[8,64,2,256]{3,1,2,0:T(8,128)(2,1)S(1)} async-done(((bf16[8,64,2,256]{3,1,2,0:T(8,128)(2,1)}), bf16[8,64,2,256]{3,1,2,0:T(8,128)(2,1)S(1)}, u32[]{:S(2)}, u32[]{:S(2)}) %all-to-all-start) | async-done | bytes 524320 | tf_op jit(solution)/shard_map/owner_share_exchange/all_to_all | solution.py:72
  25.3 1.8 %broadcast_in_dim.2 = bf16[8,2,64,2,256]{4,3,2,1,0:T(2,128)(2,1)} broadcast(bf16[2,64,2,256]{3,2,1,0:T(2,128)(2,1)S(1)} %copy.27), dimensions={1,2,3,4} | broadcast | bytes 1179648 | tf_op jit(solution)/shard_map/owner_share_exchange/broadcast_in_dim | solution.py:76
  27.1 4.4 %all-to-all-start.1 = ((bf16[8,2,64,2,256]{4,3,2,1,0:T(2,128)(2,1)}), bf16[8,2,64,2,256]{4,3,2,1,0:T(2,128)(2,1)}, u32[]{:S(2)}, u32[]{:S(2)}) async-start(bf16[8,2,64,2,256]{4,3,2,1,0:T(2,128)(2,1)} %broadcast_in_dim.2), calls=%async_computation.1 | async-start | bytes 2097152 | tf_op jit(solution)/shard_map/owner_share_exchange/all_to_all | solution.py:77
  31.9 0.5 fusion.61
  32.5 3.3 %add_convert_fusion = (bf16[32,64,512]{2,1,0:T(8,128)(2,1)}, bf16[32,64,512]{2,1,0:T(8,128)(2,1)}) fusion(f32[64,512]{1,0:T(8,128)S(1)} %get-tuple-element.29, f32[32,512]{1,0:T(8,128)S(1)} %get-tuple-element.27, f32[64,512]{1,0:T(8,128)S(1)} %get-tuple-element.28, f32[32,512]{1,0:T(8,128)S(1)} %get-tuple-element.26), kind=kLoop, calls=%fused_computation.37 | loop fusion | flops 8388608 | bytes 4587520 | tf_op jit(solution)/shard_map/lag_product/convert_element_type | solution.py:32
  35.8 3.3 %fusion.36 = bf16[512,2,2048]{2,0,1:T(8,128)(2,1)} fusion(s32[512]{0:T(512)S(1)} %bitcast.112, bf16[8,8,2,2048]{3,2,1,0:T(2,128)(2,1)S(1)} %bitcast.97), kind=kOutput, calls=%fused_computation.53 | convolution fusion | flops 268468224 | bytes 4720640 | tf_op jit(solution)/shard_map/cross_spectra/dot_general | solution.py:42
  39.1 3.3 %fusion.38 = bf16[512,2,2048]{2,0,1:T(8,128)(2,1)} fusion(s32[512]{0:T(512)S(1)} %bitcast.111, bf16[8,8,2,2048]{3,2,1,0:T(2,128)(2,1)S(1)} %bitcast.98), kind=kOutput, calls=%fused_computation.55 | convolution fusion | flops 268468224 | bytes 4720640 | tf_op jit(solution)/shard_map/cross_spectra/dot_general | solution.py:42
  42.3 14.7 %all-to-all-done.1 = bf16[8,2,64,2,256]{4,3,2,1,0:T(2,128)(2,1)} async-done(((bf16[8,2,64,2,256]{4,3,2,1,0:T(2,128)(2,1)}), bf16[8,2,64,2,256]{4,3,2,1,0:T(2,128)(2,1)}, u32[]{:S(2)}, u32[]{:S(2)}) %all-to-all-start.1) | async-done | bytes 1048608 | tf_op jit(solution)/shard_map/owner_share_exchange/all_to_all | solution.py:77
  57.0 2.0 %slice_bitcast_fusion.1 = (bf16[64,2,8,256]{3,1,0,2:T(2,128)(2,1)S(1)}, bf16[64,2,8,256]{3,1,0,2:T(2,128)(2,1)S(1)}) fusion(bf16[8,2,64,2,256]{4,3,2,1,0:T(2,128)(2,1)} %all-to-all-done.1), kind=kLoop, calls=%fused_computation.61 | loop fusion | bytes 2097152 | tf_op jit(solution)/shard_map/cross_spectra/transpose | solution.py:87
  59.0 0.6 copy.31
  59.7 0.6 copy.28
  60.5 1.3 fusion.30
  61.8 1.3 fusion.33
  63.2 0.8 copy-done.2
  64.0 4.7 %fusion.11 = (bf16[512,2048]{1,0:T(8,128)(2,1)S(1)}, bf16[512,2048]{1,0:T(8,128)(2,1)S(1)}, bf16[512,2048]{1,0:T(8,128)(2,1)S(1)}, bf16[512,2048]{1,0:T(8,128)(2,1)S(1)}) fusion(f32[2048]{0:T(1024)S(1)} %dynamic-slice-done, bf16[512,2,2048]{2,0,1:T(8,128)(2,1)S(1)} %fusion.33, bf16[512,2,2048]{2,0,1:T(8,128)(2,1)S(1)} %copy-done.2, ...), kind=kLoop, calls=%fused_computation.21 | loop fusion | flops 29360128 | bytes 25174016 | tf_op jit(solution)/shard_map/convert.4
  68.7 34.2 %fusion.24 = (bf16[256,4096]{1,0:T(8,128)(2,1)S(1)}, bf16[256,4096]{1,0:T(8,128)(2,1)S(1)}, f32[256,4096]{1,0:T(8,128)}) fusion(bf16[512,2048]{1,0:T(8,128)(2,1)S(1)} %get-tuple-element.24, bf16[512,2048]{1,0:T(8,128)(2,1)S(1)} %get-tuple-element.25, bf16[512,2048]{1,0:T(8,128)(2,1)S(1)} %get-tuple-element.9, bf16[512,2048]{1,0:T(8,128)(2,1)S(1)} %get-tuple-element.8, ...), kind=kOutput, calls=%fused_computation.34 | convolution fusion | flops 2185494528 | bytes 16781312 | tf_op jit(solution)/shard_map/bin_sums/dot_general | solution.py:97
  102.9 1.2 fusion.28
  104.2 0.3 copy-done.3
  104.5 1.3 fusion.26
  105.8 1.0 fusion.71
  106.8 5.1 %rev.4 = f32[256,512]{1,0:T(8,128)} reverse(f32[256,512]{1,0:T(8,128)} %get-tuple-element.5), dimensions={1} | reverse | bytes 1048576 | tf_op jit(solution)/shard_map/lag_product/jit(_flip)/rev | solution.py:110
  111.8 1.8 %slice_reduce_fusion = f32[256]{0:T(256)S(1)} fusion(f32[256,4096]{1,0:T(8,128)} %get-tuple-element.32), kind=kLoop, calls=%fused_computation.41 | loop fusion | flops 524032 | bytes 2098176 | tf_op jit(solution)/shard_map/lag_product/reduce_sum | solution.py:108
  113.9 1.3 pad_maximum_fusion.2
  115.2 17.0 %all_to_all.20 = f32[4,64,1024]{2,1,0:T(8,128)S(1)} all-to-all(f32[4,64,1024]{2,1,0:T(8,128)S(1)} %pad_maximum_fusion.2), channel_id=1, replica_groups=mesh['wide'=8,'narrow'=4] {'narrow'}, dimensions={0} | all-to-all | bytes 2097152 | tf_op jit(solution)/shard_map/bin_exchange/all_to_all | solution.py:115
  132.3 11.7 %all_to_all.21 = f32[8,8,1024]{2,1,0:T(8,128)S(1)} all-to-all(f32[8,8,1024]{2,1,0:T(8,128)S(1)} %bitcast.108), channel_id=1, replica_groups=mesh['wide'=8,'narrow'=4] {'wide'}, dimensions={0} | all-to-all | bytes 524288 | tf_op jit(solution)/shard_map/bin_exchange/all_to_all | solution.py:117
  144.0 0.6 multiply_bitcast_fusion
  (34 shorter events, 1.6 us)
Async XLA Ops:
  0.0 1.6 %copy-start = (bf16[64,2,8192]{2,1,0:T(2,128)(2,1)S(1)}, bf16[64,2,8192]{2,1,0:T(2,128)(2,1)}, u32[]{:S(2)}) copy-start(bf16[64,2,8192]{2,1,0:T(2,128)(2,1)} %param.6) | copy-start | bytes 6291460
  0.0 10.7 %copy-start.5 = (s32[2]{0:T(128)S(1)}, s32[2]{0:T(128)}, u32[]{:S(2)}) copy-start(s32[2]{0:T(128)} %param.8) | copy-start | bytes 28
  0.0 14.8 %copy-start.7 = (s32[1,2,128]{2,1,0:T(2,128)S(1)}, s32[1,2,128]{2,1,0:T(2,128)}, u32[]{:S(2)}) copy-start(s32[1,2,128]{2,1,0:T(2,128)} %param.10) | copy-start | bytes 3076
  0.0 14.8 %copy-start.6 = (s32[1,2,128]{2,1,0:T(2,128)S(1)}, s32[1,2,128]{2,1,0:T(2,128)}, u32[]{:S(2)}) copy-start(s32[1,2,128]{2,1,0:T(2,128)} %param.11) | copy-start | bytes 3076
  0.0 14.8 %copy-start.8 = (s32[1,2,128]{2,1,0:T(2,128)S(1)}, s32[1,2,128]{2,1,0:T(2,128)}, u32[]{:S(2)}) copy-start(s32[1,2,128]{2,1,0:T(2,128)} %param.9) | copy-start | bytes 3076
  3.4 21.8 %all-to-all-start = ((bf16[8,64,2,256]{3,1,2,0:T(8,128)(2,1)}), bf16[8,64,2,256]{3,1,2,0:T(8,128)(2,1)S(1)}, u32[]{:S(2)}, u32[]{:S(2)}) async-start(bf16[8,64,2,256]{3,1,2,0:T(8,128)(2,1)} %copy.26), calls=%async_computation | async-start | bytes 1048576 | tf_op jit(solution)/shard_map/owner_share_exchange/all_to_all | solution.py:72
  27.1 29.9 %all-to-all-start.1 = ((bf16[8,2,64,2,256]{4,3,2,1,0:T(2,128)(2,1)}), bf16[8,2,64,2,256]{4,3,2,1,0:T(2,128)(2,1)}, u32[]{:S(2)}, u32[]{:S(2)}) async-start(bf16[8,2,64,2,256]{4,3,2,1,0:T(2,128)(2,1)} %broadcast_in_dim.2), calls=%async_computation.1 | async-start | bytes 2097152 | tf_op jit(solution)/shard_map/owner_share_exchange/all_to_all | solution.py:77
  60.5 2.6 %copy-start.1 = (bf16[512,2,2048]{2,0,1:T(8,128)(2,1)S(1)}, bf16[512,2,2048]{2,0,1:T(8,128)(2,1)}, u32[]{:S(2)}) copy-start(bf16[512,2,2048]{2,0,1:T(8,128)(2,1)} %fusion.36) | copy-start | bytes 12582916
  60.5 3.5 %copy-start.2 = (bf16[512,2,2048]{2,0,1:T(8,128)(2,1)S(1)}, bf16[512,2,2048]{2,0,1:T(8,128)(2,1)}, u32[]{:S(2)}) copy-start(bf16[512,2,2048]{2,0,1:T(8,128)(2,1)} %fusion.38) | copy-start | bytes 12582916
  60.5 3.5 %dynamic-slice-start = ((f32[8192]{0:T(1024)}, s32[]{:T(128)}), f32[2048]{0:T(1024)S(1)}, s32[]{:S(2)}) async-start(f32[8192]{0:T(1024)} %param.7, s32[]{:T(128)} %select_n.44), calls=%async_computation.4 | async-start | bytes 16896 | tf_op jit(solution)/shard_map/dynamic_slice | solution.py:68
  68.7 34.2 %copy-start.4 = (bf16[32,64,512]{2,1,0:T(8,128)(2,1)S(1)}, bf16[32,64,512]{2,1,0:T(8,128)(2,1)}, u32[]{:S(2)}) copy-start(bf16[32,64,512]{2,1,0:T(8,128)(2,1)} %get-tuple-element.18) | copy-start | bytes 6291460
  102.9 1.6 %copy-start.3 = (bf16[32,64,512]{2,1,0:T(8,128)(2,1)S(1)}, bf16[32,64,512]{2,1,0:T(8,128)(2,1)}, u32[]{:S(2)}) copy-start(bf16[32,64,512]{2,1,0:T(8,128)(2,1)} %get-tuple-element.19) | copy-start | bytes 6291460

commit v4 on v3

--- a/solution.py
+++ b/solution.py
@@ -88,7 +88,7 @@
             near_rows = select_rows(near, near_ids[s])
             far_rows = select_rows(far, far_ids[s])
             pieces.append(cross_rows(near_rows, far_rows, gain))
-        cross_part = jnp.concatenate(pieces, axis=0)
+        cross_part = lax.optimization_barrier(jnp.concatenate(pieces, axis=0))
 
     with jax.named_scope("bin_sums"):
         bin_hits = (
@@ -107,7 +107,7 @@
         odd = odd[:total_bins] + odd[total_bins:]
         zero_lag = jnp.sum(bin_cross[:, :share], axis=1, keepdims=True)
         binned = jnp.concatenate(
-            [jnp.flip(even + odd, axis=1), zero_lag, (even - odd)[:, : LAGS // 2 - 1]], axis=1
+            [even + odd, zero_lag, (even - odd)[:, : LAGS // 2 - 1]], axis=1
         )
 
     with jax.named_scope("bin_exchange"):
@@ -116,6 +116,9 @@
         owned = jnp.sum(owned, axis=0).reshape(wide_count, GW, LAGS)
         owned = lax.all_to_all(owned, "wide", split_axis=0, concat_axis=0, tiled=True)
         stacked = jnp.sum(owned, axis=0)
+        stacked = jnp.concatenate(
+            [jnp.flip(stacked[:, : LAGS // 2], axis=1), stacked[:, LAGS // 2 :]], axis=1
+        )
 
     inv_root = 1.0 / freqs**0.5
     stack_scale = (GW / (steps * pair_near.shape[2])) ** 0.5

time: 145 us -> 147 us (1.014)
  other arithmetic: 13.8 us -> 49.7 us
  matrix products: 45.8 us -> 16.3 us
  local copies, waits for them, and re-layouts: 15.8 us -> 10.7 us
    concatenate x1 -> x2, other arithmetic: 1.25 us -> 36.1 us  [the longest x1 35.8 us: local(): cross_part = lax.optimization_barrier(jnp.concatenate(pieces, axis=0))]
    dot_general x1, matrix products: 34.2 us -> 2.71 us  [local(): jnp.dot(bin_hits, cross_part, preferred_element_type=jnp.float32)]
    rev x1, local copies, waits for them, and re-layouts: 5.07 us -> 0.3 us  [local(): jnp.flip(stacked[:, :LAGS // 2], axis=1)]
    reduce_sum x1, other arithmetic: 1.77 us -> 0.18 us  [local(): zero_lag = jnp.sum(bin_cross[:, :share], axis=1, keepdims=True)]
where the time goes in v4:
time: 147 us; the launch traced here: 146 us
  other arithmetic  49.7 us (34%)
  blocking collectives  34.4 us (23%)
  waiting for transfers between devices  19.6 us (13%)
  matrix products  16.3 us (11%)
  starting transfers between devices  11.7 us (8%)
  local copies, waits for them, and re-layouts  10.7 us (7%)
  between operations  4.08 us (3%)
    concatenate x1, other arithmetic, local(): cross_part = lax.optimization_barrier(jnp.concatenate(pieces, axis=0))  35.8 us
    all_to_all x1, blocking collectives, local(): lax.all_to_all(binned, 'narrow', split_axis=0, concat_axis=0, tiled=True)  17.6 us
    all_to_all x1, waiting for transfers between devices, local(): lax.all_to_all(copies, 'wide', split_axis=0, concat_axis=0, tiled=True)  14.7 us
    all_to_all x1, blocking collectives, local(): lax.all_to_all(owned, 'wide', split_axis=0, concat_axis=0, tiled=True)  11.7 us
    dot_general x4, matrix products, select_rows(): chosen = jnp.dot(picker, flat_block, preferred_element_type=jnp.bfloat16)  9.14 us
    all_to_all x1, starting transfers between devices, local(): lax.all_to_all(outgoing, 'wide', split_axis=0, concat_axis=0, tiled=True)  7.28 us
    another operation x1, other arithmetic  5.43 us
    all_gather x1, blocking collectives, local(): ids = lax.all_gather(ids, 'narrow', axis=2, tiled=True)  5.1 us
  transfers between devices with their start and end apart: 2, of which 2 were waited for; matrix products, arithmetic and copies ran while one was open for 8% of the time, Pallas kernels for 0%

profile of v4, /device:TPU:0, one launch (start us, length us, event | category | flops | bytes accessed | tf_op | source)
XLA Modules:
  0.0 146.5 jit_solution(180693663140533458)
XLA Ops:
  0.0 1.6 %copy-done = bf16[64,2,8192]{2,1,0:T(2,128)(2,1)S(1)} copy-done((bf16[64,2,8192]{2,1,0:T(2,128)(2,1)S(1)}, bf16[64,2,8192]{2,1,0:T(2,128)(2,1)}, u32[]{:S(2)}) %copy-start) | copy-done | bytes 2097176
  1.6 0.5 constant_dynamic-slice_fusion.2
  2.1 0.3 reshape.242
  2.4 0.9 copy.26
  3.4 7.3 %all-to-all-start = ((bf16[8,64,2,256]{3,1,2,0:T(8,128)(2,1)}), bf16[8,64,2,256]{3,1,2,0:T(8,128)(2,1)S(1)}, u32[]{:S(2)}, u32[]{:S(2)}) async-start(bf16[8,64,2,256]{3,1,2,0:T(8,128)(2,1)} %copy.26), calls=%async_computation | async-start | bytes 1048576 | tf_op jit(solution)/shard_map/owner_share_exchange/all_to_all | solution.py:72
  10.7 0.6 fusion.66
  15.1 5.1 %all_gather.3 = s32[3,2,512]{2,1,0:T(2,128)S(1)} all-gather(s32[3,2,128]{2,1,0:T(2,128)S(1)} %pad_add_fusion), channel_id=1, replica_groups=mesh['wide'=8,'narrow'=4] {'narrow'}, dimensions={2}, use_global_device_ids=true | all-gather | bytes 15360 | tf_op jit(solution)/shard_map/all_gather | solution.py:80
  20.2 4.9 %all-to-all-done = bf16[8,64,2,256]{3,1,2,0:T(8,128)(2,1)S(1)} async-done(((bf16[8,64,2,256]{3,1,2,0:T(8,128)(2,1)}), bf16[8,64,2,256]{3,1,2,0:T(8,128)(2,1)S(1)}, u32[]{:S(2)}, u32[]{:S(2)}) %all-to-all-start) | async-done | bytes 524320 | tf_op jit(solution)/shard_map/owner_share_exchange/all_to_all | solution.py:72
  25.3 1.8 %broadcast_in_dim.2 = bf16[8,2,64,2,256]{4,3,2,1,0:T(2,128)(2,1)} broadcast(bf16[2,64,2,256]{3,2,1,0:T(2,128)(2,1)S(1)} %copy.27), dimensions={1,2,3,4} | broadcast | bytes 1179648 | tf_op jit(solution)/shard_map/owner_share_exchange/broadcast_in_dim | solution.py:76
  27.1 4.4 %all-to-all-start.1 = ((bf16[8,2,64,2,256]{4,3,2,1,0:T(2,128)(2,1)}), bf16[8,2,64,2,256]{4,3,2,1,0:T(2,128)(2,1)}, u32[]{:S(2)}, u32[]{:S(2)}) async-start(bf16[8,2,64,2,256]{4,3,2,1,0:T(2,128)(2,1)} %broadcast_in_dim.2), calls=%async_computation.1 | async-start | bytes 2097152 | tf_op jit(solution)/shard_map/owner_share_exchange/all_to_all | solution.py:77
  31.6 0.3 fusion.60
  31.9 0.5 fusion.54
  32.4 3.3 %add_convert_fusion = (bf16[32,64,512]{2,1,0:T(8,128)(2,1)}, bf16[32,64,512]{2,1,0:T(8,128)(2,1)}) fusion(f32[64,512]{1,0:T(8,128)S(1)} %get-tuple-element.31, f32[32,512]{1,0:T(8,128)S(1)} %get-tuple-element.29, f32[64,512]{1,0:T(8,128)S(1)} %get-tuple-element.30, f32[32,512]{1,0:T(8,128)S(1)} %get-tuple-element.28), kind=kLoop, calls=%fused_computation.30 | loop fusion | flops 8388608 | bytes 4587520 | tf_op jit(solution)/shard_map/lag_product/convert_element_type | solution.py:32
  35.8 3.3 %fusion.29 = bf16[512,2,2048]{2,0,1:T(8,128)(2,1)} fusion(s32[512]{0:T(512)S(1)} %bitcast.115, bf16[8,8,2,2048]{3,2,1,0:T(2,128)(2,1)S(1)} %bitcast.99), kind=kOutput, calls=%fused_computation.47 | convolution fusion | flops 268468224 | bytes 4720640 | tf_op jit(solution)/shard_map/cross_spectra/dot_general | solution.py:42
  39.1 3.3 %fusion.31 = bf16[512,2,2048]{2,0,1:T(8,128)(2,1)} fusion(s32[512]{0:T(512)S(1)} %bitcast.114, bf16[8,8,2,2048]{3,2,1,0:T(2,128)(2,1)S(1)} %bitcast.100), kind=kOutput, calls=%fused_computation.49 | convolution fusion | flops 268468224 | bytes 4720640 | tf_op jit(solution)/shard_map/cross_spectra/dot_general | solution.py:42
  42.3 14.7 %all-to-all-done.1 = bf16[8,2,64,2,256]{4,3,2,1,0:T(2,128)(2,1)} async-done(((bf16[8,2,64,2,256]{4,3,2,1,0:T(2,128)(2,1)}), bf16[8,2,64,2,256]{4,3,2,1,0:T(2,128)(2,1)}, u32[]{:S(2)}, u32[]{:S(2)}) %all-to-all-start.1) | async-done | bytes 1048608 | tf_op jit(solution)/shard_map/owner_share_exchange/all_to_all | solution.py:77
  57.0 1.9 %slice_bitcast_fusion.1 = (bf16[64,2,8,256]{3,1,0,2:T(2,128)(2,1)S(1)}, bf16[64,2,8,256]{3,1,0,2:T(2,128)(2,1)S(1)}) fusion(bf16[8,2,64,2,256]{4,3,2,1,0:T(2,128)(2,1)} %all-to-all-done.1), kind=kLoop, calls=%fused_computation.55 | loop fusion | bytes 2097152 | tf_op jit(solution)/shard_map/cross_spectra/transpose | solution.py:87
  58.9 0.6 copy.31
  59.7 0.6 copy.28
  60.5 1.3 fusion.23
  61.8 1.3 fusion.26
  63.1 0.8 copy-done.2
  63.9 5.4 %fusion.3 = (bf16[512,2048]{1,0:T(8,128)(2,1)S(1)}, bf16[512,2048]{1,0:T(8,128)(2,1)S(1)}, bf16[512,2048]{1,0:T(8,128)(2,1)S(1)}, bf16[512,2048]{1,0:T(8,128)(2,1)S(1)}) fusion(f32[2048]{0:T(1024)S(1)} %dynamic-slice-done, bf16[512,2,2048]{2,0,1:T(8,128)(2,1)S(1)} %fusion.26, bf16[512,2,2048]{2,0,1:T(8,128)(2,1)S(1)} %copy-done.2, ...), kind=kLoop, calls=%fused_computation.14 | loop fusion | flops 29360128 | bytes 25174016 | tf_op jit(solution)/shard_map/convert.4
  69.4 35.8 %maximum_maximum_fusion = bf16[1024,4096]{1,0:T(8,128)(2,1)S(1)} fusion(bf16[512,2048]{1,0:T(8,128)(2,1)S(1)} %get-tuple-element.26, bf16[512,2048]{1,0:T(8,128)(2,1)S(1)} %get-tuple-element.27, bf16[512,2048]{1,0:T(8,128)(2,1)S(1)} %get-tuple-element.9, bf16[512,2048]{1,0:T(8,128)(2,1)S(1)} %get-tuple-element.8), kind=kLoop, calls=%fused_computation | loop fusion | flops 33554432 | bytes 16777216 | tf_op jit(solution)/shard_map/cross_spectra/concatenate | solution.py:91
  105.2 2.7 %fusion.16 = (bf16[256,4096]{1,0:T(8,128)(2,1)S(1)}, bf16[256,4096]{1,0:T(8,128)(2,1)S(1)}, f32[256,4096]{1,0:T(8,128)S(1)}) fusion(bf16[1024,4096]{1,0:T(8,128)(2,1)S(1)} %maximum_maximum_fusion, s32[1024]{0:T(1024)S(1)} %bitcast.116), kind=kOutput, calls=%fused_computation.27 | convolution fusion | flops 2151940096 | bytes 16781312 | tf_op jit(solution)/shard_map/bin_sums/dot_general | solution.py:97
  108.0 2.2 %fusion.20 = f32[512,512]{1,0:T(8,128)} fusion(bf16[2048,512]{1,0:T(8,128)(2,1)S(1)} %bitcast.106, bf16[256,4096]{1,0:T(8,128)(2,1)S(1)} %get-tuple-element.12, bf16[256,4096]{1,0:T(8,128)(2,1)S(1)} %get-tuple-element.13), kind=kOutput, calls=%fused_computation.36 | convolution fusion | flops 1077936128 | bytes 7340032 | tf_op jit(solution)/shard_map/lag_product/dot_general | solution.py:105
  110.2 2.2 %fusion.18 = f32[512,512]{1,0:T(8,128)} fusion(bf16[2048,512]{1,0:T(8,128)(2,1)S(1)} %bitcast.105, bf16[256,4096]{1,0:T(8,128)(2,1)S(1)} %get-tuple-element.13, bf16[256,4096]{1,0:T(8,128)(2,1)S(1)} %get-tuple-element.12), kind=kOutput, calls=%fused_computation.33 | convolution fusion | flops 1077936128 | bytes 7340032 | tf_op jit(solution)/shard_map/lag_product/dot_general | solution.py:104
  112.8 1.7 %fusion.63 = (f32[256,512]{1,0:T(8,128)S(1)}, f32[256,512]{1,0:T(8,128)S(1)}, f32[256,512]{1,0:T(8,128)S(1)}) fusion(f32[512,512]{1,0:T(8,128)} %fusion.18, f32[512,512]{1,0:T(8,128)} %fusion.20), kind=kLoop, calls=%fused_computation.104 | loop fusion | flops 393216 | bytes 3670016 | tf_op jit(solution)/shard_map/lag_product/add | solution.py:110
  114.9 17.6 %all_to_all.20 = f32[4,64,1024]{2,1,0:T(8,128)} all-to-all(f32[4,64,1024]{2,1,0:T(8,128)S(1)} %pad_maximum_fusion.2), channel_id=1, replica_groups=mesh['wide'=8,'narrow'=4] {'narrow'}, dimensions={0} | all-to-all | bytes 2097152 | tf_op jit(solution)/shard_map/bin_exchange/all_to_all | solution.py:115
  132.5 1.3 reduce_sum.28
  133.8 11.7 %all_to_all.21 = f32[8,8,1024]{2,1,0:T(8,128)S(1)} all-to-all(f32[8,8,1024]{2,1,0:T(8,128)S(1)} %bitcast.110), channel_id=1, replica_groups=mesh['wide'=8,'narrow'=4] {'wide'}, dimensions={0} | all-to-all | bytes 524288 | tf_op jit(solution)/shard_map/bin_exchange/all_to_all | solution.py:117
  145.9 0.6 maximum_multiply_fusion
  (36 shorter events, 1.6 us)
Async XLA Ops:
  0.0 1.6 %copy-start = (bf16[64,2,8192]{2,1,0:T(2,128)(2,1)S(1)}, bf16[64,2,8192]{2,1,0:T(2,128)(2,1)}, u32[]{:S(2)}) copy-start(bf16[64,2,8192]{2,1,0:T(2,128)(2,1)} %param.6) | copy-start | bytes 6291460
  0.0 10.7 %copy-start.5 = (s32[2]{0:T(128)S(1)}, s32[2]{0:T(128)}, u32[]{:S(2)}) copy-start(s32[2]{0:T(128)} %param.8) | copy-start | bytes 28
  0.0 15.1 %copy-start.7 = (s32[1,2,128]{2,1,0:T(2,128)S(1)}, s32[1,2,128]{2,1,0:T(2,128)}, u32[]{:S(2)}) copy-start(s32[1,2,128]{2,1,0:T(2,128)} %param.10) | copy-start | bytes 3076
  0.0 15.1 %copy-start.6 = (s32[1,2,128]{2,1,0:T(2,128)S(1)}, s32[1,2,128]{2,1,0:T(2,128)}, u32[]{:S(2)}) copy-start(s32[1,2,128]{2,1,0:T(2,128)} %param.11) | copy-start | bytes 3076
  0.0 15.1 %copy-start.8 = (s32[1,2,128]{2,1,0:T(2,128)S(1)}, s32[1,2,128]{2,1,0:T(2,128)}, u32[]{:S(2)}) copy-start(s32[1,2,128]{2,1,0:T(2,128)} %param.9) | copy-start | bytes 3076
  3.4 21.8 %all-to-all-start = ((bf16[8,64,2,256]{3,1,2,0:T(8,128)(2,1)}), bf16[8,64,2,256]{3,1,2,0:T(8,128)(2,1)S(1)}, u32[]{:S(2)}, u32[]{:S(2)}) async-start(bf16[8,64,2,256]{3,1,2,0:T(8,128)(2,1)} %copy.26), calls=%async_computation | async-start | bytes 1048576 | tf_op jit(solution)/shard_map/owner_share_exchange/all_to_all | solution.py:72
  27.1 29.9 %all-to-all-start.1 = ((bf16[8,2,64,2,256]{4,3,2,1,0:T(2,128)(2,1)}), bf16[8,2,64,2,256]{4,3,2,1,0:T(2,128)(2,1)}, u32[]{:S(2)}, u32[]{:S(2)}) async-start(bf16[8,2,64,2,256]{4,3,2,1,0:T(2,128)(2,1)} %broadcast_in_dim.2), calls=%async_computation.1 | async-start | bytes 2097152 | tf_op jit(solution)/shard_map/owner_share_exchange/all_to_all | solution.py:77
  60.4 2.6 %copy-start.1 = (bf16[512,2,2048]{2,0,1:T(8,128)(2,1)S(1)}, bf16[512,2,2048]{2,0,1:T(8,128)(2,1)}, u32[]{:S(2)}) copy-start(bf16[512,2,2048]{2,0,1:T(8,128)(2,1)} %fusion.29) | copy-start | bytes 12582916
  60.5 3.5 %copy-start.2 = (bf16[512,2,2048]{2,0,1:T(8,128)(2,1)S(1)}, bf16[512,2,2048]{2,0,1:T(8,128)(2,1)}, u32[]{:S(2)}) copy-start(bf16[512,2,2048]{2,0,1:T(8,128)(2,1)} %fusion.31) | copy-start | bytes 12582916
  60.5 3.5 %dynamic-slice-start = ((f32[8192]{0:T(1024)}, s32[]{:T(128)}), f32[2048]{0:T(1024)S(1)}, s32[]{:S(2)}) async-start(f32[8192]{0:T(1024)} %param.7, s32[]{:T(128)} %select_n.44), calls=%async_computation.4 | async-start | bytes 16896 | tf_op jit(solution)/shard_map/dynamic_slice | solution.py:68
  105.2 2.7 %copy-start.4 = (bf16[32,64,512]{2,1,0:T(8,128)(2,1)S(1)}, bf16[32,64,512]{2,1,0:T(8,128)(2,1)}, u32[]{:S(2)}) copy-start(bf16[32,64,512]{2,1,0:T(8,128)(2,1)} %get-tuple-element.18) | copy-start | bytes 6291460
  107.9 2.3 %copy-start.3 = (bf16[32,64,512]{2,1,0:T(8,128)(2,1)S(1)}, bf16[32,64,512]{2,1,0:T(8,128)(2,1)}, u32[]{:S(2)}) copy-start(bf16[32,64,512]{2,1,0:T(8,128)(2,1)} %get-tuple-element.19) | copy-start | bytes 6291460

commit v5 on v4

--- a/solution.py
+++ b/solution.py
@@ -50,7 +50,15 @@
     far_imag = far_rows[:, 1].astype(jnp.float32)
     real_part = (near_real * far_real + near_imag * far_imag) * band_gain
     imag_part = (near_imag * far_real - near_real * far_imag) * band_gain
-    return jnp.concatenate([real_part, imag_part], axis=1).astype(jnp.bfloat16)
+    return real_part.astype(jnp.bfloat16), imag_part.astype(jnp.bfloat16)
+
+
+def split_product(values, table):
+    high = lax.reduce_precision(values, exponent_bits=8, mantissa_bits=7)
+    low = values - high
+    return jnp.dot(
+        high.astype(jnp.bfloat16), table, preferred_element_type=jnp.float32
+    ) + jnp.dot(low.astype(jnp.bfloat16), table, preferred_element_type=jnp.float32)
 
 
 def local(spectra, band_gain, owners, pair_near, pair_far, stack_bins):
@@ -79,45 +87,44 @@
     ids = jnp.stack([pair_near[0], pair_far[0], stack_bins[0]])
     ids = lax.all_gather(ids, "narrow", axis=2, tiled=True)
     near_ids, far_ids = ids[0], ids[1]
-    bin_ids = ids[2].reshape(-1)
+    bin_ids = ids[2]
 
     with jax.named_scope("cross_spectra"):
-        pieces = []
+        parts = []
         for s in range(steps):
             far = gathered[:, s].transpose(1, 2, 0, 3).reshape(block_rows, 2, share)
             near_rows = select_rows(near, near_ids[s])
             far_rows = select_rows(far, far_ids[s])
-            pieces.append(cross_rows(near_rows, far_rows, gain))
-        cross_part = lax.optimization_barrier(jnp.concatenate(pieces, axis=0))
+            parts.append(lax.optimization_barrier(cross_rows(near_rows, far_rows, gain)))
 
     with jax.named_scope("bin_sums"):
-        bin_hits = (
-            jnp.arange(total_bins, dtype=jnp.int32)[:, None] == bin_ids[None, :]
-        ).astype(jnp.bfloat16)
-        bin_cross = jnp.dot(bin_hits, cross_part, preferred_element_type=jnp.float32)
-        high = lax.reduce_precision(bin_cross, exponent_bits=8, mantissa_bits=7)
-        low = bin_cross - high
-        split = jnp.concatenate([high, low], axis=0).astype(jnp.bfloat16)
+        real_sum = None
+        imag_sum = None
+        for s in range(steps):
+            bin_hits = (
+                jnp.arange(total_bins, dtype=jnp.int32)[:, None] == bin_ids[s][None, :]
+            ).astype(jnp.bfloat16)
+            real_step = jnp.dot(bin_hits, parts[s][0], preferred_element_type=jnp.float32)
+            imag_step = jnp.dot(bin_hits, parts[s][1], preferred_element_type=jnp.float32)
+            real_sum = real_step if real_sum is None else real_sum + real_step
+            imag_sum = imag_step if imag_sum is None else imag_sum + imag_step
 
     with jax.named_scope("lag_product"):
         cosine, sine = lag_halves(first_freq, share, freqs, LAGS)
-        even = jnp.dot(split[:, :share], cosine, preferred_element_type=jnp.float32)
-        odd = jnp.dot(split[:, share:], sine, preferred_element_type=jnp.float32)
-        even = even[:total_bins] + even[total_bins:]
-        odd = odd[:total_bins] + odd[total_bins:]
-        zero_lag = jnp.sum(bin_cross[:, :share], axis=1, keepdims=True)
-        binned = jnp.concatenate(
-            [even + odd, zero_lag, (even - odd)[:, : LAGS // 2 - 1]], axis=1
-        )
+        even = split_product(real_sum, cosine)
+        odd = split_product(imag_sum, sine)
+        zero_lag = jnp.sum(real_sum, axis=1, keepdims=True)
+        last = jnp.arange(LAGS // 2, dtype=jnp.int32)[None, :] == LAGS // 2 - 1
+        binned = jnp.stack([even + odd, jnp.where(last, zero_lag, even - odd)])
 
     with jax.named_scope("bin_exchange"):
-        binned = binned.reshape(narrow_count, wide_count * GW, LAGS)
-        owned = lax.all_to_all(binned, "narrow", split_axis=0, concat_axis=0, tiled=True)
-        owned = jnp.sum(owned, axis=0).reshape(wide_count, GW, LAGS)
-        owned = lax.all_to_all(owned, "wide", split_axis=0, concat_axis=0, tiled=True)
-        stacked = jnp.sum(owned, axis=0)
+        binned = binned.reshape(2, narrow_count, wide_count * GW, LAGS // 2)
+        owned = lax.all_to_all(binned, "narrow", split_axis=1, concat_axis=1, tiled=True)
+        owned = jnp.sum(owned, axis=1).reshape(2, wide_count, GW, LAGS // 2)
+        owned = lax.all_to_all(owned, "wide", split_axis=1, concat_axis=1, tiled=True)
+        plus, minus = jnp.sum(owned, axis=1)
         stacked = jnp.concatenate(
-            [jnp.flip(stacked[:, : LAGS // 2], axis=1), stacked[:, LAGS // 2 :]], axis=1
+            [jnp.flip(plus, axis=1), minus[:, LAGS // 2 - 1 :], minus[:, : LAGS // 2 - 1]], axis=1
         )
 
     inv_root = 1.0 / freqs**0.5

time: 147 us -> 109 us (0.74)
  other arithmetic: 49.7 us -> 10.7 us
  local copies, waits for them, and re-layouts: 10.7 us -> 13.2 us
    concatenate x2 -> x0, other arithmetic: 36.1 us -> none  [the longest x1 35.8 us: local(): cross_part = lax.optimization_barrier(jnp.concatenate(pieces, axis=0))]
    convert_element_type x0 -> x1, other arithmetic: none -> 5.63 us  [cross_rows(): return (real_part.astype(jnp.bfloat16), imag_part.astype(jnp.bfloat16))]
    another operation x1, other arithmetic: 5.43 us -> 0.07 us  [local(): binned = jnp.stack([even + odd, jnp.where(last, zero_lag, even - odd)])]
    all_to_all x1, waiting for transfers between devices: 4.92 us -> 10 us  [local(): lax.all_to_all(outgoing, 'wide', split_axis=0, concat_axis=0, tiled=True)]
    all_to_all x1, waiting for transfers between devices: 14.7 us -> 9.77 us  [local(): lax.all_to_all(copies, 'wide', split_axis=0, concat_axis=0, tiled=True)]
    unnamed x22, local copies, waits for them, and re-layouts: 2.78 us -> 5.41 us
    add x1 -> x0, other arithmetic: 1.74 us -> none  [local(): even + odd]
    dot_general x3 -> x8, matrix products: 7.2 us -> 5.94 us  [the longest x2 1.61 us: local(): jnp.dot(bin_hits, parts[s][0], preferred_element_type=jnp.float32)]
  transfers between devices with their start and end apart: 2 -> 2, of which waited for: 2 -> 2; matrix products, arithmetic and copies ran while one was open for 8% -> 10% of each run, Pallas kernels for 0% -> 0%
where the time goes in v5:
time: 109 us; the launch traced here: 108 us
  blocking collectives  33.9 us (31%)
  waiting for transfers between devices  19.8 us (18%)
  matrix products  15.1 us (14%)
  local copies, waits for them, and re-layouts  13.2 us (12%)
  starting transfers between devices  11.5 us (11%)
  other arithmetic  10.7 us (10%)
  between operations  4.08 us (4%)
    all_to_all x1, blocking collectives, local(): lax.all_to_all(binned, 'narrow', split_axis=1, concat_axis=1, tiled=True)  17 us
    all_to_all x1, blocking collectives, local(): lax.all_to_all(owned, 'wide', split_axis=1, concat_axis=1, tiled=True)  11.8 us
    all_to_all x1, waiting for transfers between devices, local(): lax.all_to_all(outgoing, 'wide', split_axis=0, concat_axis=0, tiled=True)  10 us
    all_to_all x1, waiting for transfers between devices, local(): lax.all_to_all(copies, 'wide', split_axis=0, concat_axis=0, tiled=True)  9.77 us
    dot_general x4, matrix products, select_rows(): chosen = jnp.dot(picker, flat_block, preferred_element_type=jnp.bfloat16)  9.14 us
    all_to_all x1, starting transfers between devices, local(): lax.all_to_all(outgoing, 'wide', split_axis=0, concat_axis=0, tiled=True)  7.28 us
    convert_element_type x1, other arithmetic, cross_rows(): return (real_part.astype(jnp.bfloat16), imag_part.astype(jnp.bfloat16))  5.63 us
    unnamed x22, local copies, waits for them, and re-layouts  5.41 us
  transfers between devices with their start and end apart: 2, of which 2 were waited for; matrix products, arithmetic and copies ran while one was open for 10% of the time, Pallas kernels for 0%

profile of v5, /device:TPU:0, one launch (start us, length us, event | category | flops | bytes accessed | tf_op | source)
XLA Modules:
  0.0 108.3 jit_solution(2294766203772576652)
XLA Ops:
  0.0 1.6 %copy-done = bf16[64,2,8192]{2,1,0:T(2,128)(2,1)S(1)} copy-done((bf16[64,2,8192]{2,1,0:T(2,128)(2,1)S(1)}, bf16[64,2,8192]{2,1,0:T(2,128)(2,1)}, u32[]{:S(2)}) %copy-start) | copy-done | bytes 2097176
  2.4 1.0 copy.29
  3.4 7.3 %all-to-all-start = ((bf16[8,64,2,256]{3,1,2,0:T(8,128)(2,1)}), bf16[8,64,2,256]{3,1,2,0:T(8,128)(2,1)S(1)}, u32[]{:S(2)}, u32[]{:S(2)}) async-start(bf16[8,64,2,256]{3,1,2,0:T(8,128)(2,1)} %copy.29), calls=%async_computation | async-start | bytes 1048576 | tf_op jit(solution)/shard_map/owner_share_exchange/all_to_all | solution.py:80
  10.7 0.6 fusion.67
  15.1 10.0 %all-to-all-done = bf16[8,64,2,256]{3,1,2,0:T(8,128)(2,1)S(1)} async-done(((bf16[8,64,2,256]{3,1,2,0:T(8,128)(2,1)}), bf16[8,64,2,256]{3,1,2,0:T(8,128)(2,1)S(1)}, u32[]{:S(2)}, u32[]{:S(2)}) %all-to-all-start) | async-done | bytes 524320 | tf_op jit(solution)/shard_map/owner_share_exchange/all_to_all | solution.py:80
  25.4 1.8 %broadcast_in_dim.12 = bf16[8,2,64,2,256]{4,3,2,1,0:T(2,128)(2,1)} broadcast(bf16[2,64,2,256]{3,2,1,0:T(2,128)(2,1)S(1)} %copy.30), dimensions={1,2,3,4} | broadcast | bytes 1179648 | tf_op jit(solution)/shard_map/owner_share_exchange/broadcast_in_dim | solution.py:84
  27.1 4.2 %all-to-all-start.1 = ((bf16[8,2,64,2,256]{4,3,2,1,0:T(2,128)(2,1)}), bf16[8,2,64,2,256]{4,3,2,1,0:T(2,128)(2,1)}, u32[]{:S(2)}, u32[]{:S(2)}) async-start(bf16[8,2,64,2,256]{4,3,2,1,0:T(2,128)(2,1)} %broadcast_in_dim.12), calls=%async_computation.1 | async-start | bytes 2097152 | tf_op jit(solution)/shard_map/owner_share_exchange/all_to_all | solution.py:85
  31.4 5.1 %all_gather.3 = s32[3,2,512]{2,1,0:T(2,128)S(1)} all-gather(s32[3,2,128]{2,1,0:T(2,128)S(1)} %pad_add_fusion), channel_id=1, replica_groups=mesh['wide'=8,'narrow'=4] {'narrow'}, dimensions={2}, use_global_device_ids=true | all-gather | bytes 15360 | tf_op jit(solution)/shard_map/all_gather | solution.py:88
  37.4 3.3 %add_convert_fusion = (bf16[32,64,512]{2,1,0:T(8,128)(2,1)}, bf16[32,64,512]{2,1,0:T(8,128)(2,1)}) fusion(f32[64,512]{1,0:T(8,128)S(1)} %get-tuple-element.38, f32[32,512]{1,0:T(8,128)S(1)} %get-tuple-element.36, f32[64,512]{1,0:T(8,128)S(1)} %get-tuple-element.37, f32[32,512]{1,0:T(8,128)S(1)} %get-tuple-element.35), kind=kLoop, calls=%fused_computation.24 | loop fusion | flops 8388608 | bytes 4587520 | tf_op jit(solution)/shard_map/lag_product/convert_element_type | solution.py:32
  40.7 3.3 %fusion.28 = bf16[512,2,2048]{2,0,1:T(8,128)(2,1)} fusion(s32[512]{0:T(512)S(1)} %bitcast.135, bf16[8,8,2,2048]{3,2,1,0:T(2,128)(2,1)S(1)} %bitcast.117), kind=kOutput, calls=%fused_computation.45 | convolution fusion | flops 268468224 | bytes 4720640 | tf_op jit(solution)/shard_map/cross_spectra/dot_general | solution.py:42
  44.0 3.3 %fusion.30 = bf16[512,2,2048]{2,0,1:T(8,128)(2,1)} fusion(s32[512]{0:T(512)S(1)} %bitcast.134, bf16[8,8,2,2048]{3,2,1,0:T(2,128)(2,1)S(1)} %bitcast.118), kind=kOutput, calls=%fused_computation.47 | convolution fusion | flops 268468224 | bytes 4720640 | tf_op jit(solution)/shard_map/cross_spectra/dot_general | solution.py:42
  47.2 9.8 %all-to-all-done.1 = bf16[8,2,64,2,256]{4,3,2,1,0:T(2,128)(2,1)} async-done(((bf16[8,2,64,2,256]{4,3,2,1,0:T(2,128)(2,1)}), bf16[8,2,64,2,256]{4,3,2,1,0:T(2,128)(2,1)}, u32[]{:S(2)}, u32[]{:S(2)}) %all-to-all-start.1) | async-done | bytes 1048608 | tf_op jit(solution)/shard_map/owner_share_exchange/all_to_all | solution.py:85
  57.0 2.0 %slice_bitcast_fusion = (bf16[64,2,8,256]{3,1,0,2:T(2,128)(2,1)S(1)}, bf16[64,2,8,256]{3,1,0,2:T(2,128)(2,1)S(1)}) fusion(bf16[8,2,64,2,256]{4,3,2,1,0:T(2,128)(2,1)} %all-to-all-done.1), kind=kLoop, calls=%fused_computation.49 | loop fusion | bytes 2097152 | tf_op jit(solution)/shard_map/cross_spectra/transpose | solution.py:95
  59.8 0.6 copy.31
  60.5 1.3 %fusion.22 = bf16[512,2,2048]{2,0,1:T(8,128)(2,1)S(1)} fusion(bf16[8,2,8,2048]{3,2,1,0:T(8,128)(2,1)S(1)} %bitcast.119, s32[512]{0:T(512)S(1)} %bitcast.133), kind=kOutput, calls=%fused_computation.39 | convolution fusion | flops 268468224 | bytes 4720640 | tf_op jit(solution)/shard_map/cross_spectra/dot_general | solution.py:42
  61.8 1.3 %fusion.25 = bf16[512,2,2048]{2,0,1:T(8,128)(2,1)S(1)} fusion(bf16[8,2,8,2048]{3,2,1,0:T(8,128)(2,1)S(1)} %bitcast.120, s32[512]{0:T(512)S(1)} %bitcast.132), kind=kOutput, calls=%fused_computation.42 | convolution fusion | flops 268468224 | bytes 4720640 | tf_op jit(solution)/shard_map/cross_spectra/dot_general | solution.py:42
  63.2 1.1 copy-done.3
  64.2 5.6 %fusion.15 = (bf16[512,2048]{1,0:T(8,128)(2,1)}, bf16[512,2048]{1,0:T(8,128)(2,1)S(1)}, bf16[512,2048]{1,0:T(8,128)(2,1)S(1)}, bf16[512,2048]{1,0:T(8,128)(2,1)S(1)}) fusion(f32[2048]{0:T(1024)S(1)} %dynamic-slice-done, bf16[512,2,2048]{2,0,1:T(8,128)(2,1)S(1)} %fusion.22, bf16[512,2,2048]{2,0,1:T(8,128)(2,1)S(1)} %copy-done.3, ...), kind=kLoop, calls=%fused_computation.23 | loop fusion | flops 29360128 | bytes 25174016 | tf_op jit(solution)/shard_map/cross_spectra/convert_element_type | solution.py:53
  69.9 0.7 fusion.33
  70.6 0.7 fusion.32
  71.3 0.8 copy-done.5
  72.2 0.8 convolution_add_fusion
  73.0 0.8 copy-done.2
  73.8 0.7 fusion.21
  74.5 0.7 convolution_add_fusion.2
  75.2 0.9 fusion.68
  76.1 0.7 copy-done.1
  76.8 0.7 fusion.20
  77.5 0.7 fusion.65
  78.3 17.0 %all_to_all.20 = f32[2,4,64,512]{3,2,0,1:T(8,128)S(1)} all-to-all(f32[2,4,64,512]{3,2,0,1:T(8,128)S(1)} %pad_maximum_fusion), channel_id=1, replica_groups=mesh['wide'=8,'narrow'=4] {'narrow'}, dimensions={1} | all-to-all | bytes 2097152 | tf_op jit(solution)/shard_map/bin_exchange/all_to_all | solution.py:122
  95.5 11.8 %all_to_all.21 = f32[2,8,8,512]{3,2,0,1:T(8,128)S(1)} all-to-all(f32[2,8,8,512]{3,2,0,1:T(8,128)S(1)} %copy.38), channel_id=1, replica_groups=mesh['wide'=8,'narrow'=4] {'wide'}, dimensions={1} | all-to-all | bytes 524288 | tf_op jit(solution)/shard_map/bin_exchange/all_to_all | solution.py:124
  107.6 0.7 maximum_multiply_fusion
  (40 shorter events, 3.4 us)
Async XLA Ops:
  0.0 1.6 %copy-start = (bf16[64,2,8192]{2,1,0:T(2,128)(2,1)S(1)}, bf16[64,2,8192]{2,1,0:T(2,128)(2,1)}, u32[]{:S(2)}) copy-start(bf16[64,2,8192]{2,1,0:T(2,128)(2,1)} %param.6) | copy-start | bytes 6291460
  1.6 9.1 %copy-start.6 = (s32[2]{0:T(128)S(1)}, s32[2]{0:T(128)}, u32[]{:S(2)}) copy-start(s32[2]{0:T(128)} %param.8) | copy-start | bytes 28
  1.6 13.5 %copy-start.7 = (s32[1,2,128]{2,1,0:T(2,128)S(1)}, s32[1,2,128]{2,1,0:T(2,128)}, u32[]{:S(2)}) copy-start(s32[1,2,128]{2,1,0:T(2,128)} %param.11) | copy-start | bytes 3076
  1.6 13.5 %copy-start.8 = (s32[1,2,128]{2,1,0:T(2,128)S(1)}, s32[1,2,128]{2,1,0:T(2,128)}, u32[]{:S(2)}) copy-start(s32[1,2,128]{2,1,0:T(2,128)} %param.10) | copy-start | bytes 3076
  1.6 13.5 %copy-start.9 = (s32[1,2,128]{2,1,0:T(2,128)S(1)}, s32[1,2,128]{2,1,0:T(2,128)}, u32[]{:S(2)}) copy-start(s32[1,2,128]{2,1,0:T(2,128)} %param.9) | copy-start | bytes 3076
  3.4 21.8 %all-to-all-start = ((bf16[8,64,2,256]{3,1,2,0:T(8,128)(2,1)}), bf16[8,64,2,256]{3,1,2,0:T(8,128)(2,1)S(1)}, u32[]{:S(2)}, u32[]{:S(2)}) async-start(bf16[8,64,2,256]{3,1,2,0:T(8,128)(2,1)} %copy.29), calls=%async_computation | async-start | bytes 1048576 | tf_op jit(solution)/shard_map/owner_share_exchange/all_to_all | solution.py:80
  27.1 29.9 %all-to-all-start.1 = ((bf16[8,2,64,2,256]{4,3,2,1,0:T(2,128)(2,1)}), bf16[8,2,64,2,256]{4,3,2,1,0:T(2,128)(2,1)}, u32[]{:S(2)}, u32[]{:S(2)}) async-start(bf16[8,2,64,2,256]{4,3,2,1,0:T(2,128)(2,1)} %broadcast_in_dim.12), calls=%async_computation.1 | async-start | bytes 2097152 | tf_op jit(solution)/shard_map/owner_share_exchange/all_to_all | solution.py:85
  60.5 2.6 %copy-start.4 = (bf16[512,2,2048]{2,0,1:T(8,128)(2,1)S(1)}, bf16[512,2,2048]{2,0,1:T(8,128)(2,1)}, u32[]{:S(2)}) copy-start(bf16[512,2,2048]{2,0,1:T(8,128)(2,1)} %fusion.30) | copy-start | bytes 12582916
  61.8 2.4 %copy-start.3 = (bf16[512,2,2048]{2,0,1:T(8,128)(2,1)S(1)}, bf16[512,2,2048]{2,0,1:T(8,128)(2,1)}, u32[]{:S(2)}) copy-start(bf16[512,2,2048]{2,0,1:T(8,128)(2,1)} %fusion.28) | copy-start | bytes 12582916
  61.8 2.4 %dynamic-slice-start = ((f32[8192]{0:T(1024)}, s32[]{:T(128)}), f32[2048]{0:T(1024)S(1)}, s32[]{:S(2)}) async-start(f32[8192]{0:T(1024)} %param.7, s32[]{:T(128)} %select_n.48), calls=%async_computation.4 | async-start | bytes 16896 | tf_op jit(solution)/shard_map/dynamic_slice | solution.py:76
  70.6 1.6 %copy-start.5 = (bf16[512,2048]{1,0:T(8,128)(2,1)S(1)}, bf16[512,2048]{1,0:T(8,128)(2,1)}, u32[]{:S(2)}) copy-start(bf16[512,2048]{1,0:T(8,128)(2,1)} %get-tuple-element.12) | copy-start | bytes 6291460
  72.2 1.6 %copy-start.2 = (bf16[32,64,512]{2,1,0:T(8,128)(2,1)S(1)}, bf16[32,64,512]{2,1,0:T(8,128)(2,1)}, u32[]{:S(2)}) copy-start(bf16[32,64,512]{2,1,0:T(8,128)(2,1)} %get-tuple-element.23) | copy-start | bytes 6291460
  75.2 1.6 %copy-start.1 = (bf16[32,64,512]{2,1,0:T(8,128)(2,1)S(1)}, bf16[32,64,512]{2,1,0:T(8,128)(2,1)}, u32[]{:S(2)}) copy-start(bf16[32,64,512]{2,1,0:T(8,128)(2,1)} %get-tuple-element.24) | copy-start | bytes 6291460

commit v6 on v5

--- a/solution.py
+++ b/solution.py
@@ -76,23 +76,23 @@
     gain = lax.dynamic_slice_in_dim(band_gain, first_freq, share, axis=0)
 
     with jax.named_scope("owner_share_exchange"):
-        outgoing = near.reshape(block_rows, 2, wide_count, piece).transpose(2, 0, 1, 3)
-        arrived = lax.all_to_all(outgoing, "wide", split_axis=0, concat_axis=0, tiled=True)
-        chosen = jnp.stack(
-            [lax.dynamic_index_in_dim(arrived, owners[s], 0, keepdims=False) for s in range(steps)]
-        )
-        copies = jnp.broadcast_to(chosen[None], (wide_count,) + chosen.shape)
-        gathered = lax.all_to_all(copies, "wide", split_axis=0, concat_axis=0, tiled=True)
+        outgoing = near.reshape(block_rows, 2, wide_count, piece)
+        arrived = lax.all_to_all(outgoing, "wide", split_axis=2, concat_axis=2, tiled=True)
+        gathered = []
+        for s in range(steps):
+            chosen = lax.dynamic_index_in_dim(arrived, owners[s], 2, keepdims=False)
+            copies = jnp.broadcast_to(chosen[None], (wide_count,) + chosen.shape)
+            gathered.append(lax.all_to_all(copies, "wide", split_axis=0, concat_axis=0, tiled=True))
 
-    ids = jnp.stack([pair_near[0], pair_far[0], stack_bins[0]])
-    ids = lax.all_gather(ids, "narrow", axis=2, tiled=True)
+    ids = jnp.stack([pair_near[0], pair_far[0], stack_bins[0]]).astype(jnp.float32)
+    ids = lax.all_gather(ids, "narrow", axis=2, tiled=True).astype(jnp.int32)
     near_ids, far_ids = ids[0], ids[1]
     bin_ids = ids[2]
 
     with jax.named_scope("cross_spectra"):
         parts = []
         for s in range(steps):
-            far = gathered[:, s].transpose(1, 2, 0, 3).reshape(block_rows, 2, share)
+            far = gathered[s].transpose(1, 2, 0, 3).reshape(block_rows, 2, share)
             near_rows = select_rows(near, near_ids[s])
             far_rows = select_rows(far, far_ids[s])
             parts.append(lax.optimization_barrier(cross_rows(near_rows, far_rows, gain)))

time: 109 us -> 115 us (1.055)
  starting transfers between devices: 11.5 us -> 15.1 us
  waiting for transfers between devices: 19.8 us -> 22.3 us
    all_to_all x1 -> x2, starting transfers between devices: 4.24 us -> 7.78 us  [local(): lax.all_to_all(copies, 'wide', split_axis=0, concat_axis=0, tiled=True)]
    all_to_all x1 -> x2, waiting for transfers between devices: 9.77 us -> 12.2 us  [local(): lax.all_to_all(copies, 'wide', split_axis=0, concat_axis=0, tiled=True)]
    transpose x4 -> x2, local copies, waits for them, and re-layouts: 4.06 us -> 2.17 us  [local(): far = gathered[s].transpose(1, 2, 0, 3).reshape(block_rows, 2, share)]
  transfers between devices with their start and end apart: 2 -> 3, of which waited for: 2 -> 3; matrix products, arithmetic and copies ran while one was open for 10% -> 11% of each run, Pallas kernels for 0% -> 0%
where the time goes in v6:
time: 115 us; the launch traced here: 114 us
  blocking collectives  34.5 us (30%)
  waiting for transfers between devices  22.3 us (19%)
  starting transfers between devices  15.1 us (13%)
  matrix products  15.1 us (13%)
  local copies, waits for them, and re-layouts  12.7 us (11%)
  other arithmetic  10.7 us (9%)
  between operations  4.07 us (4%)
    all_to_all x1, blocking collectives, local(): lax.all_to_all(binned, 'narrow', split_axis=1, concat_axis=1, tiled=True)  17 us
    all_to_all x1, blocking collectives, local(): lax.all_to_all(owned, 'wide', split_axis=1, concat_axis=1, tiled=True)  12.4 us
    all_to_all x2, waiting for transfers between devices, local(): lax.all_to_all(copies, 'wide', split_axis=0, concat_axis=0, tiled=True)  12.2 us
    all_to_all x1, waiting for transfers between devices, local(): lax.all_to_all(outgoing, 'wide', split_axis=2, concat_axis=2, tiled=True)  10.1 us
    dot_general x4, matrix products, select_rows(): chosen = jnp.dot(picker, flat_block, preferred_element_type=jnp.bfloat16)  9.14 us
    all_to_all x2, starting transfers between devices, local(): lax.all_to_all(copies, 'wide', split_axis=0, concat_axis=0, tiled=True)  7.78 us
    all_to_all x1, starting transfers between devices, local(): lax.all_to_all(outgoing, 'wide', split_axis=2, concat_axis=2, tiled=True)  7.28 us
    convert_element_type x1, other arithmetic, cross_rows(): return (real_part.astype(jnp.bfloat16), imag_part.astype(jnp.bfloat16))  5.64 us
  transfers between devices with their start and end apart: 3, of which 3 were waited for; matrix products, arithmetic and copies ran while one was open for 11% of the time, Pallas kernels for 0%

profile of v6, /device:TPU:0, one launch (start us, length us, event | category | flops | bytes accessed | tf_op | source)
XLA Modules:
  0.0 114.4 jit_solution(14257429152390539836)
XLA Ops:
  0.0 1.6 %copy-done = bf16[64,2,8192]{2,1,0:T(2,128)(2,1)S(1)} copy-done((bf16[64,2,8192]{2,1,0:T(2,128)(2,1)S(1)}, bf16[64,2,8192]{2,1,0:T(2,128)(2,1)}, u32[]{:S(2)}) %copy-start) | copy-done | bytes 2097176
  2.5 1.0 copy.40
  3.4 7.3 %all-to-all-start = ((bf16[64,2,8,256]{3,0,1,2:T(8,128)(2,1)}), bf16[64,2,8,256]{3,0,1,2:T(8,128)(2,1)S(1)}, u32[]{:S(2)}, u32[]{:S(2)}) async-start(bf16[64,2,8,256]{3,0,1,2:T(8,128)(2,1)} %copy.40), calls=%async_computation | async-start | bytes 1048576 | tf_op jit(solution)/shard_map/owner_share_exchange/all_to_all | solution.py:80
  15.1 10.1 %all-to-all-done = bf16[64,2,8,256]{3,0,1,2:T(8,128)(2,1)S(1)} async-done(((bf16[64,2,8,256]{3,0,1,2:T(8,128)(2,1)}), bf16[64,2,8,256]{3,0,1,2:T(8,128)(2,1)S(1)}, u32[]{:S(2)}, u32[]{:S(2)}) %all-to-all-start) | async-done | bytes 524320 | tf_op jit(solution)/shard_map/owner_share_exchange/all_to_all | solution.py:80
  25.3 1.1 broadcast_in_dim.21
  26.4 3.6 %all-to-all-start.2 = ((bf16[8,64,2,256]{3,2,1,0:T(2,128)(2,1)}), bf16[8,64,2,256]{3,2,1,0:T(2,128)(2,1)S(1)}, u32[]{:S(2)}, u32[]{:S(2)}) async-start(bf16[8,64,2,256]{3,2,1,0:T(2,128)(2,1)} %broadcast_in_dim.21), calls=%async_computation.2 | async-start | bytes 1048576 | tf_op jit(solution)/shard_map/owner_share_exchange/all_to_all | solution.py:85
  30.9 3.3 %add_convert_fusion = (bf16[32,64,512]{2,1,0:T(8,128)(2,1)}, bf16[32,64,512]{2,1,0:T(8,128)(2,1)}) fusion(f32[64,512]{1,0:T(8,128)S(1)} %get-tuple-element.36, f32[32,512]{1,0:T(8,128)S(1)} %get-tuple-element.34, f32[64,512]{1,0:T(8,128)S(1)} %get-tuple-element.35, f32[32,512]{1,0:T(8,128)S(1)} %get-tuple-element.33), kind=kLoop, calls=%fused_computation.24 | loop fusion | flops 8388608 | bytes 4587520 | tf_op jit(solution)/shard_map/lag_product/convert_element_type | solution.py:32
  34.3 10.4 %all-to-all-done.2 = bf16[8,64,2,256]{3,2,1,0:T(2,128)(2,1)S(1)} async-done(((bf16[8,64,2,256]{3,2,1,0:T(2,128)(2,1)}), bf16[8,64,2,256]{3,2,1,0:T(2,128)(2,1)S(1)}, u32[]{:S(2)}, u32[]{:S(2)}) %all-to-all-start.2) | async-done | bytes 524320 | tf_op jit(solution)/shard_map/owner_share_exchange/all_to_all | solution.py:85
  44.7 1.1 broadcast_in_dim.19
  45.7 4.1 %all-to-all-start.1 = ((bf16[8,64,2,256]{3,2,1,0:T(2,128)(2,1)}), bf16[8,64,2,256]{3,2,1,0:T(2,128)(2,1)}, u32[]{:S(2)}, u32[]{:S(2)}) async-start(bf16[8,64,2,256]{3,2,1,0:T(2,128)(2,1)} %broadcast_in_dim.19), calls=%async_computation.1 | async-start | bytes 1048576 | tf_op jit(solution)/shard_map/owner_share_exchange/all_to_all | solution.py:85
  49.9 5.1 %all_gather.3 = f32[3,2,512]{2,1,0:T(2,128)S(1)} all-gather(f32[3,2,128]{2,1,0:T(2,128)S(1)} %add_convert_fusion.1), channel_id=1, replica_groups=mesh['wide'=8,'narrow'=4] {'narrow'}, dimensions={2}, use_global_device_ids=true | all-gather | bytes 15360 | tf_op jit(solution)/shard_map/all_gather | solution.py:88
  55.0 3.3 %fusion.28 = bf16[512,2,2048]{2,0,1:T(8,128)(2,1)} fusion(s32[512]{0:T(512)S(1)} %bitcast.135, bf16[8,8,2,2048]{3,2,1,0:T(2,128)(2,1)S(1)} %bitcast.117), kind=kOutput, calls=%fused_computation.45 | convolution fusion | flops 268468224 | bytes 4720640 | tf_op jit(solution)/shard_map/cross_spectra/dot_general | solution.py:42
  58.3 3.3 %fusion.30 = bf16[512,2,2048]{2,0,1:T(8,128)(2,1)} fusion(s32[512]{0:T(512)S(1)} %bitcast.134, bf16[8,8,2,2048]{3,2,1,0:T(2,128)(2,1)S(1)} %bitcast.118), kind=kOutput, calls=%fused_computation.47 | convolution fusion | flops 268468224 | bytes 4720640 | tf_op jit(solution)/shard_map/cross_spectra/dot_general | solution.py:42
  62.3 1.9 %all-to-all-done.1 = bf16[8,64,2,256]{3,2,1,0:T(2,128)(2,1)} async-done(((bf16[8,64,2,256]{3,2,1,0:T(2,128)(2,1)}), bf16[8,64,2,256]{3,2,1,0:T(2,128)(2,1)}, u32[]{:S(2)}, u32[]{:S(2)}) %all-to-all-start.1) | async-done | bytes 524320 | tf_op jit(solution)/shard_map/owner_share_exchange/all_to_all | solution.py:85
  64.2 1.6 %copy.43 = bf16[64,2,8,256]{3,2,1,0:T(8,128)(2,1)S(1)} copy(bf16[64,2,8,256]{3,1,0,2:T(2,128)(2,1)} %bitcast.8) | data formatting | bytes 1048576 | tf_op jit(solution)/shard_map/cross_spectra/transpose | solution.py:95
  66.0 1.3 %fusion.22 = bf16[512,2,2048]{2,0,1:T(8,128)(2,1)S(1)} fusion(bf16[8,2,8,2048]{3,2,1,0:T(8,128)(2,1)S(1)} %bitcast.119, s32[512]{0:T(512)S(1)} %bitcast.133), kind=kOutput, calls=%fused_computation.39 | convolution fusion | flops 268468224 | bytes 4720640 | tf_op jit(solution)/shard_map/cross_spectra/dot_general | solution.py:42
  67.3 1.3 %fusion.25 = bf16[512,2,2048]{2,0,1:T(8,128)(2,1)S(1)} fusion(bf16[8,2,8,2048]{3,2,1,0:T(8,128)(2,1)S(1)} %bitcast.120, s32[512]{0:T(512)S(1)} %bitcast.132), kind=kOutput, calls=%fused_computation.42 | convolution fusion | flops 268468224 | bytes 4720640 | tf_op jit(solution)/shard_map/cross_spectra/dot_general | solution.py:42
  68.6 1.1 copy-done.3
  69.7 5.6 %fusion.15 = (bf16[512,2048]{1,0:T(8,128)(2,1)}, bf16[512,2048]{1,0:T(8,128)(2,1)S(1)}, bf16[512,2048]{1,0:T(8,128)(2,1)S(1)}, bf16[512,2048]{1,0:T(8,128)(2,1)S(1)}) fusion(f32[2048]{0:T(1024)S(1)} %dynamic-slice-done, bf16[512,2,2048]{2,0,1:T(8,128)(2,1)S(1)} %fusion.22, bf16[512,2,2048]{2,0,1:T(8,128)(2,1)S(1)} %copy-done.3, ...), kind=kLoop, calls=%fused_computation.23 | loop fusion | flops 29360128 | bytes 25174016 | tf_op jit(solution)/shard_map/cross_spectra/convert_element_type | solution.py:53
  75.3 0.7 fusion.33
  76.1 0.7 fusion.32
  76.8 0.8 copy-done.5
  77.7 0.8 convolution_add_fusion
  78.4 0.8 copy-done.2
  79.3 0.7 fusion.21
  80.0 0.7 convolution_add_fusion.2
  80.7 0.9 fusion.68
  81.6 0.7 copy-done.1
  82.3 0.7 fusion.20
  83.0 0.7 fusion.65
  83.8 17.0 %all_to_all.25 = f32[2,4,64,512]{3,2,0,1:T(8,128)S(1)} all-to-all(f32[2,4,64,512]{3,2,0,1:T(8,128)S(1)} %pad_maximum_fusion), channel_id=1, replica_groups=mesh['wide'=8,'narrow'=4] {'narrow'}, dimensions={1} | all-to-all | bytes 2097152 | tf_op jit(solution)/shard_map/bin_exchange/all_to_all | solution.py:122
  100.9 12.4 %all_to_all.26 = f32[2,8,8,512]{3,2,0,1:T(8,128)S(1)} all-to-all(f32[2,8,8,512]{3,2,0,1:T(8,128)S(1)} %copy.52), channel_id=1, replica_groups=mesh['wide'=8,'narrow'=4] {'wide'}, dimensions={1} | all-to-all | bytes 524288 | tf_op jit(solution)/shard_map/bin_exchange/all_to_all | solution.py:124
  (43 shorter events, 4.7 us)
Async XLA Ops:
  0.0 1.6 %copy-start = (bf16[64,2,8192]{2,1,0:T(2,128)(2,1)S(1)}, bf16[64,2,8192]{2,1,0:T(2,128)(2,1)}, u32[]{:S(2)}) copy-start(bf16[64,2,8192]{2,1,0:T(2,128)(2,1)} %param.6) | copy-start | bytes 6291460
  1.6 9.1 %copy-start.6 = (s32[2]{0:T(128)S(1)}, s32[2]{0:T(128)}, u32[]{:S(2)}) copy-start(s32[2]{0:T(128)} %param.8) | copy-start | bytes 28
  2.4 27.6 %copy-start.7 = (s32[1,2,128]{2,1,0:T(2,128)S(1)}, s32[1,2,128]{2,1,0:T(2,128)}, u32[]{:S(2)}) copy-start(s32[1,2,128]{2,1,0:T(2,128)} %param.11) | copy-start | bytes 3076
  2.4 27.6 %copy-start.8 = (s32[1,2,128]{2,1,0:T(2,128)S(1)}, s32[1,2,128]{2,1,0:T(2,128)}, u32[]{:S(2)}) copy-start(s32[1,2,128]{2,1,0:T(2,128)} %param.10) | copy-start | bytes 3076
  2.5 27.6 %copy-start.9 = (s32[1,2,128]{2,1,0:T(2,128)S(1)}, s32[1,2,128]{2,1,0:T(2,128)}, u32[]{:S(2)}) copy-start(s32[1,2,128]{2,1,0:T(2,128)} %param.9) | copy-start | bytes 3076
  3.4 21.8 %all-to-all-start = ((bf16[64,2,8,256]{3,0,1,2:T(8,128)(2,1)}), bf16[64,2,8,256]{3,0,1,2:T(8,128)(2,1)S(1)}, u32[]{:S(2)}, u32[]{:S(2)}) async-start(bf16[64,2,8,256]{3,0,1,2:T(8,128)(2,1)} %copy.40), calls=%async_computation | async-start | bytes 1048576 | tf_op jit(solution)/shard_map/owner_share_exchange/all_to_all | solution.py:80
  26.4 18.3 %all-to-all-start.2 = ((bf16[8,64,2,256]{3,2,1,0:T(2,128)(2,1)}), bf16[8,64,2,256]{3,2,1,0:T(2,128)(2,1)S(1)}, u32[]{:S(2)}, u32[]{:S(2)}) async-start(bf16[8,64,2,256]{3,2,1,0:T(2,128)(2,1)} %broadcast_in_dim.21), calls=%async_computation.2 | async-start | bytes 1048576 | tf_op jit(solution)/shard_map/owner_share_exchange/all_to_all | solution.py:85
  45.7 18.4 %all-to-all-start.1 = ((bf16[8,64,2,256]{3,2,1,0:T(2,128)(2,1)}), bf16[8,64,2,256]{3,2,1,0:T(2,128)(2,1)}, u32[]{:S(2)}, u32[]{:S(2)}) async-start(bf16[8,64,2,256]{3,2,1,0:T(2,128)(2,1)} %broadcast_in_dim.19), calls=%async_computation.1 | async-start | bytes 1048576 | tf_op jit(solution)/shard_map/owner_share_exchange/all_to_all | solution.py:85
  66.0 2.6 %copy-start.4 = (bf16[512,2,2048]{2,0,1:T(8,128)(2,1)S(1)}, bf16[512,2,2048]{2,0,1:T(8,128)(2,1)}, u32[]{:S(2)}) copy-start(bf16[512,2,2048]{2,0,1:T(8,128)(2,1)} %fusion.30) | copy-start | bytes 12582916
  67.3 2.4 %copy-start.3 = (bf16[512,2,2048]{2,0,1:T(8,128)(2,1)S(1)}, bf16[512,2,2048]{2,0,1:T(8,128)(2,1)}, u32[]{:S(2)}) copy-start(bf16[512,2,2048]{2,0,1:T(8,128)(2,1)} %fusion.28) | copy-start | bytes 12582916
  67.3 2.4 %dynamic-slice-start = ((f32[8192]{0:T(1024)}, s32[]{:T(128)}), f32[2048]{0:T(1024)S(1)}, s32[]{:S(2)}) async-start(f32[8192]{0:T(1024)} %param.7, s32[]{:T(128)} %select_n.48), calls=%async_computation.5 | async-start | bytes 16896 | tf_op jit(solution)/shard_map/dynamic_slice | solution.py:76
  76.1 1.6 %copy-start.5 = (bf16[512,2048]{1,0:T(8,128)(2,1)S(1)}, bf16[512,2048]{1,0:T(8,128)(2,1)}, u32[]{:S(2)}) copy-start(bf16[512,2048]{1,0:T(8,128)(2,1)} %get-tuple-element.12) | copy-start | bytes 6291460
  77.7 1.6 %copy-start.2 = (bf16[32,64,512]{2,1,0:T(8,128)(2,1)S(1)}, bf16[32,64,512]{2,1,0:T(8,128)(2,1)}, u32[]{:S(2)}) copy-start(bf16[32,64,512]{2,1,0:T(8,128)(2,1)} %get-tuple-element.21) | copy-start | bytes 6291460
  80.7 1.6 %copy-start.1 = (bf16[32,64,512]{2,1,0:T(8,128)(2,1)S(1)}, bf16[32,64,512]{2,1,0:T(8,128)(2,1)}, u32[]{:S(2)}) copy-start(bf16[32,64,512]{2,1,0:T(8,128)(2,1)} %get-tuple-element.22) | copy-start | bytes 6291460

commit v7 on v5

--- a/solution.py
+++ b/solution.py
@@ -61,6 +61,21 @@
     ) + jnp.dot(low.astype(jnp.bfloat16), table, preferred_element_type=jnp.float32)
 
 
+def halving_sum(parts, axis, count):
+    index = lax.axis_index(axis)
+    bit = 1
+    while bit < count:
+        mine = (index // bit) % 2
+        paired = parts.reshape((parts.shape[0], parts.shape[1] // 2, 2) + parts.shape[2:])
+        first, second = paired[:, :, 0], paired[:, :, 1]
+        keep = jnp.where(mine == 0, first, second)
+        send = jnp.where(mine == 0, second, first)
+        pairs = [(i, i ^ bit) for i in range(count)]
+        parts = keep + lax.ppermute(send, axis, pairs)
+        bit *= 2
+    return parts[:, 0]
+
+
 def local(spectra, band_gain, owners, pair_near, pair_far, stack_bins):
     narrow_count = lax.axis_size("narrow")
     wide_count = lax.axis_size("wide")
@@ -119,8 +134,8 @@
 
     with jax.named_scope("bin_exchange"):
         binned = binned.reshape(2, narrow_count, wide_count * GW, LAGS // 2)
-        owned = lax.all_to_all(binned, "narrow", split_axis=1, concat_axis=1, tiled=True)
-        owned = jnp.sum(owned, axis=1).reshape(2, wide_count, GW, LAGS // 2)
+        owned = halving_sum(binned, "narrow", narrow_count)
+        owned = owned.reshape(2, wide_count, GW, LAGS // 2)
         owned = lax.all_to_all(owned, "wide", split_axis=1, concat_axis=1, tiled=True)
         plus, minus = jnp.sum(owned, axis=1)
         stacked = jnp.concatenate(

time: 109 us -> 105 us (0.963)
  blocking collectives: 33.9 us -> 16.9 us
  waiting for transfers between devices: 19.8 us -> 28.7 us
  other arithmetic: 10.7 us -> 12.8 us
  starting transfers between devices: 11.5 us -> 13.1 us
    all_to_all x1 -> x0, blocking collectives: 17 us -> none  [local(): lax.all_to_all(binned, 'narrow', split_axis=1, concat_axis=1, tiled=True)]
    ppermute x0 -> x2, waiting for transfers between devices: none -> 9.11 us  [halving_sum(): parts = keep + lax.ppermute(send, axis, pairs)]
    ppermute x0 -> x2, starting transfers between devices: none -> 1.56 us  [halving_sum(): parts = keep + lax.ppermute(send, axis, pairs)]
    reshape x0 -> x1, other arithmetic: none -> 1.19 us  [halving_sum(): parts.reshape((parts.shape[0], parts.shape[1] // 2, 2) + parts.shape[2:])]
  transfers between devices with their start and end apart: 2 -> 4, of which waited for: 2 -> 4; matrix products, arithmetic and copies ran while one was open for 10% -> 11% of each run, Pallas kernels for 0% -> 0%
where the time goes in v7:
time: 105 us; the launch traced here: 104 us
  waiting for transfers between devices  28.7 us (27%)
  blocking collectives  16.9 us (16%)
  matrix products  15.1 us (14%)
  local copies, waits for them, and re-layouts  13.3 us (13%)
  starting transfers between devices  13.1 us (12%)
  other arithmetic  12.8 us (12%)
  between operations  4.21 us (4%)
    all_to_all x1, blocking collectives, local(): lax.all_to_all(owned, 'wide', split_axis=1, concat_axis=1, tiled=True)  11.8 us
    all_to_all x1, waiting for transfers between devices, local(): lax.all_to_all(outgoing, 'wide', split_axis=0, concat_axis=0, tiled=True)  9.9 us
    all_to_all x1, waiting for transfers between devices, local(): lax.all_to_all(copies, 'wide', split_axis=0, concat_axis=0, tiled=True)  9.72 us
    dot_general x4, matrix products, select_rows(): chosen = jnp.dot(picker, flat_block, preferred_element_type=jnp.bfloat16)  9.14 us
    ppermute x2, waiting for transfers between devices, halving_sum(): parts = keep + lax.ppermute(send, axis, pairs)  9.11 us
    all_to_all x1, starting transfers between devices, local(): lax.all_to_all(outgoing, 'wide', split_axis=0, concat_axis=0, tiled=True)  7.28 us
    convert_element_type x1, other arithmetic, cross_rows(): return (real_part.astype(jnp.bfloat16), imag_part.astype(jnp.bfloat16))  5.62 us
    unnamed x22, local copies, waits for them, and re-layouts  5.42 us
  transfers between devices with their start and end apart: 4, of which 4 were waited for; matrix products, arithmetic and copies ran while one was open for 11% of the time, Pallas kernels for 0%

profile of v7, /device:TPU:0, one launch (start us, length us, event | category | flops | bytes accessed | tf_op | source)
XLA Modules:
  0.0 104.1 jit_solution(17468523711169675485)
XLA Ops:
  0.0 1.6 %copy-done = bf16[64,2,8192]{2,1,0:T(2,128)(2,1)S(1)} copy-done((bf16[64,2,8192]{2,1,0:T(2,128)(2,1)S(1)}, bf16[64,2,8192]{2,1,0:T(2,128)(2,1)}, u32[]{:S(2)}) %copy-start) | copy-done | bytes 2097176
  2.4 1.0 copy.51
  3.4 7.3 %all-to-all-start = ((bf16[8,64,2,256]{3,1,2,0:T(8,128)(2,1)}), bf16[8,64,2,256]{3,1,2,0:T(8,128)(2,1)S(1)}, u32[]{:S(2)}, u32[]{:S(2)}) async-start(bf16[8,64,2,256]{3,1,2,0:T(8,128)(2,1)} %copy.51), calls=%async_computation | async-start | bytes 1048576 | tf_op jit(solution)/shard_map/owner_share_exchange/all_to_all | solution.py:95
  15.3 9.9 %all-to-all-done = bf16[8,64,2,256]{3,1,2,0:T(8,128)(2,1)S(1)} async-done(((bf16[8,64,2,256]{3,1,2,0:T(8,128)(2,1)}), bf16[8,64,2,256]{3,1,2,0:T(8,128)(2,1)S(1)}, u32[]{:S(2)}, u32[]{:S(2)}) %all-to-all-start) | async-done | bytes 524320 | tf_op jit(solution)/shard_map/owner_share_exchange/all_to_all | solution.py:95
  25.4 1.8 %broadcast_in_dim.12 = bf16[8,2,64,2,256]{4,3,2,1,0:T(2,128)(2,1)} broadcast(bf16[2,64,2,256]{3,2,1,0:T(2,128)(2,1)S(1)} %copy.52), dimensions={1,2,3,4} | broadcast | bytes 1179648 | tf_op jit(solution)/shard_map/owner_share_exchange/broadcast_in_dim | solution.py:99
  27.2 4.3 %all-to-all-start.1 = ((bf16[8,2,64,2,256]{4,3,2,1,0:T(2,128)(2,1)}), bf16[8,2,64,2,256]{4,3,2,1,0:T(2,128)(2,1)}, u32[]{:S(2)}, u32[]{:S(2)}) async-start(bf16[8,2,64,2,256]{4,3,2,1,0:T(2,128)(2,1)} %broadcast_in_dim.12), calls=%async_computation.1 | async-start | bytes 2097152 | tf_op jit(solution)/shard_map/owner_share_exchange/all_to_all | solution.py:100
  31.5 5.1 %all_gather.3 = s32[3,2,512]{2,1,0:T(2,128)S(1)} all-gather(s32[3,2,128]{2,1,0:T(2,128)S(1)} %pad_add_fusion), channel_id=1, replica_groups=mesh['wide'=8,'narrow'=4] {'narrow'}, dimensions={2}, use_global_device_ids=true | all-gather | bytes 15360 | tf_op jit(solution)/shard_map/all_gather | solution.py:103
  37.4 3.3 %add_convert_fusion = (bf16[32,64,512]{2,1,0:T(8,128)(2,1)}, bf16[32,64,512]{2,1,0:T(8,128)(2,1)}) fusion(f32[64,512]{1,0:T(8,128)S(1)} %get-tuple-element.40, f32[32,512]{1,0:T(8,128)S(1)} %get-tuple-element.38, f32[64,512]{1,0:T(8,128)S(1)} %get-tuple-element.39, f32[32,512]{1,0:T(8,128)S(1)} %get-tuple-element.37), kind=kLoop, calls=%fused_computation.24 | loop fusion | flops 8388608 | bytes 4587520 | tf_op jit(solution)/shard_map/lag_product/convert_element_type | solution.py:32
  40.8 3.2 %fusion.29 = bf16[512,2,2048]{2,0,1:T(8,128)(2,1)} fusion(s32[512]{0:T(512)S(1)} %bitcast.145, bf16[8,8,2,2048]{3,2,1,0:T(2,128)(2,1)S(1)} %bitcast.128), kind=kOutput, calls=%fused_computation.47 | convolution fusion | flops 268468224 | bytes 4720640 | tf_op jit(solution)/shard_map/cross_spectra/dot_general | solution.py:42
  44.0 3.3 %fusion.31 = bf16[512,2,2048]{2,0,1:T(8,128)(2,1)} fusion(s32[512]{0:T(512)S(1)} %bitcast.144, bf16[8,8,2,2048]{3,2,1,0:T(2,128)(2,1)S(1)} %bitcast.129), kind=kOutput, calls=%fused_computation.49 | convolution fusion | flops 268468224 | bytes 4720640 | tf_op jit(solution)/shard_map/cross_spectra/dot_general | solution.py:42
  47.3 9.7 %all-to-all-done.1 = bf16[8,2,64,2,256]{4,3,2,1,0:T(2,128)(2,1)} async-done(((bf16[8,2,64,2,256]{4,3,2,1,0:T(2,128)(2,1)}), bf16[8,2,64,2,256]{4,3,2,1,0:T(2,128)(2,1)}, u32[]{:S(2)}, u32[]{:S(2)}) %all-to-all-start.1) | async-done | bytes 1048608 | tf_op jit(solution)/shard_map/owner_share_exchange/all_to_all | solution.py:100
  57.0 2.0 %slice_bitcast_fusion = (bf16[64,2,8,256]{3,1,0,2:T(2,128)(2,1)S(1)}, bf16[64,2,8,256]{3,1,0,2:T(2,128)(2,1)S(1)}) fusion(bf16[8,2,64,2,256]{4,3,2,1,0:T(2,128)(2,1)} %all-to-all-done.1), kind=kLoop, calls=%fused_computation.52 | loop fusion | bytes 2097152 | tf_op jit(solution)/shard_map/cross_spectra/transpose | solution.py:110
  60.5 1.3 %fusion.23 = bf16[512,2,2048]{2,0,1:T(8,128)(2,1)S(1)} fusion(bf16[8,2,8,2048]{3,2,1,0:T(8,128)(2,1)S(1)} %bitcast.130, s32[512]{0:T(512)S(1)} %bitcast.143), kind=kOutput, calls=%fused_computation.41 | convolution fusion | flops 268468224 | bytes 4720640 | tf_op jit(solution)/shard_map/cross_spectra/dot_general | solution.py:42
  61.9 1.3 %fusion.26 = bf16[512,2,2048]{2,0,1:T(8,128)(2,1)S(1)} fusion(bf16[8,2,8,2048]{3,2,1,0:T(8,128)(2,1)S(1)} %bitcast.131, s32[512]{0:T(512)S(1)} %bitcast.142), kind=kOutput, calls=%fused_computation.44 | convolution fusion | flops 268468224 | bytes 4720640 | tf_op jit(solution)/shard_map/cross_spectra/dot_general | solution.py:42
  63.2 1.1 %copy-done.3 = bf16[512,2,2048]{2,0,1:T(8,128)(2,1)S(1)} copy-done((bf16[512,2,2048]{2,0,1:T(8,128)(2,1)S(1)}, bf16[512,2,2048]{2,0,1:T(8,128)(2,1)}, u32[]{:S(2)}) %copy-start.3) | copy-done | bytes 4194328
  64.3 5.6 %fusion.15 = (bf16[512,2048]{1,0:T(8,128)(2,1)}, bf16[512,2048]{1,0:T(8,128)(2,1)S(1)}, bf16[512,2048]{1,0:T(8,128)(2,1)S(1)}, bf16[512,2048]{1,0:T(8,128)(2,1)S(1)}) fusion(f32[2048]{0:T(1024)S(1)} %dynamic-slice-done, bf16[512,2,2048]{2,0,1:T(8,128)(2,1)S(1)} %fusion.23, bf16[512,2,2048]{2,0,1:T(8,128)(2,1)S(1)} %copy-done.3, ...), kind=kLoop, calls=%fused_computation.23 | loop fusion | flops 29360128 | bytes 25174016 | tf_op jit(solution)/shard_map/cross_spectra/convert_element_type | solution.py:53
  69.9 0.7 fusion.35
  70.6 0.7 fusion.34
  71.4 0.8 copy-done.5
  72.2 0.8 convolution_add_fusion
  73.0 0.8 copy-done.2
  74.5 0.7 convolution_add_fusion.2
  75.2 0.9 fusion.71
  76.1 0.7 copy-done.1
  76.8 0.7 fusion.20
  77.5 0.7 fusion.68
  78.4 0.9 select_bitcast_fusion
  79.3 2.2 %collective-permute-done = f32[2,2,64,512]{3,2,0,1:T(8,128)} collective-permute-done((f32[2,2,64,512]{3,2,0,1:T(8,128)}, f32[2,2,64,512]{3,2,0,1:T(8,128)}, u32[]{:S(2)}, u32[]{:S(2)}) %collective-permute-start) | collective-permute-done | bytes 524320 | tf_op jit(solution)/shard_map/bin_exchange/ppermute | solution.py:74
  81.5 1.2 %fusion.33 = f32[2,1,2,64,512]{4,3,0,2,1:T(8,128)S(1)} fusion(f32[2,2,64,512]{3,2,0,1:T(8,128)} %collective-permute-done, f32[2,2,1,64,512]{4,3,2,1,0:T(8,128)S(1)} %get-tuple-element.18, f32[2,2,1,64,512]{4,3,2,1,0:T(8,128)S(1)} %get-tuple-element.17, pred[]{:T(512)S(6)} %eq.117), kind=kLoop, calls=%fused_computation.55 | loop fusion | flops 262144 | bytes 2097153 | tf_op jit(solution)/shard_map/bin_exchange/reshape | solution.py:69
  82.7 1.6 %collective-permute-start.1 = (f32[2,1,64,512]{3,2,0,1:T(8,128)S(1)}, f32[2,1,64,512]{3,2,0,1:T(8,128)S(1)}, u32[]{:S(2)}, u32[]{:S(2)}) collective-permute-start(f32[2,1,64,512]{3,2,0,1:T(8,128)S(1)} %select_bitcast_fusion.1), channel_id=1, source_target_pairs={{0,2},{1,3},{2,0},{3,1},{4,6},{5,7},{6,4},{7,5},{8,10},{9,11},{10,... | collective-permute-start | bytes 786440 | tf_op jit(solution)/shard_map/bin_exchange/ppermute | solution.py:74
  84.3 6.9 %collective-permute-done.1 = f32[2,1,64,512]{3,2,0,1:T(8,128)S(1)} collective-permute-done((f32[2,1,64,512]{3,2,0,1:T(8,128)S(1)}, f32[2,1,64,512]{3,2,0,1:T(8,128)S(1)}, u32[]{:S(2)}, u32[]{:S(2)}) %collective-permute-start.1) | collective-permute-done | bytes 262176 | tf_op jit(solution)/shard_map/bin_exchange/ppermute | solution.py:74
  91.2 11.8 %all_to_all.15 = f32[2,8,8,512]{3,2,0,1:T(8,128)S(1)} all-to-all(f32[2,8,8,512]{3,2,0,1:T(8,128)S(1)} %copy.60), channel_id=1, replica_groups=mesh['wide'=8,'narrow'=4] {'wide'}, dimensions={1} | all-to-all | bytes 524288 | tf_op jit(solution)/shard_map/bin_exchange/all_to_all | solution.py:139
  (46 shorter events, 6.1 us)
Async XLA Ops:
  0.0 1.6 %copy-start = (bf16[64,2,8192]{2,1,0:T(2,128)(2,1)S(1)}, bf16[64,2,8192]{2,1,0:T(2,128)(2,1)}, u32[]{:S(2)}) copy-start(bf16[64,2,8192]{2,1,0:T(2,128)(2,1)} %param.6) | copy-start | bytes 6291460
  1.6 9.1 %copy-start.6 = (s32[2]{0:T(128)S(1)}, s32[2]{0:T(128)}, u32[]{:S(2)}) copy-start(s32[2]{0:T(128)} %param.8) | copy-start | bytes 28
  1.6 13.6 %copy-start.7 = (s32[1,2,128]{2,1,0:T(2,128)S(1)}, s32[1,2,128]{2,1,0:T(2,128)}, u32[]{:S(2)}) copy-start(s32[1,2,128]{2,1,0:T(2,128)} %param.11) | copy-start | bytes 3076
  1.6 13.7 %copy-start.8 = (s32[1,2,128]{2,1,0:T(2,128)S(1)}, s32[1,2,128]{2,1,0:T(2,128)}, u32[]{:S(2)}) copy-start(s32[1,2,128]{2,1,0:T(2,128)} %param.10) | copy-start | bytes 3076
  1.6 13.7 %copy-start.9 = (s32[1,2,128]{2,1,0:T(2,128)S(1)}, s32[1,2,128]{2,1,0:T(2,128)}, u32[]{:S(2)}) copy-start(s32[1,2,128]{2,1,0:T(2,128)} %param.9) | copy-start | bytes 3076
  3.4 21.8 %all-to-all-start = ((bf16[8,64,2,256]{3,1,2,0:T(8,128)(2,1)}), bf16[8,64,2,256]{3,1,2,0:T(8,128)(2,1)S(1)}, u32[]{:S(2)}, u32[]{:S(2)}) async-start(bf16[8,64,2,256]{3,1,2,0:T(8,128)(2,1)} %copy.51), calls=%async_computation | async-start | bytes 1048576 | tf_op jit(solution)/shard_map/owner_share_exchange/all_to_all | solution.py:95
  27.2 29.9 %all-to-all-start.1 = ((bf16[8,2,64,2,256]{4,3,2,1,0:T(2,128)(2,1)}), bf16[8,2,64,2,256]{4,3,2,1,0:T(2,128)(2,1)}, u32[]{:S(2)}, u32[]{:S(2)}) async-start(bf16[8,2,64,2,256]{4,3,2,1,0:T(2,128)(2,1)} %broadcast_in_dim.12), calls=%async_computation.1 | async-start | bytes 2097152 | tf_op jit(solution)/shard_map/owner_share_exchange/all_to_all | solution.py:100
  60.5 2.6 %copy-start.4 = (bf16[512,2,2048]{2,0,1:T(8,128)(2,1)S(1)}, bf16[512,2,2048]{2,0,1:T(8,128)(2,1)}, u32[]{:S(2)}) copy-start(bf16[512,2,2048]{2,0,1:T(8,128)(2,1)} %fusion.31) | copy-start | bytes 12582916
  61.9 2.4 %copy-start.3 = (bf16[512,2,2048]{2,0,1:T(8,128)(2,1)S(1)}, bf16[512,2,2048]{2,0,1:T(8,128)(2,1)}, u32[]{:S(2)}) copy-start(bf16[512,2,2048]{2,0,1:T(8,128)(2,1)} %fusion.29) | copy-start | bytes 12582916
  61.9 2.4 %dynamic-slice-start = ((f32[8192]{0:T(1024)}, s32[]{:T(128)}), f32[2048]{0:T(1024)S(1)}, s32[]{:S(2)}) async-start(f32[8192]{0:T(1024)} %param.7, s32[]{:T(128)} %select_n.120), calls=%async_computation.3 | async-start | bytes 16896 | tf_op jit(solution)/shard_map/dynamic_slice | solution.py:91
  70.6 1.6 %copy-start.5 = (bf16[512,2048]{1,0:T(8,128)(2,1)S(1)}, bf16[512,2048]{1,0:T(8,128)(2,1)}, u32[]{:S(2)}) copy-start(bf16[512,2048]{1,0:T(8,128)(2,1)} %get-tuple-element.12) | copy-start | bytes 6291460
  72.2 1.6 %copy-start.2 = (bf16[32,64,512]{2,1,0:T(8,128)(2,1)S(1)}, bf16[32,64,512]{2,1,0:T(8,128)(2,1)}, u32[]{:S(2)}) copy-start(bf16[32,64,512]{2,1,0:T(8,128)(2,1)} %get-tuple-element.25) | copy-start | bytes 6291460
  75.2 1.6 %copy-start.1 = (bf16[32,64,512]{2,1,0:T(8,128)(2,1)S(1)}, bf16[32,64,512]{2,1,0:T(8,128)(2,1)}, u32[]{:S(2)}) copy-start(bf16[32,64,512]{2,1,0:T(8,128)(2,1)} %get-tuple-element.26) | copy-start | bytes 6291460
  79.3 2.3 %collective-permute-start = (f32[2,2,64,512]{3,2,0,1:T(8,128)}, f32[2,2,64,512]{3,2,0,1:T(8,128)}, u32[]{:S(2)}, u32[]{:S(2)}) collective-permute-start(f32[2,2,64,512]{3,2,0,1:T(8,128)} %select_bitcast_fusion), channel_id=1, source_target_pairs={{0,1},{1,0},{2,3},{3,2},{4,5},{5,4},{6,7},{7,6},{8,9},{9,8},{10,11... | collective-permute-start | bytes 1572872 | tf_op jit(solution)/shard_map/bin_exchange/ppermute | solution.py:74
  82.7 8.4 %collective-permute-start.1 = (f32[2,1,64,512]{3,2,0,1:T(8,128)S(1)}, f32[2,1,64,512]{3,2,0,1:T(8,128)S(1)}, u32[]{:S(2)}, u32[]{:S(2)}) collective-permute-start(f32[2,1,64,512]{3,2,0,1:T(8,128)S(1)} %select_bitcast_fusion.1), channel_id=1, source_target_pairs={{0,2},{1,3},{2,0},{3,1},{4,6},{5,7},{6,4},{7,5},{8,10},{9,11},{10,... | collective-permute-start | bytes 786440 | tf_op jit(solution)/shard_map/bin_exchange/ppermute | solution.py:74

commit v8 on v7

--- a/solution.py
+++ b/solution.py
@@ -136,8 +136,7 @@
         binned = binned.reshape(2, narrow_count, wide_count * GW, LAGS // 2)
         owned = halving_sum(binned, "narrow", narrow_count)
         owned = owned.reshape(2, wide_count, GW, LAGS // 2)
-        owned = lax.all_to_all(owned, "wide", split_axis=1, concat_axis=1, tiled=True)
-        plus, minus = jnp.sum(owned, axis=1)
+        plus, minus = halving_sum(owned, "wide", wide_count)
         stacked = jnp.concatenate(
             [jnp.flip(plus, axis=1), minus[:, LAGS // 2 - 1 :], minus[:, : LAGS // 2 - 1]], axis=1
         )

time: 105 us -> 107 us (1.019)
  waiting for transfers between devices: 28.7 us -> 41.4 us
  blocking collectives: 16.9 us -> 5.1 us
  starting transfers between devices: 13.1 us -> 14.5 us
    ppermute x2 -> x5, waiting for transfers between devices: 9.11 us -> 21.7 us  [halving_sum(): parts = keep + lax.ppermute(send, axis, pairs)]
    all_to_all x1 -> x0, blocking collectives: 11.8 us -> none  [local(): lax.all_to_all(owned, 'wide', split_axis=1, concat_axis=1, tiled=True)]
    ppermute x2 -> x5, starting transfers between devices: 1.56 us -> 3.02 us  [halving_sum(): parts = keep + lax.ppermute(send, axis, pairs)]
    unnamed x22 -> x24, local copies, waits for them, and re-layouts: 5.42 us -> 6.22 us
  transfers between devices with their start and end apart: 4 -> 7, of which waited for: 4 -> 7; matrix products, arithmetic and copies ran while one was open for 11% -> 11% of each run, Pallas kernels for 0% -> 0%
where the time goes in v8:
time: 107 us
  waiting for transfers between devices  41.4 us (39%)
  matrix products  15.2 us (14%)
  starting transfers between devices  14.5 us (14%)
  local copies, waits for them, and re-layouts  14 us (13%)
  other arithmetic  12.2 us (11%)
  blocking collectives  5.1 us (5%)
  between operations  4.2 us (4%)
    ppermute x5, waiting for transfers between devices, halving_sum(): parts = keep + lax.ppermute(send, axis, pairs)  21.7 us
    all_to_all x1, waiting for transfers between devices, local(): lax.all_to_all(outgoing, 'wide', split_axis=0, concat_axis=0, tiled=True)  10.1 us
    all_to_all x1, waiting for transfers between devices, local(): lax.all_to_all(copies, 'wide', split_axis=0, concat_axis=0, tiled=True)  9.69 us
    dot_general x4, matrix products, select_rows(): chosen = jnp.dot(picker, flat_block, preferred_element_type=jnp.bfloat16)  9.18 us
    all_to_all x1, starting transfers between devices, local(): lax.all_to_all(outgoing, 'wide', split_axis=0, concat_axis=0, tiled=True)  7.28 us
    unnamed x24, local copies, waits for them, and re-layouts  6.22 us
    convert_element_type x1, other arithmetic, cross_rows(): return (real_part.astype(jnp.bfloat16), imag_part.astype(jnp.bfloat16))  5.62 us
    all_gather x1, blocking collectives, local(): ids = lax.all_gather(ids, 'narrow', axis=2, tiled=True)  5.1 us
  transfers between devices with their start and end apart: 7, of which 7 were waited for; matrix products, arithmetic and copies ran while one was open for 11% of the time, Pallas kernels for 0%

profile of v8, /device:TPU:0, one launch (start us, length us, event | category | flops | bytes accessed | tf_op | source)
XLA Modules:
  0.0 106.7 jit_solution(14283843495602667061)
XLA Ops:
  0.0 1.6 %copy-done = bf16[64,2,8192]{2,1,0:T(2,128)(2,1)S(1)} copy-done((bf16[64,2,8192]{2,1,0:T(2,128)(2,1)S(1)}, bf16[64,2,8192]{2,1,0:T(2,128)(2,1)}, u32[]{:S(2)}) %copy-start) | copy-done | bytes 2097176
  2.4 1.0 copy.67
  3.4 7.3 %all-to-all-start = ((bf16[8,64,2,256]{3,1,2,0:T(8,128)(2,1)}), bf16[8,64,2,256]{3,1,2,0:T(8,128)(2,1)S(1)}, u32[]{:S(2)}, u32[]{:S(2)}) async-start(bf16[8,64,2,256]{3,1,2,0:T(8,128)(2,1)} %copy.67), calls=%async_computation | async-start | bytes 1048576 | tf_op jit(solution)/shard_map/owner_share_exchange/all_to_all | solution.py:95
  15.1 10.1 %all-to-all-done = bf16[8,64,2,256]{3,1,2,0:T(8,128)(2,1)S(1)} async-done(((bf16[8,64,2,256]{3,1,2,0:T(8,128)(2,1)}), bf16[8,64,2,256]{3,1,2,0:T(8,128)(2,1)S(1)}, u32[]{:S(2)}, u32[]{:S(2)}) %all-to-all-start) | async-done | bytes 524320 | tf_op jit(solution)/shard_map/owner_share_exchange/all_to_all | solution.py:95
  25.4 1.8 %broadcast_in_dim.12 = bf16[8,2,64,2,256]{4,3,2,1,0:T(2,128)(2,1)} broadcast(bf16[2,64,2,256]{3,2,1,0:T(2,128)(2,1)S(1)} %copy.68), dimensions={1,2,3,4} | broadcast | bytes 1179648 | tf_op jit(solution)/shard_map/owner_share_exchange/broadcast_in_dim | solution.py:99
  27.2 4.2 %all-to-all-start.1 = ((bf16[8,2,64,2,256]{4,3,2,1,0:T(2,128)(2,1)}), bf16[8,2,64,2,256]{4,3,2,1,0:T(2,128)(2,1)}, u32[]{:S(2)}, u32[]{:S(2)}) async-start(bf16[8,2,64,2,256]{4,3,2,1,0:T(2,128)(2,1)} %broadcast_in_dim.12), calls=%async_computation.1 | async-start | bytes 2097152 | tf_op jit(solution)/shard_map/owner_share_exchange/all_to_all | solution.py:100
  31.4 5.1 %all_gather.3 = s32[3,2,512]{2,1,0:T(2,128)S(1)} all-gather(s32[3,2,128]{2,1,0:T(2,128)S(1)} %pad_add_fusion), channel_id=1, replica_groups=mesh['wide'=8,'narrow'=4] {'narrow'}, dimensions={2}, use_global_device_ids=true | all-gather | bytes 15360 | tf_op jit(solution)/shard_map/all_gather | solution.py:103
  37.4 3.3 %add_convert_fusion = (bf16[32,64,512]{2,1,0:T(8,128)(2,1)}, bf16[32,64,512]{2,1,0:T(8,128)(2,1)}) fusion(f32[64,512]{1,0:T(8,128)S(1)} %get-tuple-element.40, f32[32,512]{1,0:T(8,128)S(1)} %get-tuple-element.38, f32[64,512]{1,0:T(8,128)S(1)} %get-tuple-element.39, f32[32,512]{1,0:T(8,128)S(1)} %get-tuple-element.37), kind=kLoop, calls=%fused_computation.24 | loop fusion | flops 8388608 | bytes 4587520 | tf_op jit(solution)/shard_map/lag_product/convert_element_type | solution.py:32
  40.8 3.3 %fusion.29 = bf16[512,2,2048]{2,0,1:T(8,128)(2,1)} fusion(s32[512]{0:T(512)S(1)} %bitcast.207, bf16[8,8,2,2048]{3,2,1,0:T(2,128)(2,1)S(1)} %bitcast.186), kind=kOutput, calls=%fused_computation.47 | convolution fusion | flops 268468224 | bytes 4720640 | tf_op jit(solution)/shard_map/cross_spectra/dot_general | solution.py:42
  44.0 3.3 %fusion.31 = bf16[512,2,2048]{2,0,1:T(8,128)(2,1)} fusion(s32[512]{0:T(512)S(1)} %bitcast.206, bf16[8,8,2,2048]{3,2,1,0:T(2,128)(2,1)S(1)} %bitcast.187), kind=kOutput, calls=%fused_computation.49 | convolution fusion | flops 268468224 | bytes 4720640 | tf_op jit(solution)/shard_map/cross_spectra/dot_general | solution.py:42
  47.3 9.7 %all-to-all-done.1 = bf16[8,2,64,2,256]{4,3,2,1,0:T(2,128)(2,1)} async-done(((bf16[8,2,64,2,256]{4,3,2,1,0:T(2,128)(2,1)}), bf16[8,2,64,2,256]{4,3,2,1,0:T(2,128)(2,1)}, u32[]{:S(2)}, u32[]{:S(2)}) %all-to-all-start.1) | async-done | bytes 1048608 | tf_op jit(solution)/shard_map/owner_share_exchange/all_to_all | solution.py:100
  57.0 2.0 %slice_bitcast_fusion = (bf16[64,2,8,256]{3,1,0,2:T(2,128)(2,1)S(1)}, bf16[64,2,8,256]{3,1,0,2:T(2,128)(2,1)S(1)}) fusion(bf16[8,2,64,2,256]{4,3,2,1,0:T(2,128)(2,1)} %all-to-all-done.1), kind=kLoop, calls=%fused_computation.52 | loop fusion | bytes 2097152 | tf_op jit(solution)/shard_map/cross_spectra/transpose | solution.py:110
  60.5 1.3 %fusion.23 = bf16[512,2,2048]{2,0,1:T(8,128)(2,1)S(1)} fusion(bf16[8,2,8,2048]{3,2,1,0:T(8,128)(2,1)S(1)} %bitcast.190, s32[512]{0:T(512)S(1)} %bitcast.205), kind=kOutput, calls=%fused_computation.41 | convolution fusion | flops 268468224 | bytes 4720640 | tf_op jit(solution)/shard_map/cross_spectra/dot_general | solution.py:42
  61.9 1.3 %fusion.26 = bf16[512,2,2048]{2,0,1:T(8,128)(2,1)S(1)} fusion(bf16[8,2,8,2048]{3,2,1,0:T(8,128)(2,1)S(1)} %bitcast.191, s32[512]{0:T(512)S(1)} %bitcast.204), kind=kOutput, calls=%fused_computation.44 | convolution fusion | flops 268468224 | bytes 4720640 | tf_op jit(solution)/shard_map/cross_spectra/dot_general | solution.py:42
  63.2 1.1 %copy-done.3 = bf16[512,2,2048]{2,0,1:T(8,128)(2,1)S(1)} copy-done((bf16[512,2,2048]{2,0,1:T(8,128)(2,1)S(1)}, bf16[512,2,2048]{2,0,1:T(8,128)(2,1)}, u32[]{:S(2)}) %copy-start.3) | copy-done | bytes 4194328
  64.2 5.6 %fusion.15 = (bf16[512,2048]{1,0:T(8,128)(2,1)}, bf16[512,2048]{1,0:T(8,128)(2,1)S(1)}, bf16[512,2048]{1,0:T(8,128)(2,1)S(1)}, bf16[512,2048]{1,0:T(8,128)(2,1)S(1)}) fusion(f32[2048]{0:T(1024)S(1)} %dynamic-slice-done, bf16[512,2,2048]{2,0,1:T(8,128)(2,1)S(1)} %fusion.23, bf16[512,2,2048]{2,0,1:T(8,128)(2,1)S(1)} %copy-done.3, ...), kind=kLoop, calls=%fused_computation.23 | loop fusion | flops 29360128 | bytes 25174016 | tf_op jit(solution)/shard_map/cross_spectra/convert_element_type | solution.py:53
  69.9 0.7 fusion.35
  70.6 0.7 fusion.34
  71.4 0.8 copy-done.5
  72.2 0.8 convolution_add_fusion
  73.0 0.8 copy-done.2
  75.2 0.9 fusion.77
  77.5 0.7 fusion.74
  78.4 0.8 copy-done.6
  79.4 2.0 %collective-permute-done = f32[2,2,64,512]{3,2,0,1:T(8,128)} collective-permute-done((f32[2,2,64,512]{3,2,0,1:T(8,128)S(1)}, f32[2,2,64,512]{3,2,0,1:T(8,128)}, u32[]{:S(2)}, u32[]{:S(2)}) %collective-permute-start) | collective-permute-done | bytes 524320 | tf_op jit(solution)/shard_map/bin_exchange/ppermute | solution.py:74
  81.4 1.3 %fusion.33 = f32[2,1,2,64,512]{4,3,0,2,1:T(8,128)S(1)} fusion(f32[2,2,64,512]{3,2,0,1:T(8,128)} %collective-permute-done, f32[2,2,1,64,512]{4,3,2,1,0:T(8,128)} %copy-done.6, f32[2,2,1,64,512]{4,3,2,1,0:T(8,128)S(1)} %get-tuple-element.17, pred[]{:T(512)S(6)} %eq.135), kind=kLoop, calls=%fused_computation.55 | loop fusion | flops 262144 | bytes 2097153 | tf_op jit(solution)/shard_map/bin_exchange/reshape | solution.py:69
  82.8 1.5 %collective-permute-start.1 = (f32[2,1,64,512]{3,2,0,1:T(8,128)S(1)}, f32[2,1,64,512]{3,2,0,1:T(8,128)S(1)}, u32[]{:S(2)}, u32[]{:S(2)}) collective-permute-start(f32[2,1,64,512]{3,2,0,1:T(8,128)S(1)} %select_bitcast_fusion.1), channel_id=1, source_target_pairs={{0,2},{1,3},{2,0},{3,1},{4,6},{5,7},{6,4},{7,5},{8,10},{9,11},{10,... | collective-permute-start | bytes 786440 | tf_op jit(solution)/shard_map/bin_exchange/ppermute | solution.py:74
  84.3 6.9 %collective-permute-done.1 = f32[2,1,64,512]{3,2,0,1:T(8,128)S(1)} collective-permute-done((f32[2,1,64,512]{3,2,0,1:T(8,128)S(1)}, f32[2,1,64,512]{3,2,0,1:T(8,128)S(1)}, u32[]{:S(2)}, u32[]{:S(2)}) %collective-permute-start.1) | collective-permute-done | bytes 262176 | tf_op jit(solution)/shard_map/bin_exchange/ppermute | solution.py:74
  91.3 1.3 %collective-permute-start.2 = (f32[2,4,8,512]{3,2,1,0:T(8,128)S(1)}, f32[2,4,8,512]{3,2,1,0:T(8,128)S(1)}, u32[]{:S(2)}, u32[]{:S(2)}) collective-permute-start(f32[2,4,8,512]{3,2,1,0:T(8,128)S(1)} %select_bitcast_fusion.2), channel_id=1, source_target_pairs={{0,4},{4,0},{8,12},{12,8},{16,20},{20,16},{24,28},{28,24},{1,5},{5... | collective-permute-start | bytes 393224 | tf_op jit(solution)/shard_map/bin_exchange/ppermute | solution.py:74
  92.6 3.8 %collective-permute-done.2 = f32[2,4,8,512]{3,2,1,0:T(8,128)S(1)} collective-permute-done((f32[2,4,8,512]{3,2,1,0:T(8,128)S(1)}, f32[2,4,8,512]{3,2,1,0:T(8,128)S(1)}, u32[]{:S(2)}, u32[]{:S(2)}) %collective-permute-start.2) | collective-permute-done | bytes 131104 | tf_op jit(solution)/shard_map/bin_exchange/ppermute | solution.py:74
  96.5 4.2 %collective-permute-done.3 = f32[2,2,8,512]{3,2,1,0:T(8,128)S(1)} collective-permute-done((f32[2,2,8,512]{3,2,1,0:T(8,128)S(1)}, f32[2,2,8,512]{3,2,1,0:T(8,128)S(1)}, u32[]{:S(2)}, u32[]{:S(2)}) %collective-permute-start.3) | collective-permute-done | bytes 65568 | tf_op jit(solution)/shard_map/bin_exchange/ppermute | solution.py:74
  100.8 4.8 %collective-permute-done.4 = f32[2,1,8,512]{3,2,0,1:T(8,128)S(1)} collective-permute-done((f32[2,1,8,512]{3,2,0,1:T(8,128)S(1)}, f32[2,1,8,512]{3,2,0,1:T(8,128)S(1)}, u32[]{:S(2)}, u32[]{:S(2)}) %collective-permute-start.4) | collective-permute-done | bytes 32800 | tf_op jit(solution)/shard_map/bin_exchange/ppermute | solution.py:74
  (57 shorter events, 8.4 us)
Async XLA Ops:
  0.0 1.6 %copy-start = (bf16[64,2,8192]{2,1,0:T(2,128)(2,1)S(1)}, bf16[64,2,8192]{2,1,0:T(2,128)(2,1)}, u32[]{:S(2)}) copy-start(bf16[64,2,8192]{2,1,0:T(2,128)(2,1)} %param.6) | copy-start | bytes 6291460
  1.6 9.1 %copy-start.7 = (s32[2]{0:T(128)S(1)}, s32[2]{0:T(128)}, u32[]{:S(2)}) copy-start(s32[2]{0:T(128)} %param.8) | copy-start | bytes 28
  1.6 13.5 %copy-start.8 = (s32[1,2,128]{2,1,0:T(2,128)S(1)}, s32[1,2,128]{2,1,0:T(2,128)}, u32[]{:S(2)}) copy-start(s32[1,2,128]{2,1,0:T(2,128)} %param.11) | copy-start | bytes 3076
  1.6 13.5 %copy-start.9 = (s32[1,2,128]{2,1,0:T(2,128)S(1)}, s32[1,2,128]{2,1,0:T(2,128)}, u32[]{:S(2)}) copy-start(s32[1,2,128]{2,1,0:T(2,128)} %param.10) | copy-start | bytes 3076
  1.6 13.5 %copy-start.10 = (s32[1,2,128]{2,1,0:T(2,128)S(1)}, s32[1,2,128]{2,1,0:T(2,128)}, u32[]{:S(2)}) copy-start(s32[1,2,128]{2,1,0:T(2,128)} %param.9) | copy-start | bytes 3076
  3.4 21.8 %all-to-all-start = ((bf16[8,64,2,256]{3,1,2,0:T(8,128)(2,1)}), bf16[8,64,2,256]{3,1,2,0:T(8,128)(2,1)S(1)}, u32[]{:S(2)}, u32[]{:S(2)}) async-start(bf16[8,64,2,256]{3,1,2,0:T(8,128)(2,1)} %copy.67), calls=%async_computation | async-start | bytes 1048576 | tf_op jit(solution)/shard_map/owner_share_exchange/all_to_all | solution.py:95
  27.2 29.9 %all-to-all-start.1 = ((bf16[8,2,64,2,256]{4,3,2,1,0:T(2,128)(2,1)}), bf16[8,2,64,2,256]{4,3,2,1,0:T(2,128)(2,1)}, u32[]{:S(2)}, u32[]{:S(2)}) async-start(bf16[8,2,64,2,256]{4,3,2,1,0:T(2,128)(2,1)} %broadcast_in_dim.12), calls=%async_computation.1 | async-start | bytes 2097152 | tf_op jit(solution)/shard_map/owner_share_exchange/all_to_all | solution.py:100
  60.5 2.6 %copy-start.4 = (bf16[512,2,2048]{2,0,1:T(8,128)(2,1)S(1)}, bf16[512,2,2048]{2,0,1:T(8,128)(2,1)}, u32[]{:S(2)}) copy-start(bf16[512,2,2048]{2,0,1:T(8,128)(2,1)} %fusion.31) | copy-start | bytes 12582916
  61.8 2.4 %copy-start.3 = (bf16[512,2,2048]{2,0,1:T(8,128)(2,1)S(1)}, bf16[512,2,2048]{2,0,1:T(8,128)(2,1)}, u32[]{:S(2)}) copy-start(bf16[512,2,2048]{2,0,1:T(8,128)(2,1)} %fusion.29) | copy-start | bytes 12582916
  61.8 2.4 %dynamic-slice-start = ((f32[8192]{0:T(1024)}, s32[]{:T(128)}), f32[2048]{0:T(1024)S(1)}, s32[]{:S(2)}) async-start(f32[8192]{0:T(1024)} %param.7, s32[]{:T(128)} %select_n.217), calls=%async_computation.2 | async-start | bytes 16896 | tf_op jit(solution)/shard_map/dynamic_slice | solution.py:91
  70.6 1.6 %copy-start.5 = (bf16[512,2048]{1,0:T(8,128)(2,1)S(1)}, bf16[512,2048]{1,0:T(8,128)(2,1)}, u32[]{:S(2)}) copy-start(bf16[512,2048]{1,0:T(8,128)(2,1)} %get-tuple-element.12) | copy-start | bytes 6291460
  72.2 1.6 %copy-start.2 = (bf16[32,64,512]{2,1,0:T(8,128)(2,1)S(1)}, bf16[32,64,512]{2,1,0:T(8,128)(2,1)}, u32[]{:S(2)}) copy-start(bf16[32,64,512]{2,1,0:T(8,128)(2,1)} %get-tuple-element.25) | copy-start | bytes 6291460
  75.2 1.6 %copy-start.1 = (bf16[32,64,512]{2,1,0:T(8,128)(2,1)S(1)}, bf16[32,64,512]{2,1,0:T(8,128)(2,1)}, u32[]{:S(2)}) copy-start(bf16[32,64,512]{2,1,0:T(8,128)(2,1)} %get-tuple-element.26) | copy-start | bytes 6291460
  78.4 0.8 copy-start.6
  79.3 2.1 %collective-permute-start = (f32[2,2,64,512]{3,2,0,1:T(8,128)S(1)}, f32[2,2,64,512]{3,2,0,1:T(8,128)}, u32[]{:S(2)}, u32[]{:S(2)}) collective-permute-start(f32[2,2,64,512]{3,2,0,1:T(8,128)S(1)} %select_bitcast_fusion), channel_id=1, source_target_pairs={{0,1},{1,0},{2,3},{3,2},{4,5},{5,4},{6,7},{7,6},{8,9},{9,8},{10,11... | collective-permute-start | bytes 1572872 | tf_op jit(solution)/shard_map/bin_exchange/ppermute | solution.py:74
  82.8 8.4 %collective-permute-start.1 = (f32[2,1,64,512]{3,2,0,1:T(8,128)S(1)}, f32[2,1,64,512]{3,2,0,1:T(8,128)S(1)}, u32[]{:S(2)}, u32[]{:S(2)}) collective-permute-start(f32[2,1,64,512]{3,2,0,1:T(8,128)S(1)} %select_bitcast_fusion.1), channel_id=1, source_target_pairs={{0,2},{1,3},{2,0},{3,1},{4,6},{5,7},{6,4},{7,5},{8,10},{9,11},{10,... | collective-permute-start | bytes 786440 | tf_op jit(solution)/shard_map/bin_exchange/ppermute | solution.py:74
  91.3 5.0 %collective-permute-start.2 = (f32[2,4,8,512]{3,2,1,0:T(8,128)S(1)}, f32[2,4,8,512]{3,2,1,0:T(8,128)S(1)}, u32[]{:S(2)}, u32[]{:S(2)}) collective-permute-start(f32[2,4,8,512]{3,2,1,0:T(8,128)S(1)} %select_bitcast_fusion.2), channel_id=1, source_target_pairs={{0,4},{4,0},{8,12},{12,8},{16,20},{20,16},{24,28},{28,24},{1,5},{5... | collective-permute-start | bytes 393224 | tf_op jit(solution)/shard_map/bin_exchange/ppermute | solution.py:74
  96.4 4.3 %collective-permute-start.3 = (f32[2,2,8,512]{3,2,1,0:T(8,128)S(1)}, f32[2,2,8,512]{3,2,1,0:T(8,128)S(1)}, u32[]{:S(2)}, u32[]{:S(2)}) collective-permute-start(f32[2,2,8,512]{3,2,1,0:T(8,128)S(1)} %select_bitcast_fusion.3), channel_id=1, source_target_pairs={{0,8},{4,12},{8,0},{12,4},{16,24},{20,28},{24,16},{28,20},{1,9},{5... | collective-permute-start | bytes 196616 | tf_op jit(solution)/shard_map/bin_exchange/ppermute | solution.py:74
  100.7 4.9 %collective-permute-start.4 = (f32[2,1,8,512]{3,2,0,1:T(8,128)S(1)}, f32[2,1,8,512]{3,2,0,1:T(8,128)S(1)}, u32[]{:S(2)}, u32[]{:S(2)}) collective-permute-start(f32[2,1,8,512]{3,2,0,1:T(8,128)S(1)} %select_bitcast_fusion.4), channel_id=1, source_target_pairs={{0,16},{4,20},{8,24},{12,28},{16,0},{20,4},{24,8},{28,12},{1,17},{... | collective-permute-start | bytes 98312 | tf_op jit(solution)/shard_map/bin_exchange/ppermute | solution.py:74

commit v9 on v7

--- a/solution.py
+++ b/solution.py
@@ -56,9 +56,9 @@
 def split_product(values, table):
     high = lax.reduce_precision(values, exponent_bits=8, mantissa_bits=7)
     low = values - high
-    return jnp.dot(
-        high.astype(jnp.bfloat16), table, preferred_element_type=jnp.float32
-    ) + jnp.dot(low.astype(jnp.bfloat16), table, preferred_element_type=jnp.float32)
+    split = jnp.concatenate([high, low], axis=0).astype(jnp.bfloat16)
+    both = jnp.dot(split, table, preferred_element_type=jnp.float32)
+    return both[: values.shape[0]] + both[values.shape[0] :]
 
 
 def halving_sum(parts, axis, count):
@@ -97,7 +97,7 @@
             [lax.dynamic_index_in_dim(arrived, owners[s], 0, keepdims=False) for s in range(steps)]
         )
         copies = jnp.broadcast_to(chosen[None], (wide_count,) + chosen.shape)
-        gathered = lax.all_to_all(copies, "wide", split_axis=0, concat_axis=0, tiled=True)
+        gathered = lax.all_to_all(copies, "wide", split_axis=0, concat_axis=4, tiled=True)
 
     ids = jnp.stack([pair_near[0], pair_far[0], stack_bins[0]])
     ids = lax.all_gather(ids, "narrow", axis=2, tiled=True)
@@ -107,7 +107,7 @@
     with jax.named_scope("cross_spectra"):
         parts = []
         for s in range(steps):
-            far = gathered[:, s].transpose(1, 2, 0, 3).reshape(block_rows, 2, share)
+            far = gathered[0, s]
             near_rows = select_rows(near, near_ids[s])
             far_rows = select_rows(far, far_ids[s])
             parts.append(lax.optimization_barrier(cross_rows(near_rows, far_rows, gain)))

time: 105 us -> 101 us (0.962)
  local copies, waits for them, and re-layouts: 13.3 us -> 10.2 us
    transpose x3 -> x0, local copies, waits for them, and re-layouts: 3.1 us -> none  [local(): far = gathered[:, s].transpose(1, 2, 0, 3).reshape(block_rows, 2, share)]
    unnamed x22 -> x18, local copies, waits for them, and re-layouts: 5.42 us -> 3.67 us
    all_to_all x0 -> x1, local copies, waits for them, and re-layouts: none -> 1.35 us  [local(): lax.all_to_all(copies, 'wide', split_axis=0, concat_axis=4, tiled=True)]
    slice x0 -> x3, local copies, waits for them, and re-layouts: none -> 1.19 us  [local(): far = gathered[0, s]]
    dot_general x4 -> x2, matrix products: 2.83 us -> 2.5 us  [split_product(): both = jnp.dot(split, table, preferred_element_type=jnp.float32)]
where the time goes in v9:
time: 101 us
  waiting for transfers between devices  28.7 us (28%)
  blocking collectives  16.8 us (17%)
  matrix products  14.9 us (15%)
  starting transfers between devices  13.1 us (13%)
  other arithmetic  12.8 us (13%)
  local copies, waits for them, and re-layouts  10.2 us (10%)
  between operations  4.18 us (4%)
    all_to_all x1, blocking collectives, local(): lax.all_to_all(owned, 'wide', split_axis=1, concat_axis=1, tiled=True)  11.7 us
    all_to_all x1, waiting for transfers between devices, local(): lax.all_to_all(outgoing, 'wide', split_axis=0, concat_axis=0, tiled=True)  9.9 us
    all_to_all x1, waiting for transfers between devices, local(): lax.all_to_all(copies, 'wide', split_axis=0, concat_axis=4, tiled=True)  9.73 us
    dot_general x4, matrix products, select_rows(): chosen = jnp.dot(picker, flat_block, preferred_element_type=jnp.bfloat16)  9.15 us
    ppermute x2, waiting for transfers between devices, halving_sum(): parts = keep + lax.ppermute(send, axis, pairs)  9.1 us
    all_to_all x1, starting transfers between devices, local(): lax.all_to_all(outgoing, 'wide', split_axis=0, concat_axis=0, tiled=True)  7.28 us
    convert_element_type x1, other arithmetic, cross_rows(): return (real_part.astype(jnp.bfloat16), imag_part.astype(jnp.bfloat16))  5.43 us
    all_gather x1, blocking collectives, local(): ids = lax.all_gather(ids, 'narrow', axis=2, tiled=True)  5.1 us
  transfers between devices with their start and end apart: 4, of which 4 were waited for; matrix products, arithmetic and copies ran while one was open for 11% of the time, Pallas kernels for 0%

profile of v9, /device:TPU:0, one launch (start us, length us, event | category | flops | bytes accessed | tf_op | source)
XLA Modules:
  0.0 100.7 jit_solution(3957996936102016358)
XLA Ops:
  0.0 1.6 %copy-done = bf16[64,2,8192]{2,1,0:T(2,128)(2,1)S(1)} copy-done((bf16[64,2,8192]{2,1,0:T(2,128)(2,1)S(1)}, bf16[64,2,8192]{2,1,0:T(2,128)(2,1)}, u32[]{:S(2)}) %copy-start) | copy-done | bytes 2097176
  2.4 1.0 copy.68
  3.4 7.3 %all-to-all-start = ((bf16[8,64,2,256]{3,1,2,0:T(8,128)(2,1)}), bf16[8,64,2,256]{3,1,2,0:T(8,128)(2,1)S(1)}, u32[]{:S(2)}, u32[]{:S(2)}) async-start(bf16[8,64,2,256]{3,1,2,0:T(8,128)(2,1)} %copy.68), calls=%async_computation | async-start | bytes 1048576 | tf_op jit(solution)/shard_map/owner_share_exchange/all_to_all | solution.py:95
  10.7 0.6 fusion.77
  15.3 9.9 %all-to-all-done = bf16[8,64,2,256]{3,1,2,0:T(8,128)(2,1)S(1)} async-done(((bf16[8,64,2,256]{3,1,2,0:T(8,128)(2,1)}), bf16[8,64,2,256]{3,1,2,0:T(8,128)(2,1)S(1)}, u32[]{:S(2)}, u32[]{:S(2)}) %all-to-all-start) | async-done | bytes 524320 | tf_op jit(solution)/shard_map/owner_share_exchange/all_to_all | solution.py:95
  25.2 1.1 %broadcast_in_dim.12 = bf16[8,2,64,2,256]{4,2,3,1,0:T(8,128)(2,1)} broadcast(bf16[2,64,2,256]{3,1,2,0:T(8,128)(2,1)S(1)} %pad_maximum_fusion.1), dimensions={1,2,3,4} | broadcast | bytes 1179648 | tf_op jit(solution)/shard_map/owner_share_exchange/broadcast_in_dim | solution.py:99
  26.3 4.3 %all-to-all-start.1 = ((bf16[8,2,64,2,256]{4,2,3,1,0:T(8,128)(2,1)}), bf16[8,2,64,2,256]{4,2,3,1,0:T(8,128)(2,1)}, u32[]{:S(2)}, u32[]{:S(2)}) async-start(bf16[8,2,64,2,256]{4,2,3,1,0:T(8,128)(2,1)} %broadcast_in_dim.12), calls=%async_computation.1 | async-start | bytes 2097152 | tf_op jit(solution)/shard_map/owner_share_exchange/all_to_all | solution.py:100
  30.6 5.1 %all_gather.3 = s32[3,2,512]{2,1,0:T(2,128)S(1)} all-gather(s32[3,2,128]{2,1,0:T(2,128)S(1)} %pad_add_fusion), channel_id=1, replica_groups=mesh['wide'=8,'narrow'=4] {'narrow'}, dimensions={2}, use_global_device_ids=true | all-gather | bytes 15360 | tf_op jit(solution)/shard_map/all_gather | solution.py:103
  36.6 3.3 %add_convert_fusion = (bf16[32,64,512]{2,1,0:T(8,128)(2,1)}, bf16[32,64,512]{2,1,0:T(8,128)(2,1)}) fusion(f32[64,512]{1,0:T(8,128)S(1)} %get-tuple-element.45, f32[32,512]{1,0:T(8,128)S(1)} %get-tuple-element.43, f32[64,512]{1,0:T(8,128)S(1)} %get-tuple-element.44, f32[32,512]{1,0:T(8,128)S(1)} %get-tuple-element.42), kind=kLoop, calls=%fused_computation.24 | loop fusion | flops 8388608 | bytes 4587520 | tf_op jit(solution)/shard_map/lag_product/convert_element_type | solution.py:32
  39.9 3.2 %fusion.33 = bf16[512,2,2048]{2,0,1:T(8,128)(2,1)} fusion(s32[512]{0:T(512)S(1)} %bitcast.143, bf16[8,8,2,2048]{3,2,1,0:T(2,128)(2,1)S(1)} %bitcast.125), kind=kOutput, calls=%fused_computation.51 | convolution fusion | flops 268468224 | bytes 4720640 | tf_op jit(solution)/shard_map/cross_spectra/dot_general | solution.py:42
  43.2 3.3 %fusion.35 = bf16[512,2,2048]{2,0,1:T(8,128)(2,1)} fusion(s32[512]{0:T(512)S(1)} %bitcast.142, bf16[8,8,2,2048]{3,2,1,0:T(2,128)(2,1)S(1)} %bitcast.126), kind=kOutput, calls=%fused_computation.53 | convolution fusion | flops 268468224 | bytes 4720640 | tf_op jit(solution)/shard_map/cross_spectra/dot_general | solution.py:42
  46.5 9.7 %all-to-all-done.1 = bf16[8,2,64,2,256]{4,2,3,1,0:T(8,128)(2,1)} async-done(((bf16[8,2,64,2,256]{4,2,3,1,0:T(8,128)(2,1)}), bf16[8,2,64,2,256]{4,2,3,1,0:T(8,128)(2,1)}, u32[]{:S(2)}, u32[]{:S(2)}) %all-to-all-start.1) | async-done | bytes 1048608 | tf_op jit(solution)/shard_map/owner_share_exchange/all_to_all | solution.py:100
  56.2 1.3 %copy.87 = bf16[1,8,2,2,8,8,256]{6,5,1,4,3,2,0:T(8,128)(2,1)S(1)} copy(bf16[1,8,2,2,8,8,256]{6,5,4,3,2,1,0:T(8,128)(2,1)} %bitcast.45) | data formatting | bytes 2097152 | tf_op jit(solution)/shard_map/owner_share_exchange/all_to_all | solution.py:100
  57.7 0.5 copy.73
  58.8 1.3 %fusion.27 = bf16[512,2,2048]{2,0,1:T(8,128)(2,1)S(1)} fusion(s32[512]{0:T(512)S(1)} %bitcast.141, bf16[8,8,2,2048]{3,2,1,0:T(2,128)(2,1)S(1)} %bitcast.128), kind=kOutput, calls=%fused_computation.45 | convolution fusion | flops 268468224 | bytes 4720640 | tf_op jit(solution)/shard_map/cross_spectra/dot_general | solution.py:42
  60.1 1.3 %fusion.30 = bf16[512,2,2048]{2,0,1:T(8,128)(2,1)S(1)} fusion(s32[512]{0:T(512)S(1)} %bitcast.140, bf16[8,8,2,2048]{3,2,1,0:T(2,128)(2,1)S(1)} %bitcast.129), kind=kOutput, calls=%fused_computation.48 | convolution fusion | flops 268468224 | bytes 4720640 | tf_op jit(solution)/shard_map/cross_spectra/dot_general | solution.py:42
  61.4 1.1 %copy-done.1 = bf16[512,2,2048]{2,0,1:T(8,128)(2,1)S(1)} copy-done((bf16[512,2,2048]{2,0,1:T(8,128)(2,1)S(1)}, bf16[512,2,2048]{2,0,1:T(8,128)(2,1)}, u32[]{:S(2)}) %copy-start.1) | copy-done | bytes 4194328
  62.5 5.4 %fusion.15 = (bf16[512,2048]{1,0:T(8,128)(2,1)S(1)}, bf16[512,2048]{1,0:T(8,128)(2,1)S(1)}, bf16[512,2048]{1,0:T(8,128)(2,1)S(1)}, bf16[512,2048]{1,0:T(8,128)(2,1)S(1)}) fusion(f32[2048]{0:T(1024)S(1)} %dynamic-slice-done, bf16[512,2,2048]{2,0,1:T(8,128)(2,1)S(1)} %fusion.27, bf16[512,2,2048]{2,0,1:T(8,128)(2,1)S(1)} %copy-done.1, ...), kind=kLoop, calls=%fused_computation.23 | loop fusion | flops 29360128 | bytes 25174016 | tf_op jit(solution)/shard_map/cross_spectra/convert_element_type | solution.py:53
  67.9 0.7 fusion.38
  68.7 0.7 fusion.39
  69.4 0.8 reduce-precision_convert_fusion
  70.3 0.9 reduce-precision_convert_fusion.1
  71.2 0.6 copy-done.4
  71.8 1.2 %fusion.22 = f32[512,512]{1,0:T(8,128)S(1)} fusion(bf16[2048,512]{1,0:T(8,128)(2,1)S(1)} %bitcast.131, bf16[256,2048]{1,0:T(8,128)(2,1)S(1)} %get-tuple-element.20, bf16[256,2048]{1,0:T(8,128)(2,1)S(1)} %get-tuple-element.19), kind=kOutput, calls=%fused_computation.38 | convolution fusion | flops 1077936128 | bytes 5242880 | tf_op jit(solution)/shard_map/lag_product/dot_general | solution.py:60
  73.4 1.3 %fusion.18 = f32[512,512]{1,0:T(8,128)S(1)} fusion(bf16[2048,512]{1,0:T(8,128)(2,1)S(1)} %bitcast.130, bf16[256,2048]{1,0:T(8,128)(2,1)S(1)} %get-tuple-element.23, bf16[256,2048]{1,0:T(8,128)(2,1)S(1)} %get-tuple-element.21), kind=kOutput, calls=%fused_computation.34 | convolution fusion | flops 1077936128 | bytes 5242880 | tf_op jit(solution)/shard_map/lag_product/dot_general | solution.py:60
  75.0 0.9 select_bitcast_fusion
  75.9 2.2 %collective-permute-done = f32[2,2,64,512]{3,2,0,1:T(8,128)} collective-permute-done((f32[2,2,64,512]{3,2,0,1:T(8,128)}, f32[2,2,64,512]{3,2,0,1:T(8,128)}, u32[]{:S(2)}, u32[]{:S(2)}) %collective-permute-start) | collective-permute-done | bytes 524320 | tf_op jit(solution)/shard_map/bin_exchange/ppermute | solution.py:74
  78.1 1.2 %fusion.37 = f32[2,1,2,64,512]{4,3,0,2,1:T(8,128)S(1)} fusion(f32[2,2,64,512]{3,2,0,1:T(8,128)} %collective-permute-done, f32[2,2,1,64,512]{4,3,2,1,0:T(8,128)S(1)} %get-tuple-element.25, f32[2,2,1,64,512]{4,3,2,1,0:T(8,128)S(1)} %get-tuple-element.24, pred[]{:T(512)S(6)} %eq.117), kind=kLoop, calls=%fused_computation.59 | loop fusion | flops 262144 | bytes 2097153 | tf_op jit(solution)/shard_map/bin_exchange/reshape | solution.py:69
  79.4 1.6 %collective-permute-start.1 = (f32[2,1,64,512]{3,2,0,1:T(8,128)S(1)}, f32[2,1,64,512]{3,2,0,1:T(8,128)S(1)}, u32[]{:S(2)}, u32[]{:S(2)}) collective-permute-start(f32[2,1,64,512]{3,2,0,1:T(8,128)S(1)} %select_bitcast_fusion.1), channel_id=1, source_target_pairs={{0,2},{1,3},{2,0},{3,1},{4,6},{5,7},{6,4},{7,5},{8,10},{9,11},{10,... | collective-permute-start | bytes 786440 | tf_op jit(solution)/shard_map/bin_exchange/ppermute | solution.py:74
  80.9 6.8 %collective-permute-done.1 = f32[2,1,64,512]{3,2,0,1:T(8,128)S(1)} collective-permute-done((f32[2,1,64,512]{3,2,0,1:T(8,128)S(1)}, f32[2,1,64,512]{3,2,0,1:T(8,128)S(1)}, u32[]{:S(2)}, u32[]{:S(2)}) %collective-permute-start.1) | collective-permute-done | bytes 262176 | tf_op jit(solution)/shard_map/bin_exchange/ppermute | solution.py:74
  87.9 11.7 %all_to_all.28 = f32[2,8,8,512]{3,2,0,1:T(8,128)S(1)} all-to-all(f32[2,8,8,512]{3,2,0,1:T(8,128)S(1)} %copy.77), channel_id=1, replica_groups=mesh['wide'=8,'narrow'=4] {'wide'}, dimensions={1} | all-to-all | bytes 524288 | tf_op jit(solution)/shard_map/bin_exchange/all_to_all | solution.py:139
  100.0 0.7 maximum_multiply_fusion
  (41 shorter events, 3.6 us)
Async XLA Ops:
  0.0 1.6 %copy-start = (bf16[64,2,8192]{2,1,0:T(2,128)(2,1)S(1)}, bf16[64,2,8192]{2,1,0:T(2,128)(2,1)}, u32[]{:S(2)}) copy-start(bf16[64,2,8192]{2,1,0:T(2,128)(2,1)} %param.6) | copy-start | bytes 6291460
  1.6 9.1 %copy-start.5 = (s32[2]{0:T(128)S(1)}, s32[2]{0:T(128)}, u32[]{:S(2)}) copy-start(s32[2]{0:T(128)} %param.8) | copy-start | bytes 28
  1.6 13.6 %copy-start.6 = (s32[1,2,128]{2,1,0:T(2,128)S(1)}, s32[1,2,128]{2,1,0:T(2,128)}, u32[]{:S(2)}) copy-start(s32[1,2,128]{2,1,0:T(2,128)} %param.11) | copy-start | bytes 3076
  1.6 13.7 %copy-start.7 = (s32[1,2,128]{2,1,0:T(2,128)S(1)}, s32[1,2,128]{2,1,0:T(2,128)}, u32[]{:S(2)}) copy-start(s32[1,2,128]{2,1,0:T(2,128)} %param.10) | copy-start | bytes 3076
  1.6 13.7 %copy-start.8 = (s32[1,2,128]{2,1,0:T(2,128)S(1)}, s32[1,2,128]{2,1,0:T(2,128)}, u32[]{:S(2)}) copy-start(s32[1,2,128]{2,1,0:T(2,128)} %param.9) | copy-start | bytes 3076
  3.4 21.8 %all-to-all-start = ((bf16[8,64,2,256]{3,1,2,0:T(8,128)(2,1)}), bf16[8,64,2,256]{3,1,2,0:T(8,128)(2,1)S(1)}, u32[]{:S(2)}, u32[]{:S(2)}) async-start(bf16[8,64,2,256]{3,1,2,0:T(8,128)(2,1)} %copy.68), calls=%async_computation | async-start | bytes 1048576 | tf_op jit(solution)/shard_map/owner_share_exchange/all_to_all | solution.py:95
  26.3 29.9 %all-to-all-start.1 = ((bf16[8,2,64,2,256]{4,2,3,1,0:T(8,128)(2,1)}), bf16[8,2,64,2,256]{4,2,3,1,0:T(8,128)(2,1)}, u32[]{:S(2)}, u32[]{:S(2)}) async-start(bf16[8,2,64,2,256]{4,2,3,1,0:T(8,128)(2,1)} %broadcast_in_dim.12), calls=%async_computation.1 | async-start | bytes 2097152 | tf_op jit(solution)/shard_map/owner_share_exchange/all_to_all | solution.py:100
  58.8 2.7 %copy-start.2 = (bf16[512,2,2048]{2,0,1:T(8,128)(2,1)S(1)}, bf16[512,2,2048]{2,0,1:T(8,128)(2,1)}, u32[]{:S(2)}) copy-start(bf16[512,2,2048]{2,0,1:T(8,128)(2,1)} %fusion.35) | copy-start | bytes 12582916
  60.1 2.4 %copy-start.1 = (bf16[512,2,2048]{2,0,1:T(8,128)(2,1)S(1)}, bf16[512,2,2048]{2,0,1:T(8,128)(2,1)}, u32[]{:S(2)}) copy-start(bf16[512,2,2048]{2,0,1:T(8,128)(2,1)} %fusion.33) | copy-start | bytes 12582916
  60.1 2.4 %dynamic-slice-start = ((f32[8192]{0:T(1024)}, s32[]{:T(128)}), f32[2048]{0:T(1024)S(1)}, s32[]{:S(2)}) async-start(f32[8192]{0:T(1024)} %param.7, s32[]{:T(128)} %select_n.120), calls=%async_computation.3 | async-start | bytes 16896 | tf_op jit(solution)/shard_map/dynamic_slice | solution.py:91
  70.2 1.6 %copy-start.4 = (bf16[32,64,512]{2,1,0:T(8,128)(2,1)S(1)}, bf16[32,64,512]{2,1,0:T(8,128)(2,1)}, u32[]{:S(2)}) copy-start(bf16[32,64,512]{2,1,0:T(8,128)(2,1)} %get-tuple-element.30) | copy-start | bytes 6291460
  71.8 1.6 %copy-start.3 = (bf16[32,64,512]{2,1,0:T(8,128)(2,1)S(1)}, bf16[32,64,512]{2,1,0:T(8,128)(2,1)}, u32[]{:S(2)}) copy-start(bf16[32,64,512]{2,1,0:T(8,128)(2,1)} %get-tuple-element.31) | copy-start | bytes 6291460
  75.9 2.3 %collective-permute-start = (f32[2,2,64,512]{3,2,0,1:T(8,128)}, f32[2,2,64,512]{3,2,0,1:T(8,128)}, u32[]{:S(2)}, u32[]{:S(2)}) collective-permute-start(f32[2,2,64,512]{3,2,0,1:T(8,128)} %select_bitcast_fusion), channel_id=1, source_target_pairs={{0,1},{1,0},{2,3},{3,2},{4,5},{5,4},{6,7},{7,6},{8,9},{9,8},{10,11... | collective-permute-start | bytes 1572872 | tf_op jit(solution)/shard_map/bin_exchange/ppermute | solution.py:74
  79.4 8.4 %collective-permute-start.1 = (f32[2,1,64,512]{3,2,0,1:T(8,128)S(1)}, f32[2,1,64,512]{3,2,0,1:T(8,128)S(1)}, u32[]{:S(2)}, u32[]{:S(2)}) collective-permute-start(f32[2,1,64,512]{3,2,0,1:T(8,128)S(1)} %select_bitcast_fusion.1), channel_id=1, source_target_pairs={{0,2},{1,3},{2,0},{3,1},{4,6},{5,7},{6,4},{7,5},{8,10},{9,11},{10,... | collective-permute-start | bytes 786440 | tf_op jit(solution)/shard_map/bin_exchange/ppermute | solution.py:74

commit v10 on v9

--- a/solution.py
+++ b/solution.py
@@ -2,6 +2,8 @@
 import jax.numpy as jnp
 from jax import lax
 from jax.sharding import PartitionSpec as P
+from jax.experimental import pallas as pl
+from jax.experimental.pallas import tpu as pltpu
 
 LAGS = 1024
 GW = 8
@@ -76,6 +78,63 @@
     return parts[:, 0]
 
 
+def bin_cross_kernel(near_re, near_im, far_re, far_im, far_pick, gain, bin_pick, out_re, out_im):
+    step = pl.program_id(1)
+    picker = far_pick[0]
+    far_real = jnp.dot(picker, far_re[0], preferred_element_type=jnp.float32)
+    far_imag = jnp.dot(picker, far_im[0], preferred_element_type=jnp.float32)
+    near_real = near_re[0].astype(jnp.float32)
+    near_imag = near_im[0].astype(jnp.float32)
+    weight = gain[...]
+    real_part = ((near_real * far_real + near_imag * far_imag) * weight).astype(jnp.bfloat16)
+    imag_part = ((near_imag * far_real - near_real * far_imag) * weight).astype(jnp.bfloat16)
+    bins = bin_pick[0]
+    real_sum = jnp.dot(bins, real_part, preferred_element_type=jnp.float32)
+    imag_sum = jnp.dot(bins, imag_part, preferred_element_type=jnp.float32)
+
+    @pl.when(step == 0)
+    def _():
+        out_re[...] = real_sum
+        out_im[...] = imag_sum
+
+    @pl.when(step > 0)
+    def _():
+        out_re[...] += real_sum
+        out_im[...] += imag_sum
+
+
+def bin_cross(near_rows, far_blocks, far_pick, gain, bin_pick, tile):
+    steps, pairs, width = near_rows.shape
+    share = width // 2
+    block_rows = far_blocks.shape[1]
+    bins = bin_pick.shape[1]
+    tiles = share // tile
+    row_spec = lambda offset: pl.BlockSpec((1, pairs, tile), lambda t, s: (s, 0, t + offset))
+    block_spec = lambda offset: pl.BlockSpec((1, block_rows, tile), lambda t, s: (s, 0, t + offset))
+    out_spec = pl.BlockSpec((bins, tile), lambda t, s: (0, t))
+    return pl.pallas_call(
+        bin_cross_kernel,
+        grid=(tiles, steps),
+        in_specs=[
+            row_spec(0),
+            row_spec(tiles),
+            block_spec(0),
+            block_spec(tiles),
+            pl.BlockSpec((1, pairs, block_rows), lambda t, s: (s, 0, 0)),
+            pl.BlockSpec((1, tile), lambda t, s: (0, t)),
+            pl.BlockSpec((1, bins, pairs), lambda t, s: (s, 0, 0)),
+        ],
+        out_specs=[out_spec, out_spec],
+        out_shape=[jax.ShapeDtypeStruct((bins, share), jnp.float32)] * 2,
+        compiler_params=pltpu.CompilerParams(dimension_semantics=("parallel", "arbitrary")),
+        cost_estimate=pl.CostEstimate(
+            flops=2 * steps * share * (2 * pairs * block_rows + 2 * bins * pairs),
+            transcendentals=0,
+            bytes_accessed=2 * steps * pairs * width + 2 * steps * block_rows * width + 8 * bins * share,
+        ),
+    )(near_rows, near_rows, far_blocks, far_blocks, far_pick, gain, bin_pick)
+
+
 def local(spectra, band_gain, owners, pair_near, pair_far, stack_bins):
     narrow_count = lax.axis_size("narrow")
     wide_count = lax.axis_size("wide")
@@ -104,25 +163,20 @@
     near_ids, far_ids = ids[0], ids[1]
     bin_ids = ids[2]
 
-    with jax.named_scope("cross_spectra"):
-        parts = []
-        for s in range(steps):
-            far = gathered[0, s]
-            near_rows = select_rows(near, near_ids[s])
-            far_rows = select_rows(far, far_ids[s])
-            parts.append(lax.optimization_barrier(cross_rows(near_rows, far_rows, gain)))
-
-    with jax.named_scope("bin_sums"):
-        real_sum = None
-        imag_sum = None
-        for s in range(steps):
-            bin_hits = (
-                jnp.arange(total_bins, dtype=jnp.int32)[:, None] == bin_ids[s][None, :]
-            ).astype(jnp.bfloat16)
-            real_step = jnp.dot(bin_hits, parts[s][0], preferred_element_type=jnp.float32)
-            imag_step = jnp.dot(bin_hits, parts[s][1], preferred_element_type=jnp.float32)
-            real_sum = real_step if real_sum is None else real_sum + real_step
-            imag_sum = imag_step if imag_sum is None else imag_sum + imag_step
+    with jax.named_scope("near_rows"):
+        near_rows = jnp.stack(
+            [select_rows(near, near_ids[s]).reshape(near_ids.shape[1], 2 * share) for s in range(steps)]
+        )
+        rows = jnp.arange(block_rows, dtype=jnp.int32)[None, None, :]
+        far_pick = (far_ids[:, :, None] == rows).astype(jnp.bfloat16)
+        bins = jnp.arange(total_bins, dtype=jnp.int32)[None, :, None]
+        bin_pick = (bins == bin_ids[:, None, :]).astype(jnp.bfloat16)
+
+    with jax.named_scope("bin_cross"):
+        far_blocks = gathered[0].reshape(steps, block_rows, 2 * share)
+        real_sum, imag_sum = bin_cross(
+            near_rows, far_blocks, far_pick, gain.reshape(1, share), bin_pick, 512
+        )
 
     with jax.named_scope("lag_product"):
         cosine, sine = lag_halves(first_freq, share, freqs, LAGS)

time: 101 us -> 110 us (1.089)
  Pallas kernels: 0 us -> 13.8 us
  waiting for transfers between devices: 28.7 us -> 20.5 us
  other arithmetic: 12.8 us -> 18.7 us
  matrix products: 14.9 us -> 9.02 us
  local copies, waits for them, and re-layouts: 10.2 us -> 12.6 us
    pallas_call x0 -> x1, Pallas kernels: none -> 13.8 us  [bin_cross(): pl.pallas_call(bin_cross_kernel, grid=(tiles, steps), in_specs=[row_spec(...]
    another operation x0 -> x2, other arithmetic: none -> 9.54 us  [the longest x1 6.18 us: local(): jnp.stack([select_rows(near, near_ids[s]).reshape(near_ids.shape[1], 2 *...]
    all_to_all x1, waiting for transfers between devices: 9.9 us -> 1.44 us  [local(): lax.all_to_all(outgoing, 'wide', split_axis=0, concat_axis=0, tiled=True)]
    convert_element_type x1 -> x2, other arithmetic: 5.43 us -> 1.86 us  [the longest x1 0.93 us: local(): far_pick = (far_ids[:, :, None] == rows).astype(jnp.bfloat16)]
    dot_general x4 -> x0, matrix products: 3.23 us -> none  [the longest x2 1.67 us: local(): jnp.dot(bin_hits, parts[s][0], preferred_element_type=jnp.float32)]
    dot_general x4 -> x2, matrix products: 9.15 us -> 6.51 us  [select_rows(): chosen = jnp.dot(picker, flat_block, preferred_element_type=jnp.bfloat16)]
    unnamed x18 -> x17, local copies, waits for them, and re-layouts: 3.67 us -> 2.12 us
    squeeze x0 -> x1, local copies, waits for them, and re-layouts: none -> 1.31 us  [local(): far_blocks = gathered[0].reshape(steps, block_rows, 2 * share)]
  transfers between devices with their start and end apart: 4 -> 4, of which waited for: 4 -> 4; matrix products, arithmetic and copies ran while one was open for 11% -> 19% of each run, Pallas kernels for 0% -> 0%
where the time goes in v10:
time: 110 us; the launch traced here: 109 us
  waiting for transfers between devices  20.5 us (19%)
  other arithmetic  18.7 us (17%)
  blocking collectives  17.1 us (16%)
  Pallas kernels  13.8 us (13%)
  starting transfers between devices  13.4 us (12%)
  local copies, waits for them, and re-layouts  12.6 us (11%)
  matrix products  9.02 us (8%)
  between operations  3.85 us (4%)
    pallas_call x1, Pallas kernels, bin_cross(): pl.pallas_call(bin_cross_kernel, grid=(tiles, steps), in_specs=[row_spec(...  13.8 us
    all_to_all x1, blocking collectives, local(): lax.all_to_all(owned, 'wide', split_axis=1, concat_axis=1, tiled=True)  12 us
    all_to_all x1, waiting for transfers between devices, local(): lax.all_to_all(copies, 'wide', split_axis=0, concat_axis=4, tiled=True)  9.97 us
    ppermute x2, waiting for transfers between devices, halving_sum(): parts = keep + lax.ppermute(send, axis, pairs)  9.12 us
    all_to_all x1, starting transfers between devices, local(): lax.all_to_all(outgoing, 'wide', split_axis=0, concat_axis=0, tiled=True)  7.28 us
    dot_general x2, matrix products, select_rows(): chosen = jnp.dot(picker, flat_block, preferred_element_type=jnp.bfloat16)  6.51 us
    another operation x1, other arithmetic, local(): jnp.stack([select_rows(near, near_ids[s]).reshape(near_ids.shape[1], 2 *...  6.18 us
    all_gather x1, blocking collectives, local(): ids = lax.all_gather(ids, 'narrow', axis=2, tiled=True)  5.1 us
  transfers between devices with their start and end apart: 4, of which 4 were waited for; matrix products, arithmetic and copies ran while one was open for 19% of the time, Pallas kernels for 0%

profile of v10, /device:TPU:0, one launch (start us, length us, event | category | flops | bytes accessed | tf_op | source)
XLA Modules:
  0.0 109.0 jit_solution(17908406672590834911)
XLA Ops:
  0.0 1.6 %copy-done = bf16[64,2,8192]{2,1,0:T(2,128)(2,1)S(1)} copy-done((bf16[64,2,8192]{2,1,0:T(2,128)(2,1)S(1)}, bf16[64,2,8192]{2,1,0:T(2,128)(2,1)}, u32[]{:S(2)}) %copy-start) | copy-done | bytes 2097176
  1.6 0.5 constant_dynamic-slice_fusion.2
  2.5 1.0 copy.41
  3.4 7.3 %all-to-all-start = ((bf16[8,64,2,256]{3,1,2,0:T(8,128)(2,1)}), bf16[8,64,2,256]{3,1,2,0:T(8,128)(2,1)}, u32[]{:S(2)}, u32[]{:S(2)}) async-start(bf16[8,64,2,256]{3,1,2,0:T(8,128)(2,1)} %copy.41), calls=%async_computation | async-start | bytes 1048576 | tf_op jit(solution)/shard_map/owner_share_exchange/all_to_all | solution.py:154
  10.7 0.6 fusion.34
  13.9 5.1 %all_gather.3 = s32[3,2,512]{2,1,0:T(2,128)S(1)} all-gather(s32[3,2,128]{2,1,0:T(2,128)S(1)} %pad_add_fusion), channel_id=1, replica_groups=mesh['wide'=8,'narrow'=4] {'narrow'}, dimensions={2}, use_global_device_ids=true | all-gather | bytes 15360 | tf_op jit(solution)/shard_map/all_gather | solution.py:162
  20.3 3.2 %convolution_bitcast_fusion = bf16[1,512,4096]{2,1,0:T(8,128)(2,1)} fusion(bf16[64,4096]{1,0:T(8,128)(2,1)S(1)} %bitcast.55, s32[512]{0:T(512)S(1)} %bitcast.65), kind=kOutput, calls=%fused_computation.1 | convolution fusion | flops 268468224 | bytes 4720640 | tf_op jit(solution)/shard_map/near_rows/dot_general | solution.py:44
  23.9 1.4 %all-to-all-done = bf16[8,64,2,256]{3,1,2,0:T(8,128)(2,1)} async-done(((bf16[8,64,2,256]{3,1,2,0:T(8,128)(2,1)}), bf16[8,64,2,256]{3,1,2,0:T(8,128)(2,1)}, u32[]{:S(2)}, u32[]{:S(2)}) %all-to-all-start) | async-done | bytes 524320 | tf_op jit(solution)/shard_map/owner_share_exchange/all_to_all | solution.py:154
  25.3 0.9 constant_dynamic-slice_fusion.1
  26.4 1.8 %broadcast_in_dim.12 = bf16[8,2,64,2,256]{4,3,2,1,0:T(2,128)(2,1)} broadcast(bf16[2,64,2,256]{3,2,1,0:T(2,128)(2,1)S(1)} %copy.42), dimensions={1,2,3,4} | broadcast | bytes 1179648 | tf_op jit(solution)/shard_map/owner_share_exchange/broadcast_in_dim | solution.py:158
  28.1 4.6 %all-to-all-start.1 = ((bf16[8,2,64,2,256]{4,3,2,1,0:T(2,128)(2,1)}), bf16[8,2,64,2,256]{4,3,2,1,0:T(2,128)(2,1)}, u32[]{:S(2)}, u32[]{:S(2)}) async-start(bf16[8,2,64,2,256]{4,3,2,1,0:T(2,128)(2,1)} %broadcast_in_dim.12), calls=%async_computation.1 | async-start | bytes 2097152 | tf_op jit(solution)/shard_map/owner_share_exchange/all_to_all | solution.py:159
  32.7 3.3 %convolution_bitcast_fusion.1 = bf16[1,512,4096]{2,1,0:T(8,128)(2,1)} fusion(bf16[64,4096]{1,0:T(8,128)(2,1)S(1)} %bitcast.56, s32[512]{0:T(512)S(1)} %bitcast.64), kind=kOutput, calls=%fused_computation.2 | convolution fusion | flops 268468224 | bytes 4720640 | tf_op jit(solution)/shard_map/near_rows/dot_general | solution.py:44
  36.0 1.3 %dynamic_slice.16 = f32[2048]{0:T(1024)} dynamic-slice(f32[8192]{0:T(1024)} %param.7, s32[]{:T(128)S(6)} %select_n.120), dynamic_slice_sizes={2048} | dynamic-slice | bytes 16388 | tf_op jit(solution)/shard_map/dynamic_slice | solution.py:150
  37.3 0.5 fusion.28
  37.8 0.9 fusion.13.far_pick
  38.7 0.9 fusion.10.bin_pick
  39.7 3.3 %add_convert_fusion = (bf16[32,64,512]{2,1,0:T(8,128)(2,1)}, bf16[32,64,512]{2,1,0:T(8,128)(2,1)}) fusion(f32[64,512]{1,0:T(8,128)S(1)} %get-tuple-element.31, f32[32,512]{1,0:T(8,128)S(1)} %get-tuple-element.29, f32[64,512]{1,0:T(8,128)S(1)} %get-tuple-element.30, f32[32,512]{1,0:T(8,128)S(1)} %get-tuple-element.28), kind=kLoop, calls=%fused_computation.3 | loop fusion | flops 8388608 | bytes 4587520 | tf_op jit(solution)/shard_map/lag_product/convert_element_type | solution.py:34
  42.9 6.2 %pad_maximum_fusion.near_re.near_im = bf16[2,512,4096]{2,1,0:T(8,128)(2,1)} fusion(bf16[1,512,4096]{2,1,0:T(8,128)(2,1)S(1)} %copy-done.1, bf16[1,512,4096]{2,1,0:T(8,128)(2,1)} %convolution_bitcast_fusion.1), kind=kLoop, calls=%fused_computation | loop fusion | flops 4194304 | bytes 16777216 | tf_op jit(solution)/shard_map/near_rows/stack | solution.py:167
  49.1 10.0 %all-to-all-done.1 = bf16[8,2,64,2,256]{4,3,2,1,0:T(2,128)(2,1)} async-done(((bf16[8,2,64,2,256]{4,3,2,1,0:T(2,128)(2,1)}), bf16[8,2,64,2,256]{4,3,2,1,0:T(2,128)(2,1)}, u32[]{:S(2)}, u32[]{:S(2)}) %all-to-all-start.1) | async-done | bytes 1048608 | tf_op jit(solution)/shard_map/owner_share_exchange/all_to_all | solution.py:159
  59.1 2.3 %copy.43 = bf16[1,2,64,2,8,256]{5,4,3,2,1,0:T(8,128)(2,1)S(1)} copy(bf16[1,2,64,2,8,256]{5,3,2,1,4,0:T(2,128)(2,1)} %bitcast.9) | data formatting | bytes 2097152 | tf_op jit(solution)/shard_map/owner_share_exchange/all_to_all | solution.py:159
  61.4 1.3 %squeeze.24.far_re.far_im = bf16[2,64,4096]{2,1,0:T(8,128)(2,1)} reshape(bf16[1,2,64,2,8,256]{5,4,3,2,1,0:T(8,128)(2,1)S(1)} %copy.43) | data formatting | bytes 2097152 | tf_op jit(solution)/shard_map/bin_cross/reshape;bin_cross/squeeze | solution.py:176
  62.7 13.8 %bin_cross.1 = (f32[256,2048]{1,0:T(8,128)}, f32[256,2048]{1,0:T(8,128)}) custom-call(bf16[2,512,4096]{2,1,0:T(8,128)(2,1)} %pad_maximum_fusion.near_re.near_im, bf16[2,512,4096]{2,1,0:T(8,128)(2,1)} %pad_maximum_fusion.near_re.near_im, bf16[2,64,4096]{2,1,0:T(8,128)(2,1)} %squeeze.24.far_re.far_im, bf16[2,64,4096]{2,1,0:T(8,128)(2,1)} %squeeze.24.far_re.far_im, ...), custom_call_target="tpu_custom_call" | custom-call | flops 2684354560 | bytes 13631488 | tf_op jit(solution)/shard_map/bin_cross/pallas_call | solution.py:115
  76.6 3.4 %reduce-precision_convert_fusion = (bf16[256,2048]{1,0:T(8,128)(2,1)S(1)}, bf16[256,2048]{1,0:T(8,128)(2,1)S(1)}, bf16[256,2048]{1,0:T(8,128)(2,1)S(1)}, f32[256]{0:T(256)S(1)}, bf16[256,2048]{1,0:T(8,128)(2,1)S(1)}) fusion(f32[256,2048]{1,0:T(8,128)} %get-tuple-element.8, f32[256,2048]{1,0:T(8,128)} %get-tuple-element.7), kind=kLoop, calls=%fused_computation.6 | loop fusion | flops 4718336 | bytes 8389632 | tf_op jit(solution)/shard_map/convert
  80.0 1.2 %fusion.6 = f32[512,512]{1,0:T(8,128)S(1)} fusion(bf16[2048,512]{1,0:T(8,128)(2,1)S(1)} %bitcast.59, bf16[256,2048]{1,0:T(8,128)(2,1)S(1)} %get-tuple-element.12, bf16[256,2048]{1,0:T(8,128)(2,1)S(1)} %get-tuple-element.11), kind=kOutput, calls=%fused_computation.15 | convolution fusion | flops 1077936128 | bytes 5242880 | tf_op jit(solution)/shard_map/lag_product/dot_general | solution.py:62
  81.5 1.3 %fusion.2 = f32[512,512]{1,0:T(8,128)S(1)} fusion(bf16[2048,512]{1,0:T(8,128)(2,1)S(1)} %bitcast.58, bf16[256,2048]{1,0:T(8,128)(2,1)S(1)} %get-tuple-element.34, bf16[256,2048]{1,0:T(8,128)(2,1)S(1)} %get-tuple-element.36), kind=kOutput, calls=%fused_computation.11 | convolution fusion | flops 1077936128 | bytes 5242880 | tf_op jit(solution)/shard_map/lag_product/dot_general | solution.py:62
  83.1 0.9 select_bitcast_fusion
  84.0 2.2 %collective-permute-done = f32[2,2,64,512]{3,2,0,1:T(8,128)} collective-permute-done((f32[2,2,64,512]{3,2,0,1:T(8,128)}, f32[2,2,64,512]{3,2,0,1:T(8,128)}, u32[]{:S(2)}, u32[]{:S(2)}) %collective-permute-start) | collective-permute-done | bytes 524320 | tf_op jit(solution)/shard_map/bin_exchange/ppermute | solution.py:76
  86.2 1.2 %fusion.12 = f32[2,1,2,64,512]{4,3,0,2,1:T(8,128)S(1)} fusion(f32[2,2,64,512]{3,2,0,1:T(8,128)} %collective-permute-done, f32[2,2,1,64,512]{4,3,2,1,0:T(8,128)S(1)} %get-tuple-element.17, f32[2,2,1,64,512]{4,3,2,1,0:T(8,128)S(1)} %get-tuple-element.16, pred[]{:T(512)S(6)} %eq.87), kind=kLoop, calls=%fused_computation.28 | loop fusion | flops 262144 | bytes 2097153 | tf_op jit(solution)/shard_map/bin_exchange/reshape | solution.py:71
  87.5 1.5 %collective-permute-start.1 = (f32[2,1,64,512]{3,2,0,1:T(8,128)S(1)}, f32[2,1,64,512]{3,2,0,1:T(8,128)S(1)}, u32[]{:S(2)}, u32[]{:S(2)}) collective-permute-start(f32[2,1,64,512]{3,2,0,1:T(8,128)S(1)} %select_bitcast_fusion.1), channel_id=1, source_target_pairs={{0,2},{1,3},{2,0},{3,1},{4,6},{5,7},{6,4},{7,5},{8,10},{9,11},{10,... | collective-permute-start | bytes 786440 | tf_op jit(solution)/shard_map/bin_exchange/ppermute | solution.py:76
  89.0 6.9 %collective-permute-done.1 = f32[2,1,64,512]{3,2,0,1:T(8,128)S(1)} collective-permute-done((f32[2,1,64,512]{3,2,0,1:T(8,128)S(1)}, f32[2,1,64,512]{3,2,0,1:T(8,128)S(1)}, u32[]{:S(2)}, u32[]{:S(2)}) %collective-permute-start.1) | collective-permute-done | bytes 262176 | tf_op jit(solution)/shard_map/bin_exchange/ppermute | solution.py:76
  96.0 12.0 %all_to_all.25 = f32[2,8,8,512]{3,2,0,1:T(8,128)S(1)} all-to-all(f32[2,8,8,512]{3,2,0,1:T(8,128)S(1)} %copy.46), channel_id=1, replica_groups=mesh['wide'=8,'narrow'=4] {'wide'}, dimensions={1} | all-to-all | bytes 524288 | tf_op jit(solution)/shard_map/bin_exchange/all_to_all | solution.py:193
  108.3 0.7 maximum_multiply_fusion
  (37 shorter events, 2.2 us)
Async XLA Ops:
  0.0 1.6 %copy-start = (bf16[64,2,8192]{2,1,0:T(2,128)(2,1)S(1)}, bf16[64,2,8192]{2,1,0:T(2,128)(2,1)}, u32[]{:S(2)}) copy-start(bf16[64,2,8192]{2,1,0:T(2,128)(2,1)} %param.6) | copy-start | bytes 6291460
  1.6 9.1 %copy-start.4 = (s32[2]{0:T(128)S(1)}, s32[2]{0:T(128)}, u32[]{:S(2)}) copy-start(s32[2]{0:T(128)} %param.8) | copy-start | bytes 28
  2.1 11.8 %copy-start.5 = (s32[1,2,128]{2,1,0:T(2,128)S(1)}, s32[1,2,128]{2,1,0:T(2,128)}, u32[]{:S(2)}) copy-start(s32[1,2,128]{2,1,0:T(2,128)} %param.11) | copy-start | bytes 3076
  2.1 11.8 %copy-start.6 = (s32[1,2,128]{2,1,0:T(2,128)S(1)}, s32[1,2,128]{2,1,0:T(2,128)}, u32[]{:S(2)}) copy-start(s32[1,2,128]{2,1,0:T(2,128)} %param.10) | copy-start | bytes 3076
  2.1 11.8 %copy-start.7 = (s32[1,2,128]{2,1,0:T(2,128)S(1)}, s32[1,2,128]{2,1,0:T(2,128)}, u32[]{:S(2)}) copy-start(s32[1,2,128]{2,1,0:T(2,128)} %param.9) | copy-start | bytes 3076
  3.4 21.9 %all-to-all-start = ((bf16[8,64,2,256]{3,1,2,0:T(8,128)(2,1)}), bf16[8,64,2,256]{3,1,2,0:T(8,128)(2,1)}, u32[]{:S(2)}, u32[]{:S(2)}) async-start(bf16[8,64,2,256]{3,1,2,0:T(8,128)(2,1)} %copy.41), calls=%async_computation | async-start | bytes 1048576 | tf_op jit(solution)/shard_map/owner_share_exchange/all_to_all | solution.py:154
  28.1 31.0 %all-to-all-start.1 = ((bf16[8,2,64,2,256]{4,3,2,1,0:T(2,128)(2,1)}), bf16[8,2,64,2,256]{4,3,2,1,0:T(2,128)(2,1)}, u32[]{:S(2)}, u32[]{:S(2)}) async-start(bf16[8,2,64,2,256]{4,3,2,1,0:T(2,128)(2,1)} %broadcast_in_dim.12), calls=%async_computation.1 | async-start | bytes 2097152 | tf_op jit(solution)/shard_map/owner_share_exchange/all_to_all | solution.py:159
  39.7 3.3 %copy-start.1 = (bf16[1,512,4096]{2,1,0:T(8,128)(2,1)S(1)}, bf16[1,512,4096]{2,1,0:T(8,128)(2,1)}, u32[]{:S(2)}) copy-start(bf16[1,512,4096]{2,1,0:T(8,128)(2,1)} %convolution_bitcast_fusion) | copy-start | bytes 12582916
  76.6 3.4 %copy-start.3 = (bf16[32,64,512]{2,1,0:T(8,128)(2,1)S(1)}, bf16[32,64,512]{2,1,0:T(8,128)(2,1)}, u32[]{:S(2)}) copy-start(bf16[32,64,512]{2,1,0:T(8,128)(2,1)} %get-tuple-element.20) | copy-start | bytes 6291460
  80.0 1.6 %copy-start.2 = (bf16[32,64,512]{2,1,0:T(8,128)(2,1)S(1)}, bf16[32,64,512]{2,1,0:T(8,128)(2,1)}, u32[]{:S(2)}) copy-start(bf16[32,64,512]{2,1,0:T(8,128)(2,1)} %get-tuple-element.21) | copy-start | bytes 6291460
  84.0 2.3 %collective-permute-start = (f32[2,2,64,512]{3,2,0,1:T(8,128)}, f32[2,2,64,512]{3,2,0,1:T(8,128)}, u32[]{:S(2)}, u32[]{:S(2)}) collective-permute-start(f32[2,2,64,512]{3,2,0,1:T(8,128)} %select_bitcast_fusion), channel_id=1, source_target_pairs={{0,1},{1,0},{2,3},{3,2},{4,5},{5,4},{6,7},{7,6},{8,9},{9,8},{10,11... | collective-permute-start | bytes 1572872 | tf_op jit(solution)/shard_map/bin_exchange/ppermute | solution.py:76
  87.5 8.4 %collective-permute-start.1 = (f32[2,1,64,512]{3,2,0,1:T(8,128)S(1)}, f32[2,1,64,512]{3,2,0,1:T(8,128)S(1)}, u32[]{:S(2)}, u32[]{:S(2)}) collective-permute-start(f32[2,1,64,512]{3,2,0,1:T(8,128)S(1)} %select_bitcast_fusion.1), channel_id=1, source_target_pairs={{0,2},{1,3},{2,0},{3,1},{4,6},{5,7},{6,4},{7,5},{8,10},{9,11},{10,... | collective-permute-start | bytes 786440 | tf_op jit(solution)/shard_map/bin_exchange/ppermute | solution.py:76

commit v11 on v9

--- a/solution.py
+++ b/solution.py
@@ -93,36 +93,39 @@
     with jax.named_scope("owner_share_exchange"):
         outgoing = near.reshape(block_rows, 2, wide_count, piece).transpose(2, 0, 1, 3)
         arrived = lax.all_to_all(outgoing, "wide", split_axis=0, concat_axis=0, tiled=True)
-        chosen = jnp.stack(
-            [lax.dynamic_index_in_dim(arrived, owners[s], 0, keepdims=False) for s in range(steps)]
-        )
-        copies = jnp.broadcast_to(chosen[None], (wide_count,) + chosen.shape)
-        gathered = lax.all_to_all(copies, "wide", split_axis=0, concat_axis=4, tiled=True)
+        chosen = [
+            lax.dynamic_index_in_dim(arrived, owners[s], 0, keepdims=False) for s in range(steps)
+        ]
 
     ids = jnp.stack([pair_near[0], pair_far[0], stack_bins[0]])
     ids = lax.all_gather(ids, "narrow", axis=2, tiled=True)
     near_ids, far_ids = ids[0], ids[1]
     bin_ids = ids[2]
 
-    with jax.named_scope("cross_spectra"):
-        parts = []
-        for s in range(steps):
-            far = gathered[0, s]
-            near_rows = select_rows(near, near_ids[s])
-            far_rows = select_rows(far, far_ids[s])
-            parts.append(lax.optimization_barrier(cross_rows(near_rows, far_rows, gain)))
+    with jax.named_scope("near_rows"):
+        near_rows = [select_rows(near, near_ids[s]) for s in range(steps)]
 
-    with jax.named_scope("bin_sums"):
-        real_sum = None
-        imag_sum = None
-        for s in range(steps):
+    sums = None
+    for s in range(steps):
+        with jax.named_scope("owner_share_gather"):
+            copies = jnp.broadcast_to(chosen[s][None], (wide_count,) + chosen[s].shape)
+            gathered = lax.all_to_all(copies, "wide", split_axis=0, concat_axis=3, tiled=True)
+            if sums is not None:
+                gathered, sums = lax.optimization_barrier((gathered, sums))
+        with jax.named_scope("cross_spectra"):
+            far_rows = select_rows(gathered[0], far_ids[s])
+            real_part, imag_part = lax.optimization_barrier(cross_rows(near_rows[s], far_rows, gain))
+        with jax.named_scope("bin_sums"):
             bin_hits = (
                 jnp.arange(total_bins, dtype=jnp.int32)[:, None] == bin_ids[s][None, :]
             ).astype(jnp.bfloat16)
-            real_step = jnp.dot(bin_hits, parts[s][0], preferred_element_type=jnp.float32)
-            imag_step = jnp.dot(bin_hits, parts[s][1], preferred_element_type=jnp.float32)
-            real_sum = real_step if real_sum is None else real_sum + real_step
-            imag_sum = imag_step if imag_sum is None else imag_sum + imag_step
+            real_step = jnp.dot(bin_hits, real_part, preferred_element_type=jnp.float32)
+            imag_step = jnp.dot(bin_hits, imag_part, preferred_element_type=jnp.float32)
+            if sums is None:
+                sums = (real_step, imag_step)
+            else:
+                sums = (sums[0] + real_step, sums[1] + imag_step)
+    real_sum, imag_sum = sums
 
     with jax.named_scope("lag_product"):
         cosine, sine = lag_halves(first_freq, share, freqs, LAGS)

time: 101 us -> 104 us (1.030)
  waiting for transfers between devices: 28.7 us -> 20 us
  local copies, waits for them, and re-layouts: 10.2 us -> 14.9 us
  starting transfers between devices: 13.1 us -> 16.8 us
  matrix products: 14.9 us -> 17.6 us
    all_to_all x1 -> x2, waiting for transfers between devices: 9.73 us -> 5.12 us  [local(): lax.all_to_all(copies, 'wide', split_axis=0, concat_axis=3, tiled=True)]
    all_to_all x1, waiting for transfers between devices: 9.9 us -> 5.76 us  [local(): lax.all_to_all(outgoing, 'wide', split_axis=0, concat_axis=0, tiled=True)]
    all_to_all x1 -> x2, starting transfers between devices: 4.25 us -> 7.97 us  [local(): lax.all_to_all(copies, 'wide', split_axis=0, concat_axis=3, tiled=True)]
    dot_general x4, matrix products: 3.23 us -> 5.97 us  [the longest x2 3.03 us: local(): real_step = jnp.dot(bin_hits, real_part, preferred_element_type=jnp.float32)]
    unnamed x18 -> x22, local copies, waits for them, and re-layouts: 3.67 us -> 5.13 us
    squeeze x0 -> x1, local copies, waits for them, and re-layouts: none -> 1.28 us  [select_rows(): flat_block = block.reshape(block_rows, -1)]
    slice x3 -> x0, local copies, waits for them, and re-layouts: 1.19 us -> none  [local(): far = gathered[0, s]]
    all_to_all x1 -> x2, local copies, waits for them, and re-layouts: 1.35 us -> 2.45 us  [local(): lax.all_to_all(copies, 'wide', split_axis=0, concat_axis=3, tiled=True)]
  transfers between devices with their start and end apart: 4 -> 5, of which waited for: 4 -> 5; matrix products, arithmetic and copies ran while one was open for 11% -> 22% of each run, Pallas kernels for 0% -> 0%
where the time goes in v11:
time: 104 us; the launch traced here: 103 us
  waiting for transfers between devices  20 us (19%)
  matrix products  17.6 us (17%)
  blocking collectives  17.1 us (16%)
  starting transfers between devices  16.8 us (16%)
  local copies, waits for them, and re-layouts  14.9 us (14%)
  other arithmetic  12.5 us (12%)
  between operations  4.12 us (4%)
    all_to_all x1, blocking collectives, local(): lax.all_to_all(owned, 'wide', split_axis=1, concat_axis=1, tiled=True)  12 us
    dot_general x4, matrix products, select_rows(): chosen = jnp.dot(picker, flat_block, preferred_element_type=jnp.bfloat16)  9.16 us
    ppermute x2, waiting for transfers between devices, halving_sum(): parts = keep + lax.ppermute(send, axis, pairs)  9.11 us
    all_to_all x2, starting transfers between devices, local(): lax.all_to_all(copies, 'wide', split_axis=0, concat_axis=3, tiled=True)  7.97 us
    all_to_all x1, starting transfers between devices, local(): lax.all_to_all(outgoing, 'wide', split_axis=0, concat_axis=0, tiled=True)  7.28 us
    all_to_all x1, waiting for transfers between devices, local(): lax.all_to_all(outgoing, 'wide', split_axis=0, concat_axis=0, tiled=True)  5.76 us
    unnamed x22, local copies, waits for them, and re-layouts  5.13 us
    all_to_all x2, waiting for transfers between devices, local(): lax.all_to_all(copies, 'wide', split_axis=0, concat_axis=3, tiled=True)  5.12 us
  transfers between devices with their start and end apart: 5, of which 5 were waited for; matrix products, arithmetic and copies ran while one was open for 22% of the time, Pallas kernels for 0%

profile of v11, /device:TPU:0, one launch (start us, length us, event | category | flops | bytes accessed | tf_op | source)
XLA Modules:
  0.0 103.0 jit_solution(13086832140217767927)
XLA Ops:
  0.0 1.6 %copy-done = bf16[64,2,8192]{2,1,0:T(2,128)(2,1)S(1)} copy-done((bf16[64,2,8192]{2,1,0:T(2,128)(2,1)S(1)}, bf16[64,2,8192]{2,1,0:T(2,128)(2,1)}, u32[]{:S(2)}) %copy-start) | copy-done | bytes 2097176
  2.4 1.0 copy.66
  3.4 7.3 %all-to-all-start = ((bf16[8,64,2,256]{3,1,2,0:T(8,128)(2,1)}), bf16[8,64,2,256]{3,1,2,0:T(8,128)(2,1)S(1)}, u32[]{:S(2)}, u32[]{:S(2)}) async-start(bf16[8,64,2,256]{3,1,2,0:T(8,128)(2,1)} %copy.66), calls=%async_computation | async-start | bytes 1048576 | tf_op jit(solution)/shard_map/owner_share_exchange/all_to_all | solution.py:95
  16.1 3.3 %add_convert_fusion = (bf16[32,64,512]{2,1,0:T(8,128)(2,1)}, bf16[32,64,512]{2,1,0:T(8,128)(2,1)}) fusion(f32[64,512]{1,0:T(8,128)S(1)} %get-tuple-element.47, f32[32,512]{1,0:T(8,128)S(1)} %get-tuple-element.45, f32[64,512]{1,0:T(8,128)S(1)} %get-tuple-element.46, f32[32,512]{1,0:T(8,128)S(1)} %get-tuple-element.44), kind=kLoop, calls=%fused_computation.24 | loop fusion | flops 8388608 | bytes 4587520 | tf_op jit(solution)/shard_map/lag_product/convert_element_type | solution.py:32
  19.4 5.8 %all-to-all-done = bf16[8,64,2,256]{3,1,2,0:T(8,128)(2,1)S(1)} async-done(((bf16[8,64,2,256]{3,1,2,0:T(8,128)(2,1)}), bf16[8,64,2,256]{3,1,2,0:T(8,128)(2,1)S(1)}, u32[]{:S(2)}, u32[]{:S(2)}) %all-to-all-start) | async-done | bytes 524320 | tf_op jit(solution)/shard_map/owner_share_exchange/all_to_all | solution.py:95
  25.3 1.1 %broadcast_in_dim.21 = bf16[8,64,2,256]{3,2,1,0:T(2,128)(2,1)} broadcast(bf16[64,2,256]{2,1,0:T(2,128)(2,1)S(1)} %copy.69), dimensions={1,2,3} | broadcast | bytes 589824 | tf_op jit(solution)/shard_map/owner_share_gather/broadcast_in_dim | solution.py:111
  26.4 3.6 %all-to-all-start.2 = ((bf16[8,64,2,256]{3,2,1,0:T(2,128)(2,1)}), bf16[8,64,2,256]{3,2,1,0:T(2,128)(2,1)S(1)}, u32[]{:S(2)}, u32[]{:S(2)}) async-start(bf16[8,64,2,256]{3,2,1,0:T(2,128)(2,1)} %broadcast_in_dim.21), calls=%async_computation.2 | async-start | bytes 1048576 | tf_op jit(solution)/shard_map/owner_share_gather/all_to_all | solution.py:112
  30.7 5.1 %all_gather.3 = s32[3,2,512]{2,1,0:T(2,128)S(1)} all-gather(s32[3,2,128]{2,1,0:T(2,128)S(1)} %pad_add_fusion), channel_id=1, replica_groups=mesh['wide'=8,'narrow'=4] {'narrow'}, dimensions={2}, use_global_device_ids=true | all-gather | bytes 15360 | tf_op jit(solution)/shard_map/all_gather | solution.py:101
  35.8 3.3 %fusion.35 = bf16[512,2,2048]{2,0,1:T(8,128)(2,1)} fusion(s32[512]{0:T(512)S(1)} %bitcast.146, bf16[8,8,2,2048]{3,2,1,0:T(2,128)(2,1)S(1)} %bitcast.127), kind=kOutput, calls=%fused_computation.53 | convolution fusion | flops 268468224 | bytes 4720640 | tf_op jit(solution)/shard_map/near_rows/dot_general | solution.py:42
  39.2 3.2 %fusion.33 = bf16[512,2,2048]{2,0,1:T(8,128)(2,1)} fusion(s32[512]{0:T(512)S(1)} %bitcast.145, bf16[8,8,2,2048]{3,2,1,0:T(2,128)(2,1)S(1)} %bitcast.128), kind=kOutput, calls=%fused_computation.51 | convolution fusion | flops 268468224 | bytes 4720640 | tf_op jit(solution)/shard_map/near_rows/dot_general | solution.py:42
  42.4 2.3 %all-to-all-done.2 = bf16[8,64,2,256]{3,2,1,0:T(2,128)(2,1)S(1)} async-done(((bf16[8,64,2,256]{3,2,1,0:T(2,128)(2,1)}), bf16[8,64,2,256]{3,2,1,0:T(2,128)(2,1)S(1)}, u32[]{:S(2)}, u32[]{:S(2)}) %all-to-all-start.2) | async-done | bytes 524320 | tf_op jit(solution)/shard_map/owner_share_gather/all_to_all | solution.py:112
  45.5 4.3 %all-to-all-start.1 = ((bf16[8,64,2,256]{3,1,2,0:T(8,128)(2,1)}), bf16[8,64,2,256]{3,1,2,0:T(8,128)(2,1)}, u32[]{:S(2)}, u32[]{:S(2)}) async-start(bf16[8,64,2,256]{3,1,2,0:T(8,128)(2,1)} %broadcast_in_dim.19), calls=%async_computation.1 | async-start | bytes 1048576 | tf_op jit(solution)/shard_map/owner_share_gather/all_to_all | solution.py:112
  49.9 1.4 %copy.70 = bf16[1,64,2,8,256]{4,3,2,1,0:T(8,128)(2,1)} copy(bf16[1,64,2,8,256]{4,2,1,3,0:T(2,128)(2,1)S(1)} %bitcast.133) | data formatting | bytes 1048576 | tf_op jit(solution)/shard_map/owner_share_gather/all_to_all | solution.py:112
  51.2 1.3 %squeeze.15 = bf16[64,4096]{1,0:T(8,128)(2,1)S(1)} reshape(bf16[1,64,2,8,256]{4,3,2,1,0:T(8,128)(2,1)} %copy.70) | data formatting | bytes 1048576 | tf_op jit(solution)/shard_map/cross_spectra/reshape;cross_spectra/squeeze | solution.py:38
  52.5 1.3 %fusion.30 = bf16[512,2,2048]{2,0,1:T(8,128)(2,1)S(1)} fusion(bf16[8,2,8,2048]{3,2,1,0:T(8,128)(2,1)S(1)} %bitcast.129, s32[512]{0:T(512)S(1)} %bitcast.144), kind=kOutput, calls=%fused_computation.48 | convolution fusion | flops 268468224 | bytes 4720640 | tf_op jit(solution)/shard_map/cross_spectra/dot_general | solution.py:42
  53.8 0.9 copy-done.2
  54.7 2.5 %fusion.7 = (bf16[512,2048]{1,0:T(8,128)(2,1)S(1)}, bf16[512,2048]{1,0:T(8,128)(2,1)S(1)}) fusion(f32[2048]{0:T(1024)S(1)} %dynamic_slice.16, bf16[512,2,2048]{2,0,1:T(8,128)(2,1)S(1)} %fusion.30, bf16[512,2,2048]{2,0,1:T(8,128)(2,1)S(1)} %copy-done.2), kind=kLoop, calls=%fused_computation.15 | loop fusion | flops 14680064 | bytes 12591104 | tf_op jit(solution)/shard_map/cross_spectra/convert_element_type | solution.py:53
  57.3 2.1 %fusion.38 = f32[256,2048]{1,0:T(8,128)} fusion(bf16[512,2048]{1,0:T(8,128)(2,1)S(1)} %get-tuple-element.13, s32[512]{0:T(512)S(1)} %bitcast.139), kind=kOutput, calls=%fused_computation.64 | convolution fusion | flops 537001984 | bytes 4196352 | tf_op jit(solution)/shard_map/bin_sums/dot_general | solution.py:123
  59.4 2.1 %fusion.39 = f32[256,2048]{1,0:T(8,128)} fusion(bf16[512,2048]{1,0:T(8,128)(2,1)S(1)} %get-tuple-element.12, s32[512]{0:T(512)S(1)} %bitcast.140), kind=kOutput, calls=%fused_computation.65 | convolution fusion | flops 537001984 | bytes 4196352 | tf_op jit(solution)/shard_map/bin_sums/dot_general | solution.py:122
  61.5 2.8 %all-to-all-done.1 = bf16[8,64,2,256]{3,1,2,0:T(8,128)(2,1)} async-done(((bf16[8,64,2,256]{3,1,2,0:T(8,128)(2,1)}), bf16[8,64,2,256]{3,1,2,0:T(8,128)(2,1)}, u32[]{:S(2)}, u32[]{:S(2)}) %all-to-all-start.1) | async-done | bytes 524320 | tf_op jit(solution)/shard_map/owner_share_gather/all_to_all | solution.py:112
  64.3 1.1 %copy.87 = bf16[1,8,2,8,8,256]{5,4,1,3,2,0:T(8,128)(2,1)S(1)} copy(bf16[1,8,2,8,8,256]{5,4,3,2,1,0:T(8,128)(2,1)} %bitcast.50) | data formatting | bytes 1048576 | tf_op jit(solution)/shard_map/owner_share_gather/all_to_all | solution.py:112
  66.0 1.3 %fusion.27 = bf16[512,2,2048]{2,0,1:T(8,128)(2,1)S(1)} fusion(s32[512]{0:T(512)S(1)} %bitcast.143, bf16[8,8,2,2048]{3,2,1,0:T(2,128)(2,1)S(1)} %bitcast.130), kind=kOutput, calls=%fused_computation.45 | convolution fusion | flops 268468224 | bytes 4720640 | tf_op jit(solution)/shard_map/cross_spectra/dot_general | solution.py:42
  68.2 2.6 %fusion.15 = (bf16[512,2048]{1,0:T(8,128)(2,1)S(1)}, bf16[512,2048]{1,0:T(8,128)(2,1)S(1)}) fusion(f32[2048]{0:T(1024)S(1)} %dynamic_slice.16, bf16[512,2,2048]{2,0,1:T(8,128)(2,1)S(1)} %fusion.27, bf16[512,2,2048]{2,0,1:T(8,128)(2,1)S(1)} %copy-done.1), kind=kLoop, calls=%fused_computation.23 | loop fusion | flops 14680064 | bytes 12591104 | tf_op jit(solution)/shard_map/cross_spectra/convert_element_type | solution.py:53
  72.3 0.9 reduce-precision_convert_fusion.1
  73.9 1.2 %fusion.22 = f32[512,512]{1,0:T(8,128)S(1)} fusion(bf16[2048,512]{1,0:T(8,128)(2,1)S(1)} %bitcast.132, bf16[256,2048]{1,0:T(8,128)(2,1)S(1)} %get-tuple-element.26, bf16[256,2048]{1,0:T(8,128)(2,1)S(1)} %get-tuple-element.25), kind=kOutput, calls=%fused_computation.38 | convolution fusion | flops 1077936128 | bytes 5242880 | tf_op jit(solution)/shard_map/lag_product/dot_general | solution.py:60
  75.5 1.2 %fusion.18 = f32[512,512]{1,0:T(8,128)S(1)} fusion(bf16[2048,512]{1,0:T(8,128)(2,1)S(1)} %bitcast.131, bf16[256,2048]{1,0:T(8,128)(2,1)S(1)} %get-tuple-element.29, bf16[256,2048]{1,0:T(8,128)(2,1)S(1)} %get-tuple-element.27), kind=kOutput, calls=%fused_computation.34 | convolution fusion | flops 1077936128 | bytes 5242880 | tf_op jit(solution)/shard_map/lag_product/dot_general | solution.py:60
  77.1 0.9 select_bitcast_fusion
  78.0 2.2 %collective-permute-done = f32[2,2,64,512]{3,2,0,1:T(8,128)} collective-permute-done((f32[2,2,64,512]{3,2,0,1:T(8,128)}, f32[2,2,64,512]{3,2,0,1:T(8,128)}, u32[]{:S(2)}, u32[]{:S(2)}) %collective-permute-start) | collective-permute-done | bytes 524320 | tf_op jit(solution)/shard_map/bin_exchange/ppermute | solution.py:74
  80.2 1.2 %fusion.37 = f32[2,1,2,64,512]{4,3,0,2,1:T(8,128)S(1)} fusion(f32[2,2,64,512]{3,2,0,1:T(8,128)} %collective-permute-done, f32[2,2,1,64,512]{4,3,2,1,0:T(8,128)S(1)} %get-tuple-element.31, f32[2,2,1,64,512]{4,3,2,1,0:T(8,128)S(1)} %get-tuple-element.30, pred[]{:T(512)S(6)} %eq.117), kind=kLoop, calls=%fused_computation.59 | loop fusion | flops 262144 | bytes 2097153 | tf_op jit(solution)/shard_map/bin_exchange/reshape | solution.py:69
  81.4 1.6 %collective-permute-start.1 = (f32[2,1,64,512]{3,2,0,1:T(8,128)S(1)}, f32[2,1,64,512]{3,2,0,1:T(8,128)S(1)}, u32[]{:S(2)}, u32[]{:S(2)}) collective-permute-start(f32[2,1,64,512]{3,2,0,1:T(8,128)S(1)} %select_bitcast_fusion.1), channel_id=1, source_target_pairs={{0,2},{1,3},{2,0},{3,1},{4,6},{5,7},{6,4},{7,5},{8,10},{9,11},{10,... | collective-permute-start | bytes 786440 | tf_op jit(solution)/shard_map/bin_exchange/ppermute | solution.py:74
  83.0 6.9 %collective-permute-done.1 = f32[2,1,64,512]{3,2,0,1:T(8,128)S(1)} collective-permute-done((f32[2,1,64,512]{3,2,0,1:T(8,128)S(1)}, f32[2,1,64,512]{3,2,0,1:T(8,128)S(1)}, u32[]{:S(2)}, u32[]{:S(2)}) %collective-permute-start.1) | collective-permute-done | bytes 262176 | tf_op jit(solution)/shard_map/bin_exchange/ppermute | solution.py:74
  89.9 12.0 %all_to_all.43 = f32[2,8,8,512]{3,2,0,1:T(8,128)S(1)} all-to-all(f32[2,8,8,512]{3,2,0,1:T(8,128)S(1)} %copy.77), channel_id=1, replica_groups=mesh['wide'=8,'narrow'=4] {'wide'}, dimensions={1} | all-to-all | bytes 524288 | tf_op jit(solution)/shard_map/bin_exchange/all_to_all | solution.py:142
  (48 shorter events, 9.5 us)
Async XLA Ops:
  0.0 1.6 %copy-start = (bf16[64,2,8192]{2,1,0:T(2,128)(2,1)S(1)}, bf16[64,2,8192]{2,1,0:T(2,128)(2,1)}, u32[]{:S(2)}) copy-start(bf16[64,2,8192]{2,1,0:T(2,128)(2,1)} %param.6) | copy-start | bytes 6291460
  1.6 9.1 %copy-start.7 = (s32[2]{0:T(128)S(1)}, s32[2]{0:T(128)}, u32[]{:S(2)}) copy-start(s32[2]{0:T(128)} %param.8) | copy-start | bytes 28
  1.6 13.6 %copy-start.8 = (s32[1,2,128]{2,1,0:T(2,128)S(1)}, s32[1,2,128]{2,1,0:T(2,128)}, u32[]{:S(2)}) copy-start(s32[1,2,128]{2,1,0:T(2,128)} %param.11) | copy-start | bytes 3076
  1.6 13.6 %copy-start.9 = (s32[1,2,128]{2,1,0:T(2,128)S(1)}, s32[1,2,128]{2,1,0:T(2,128)}, u32[]{:S(2)}) copy-start(s32[1,2,128]{2,1,0:T(2,128)} %param.10) | copy-start | bytes 3076
  1.6 13.6 %copy-start.10 = (s32[1,2,128]{2,1,0:T(2,128)S(1)}, s32[1,2,128]{2,1,0:T(2,128)}, u32[]{:S(2)}) copy-start(s32[1,2,128]{2,1,0:T(2,128)} %param.9) | copy-start | bytes 3076
  3.4 21.8 %all-to-all-start = ((bf16[8,64,2,256]{3,1,2,0:T(8,128)(2,1)}), bf16[8,64,2,256]{3,1,2,0:T(8,128)(2,1)S(1)}, u32[]{:S(2)}, u32[]{:S(2)}) async-start(bf16[8,64,2,256]{3,1,2,0:T(8,128)(2,1)} %copy.66), calls=%async_computation | async-start | bytes 1048576 | tf_op jit(solution)/shard_map/owner_share_exchange/all_to_all | solution.py:95
  26.4 18.3 %all-to-all-start.2 = ((bf16[8,64,2,256]{3,2,1,0:T(2,128)(2,1)}), bf16[8,64,2,256]{3,2,1,0:T(2,128)(2,1)S(1)}, u32[]{:S(2)}, u32[]{:S(2)}) async-start(bf16[8,64,2,256]{3,2,1,0:T(2,128)(2,1)} %broadcast_in_dim.21), calls=%async_computation.2 | async-start | bytes 1048576 | tf_op jit(solution)/shard_map/owner_share_gather/all_to_all | solution.py:112
  45.5 18.8 %all-to-all-start.1 = ((bf16[8,64,2,256]{3,1,2,0:T(8,128)(2,1)}), bf16[8,64,2,256]{3,1,2,0:T(8,128)(2,1)}, u32[]{:S(2)}, u32[]{:S(2)}) async-start(bf16[8,64,2,256]{3,1,2,0:T(8,128)(2,1)} %broadcast_in_dim.19), calls=%async_computation.1 | async-start | bytes 1048576 | tf_op jit(solution)/shard_map/owner_share_gather/all_to_all | solution.py:112
  52.5 2.2 %copy-start.2 = (bf16[512,2,2048]{2,0,1:T(8,128)(2,1)S(1)}, bf16[512,2,2048]{2,0,1:T(8,128)(2,1)}, u32[]{:S(2)}) copy-start(bf16[512,2,2048]{2,0,1:T(8,128)(2,1)} %fusion.35) | copy-start | bytes 12582916
  66.0 2.2 %copy-start.1 = (bf16[512,2,2048]{2,0,1:T(8,128)(2,1)S(1)}, bf16[512,2,2048]{2,0,1:T(8,128)(2,1)}, u32[]{:S(2)}) copy-start(bf16[512,2,2048]{2,0,1:T(8,128)(2,1)} %fusion.33) | copy-start | bytes 12582916
  68.2 2.6 %copy-start.4 = (f32[256,2048]{1,0:T(8,128)S(1)}, f32[256,2048]{1,0:T(8,128)}, u32[]{:S(2)}) copy-start(f32[256,2048]{1,0:T(8,128)} %fusion.38) | copy-start | bytes 6291460
  70.7 1.6 %copy-start.3 = (f32[256,2048]{1,0:T(8,128)S(1)}, f32[256,2048]{1,0:T(8,128)}, u32[]{:S(2)}) copy-start(f32[256,2048]{1,0:T(8,128)} %fusion.39) | copy-start | bytes 6291460
  72.3 1.6 %copy-start.6 = (bf16[32,64,512]{2,1,0:T(8,128)(2,1)S(1)}, bf16[32,64,512]{2,1,0:T(8,128)(2,1)}, u32[]{:S(2)}) copy-start(bf16[32,64,512]{2,1,0:T(8,128)(2,1)} %get-tuple-element.34) | copy-start | bytes 6291460
  73.9 1.6 %copy-start.5 = (bf16[32,64,512]{2,1,0:T(8,128)(2,1)S(1)}, bf16[32,64,512]{2,1,0:T(8,128)(2,1)}, u32[]{:S(2)}) copy-start(bf16[32,64,512]{2,1,0:T(8,128)(2,1)} %get-tuple-element.35) | copy-start | bytes 6291460
  77.9 2.3 %collective-permute-start = (f32[2,2,64,512]{3,2,0,1:T(8,128)}, f32[2,2,64,512]{3,2,0,1:T(8,128)}, u32[]{:S(2)}, u32[]{:S(2)}) collective-permute-start(f32[2,2,64,512]{3,2,0,1:T(8,128)} %select_bitcast_fusion), channel_id=1, source_target_pairs={{0,1},{1,0},{2,3},{3,2},{4,5},{5,4},{6,7},{7,6},{8,9},{9,8},{10,11... | collective-permute-start | bytes 1572872 | tf_op jit(solution)/shard_map/bin_exchange/ppermute | solution.py:74
  81.4 8.4 %collective-permute-start.1 = (f32[2,1,64,512]{3,2,0,1:T(8,128)S(1)}, f32[2,1,64,512]{3,2,0,1:T(8,128)S(1)}, u32[]{:S(2)}, u32[]{:S(2)}) collective-permute-start(f32[2,1,64,512]{3,2,0,1:T(8,128)S(1)} %select_bitcast_fusion.1), channel_id=1, source_target_pairs={{0,2},{1,3},{2,0},{3,1},{4,6},{5,7},{6,4},{7,5},{8,10},{9,11},{10,... | collective-permute-start | bytes 786440 | tf_op jit(solution)/shard_map/bin_exchange/ppermute | solution.py:74

commit v12 on v9

--- a/solution.py
+++ b/solution.py
@@ -43,11 +43,18 @@
     return chosen.reshape(indices.shape[0], 2, -1)
 
 
-def cross_rows(near_rows, far_rows, band_gain):
+def pick_rows(block, indices):
+    picker = (indices[:, None] == jnp.arange(block.shape[0], dtype=jnp.int32)[None, :]).astype(
+        jnp.bfloat16
+    )
+    return jnp.dot(picker, block, preferred_element_type=jnp.bfloat16)
+
+
+def cross_rows(near_rows, far_real, far_imag, band_gain):
     near_real = near_rows[:, 0].astype(jnp.float32)
     near_imag = near_rows[:, 1].astype(jnp.float32)
-    far_real = far_rows[:, 0].astype(jnp.float32)
-    far_imag = far_rows[:, 1].astype(jnp.float32)
+    far_real = far_real.astype(jnp.float32)
+    far_imag = far_imag.astype(jnp.float32)
     real_part = (near_real * far_real + near_imag * far_imag) * band_gain
     imag_part = (near_imag * far_real - near_real * far_imag) * band_gain
     return real_part.astype(jnp.bfloat16), imag_part.astype(jnp.bfloat16)
@@ -91,7 +98,7 @@
     gain = lax.dynamic_slice_in_dim(band_gain, first_freq, share, axis=0)
 
     with jax.named_scope("owner_share_exchange"):
-        outgoing = near.reshape(block_rows, 2, wide_count, piece).transpose(2, 0, 1, 3)
+        outgoing = near.reshape(block_rows, 2, wide_count, piece).transpose(2, 1, 0, 3)
         arrived = lax.all_to_all(outgoing, "wide", split_axis=0, concat_axis=0, tiled=True)
         chosen = jnp.stack(
             [lax.dynamic_index_in_dim(arrived, owners[s], 0, keepdims=False) for s in range(steps)]
@@ -107,10 +114,12 @@
     with jax.named_scope("cross_spectra"):
         parts = []
         for s in range(steps):
-            far = gathered[0, s]
             near_rows = select_rows(near, near_ids[s])
-            far_rows = select_rows(far, far_ids[s])
-            parts.append(lax.optimization_barrier(cross_rows(near_rows, far_rows, gain)))
+            far_real = pick_rows(gathered[0, s, 0], far_ids[s])
+            far_imag = pick_rows(gathered[0, s, 1], far_ids[s])
+            parts.append(
+                lax.optimization_barrier(cross_rows(near_rows, far_real, far_imag, gain))
+            )
 
     with jax.named_scope("bin_sums"):
         real_sum = None

time: 101 us -> 99.1 us (0.981)
  other arithmetic: 12.8 us -> 7.39 us
  matrix products: 14.9 us -> 19.7 us
  local copies, waits for them, and re-layouts: 10.2 us -> 8.75 us
    dot_general x0 -> x4, matrix products: none -> 7.39 us  [pick_rows(): return jnp.dot(picker, block, preferred_element_type=jnp.bfloat16)]
    convert_element_type x1 -> x0, other arithmetic: 5.43 us -> none  [cross_rows(): return (real_part.astype(jnp.bfloat16), imag_part.astype(jnp.bfloat16))]
    dot_general x4 -> x2, matrix products: 9.15 us -> 6.54 us  [select_rows(): chosen = jnp.dot(picker, flat_block, preferred_element_type=jnp.bfloat16)]
    slice x3 -> x0, local copies, waits for them, and re-layouts: 1.19 us -> none  [local(): far = gathered[0, s]]
  transfers between devices with their start and end apart: 4 -> 4, of which waited for: 4 -> 4; matrix products, arithmetic and copies ran while one was open for 11% -> 12% of each run, Pallas kernels for 0% -> 0%
where the time goes in v12:
time: 99.1 us; the launch traced here: 98.6 us
  waiting for transfers between devices  28.8 us (29%)
  matrix products  19.7 us (20%)
  blocking collectives  16.8 us (17%)
  starting transfers between devices  13.1 us (13%)
  local copies, waits for them, and re-layouts  8.75 us (9%)
  other arithmetic  7.39 us (7%)
  between operations  4.1 us (4%)
    all_to_all x1, blocking collectives, local(): lax.all_to_all(owned, 'wide', split_axis=1, concat_axis=1, tiled=True)  11.7 us
    all_to_all x1, waiting for transfers between devices, local(): lax.all_to_all(outgoing, 'wide', split_axis=0, concat_axis=0, tiled=True)  9.95 us
    all_to_all x1, waiting for transfers between devices, local(): lax.all_to_all(copies, 'wide', split_axis=0, concat_axis=4, tiled=True)  9.75 us
    ppermute x2, waiting for transfers between devices, halving_sum(): parts = keep + lax.ppermute(send, axis, pairs)  9.1 us
    dot_general x4, matrix products, pick_rows(): return jnp.dot(picker, block, preferred_element_type=jnp.bfloat16)  7.39 us
    all_to_all x1, starting transfers between devices, local(): lax.all_to_all(outgoing, 'wide', split_axis=0, concat_axis=0, tiled=True)  7.28 us
    dot_general x2, matrix products, select_rows(): chosen = jnp.dot(picker, flat_block, preferred_element_type=jnp.bfloat16)  6.54 us
    all_gather x1, blocking collectives, local(): ids = lax.all_gather(ids, 'narrow', axis=2, tiled=True)  5.1 us
  transfers between devices with their start and end apart: 4, of which 4 were waited for; matrix products, arithmetic and copies ran while one was open for 12% of the time, Pallas kernels for 0%

profile of v12, /device:TPU:0, one launch (start us, length us, event | category | flops | bytes accessed | tf_op | source)
XLA Modules:
  0.0 98.6 jit_solution(9662212391486438708)
XLA Ops:
  0.0 1.6 %copy-done = bf16[64,2,8192]{2,1,0:T(2,128)(2,1)S(1)} copy-done((bf16[64,2,8192]{2,1,0:T(2,128)(2,1)S(1)}, bf16[64,2,8192]{2,1,0:T(2,128)(2,1)}, u32[]{:S(2)}) %copy-start) | copy-done | bytes 2097176
  2.4 1.0 copy.45
  3.4 7.3 %all-to-all-start = ((bf16[8,2,64,256]{3,2,1,0:T(8,128)(2,1)}), bf16[8,2,64,256]{3,2,1,0:T(8,128)(2,1)S(1)}, u32[]{:S(2)}, u32[]{:S(2)}) async-start(bf16[8,2,64,256]{3,2,1,0:T(8,128)(2,1)} %copy.45), calls=%async_computation | async-start | bytes 1048576 | tf_op jit(solution)/shard_map/owner_share_exchange/all_to_all | solution.py:102
  10.7 0.6 fusion.68
  15.2 9.9 %all-to-all-done = bf16[8,2,64,256]{3,2,1,0:T(8,128)(2,1)S(1)} async-done(((bf16[8,2,64,256]{3,2,1,0:T(8,128)(2,1)}), bf16[8,2,64,256]{3,2,1,0:T(8,128)(2,1)S(1)}, u32[]{:S(2)}, u32[]{:S(2)}) %all-to-all-start) | async-done | bytes 524320 | tf_op jit(solution)/shard_map/owner_share_exchange/all_to_all | solution.py:102
  25.2 1.1 %broadcast_in_dim.12 = bf16[8,2,2,64,256]{4,3,2,1,0:T(8,128)(2,1)} broadcast(bf16[2,2,64,256]{3,2,1,0:T(8,128)(2,1)S(1)} %pad_maximum_fusion.1), dimensions={1,2,3,4} | broadcast | bytes 1179648 | tf_op jit(solution)/shard_map/owner_share_exchange/broadcast_in_dim | solution.py:106
  26.3 4.2 %all-to-all-start.1 = ((bf16[8,2,2,64,256]{4,3,2,1,0:T(8,128)(2,1)}), bf16[8,2,2,64,256]{4,3,2,1,0:T(8,128)(2,1)}, u32[]{:S(2)}, u32[]{:S(2)}) async-start(bf16[8,2,2,64,256]{4,3,2,1,0:T(8,128)(2,1)} %broadcast_in_dim.12), calls=%async_computation.1 | async-start | bytes 2097152 | tf_op jit(solution)/shard_map/owner_share_exchange/all_to_all | solution.py:107
  30.6 5.1 %all_gather.3 = s32[3,2,512]{2,1,0:T(2,128)S(1)} all-gather(s32[3,2,128]{2,1,0:T(2,128)S(1)} %pad_add_fusion), channel_id=1, replica_groups=mesh['wide'=8,'narrow'=4] {'narrow'}, dimensions={2}, use_global_device_ids=true | all-gather | bytes 15360 | tf_op jit(solution)/shard_map/all_gather | solution.py:110
  36.6 3.3 %add_convert_fusion = (bf16[32,64,512]{2,1,0:T(8,128)(2,1)}, bf16[32,64,512]{2,1,0:T(8,128)(2,1)}) fusion(f32[64,512]{1,0:T(8,128)S(1)} %get-tuple-element.43, f32[32,512]{1,0:T(8,128)S(1)} %get-tuple-element.41, f32[64,512]{1,0:T(8,128)S(1)} %get-tuple-element.42, f32[32,512]{1,0:T(8,128)S(1)} %get-tuple-element.40), kind=kLoop, calls=%fused_computation.20 | loop fusion | flops 8388608 | bytes 4587520 | tf_op jit(solution)/shard_map/lag_product/convert_element_type | solution.py:32
  39.9 3.2 %fusion.23 = bf16[512,2,2048]{2,0,1:T(8,128)(2,1)} fusion(s32[512]{0:T(512)S(1)} %bitcast.132, bf16[8,8,2,2048]{3,2,1,0:T(2,128)(2,1)S(1)} %bitcast.113), kind=kOutput, calls=%fused_computation.45 | convolution fusion | flops 268468224 | bytes 4720640 | tf_op jit(solution)/shard_map/cross_spectra/dot_general | solution.py:42
  43.1 3.3 %fusion.25 = bf16[512,2,2048]{2,0,1:T(8,128)(2,1)} fusion(s32[512]{0:T(512)S(1)} %bitcast.131, bf16[8,8,2,2048]{3,2,1,0:T(2,128)(2,1)S(1)} %bitcast.114), kind=kOutput, calls=%fused_computation.47 | convolution fusion | flops 268468224 | bytes 4720640 | tf_op jit(solution)/shard_map/cross_spectra/dot_general | solution.py:42
  46.5 9.8 %all-to-all-done.1 = bf16[8,2,2,64,256]{4,3,2,1,0:T(8,128)(2,1)} async-done(((bf16[8,2,2,64,256]{4,3,2,1,0:T(8,128)(2,1)}), bf16[8,2,2,64,256]{4,3,2,1,0:T(8,128)(2,1)}, u32[]{:S(2)}, u32[]{:S(2)}) %all-to-all-start.1) | async-done | bytes 1048608 | tf_op jit(solution)/shard_map/owner_share_exchange/all_to_all | solution.py:107
  56.2 1.5 %copy.58 = bf16[1,8,2,2,8,8,256]{6,5,1,4,3,2,0:T(8,128)(2,1)S(1)} copy(bf16[1,8,2,2,8,8,256]{6,5,4,3,2,1,0:T(8,128)(2,1)} %bitcast.45) | data formatting | bytes 2097152 | tf_op jit(solution)/shard_map/owner_share_exchange/all_to_all | solution.py:107
  57.7 0.8 fusion.34
  58.5 0.8 fusion.35
  59.2 0.7 fusion.32
  60.0 0.7 copy-done.1
  60.7 5.1 %fusion.11 = (bf16[512,2048]{1,0:T(8,128)(2,1)S(1)}, bf16[512,2048]{1,0:T(8,128)(2,1)S(1)}, bf16[512,2048]{1,0:T(8,128)(2,1)S(1)}, bf16[512,2048]{1,0:T(8,128)(2,1)S(1)}) fusion(bf16[512,2048]{1,0:T(8,128)(2,1)S(1)} %fusion.32, f32[2048]{0:T(1024)S(1)} %dynamic-slice-done, bf16[512,2,2048]{2,0,1:T(8,128)(2,1)S(1)} %copy-done.1, ...), kind=kOutput, calls=%fused_computation.19 | convolution fusion | flops 163610624 | bytes 23341056 | tf_op jit(solution)/shard_map/cross_spectra/dot_general | solution.py:50
  65.9 0.7 fusion.28
  66.6 0.7 fusion.29
  67.3 0.8 reduce-precision_convert_fusion
  68.2 0.9 reduce-precision_convert_fusion.1
  69.1 0.6 copy-done.4
  69.8 1.2 %fusion.18 = f32[512,512]{1,0:T(8,128)S(1)} fusion(bf16[2048,512]{1,0:T(8,128)(2,1)S(1)} %bitcast.120, bf16[256,2048]{1,0:T(8,128)(2,1)S(1)} %get-tuple-element.20, bf16[256,2048]{1,0:T(8,128)(2,1)S(1)} %get-tuple-element.19), kind=kOutput, calls=%fused_computation.38 | convolution fusion | flops 1077936128 | bytes 5242880 | tf_op jit(solution)/shard_map/lag_product/dot_general | solution.py:67
  71.4 1.3 %fusion.14 = f32[512,512]{1,0:T(8,128)S(1)} fusion(bf16[2048,512]{1,0:T(8,128)(2,1)S(1)} %bitcast.119, bf16[256,2048]{1,0:T(8,128)(2,1)S(1)} %get-tuple-element.23, bf16[256,2048]{1,0:T(8,128)(2,1)S(1)} %get-tuple-element.21), kind=kOutput, calls=%fused_computation.34 | convolution fusion | flops 1077936128 | bytes 5242880 | tf_op jit(solution)/shard_map/lag_product/dot_general | solution.py:67
  72.9 0.9 select_bitcast_fusion
  73.8 2.2 %collective-permute-done = f32[2,2,64,512]{3,2,0,1:T(8,128)} collective-permute-done((f32[2,2,64,512]{3,2,0,1:T(8,128)}, f32[2,2,64,512]{3,2,0,1:T(8,128)}, u32[]{:S(2)}, u32[]{:S(2)}) %collective-permute-start) | collective-permute-done | bytes 524320 | tf_op jit(solution)/shard_map/bin_exchange/ppermute | solution.py:81
  76.1 1.2 %fusion.27 = f32[2,1,2,64,512]{4,3,0,2,1:T(8,128)S(1)} fusion(f32[2,2,64,512]{3,2,0,1:T(8,128)} %collective-permute-done, f32[2,2,1,64,512]{4,3,2,1,0:T(8,128)S(1)} %get-tuple-element.25, f32[2,2,1,64,512]{4,3,2,1,0:T(8,128)S(1)} %get-tuple-element.24, pred[]{:T(512)S(6)} %eq.131), kind=kLoop, calls=%fused_computation.53 | loop fusion | flops 262144 | bytes 2097153 | tf_op jit(solution)/shard_map/bin_exchange/reshape | solution.py:76
  77.3 1.6 %collective-permute-start.1 = (f32[2,1,64,512]{3,2,0,1:T(8,128)S(1)}, f32[2,1,64,512]{3,2,0,1:T(8,128)S(1)}, u32[]{:S(2)}, u32[]{:S(2)}) collective-permute-start(f32[2,1,64,512]{3,2,0,1:T(8,128)S(1)} %select_bitcast_fusion.1), channel_id=1, source_target_pairs={{0,2},{1,3},{2,0},{3,1},{4,6},{5,7},{6,4},{7,5},{8,10},{9,11},{10,... | collective-permute-start | bytes 786440 | tf_op jit(solution)/shard_map/bin_exchange/ppermute | solution.py:81
  78.9 6.8 %collective-permute-done.1 = f32[2,1,64,512]{3,2,0,1:T(8,128)S(1)} collective-permute-done((f32[2,1,64,512]{3,2,0,1:T(8,128)S(1)}, f32[2,1,64,512]{3,2,0,1:T(8,128)S(1)}, u32[]{:S(2)}, u32[]{:S(2)}) %collective-permute-start.1) | collective-permute-done | bytes 262176 | tf_op jit(solution)/shard_map/bin_exchange/ppermute | solution.py:81
  85.8 11.7 %all_to_all.28 = f32[2,8,8,512]{3,2,0,1:T(8,128)S(1)} all-to-all(f32[2,8,8,512]{3,2,0,1:T(8,128)S(1)} %copy.50), channel_id=1, replica_groups=mesh['wide'=8,'narrow'=4] {'wide'}, dimensions={1} | all-to-all | bytes 524288 | tf_op jit(solution)/shard_map/bin_exchange/all_to_all | solution.py:148
  97.9 0.7 maximum_multiply_fusion
  (39 shorter events, 2.9 us)
Async XLA Ops:
  0.0 1.6 %copy-start = (bf16[64,2,8192]{2,1,0:T(2,128)(2,1)S(1)}, bf16[64,2,8192]{2,1,0:T(2,128)(2,1)}, u32[]{:S(2)}) copy-start(bf16[64,2,8192]{2,1,0:T(2,128)(2,1)} %param.6) | copy-start | bytes 6291460
  1.6 9.1 %copy-start.5 = (s32[2]{0:T(128)S(1)}, s32[2]{0:T(128)}, u32[]{:S(2)}) copy-start(s32[2]{0:T(128)} %param.8) | copy-start | bytes 28
  1.6 13.6 %copy-start.6 = (s32[1,2,128]{2,1,0:T(2,128)S(1)}, s32[1,2,128]{2,1,0:T(2,128)}, u32[]{:S(2)}) copy-start(s32[1,2,128]{2,1,0:T(2,128)} %param.11) | copy-start | bytes 3076
  1.6 13.6 %copy-start.7 = (s32[1,2,128]{2,1,0:T(2,128)S(1)}, s32[1,2,128]{2,1,0:T(2,128)}, u32[]{:S(2)}) copy-start(s32[1,2,128]{2,1,0:T(2,128)} %param.10) | copy-start | bytes 3076
  1.6 13.6 %copy-start.8 = (s32[1,2,128]{2,1,0:T(2,128)S(1)}, s32[1,2,128]{2,1,0:T(2,128)}, u32[]{:S(2)}) copy-start(s32[1,2,128]{2,1,0:T(2,128)} %param.9) | copy-start | bytes 3076
  3.4 21.8 %all-to-all-start = ((bf16[8,2,64,256]{3,2,1,0:T(8,128)(2,1)}), bf16[8,2,64,256]{3,2,1,0:T(8,128)(2,1)S(1)}, u32[]{:S(2)}, u32[]{:S(2)}) async-start(bf16[8,2,64,256]{3,2,1,0:T(8,128)(2,1)} %copy.45), calls=%async_computation | async-start | bytes 1048576 | tf_op jit(solution)/shard_map/owner_share_exchange/all_to_all | solution.py:102
  26.3 29.9 %all-to-all-start.1 = ((bf16[8,2,2,64,256]{4,3,2,1,0:T(8,128)(2,1)}), bf16[8,2,2,64,256]{4,3,2,1,0:T(8,128)(2,1)}, u32[]{:S(2)}, u32[]{:S(2)}) async-start(bf16[8,2,2,64,256]{4,3,2,1,0:T(8,128)(2,1)} %broadcast_in_dim.12), calls=%async_computation.1 | async-start | bytes 2097152 | tf_op jit(solution)/shard_map/owner_share_exchange/all_to_all | solution.py:107
  56.2 3.8 %copy-start.2 = (bf16[512,2,2048]{2,0,1:T(8,128)(2,1)S(1)}, bf16[512,2,2048]{2,0,1:T(8,128)(2,1)}, u32[]{:S(2)}) copy-start(bf16[512,2,2048]{2,0,1:T(8,128)(2,1)} %fusion.25) | copy-start | bytes 12582916
  58.5 2.2 %copy-start.1 = (bf16[512,2,2048]{2,0,1:T(8,128)(2,1)S(1)}, bf16[512,2,2048]{2,0,1:T(8,128)(2,1)}, u32[]{:S(2)}) copy-start(bf16[512,2,2048]{2,0,1:T(8,128)(2,1)} %fusion.23) | copy-start | bytes 12582916
  58.5 2.2 %dynamic-slice-start = ((f32[8192]{0:T(1024)}, s32[]{:T(128)}), f32[2048]{0:T(1024)S(1)}, s32[]{:S(2)}) async-start(f32[8192]{0:T(1024)} %param.7, s32[]{:T(128)} %select_n.120), calls=%async_computation.3 | async-start | bytes 16896 | tf_op jit(solution)/shard_map/dynamic_slice | solution.py:98
  68.2 1.6 %copy-start.4 = (bf16[32,64,512]{2,1,0:T(8,128)(2,1)S(1)}, bf16[32,64,512]{2,1,0:T(8,128)(2,1)}, u32[]{:S(2)}) copy-start(bf16[32,64,512]{2,1,0:T(8,128)(2,1)} %get-tuple-element.28) | copy-start | bytes 6291460
  69.8 1.6 %copy-start.3 = (bf16[32,64,512]{2,1,0:T(8,128)(2,1)S(1)}, bf16[32,64,512]{2,1,0:T(8,128)(2,1)}, u32[]{:S(2)}) copy-start(bf16[32,64,512]{2,1,0:T(8,128)(2,1)} %get-tuple-element.29) | copy-start | bytes 6291460
  73.8 2.3 %collective-permute-start = (f32[2,2,64,512]{3,2,0,1:T(8,128)}, f32[2,2,64,512]{3,2,0,1:T(8,128)}, u32[]{:S(2)}, u32[]{:S(2)}) collective-permute-start(f32[2,2,64,512]{3,2,0,1:T(8,128)} %select_bitcast_fusion), channel_id=1, source_target_pairs={{0,1},{1,0},{2,3},{3,2},{4,5},{5,4},{6,7},{7,6},{8,9},{9,8},{10,11... | collective-permute-start | bytes 1572872 | tf_op jit(solution)/shard_map/bin_exchange/ppermute | solution.py:81
  77.3 8.4 %collective-permute-start.1 = (f32[2,1,64,512]{3,2,0,1:T(8,128)S(1)}, f32[2,1,64,512]{3,2,0,1:T(8,128)S(1)}, u32[]{:S(2)}, u32[]{:S(2)}) collective-permute-start(f32[2,1,64,512]{3,2,0,1:T(8,128)S(1)} %select_bitcast_fusion.1), channel_id=1, source_target_pairs={{0,2},{1,3},{2,0},{3,1},{4,6},{5,7},{6,4},{7,5},{8,10},{9,11},{10,... | collective-permute-start | bytes 786440 | tf_op jit(solution)/shard_map/bin_exchange/ppermute | solution.py:81

commit v13 on v12

--- a/solution.py
+++ b/solution.py
@@ -98,7 +98,12 @@
     gain = lax.dynamic_slice_in_dim(band_gain, first_freq, share, axis=0)
 
     with jax.named_scope("owner_share_exchange"):
-        outgoing = near.reshape(block_rows, 2, wide_count, piece).transpose(2, 1, 0, 3)
+        outgoing = lax.dynamic_index_in_dim(
+            spectra.reshape(block_rows, 2, narrow_count, wide_count, piece),
+            narrow_index,
+            2,
+            keepdims=False,
+        ).transpose(2, 1, 0, 3)
         arrived = lax.all_to_all(outgoing, "wide", split_axis=0, concat_axis=0, tiled=True)
         chosen = jnp.stack(
             [lax.dynamic_index_in_dim(arrived, owners[s], 0, keepdims=False) for s in range(steps)]

time: 99.1 us -> 97.3 us (0.982)
  other arithmetic: 7.39 us -> 5.15 us
  local copies, waits for them, and re-layouts: 8.75 us -> 10.1 us
    all_to_all x1, waiting for transfers between devices: 9.95 us -> 5.11 us  [local(): lax.all_to_all(outgoing, 'wide', split_axis=0, concat_axis=0, tiled=True)]
    all_to_all x1, waiting for transfers between devices: 9.75 us -> 14.4 us  [local(): lax.all_to_all(copies, 'wide', split_axis=0, concat_axis=4, tiled=True)]
    reshape x1, local copies, waits for them, and re-layouts: 0.33 us -> 3.15 us  [local(): spectra.reshape(block_rows, 2, narrow_count, wide_count, piece)]
    unnamed x18 -> x14, local copies, waits for them, and re-layouts: 3.3 us -> 1.92 us
    all_to_all x1, local copies, waits for them, and re-layouts: 1.49 us -> 0.12 us  [local(): lax.all_to_all(copies, 'wide', split_axis=0, concat_axis=4, tiled=True)]
    reshape x1, other arithmetic: 1.19 us -> 0.15 us  [halving_sum(): parts.reshape((parts.shape[0], parts.shape[1] // 2, 2) + parts.shape[2:])]
  transfers between devices with their start and end apart: 4 -> 4, of which waited for: 4 -> 4; matrix products, arithmetic and copies ran while one was open for 12% -> 13% of each run, Pallas kernels for 0% -> 0%
where the time goes in v13:
time: 97.3 us; the launch traced here: 96.9 us
  waiting for transfers between devices  28.2 us (29%)
  matrix products  19.9 us (20%)
  blocking collectives  17.1 us (18%)
  starting transfers between devices  12.5 us (13%)
  local copies, waits for them, and re-layouts  10.1 us (10%)
  other arithmetic  5.15 us (5%)
  between operations  3.95 us (4%)
    all_to_all x1, waiting for transfers between devices, local(): lax.all_to_all(copies, 'wide', split_axis=0, concat_axis=4, tiled=True)  14.4 us
    all_to_all x1, blocking collectives, local(): lax.all_to_all(owned, 'wide', split_axis=1, concat_axis=1, tiled=True)  12 us
    ppermute x2, waiting for transfers between devices, halving_sum(): parts = keep + lax.ppermute(send, axis, pairs)  8.72 us
    dot_general x4, matrix products, pick_rows(): return jnp.dot(picker, block, preferred_element_type=jnp.bfloat16)  7.58 us
    all_to_all x1, starting transfers between devices, local(): lax.all_to_all(outgoing, 'wide', split_axis=0, concat_axis=0, tiled=True)  7.28 us
    dot_general x2, matrix products, select_rows(): chosen = jnp.dot(picker, flat_block, preferred_element_type=jnp.bfloat16)  6.57 us
    all_to_all x1, waiting for transfers between devices, local(): lax.all_to_all(outgoing, 'wide', split_axis=0, concat_axis=0, tiled=True)  5.11 us
    all_gather x1, blocking collectives, local(): ids = lax.all_gather(ids, 'narrow', axis=2, tiled=True)  5.1 us
  transfers between devices with their start and end apart: 4, of which 4 were waited for; matrix products, arithmetic and copies ran while one was open for 13% of the time, Pallas kernels for 0%

profile of v13, /device:TPU:0, one launch (start us, length us, event | category | flops | bytes accessed | tf_op | source)
XLA Modules:
  0.0 96.9 jit_solution(5585129990312009815)
XLA Ops:
  0.0 3.1 %reshape.290 = bf16[64,2,4,8,256]{4,3,2,1,0:T(8,128)(2,1)S(1)} reshape(bf16[64,2,8192]{2,1,0:T(2,128)(2,1)} %param.6) | data formatting | bytes 4194304 | tf_op jit(solution)/shard_map/owner_share_exchange/reshape | solution.py:102
  3.3 1.2 %copy.61 = bf16[8,2,64,256]{3,1,2,0:T(2,128)(2,1)} copy(bf16[8,2,64,256]{3,0,1,2:T(8,128)(2,1)S(1)} %dynamic-slice_bitcast_fusion) | data formatting | bytes 1048576 | tf_op jit(solution)/shard_map/owner_share_exchange/transpose | solution.py:106
  4.5 7.3 %all-to-all-start = ((bf16[8,2,64,256]{3,1,2,0:T(2,128)(2,1)}), bf16[8,2,64,256]{3,1,2,0:T(2,128)(2,1)S(1)}, u32[]{:S(2)}, u32[]{:S(2)}) async-start(bf16[8,2,64,256]{3,1,2,0:T(2,128)(2,1)} %copy.61), calls=%async_computation | async-start | bytes 1048576 | tf_op jit(solution)/shard_map/owner_share_exchange/all_to_all | solution.py:107
  11.8 0.6 fusion.68
  16.0 5.1 %all_gather.3 = s32[3,2,512]{2,1,0:T(2,128)S(1)} all-gather(s32[3,2,128]{2,1,0:T(2,128)S(1)} %pad_add_fusion), channel_id=1, replica_groups=mesh['wide'=8,'narrow'=4] {'narrow'}, dimensions={2}, use_global_device_ids=true | all-gather | bytes 15360 | tf_op jit(solution)/shard_map/all_gather | solution.py:115
  21.2 5.1 %all-to-all-done = bf16[8,2,64,256]{3,1,2,0:T(2,128)(2,1)S(1)} async-done(((bf16[8,2,64,256]{3,1,2,0:T(2,128)(2,1)}), bf16[8,2,64,256]{3,1,2,0:T(2,128)(2,1)S(1)}, u32[]{:S(2)}, u32[]{:S(2)}) %all-to-all-start) | async-done | bytes 524320 | tf_op jit(solution)/shard_map/owner_share_exchange/all_to_all | solution.py:107
  26.6 1.1 %broadcast_in_dim.12 = bf16[8,2,2,64,256]{4,3,2,1,0:T(8,128)(2,1)} broadcast(bf16[2,2,64,256]{3,2,1,0:T(8,128)(2,1)S(1)} %copy.62), dimensions={1,2,3,4} | broadcast | bytes 1179648 | tf_op jit(solution)/shard_map/owner_share_exchange/broadcast_in_dim | solution.py:111
  27.7 3.6 %all-to-all-start.1 = ((bf16[8,2,2,64,256]{4,3,2,1,0:T(8,128)(2,1)}), bf16[8,2,2,64,256]{4,3,2,1,0:T(8,128)(2,1)S(1)}, u32[]{:S(2)}, u32[]{:S(2)}) async-start(bf16[8,2,2,64,256]{4,3,2,1,0:T(8,128)(2,1)} %broadcast_in_dim.12), calls=%async_computation.1 | async-start | bytes 2097152 | tf_op jit(solution)/shard_map/owner_share_exchange/all_to_all | solution.py:112
  31.3 0.3 fusion.64
  31.7 0.5 fusion.60
  32.2 1.4 %constant_dynamic-slice_fusion.2 = bf16[64,2,2048]{2,1,0:T(2,128)(2,1)S(1)} fusion(bf16[64,2,8192]{2,1,0:T(2,128)(2,1)} %param.6, s32[]{:T(128)} %select_n.124), kind=kLoop, calls=%fused_computation.123 | loop fusion | bytes 1048580 | tf_op jit(solution)/shard_map/dynamic_slice | solution.py:97
  33.6 2.7 %add_convert_fusion = (bf16[32,64,512]{2,1,0:T(8,128)(2,1)}, bf16[32,64,512]{2,1,0:T(8,128)(2,1)S(1)}) fusion(f32[64,512]{1,0:T(8,128)S(1)} %get-tuple-element.43, f32[32,512]{1,0:T(8,128)S(1)} %get-tuple-element.41, f32[64,512]{1,0:T(8,128)S(1)} %get-tuple-element.42, f32[32,512]{1,0:T(8,128)S(1)} %get-tuple-element.40), kind=kLoop, calls=%fused_computation.20 | loop fusion | flops 8388608 | bytes 4587520 | tf_op jit(solution)/shard_map/lag_product/convert_element_type | solution.py:32
  36.3 3.3 %fusion.23 = bf16[512,2,2048]{2,0,1:T(8,128)(2,1)} fusion(s32[512]{0:T(512)S(1)} %bitcast.135, bf16[8,8,2,2048]{3,2,1,0:T(2,128)(2,1)S(1)} %bitcast.116), kind=kOutput, calls=%fused_computation.45 | convolution fusion | flops 268468224 | bytes 4720640 | tf_op jit(solution)/shard_map/cross_spectra/dot_general | solution.py:42
  39.6 3.3 %fusion.25 = bf16[512,2,2048]{2,0,1:T(8,128)(2,1)} fusion(s32[512]{0:T(512)S(1)} %bitcast.134, bf16[8,8,2,2048]{3,2,1,0:T(2,128)(2,1)S(1)} %bitcast.117), kind=kOutput, calls=%fused_computation.47 | convolution fusion | flops 268468224 | bytes 4720640 | tf_op jit(solution)/shard_map/cross_spectra/dot_general | solution.py:42
  42.9 14.4 %all-to-all-done.1 = bf16[8,2,2,64,256]{4,3,2,1,0:T(8,128)(2,1)S(1)} async-done(((bf16[8,2,2,64,256]{4,3,2,1,0:T(8,128)(2,1)}), bf16[8,2,2,64,256]{4,3,2,1,0:T(8,128)(2,1)S(1)}, u32[]{:S(2)}, u32[]{:S(2)}) %all-to-all-start.1) | async-done | bytes 1048608 | tf_op jit(solution)/shard_map/owner_share_exchange/all_to_all | solution.py:112
  57.4 0.8 fusion.34
  58.2 0.8 fusion.35
  58.9 0.8 fusion.32
  59.7 1.3 %copy-done = bf16[512,2,2048]{2,0,1:T(8,128)(2,1)S(1)} copy-done((bf16[512,2,2048]{2,0,1:T(8,128)(2,1)S(1)}, bf16[512,2,2048]{2,0,1:T(8,128)(2,1)}, u32[]{:S(2)}) %copy-start) | copy-done | bytes 4194328
  61.0 5.3 %fusion.11 = (bf16[512,2048]{1,0:T(8,128)(2,1)S(1)}, bf16[512,2048]{1,0:T(8,128)(2,1)S(1)}, bf16[512,2048]{1,0:T(8,128)(2,1)S(1)}, bf16[512,2048]{1,0:T(8,128)(2,1)S(1)}) fusion(bf16[512,2048]{1,0:T(8,128)(2,1)S(1)} %fusion.32, f32[2048]{0:T(1024)S(1)} %dynamic-slice-done, bf16[512,2,2048]{2,0,1:T(8,128)(2,1)S(1)} %copy-done, ...), kind=kOutput, calls=%fused_computation.19 | convolution fusion | flops 163610624 | bytes 23341056 | tf_op jit(solution)/shard_map/cross_spectra/dot_general | solution.py:50
  66.3 0.7 fusion.28
  67.0 0.7 fusion.29
  67.8 0.8 reduce-precision_convert_fusion
  68.6 0.9 reduce-precision_convert_fusion.1
  69.5 0.6 copy-done.2
  70.2 1.3 %fusion.18 = f32[512,512]{1,0:T(8,128)S(1)} fusion(bf16[2048,512]{1,0:T(8,128)(2,1)S(1)} %bitcast.124, bf16[256,2048]{1,0:T(8,128)(2,1)S(1)} %get-tuple-element.20, bf16[256,2048]{1,0:T(8,128)(2,1)S(1)} %get-tuple-element.19), kind=kOutput, calls=%fused_computation.38 | convolution fusion | flops 1077936128 | bytes 5242880 | tf_op jit(solution)/shard_map/lag_product/dot_general | solution.py:67
  71.4 1.3 %fusion.14 = f32[512,512]{1,0:T(8,128)S(1)} fusion(bf16[2048,512]{1,0:T(8,128)(2,1)S(1)} %bitcast.123, bf16[256,2048]{1,0:T(8,128)(2,1)S(1)} %get-tuple-element.23, bf16[256,2048]{1,0:T(8,128)(2,1)S(1)} %get-tuple-element.21), kind=kOutput, calls=%fused_computation.34 | convolution fusion | flops 1077936128 | bytes 5242880 | tf_op jit(solution)/shard_map/lag_product/dot_general | solution.py:67
  73.2 1.9 %collective-permute-done = f32[2,2,64,512]{3,2,0,1:T(8,128)S(1)} collective-permute-done((f32[2,2,64,512]{3,2,0,1:T(8,128)S(1)}, f32[2,2,64,512]{3,2,0,1:T(8,128)S(1)}, u32[]{:S(2)}, u32[]{:S(2)}) %collective-permute-start) | collective-permute-done | bytes 524320 | tf_op jit(solution)/shard_map/bin_exchange/ppermute | solution.py:81
  75.3 1.6 %collective-permute-start.1 = (f32[2,1,64,512]{3,2,0,1:T(8,128)S(1)}, f32[2,1,64,512]{3,2,0,1:T(8,128)S(1)}, u32[]{:S(2)}, u32[]{:S(2)}) collective-permute-start(f32[2,1,64,512]{3,2,0,1:T(8,128)S(1)} %select_bitcast_fusion.1), channel_id=1, source_target_pairs={{0,2},{1,3},{2,0},{3,1},{4,6},{5,7},{6,4},{7,5},{8,10},{9,11},{10,... | collective-permute-start | bytes 786440 | tf_op jit(solution)/shard_map/bin_exchange/ppermute | solution.py:81
  76.9 6.9 %collective-permute-done.1 = f32[2,1,64,512]{3,2,0,1:T(8,128)S(1)} collective-permute-done((f32[2,1,64,512]{3,2,0,1:T(8,128)S(1)}, f32[2,1,64,512]{3,2,0,1:T(8,128)S(1)}, u32[]{:S(2)}, u32[]{:S(2)}) %collective-permute-start.1) | collective-permute-done | bytes 262176 | tf_op jit(solution)/shard_map/bin_exchange/ppermute | solution.py:81
  83.8 12.0 %all_to_all.28 = f32[2,8,8,512]{3,2,0,1:T(8,128)S(1)} all-to-all(f32[2,8,8,512]{3,2,0,1:T(8,128)S(1)} %copy.67), channel_id=1, replica_groups=mesh['wide'=8,'narrow'=4] {'wide'}, dimensions={1} | all-to-all | bytes 524288 | tf_op jit(solution)/shard_map/bin_exchange/all_to_all | solution.py:153
  96.2 0.7 maximum_multiply_fusion
  (37 shorter events, 1.7 us)
Async XLA Ops:
  3.2 8.6 %copy-start.3 = (s32[2]{0:T(128)S(1)}, s32[2]{0:T(128)}, u32[]{:S(2)}) copy-start(s32[2]{0:T(128)} %param.8) | copy-start | bytes 28
  3.2 12.8 %copy-start.4 = (s32[1,2,128]{2,1,0:T(2,128)S(1)}, s32[1,2,128]{2,1,0:T(2,128)}, u32[]{:S(2)}) copy-start(s32[1,2,128]{2,1,0:T(2,128)} %param.11) | copy-start | bytes 3076
  3.2 12.8 %copy-start.5 = (s32[1,2,128]{2,1,0:T(2,128)S(1)}, s32[1,2,128]{2,1,0:T(2,128)}, u32[]{:S(2)}) copy-start(s32[1,2,128]{2,1,0:T(2,128)} %param.10) | copy-start | bytes 3076
  3.2 12.8 %copy-start.6 = (s32[1,2,128]{2,1,0:T(2,128)S(1)}, s32[1,2,128]{2,1,0:T(2,128)}, u32[]{:S(2)}) copy-start(s32[1,2,128]{2,1,0:T(2,128)} %param.9) | copy-start | bytes 3076
  4.5 21.8 %all-to-all-start = ((bf16[8,2,64,256]{3,1,2,0:T(2,128)(2,1)}), bf16[8,2,64,256]{3,1,2,0:T(2,128)(2,1)S(1)}, u32[]{:S(2)}, u32[]{:S(2)}) async-start(bf16[8,2,64,256]{3,1,2,0:T(2,128)(2,1)} %copy.61), calls=%async_computation | async-start | bytes 1048576 | tf_op jit(solution)/shard_map/owner_share_exchange/all_to_all | solution.py:107
  27.7 29.6 %all-to-all-start.1 = ((bf16[8,2,2,64,256]{4,3,2,1,0:T(8,128)(2,1)}), bf16[8,2,2,64,256]{4,3,2,1,0:T(8,128)(2,1)S(1)}, u32[]{:S(2)}, u32[]{:S(2)}) async-start(bf16[8,2,2,64,256]{4,3,2,1,0:T(8,128)(2,1)} %broadcast_in_dim.12), calls=%async_computation.1 | async-start | bytes 2097152 | tf_op jit(solution)/shard_map/owner_share_exchange/all_to_all | solution.py:112
  57.3 2.4 %copy-start.1 = (bf16[512,2,2048]{2,0,1:T(8,128)(2,1)S(1)}, bf16[512,2,2048]{2,0,1:T(8,128)(2,1)}, u32[]{:S(2)}) copy-start(bf16[512,2,2048]{2,0,1:T(8,128)(2,1)} %fusion.25) | copy-start | bytes 12582916
  58.1 2.8 %copy-start = (bf16[512,2,2048]{2,0,1:T(8,128)(2,1)S(1)}, bf16[512,2,2048]{2,0,1:T(8,128)(2,1)}, u32[]{:S(2)}) copy-start(bf16[512,2,2048]{2,0,1:T(8,128)(2,1)} %fusion.23) | copy-start | bytes 12582916
  58.2 2.8 %dynamic-slice-start = ((f32[8192]{0:T(1024)}, s32[]{:T(128)}), f32[2048]{0:T(1024)S(1)}, s32[]{:S(2)}) async-start(f32[8192]{0:T(1024)} %param.7, s32[]{:T(128)} %select_n.124), calls=%async_computation.3 | async-start | bytes 16896 | tf_op jit(solution)/shard_map/dynamic_slice | solution.py:98
  68.6 1.6 %copy-start.2 = (bf16[32,64,512]{2,1,0:T(8,128)(2,1)S(1)}, bf16[32,64,512]{2,1,0:T(8,128)(2,1)}, u32[]{:S(2)}) copy-start(bf16[32,64,512]{2,1,0:T(8,128)(2,1)} %get-tuple-element.28) | copy-start | bytes 6291460
  73.1 2.0 %collective-permute-start = (f32[2,2,64,512]{3,2,0,1:T(8,128)S(1)}, f32[2,2,64,512]{3,2,0,1:T(8,128)S(1)}, u32[]{:S(2)}, u32[]{:S(2)}) collective-permute-start(f32[2,2,64,512]{3,2,0,1:T(8,128)S(1)} %select_bitcast_fusion), channel_id=1, source_target_pairs={{0,1},{1,0},{2,3},{3,2},{4,5},{5,4},{6,7},{7,6},{8,9},{9,8},{10,11... | collective-permute-start | bytes 1572872 | tf_op jit(solution)/shard_map/bin_exchange/ppermute | solution.py:81
  75.3 8.4 %collective-permute-start.1 = (f32[2,1,64,512]{3,2,0,1:T(8,128)S(1)}, f32[2,1,64,512]{3,2,0,1:T(8,128)S(1)}, u32[]{:S(2)}, u32[]{:S(2)}) collective-permute-start(f32[2,1,64,512]{3,2,0,1:T(8,128)S(1)} %select_bitcast_fusion.1), channel_id=1, source_target_pairs={{0,2},{1,3},{2,0},{3,1},{4,6},{5,7},{6,4},{7,5},{8,10},{9,11},{10,... | collective-permute-start | bytes 786440 | tf_op jit(solution)/shard_map/bin_exchange/ppermute | solution.py:81

commit v14 on v12

--- a/solution.py
+++ b/solution.py
@@ -90,7 +90,6 @@
     block_rows, _, freqs = spectra.shape
     steps = owners.shape[0]
     share = freqs // narrow_count
-    piece = share // wide_count
     total_bins = narrow_count * wide_count * GW
     first_freq = narrow_index * share
 
@@ -98,13 +97,17 @@
     gain = lax.dynamic_slice_in_dim(band_gain, first_freq, share, axis=0)
 
     with jax.named_scope("owner_share_exchange"):
-        outgoing = near.reshape(block_rows, 2, wide_count, piece).transpose(2, 1, 0, 3)
+        group = block_rows // wide_count
+        outgoing = near.reshape(wide_count, group, 2, share)
         arrived = lax.all_to_all(outgoing, "wide", split_axis=0, concat_axis=0, tiled=True)
         chosen = jnp.stack(
             [lax.dynamic_index_in_dim(arrived, owners[s], 0, keepdims=False) for s in range(steps)]
         )
         copies = jnp.broadcast_to(chosen[None], (wide_count,) + chosen.shape)
-        gathered = lax.all_to_all(copies, "wide", split_axis=0, concat_axis=4, tiled=True)
+        gathered = lax.all_to_all(copies, "wide", split_axis=0, concat_axis=0, tiled=True)
+        far_blocks = [
+            gathered[:, s].reshape(block_rows, 2, share) for s in range(steps)
+        ]
 
     ids = jnp.stack([pair_near[0], pair_far[0], stack_bins[0]])
     ids = lax.all_gather(ids, "narrow", axis=2, tiled=True)
@@ -115,8 +118,8 @@
         parts = []
         for s in range(steps):
             near_rows = select_rows(near, near_ids[s])
-            far_real = pick_rows(gathered[0, s, 0], far_ids[s])
-            far_imag = pick_rows(gathered[0, s, 1], far_ids[s])
+            far_real = pick_rows(far_blocks[s][:, 0], far_ids[s])
+            far_imag = pick_rows(far_blocks[s][:, 1], far_ids[s])
             parts.append(
                 lax.optimization_barrier(cross_rows(near_rows, far_real, far_imag, gain))
             )

time: 99.1 us -> 99.3 us (level)
    all_to_all x1 -> x0, local copies, waits for them, and re-layouts: 1.49 us -> none  [local(): lax.all_to_all(copies, 'wide', split_axis=0, concat_axis=4, tiled=True)]
    slice x0 -> x3, local copies, waits for them, and re-layouts: none -> 1.38 us  [local(): gathered[:, s].reshape(block_rows, 2, share)]
    unnamed x18 -> x19, local copies, waits for them, and re-layouts: 3.3 us -> 4.02 us
where the time goes in v14:
time: 99.3 us; the launch traced here: 98.8 us
  waiting for transfers between devices  28.7 us (29%)
  matrix products  19.7 us (20%)
  blocking collectives  16.8 us (17%)
  starting transfers between devices  13.1 us (13%)
  local copies, waits for them, and re-layouts  8.9 us (9%)
  other arithmetic  7.41 us (7%)
  between operations  4.17 us (4%)
    all_to_all x1, blocking collectives, local(): lax.all_to_all(owned, 'wide', split_axis=1, concat_axis=1, tiled=True)  11.7 us
    all_to_all x1, waiting for transfers between devices, local(): lax.all_to_all(outgoing, 'wide', split_axis=0, concat_axis=0, tiled=True)  9.9 us
    all_to_all x1, waiting for transfers between devices, local(): lax.all_to_all(copies, 'wide', split_axis=0, concat_axis=0, tiled=True)  9.72 us
    ppermute x2, waiting for transfers between devices, halving_sum(): parts = keep + lax.ppermute(send, axis, pairs)  9.1 us
    dot_general x4, matrix products, pick_rows(): return jnp.dot(picker, block, preferred_element_type=jnp.bfloat16)  7.39 us
    all_to_all x1, starting transfers between devices, local(): lax.all_to_all(outgoing, 'wide', split_axis=0, concat_axis=0, tiled=True)  7.28 us
    dot_general x2, matrix products, select_rows(): chosen = jnp.dot(picker, flat_block, preferred_element_type=jnp.bfloat16)  6.55 us
    all_gather x1, blocking collectives, local(): ids = lax.all_gather(ids, 'narrow', axis=2, tiled=True)  5.1 us
  transfers between devices with their start and end apart: 4, of which 4 were waited for; matrix products, arithmetic and copies ran while one was open for 12% of the time, Pallas kernels for 0%

profile of v14, /device:TPU:0, one launch (start us, length us, event | category | flops | bytes accessed | tf_op | source)
XLA Modules:
  0.0 98.8 jit_solution(10955524658712924086)
XLA Ops:
  0.0 1.6 %copy-done = bf16[64,2,8192]{2,1,0:T(2,128)(2,1)S(1)} copy-done((bf16[64,2,8192]{2,1,0:T(2,128)(2,1)S(1)}, bf16[64,2,8192]{2,1,0:T(2,128)(2,1)}, u32[]{:S(2)}) %copy-start) | copy-done | bytes 2097176
  2.3 0.8 copy.73
  3.1 7.3 %all-to-all-start = ((bf16[8,8,2,2048]{3,1,2,0:T(8,128)(2,1)}), bf16[8,8,2,2048]{3,1,2,0:T(8,128)(2,1)S(1)}, u32[]{:S(2)}, u32[]{:S(2)}) async-start(bf16[8,8,2,2048]{3,1,2,0:T(8,128)(2,1)} %copy.73), calls=%async_computation | async-start | bytes 1048576 | tf_op jit(solution)/shard_map/owner_share_exchange/all_to_all | solution.py:102
  10.4 0.6 fusion.69
  15.0 9.9 %all-to-all-done = bf16[8,8,2,2048]{3,1,2,0:T(8,128)(2,1)S(1)} async-done(((bf16[8,8,2,2048]{3,1,2,0:T(8,128)(2,1)}), bf16[8,8,2,2048]{3,1,2,0:T(8,128)(2,1)S(1)}, u32[]{:S(2)}, u32[]{:S(2)}) %all-to-all-start) | async-done | bytes 524320 | tf_op jit(solution)/shard_map/owner_share_exchange/all_to_all | solution.py:102
  24.9 1.1 %broadcast_in_dim.12 = bf16[8,2,8,2,2048]{4,2,3,1,0:T(8,128)(2,1)} broadcast(bf16[2,8,2,2048]{3,1,2,0:T(8,128)(2,1)S(1)} %pad_maximum_fusion.1), dimensions={1,2,3,4} | broadcast | bytes 1179648 | tf_op jit(solution)/shard_map/owner_share_exchange/broadcast_in_dim | solution.py:106
  26.0 4.3 %all-to-all-start.1 = ((bf16[8,2,8,2,2048]{4,2,3,1,0:T(8,128)(2,1)}), bf16[8,2,8,2,2048]{4,2,3,1,0:T(8,128)(2,1)}, u32[]{:S(2)}, u32[]{:S(2)}) async-start(bf16[8,2,8,2,2048]{4,2,3,1,0:T(8,128)(2,1)} %broadcast_in_dim.12), calls=%async_computation.1 | async-start | bytes 2097152 | tf_op jit(solution)/shard_map/owner_share_exchange/all_to_all | solution.py:107
  30.3 5.1 %all_gather.3 = s32[3,2,512]{2,1,0:T(2,128)S(1)} all-gather(s32[3,2,128]{2,1,0:T(2,128)S(1)} %pad_add_fusion), channel_id=1, replica_groups=mesh['wide'=8,'narrow'=4] {'narrow'}, dimensions={2}, use_global_device_ids=true | all-gather | bytes 15360 | tf_op jit(solution)/shard_map/all_gather | solution.py:113
  36.3 3.3 %add_convert_fusion = (bf16[32,64,512]{2,1,0:T(8,128)(2,1)}, bf16[32,64,512]{2,1,0:T(8,128)(2,1)}) fusion(f32[64,512]{1,0:T(8,128)S(1)} %get-tuple-element.45, f32[32,512]{1,0:T(8,128)S(1)} %get-tuple-element.43, f32[64,512]{1,0:T(8,128)S(1)} %get-tuple-element.44, f32[32,512]{1,0:T(8,128)S(1)} %get-tuple-element.42), kind=kLoop, calls=%fused_computation.20 | loop fusion | flops 8388608 | bytes 4587520 | tf_op jit(solution)/shard_map/lag_product/convert_element_type | solution.py:32
  39.6 3.2 %fusion.23 = bf16[512,2,2048]{2,0,1:T(8,128)(2,1)} fusion(s32[512]{0:T(512)S(1)} %bitcast.134, bf16[8,8,2,2048]{3,2,1,0:T(2,128)(2,1)S(1)} %bitcast.115), kind=kOutput, calls=%fused_computation.45 | convolution fusion | flops 268468224 | bytes 4720640 | tf_op jit(solution)/shard_map/cross_spectra/dot_general | solution.py:42
  42.9 3.3 %fusion.25 = bf16[512,2,2048]{2,0,1:T(8,128)(2,1)} fusion(s32[512]{0:T(512)S(1)} %bitcast.133, bf16[8,8,2,2048]{3,2,1,0:T(2,128)(2,1)S(1)} %bitcast.116), kind=kOutput, calls=%fused_computation.47 | convolution fusion | flops 268468224 | bytes 4720640 | tf_op jit(solution)/shard_map/cross_spectra/dot_general | solution.py:42
  46.2 9.7 %all-to-all-done.1 = bf16[8,2,8,2,2048]{4,2,3,1,0:T(8,128)(2,1)} async-done(((bf16[8,2,8,2,2048]{4,2,3,1,0:T(8,128)(2,1)}), bf16[8,2,8,2,2048]{4,2,3,1,0:T(8,128)(2,1)}, u32[]{:S(2)}, u32[]{:S(2)}) %all-to-all-start.1) | async-done | bytes 1048608 | tf_op jit(solution)/shard_map/owner_share_exchange/all_to_all | solution.py:107
  55.9 1.3 %fusion.67 = (bf16[8,1,8,2,2048]{4,2,3,1,0:T(8,128)(2,1)S(1)}, bf16[8,1,8,2,2048]{4,2,3,1,0:T(8,128)(2,1)S(1)}) fusion(bf16[8,2,8,2,2048]{4,2,3,1,0:T(8,128)(2,1)} %all-to-all-done.1), kind=kLoop, calls=%fused_computation.129 | loop fusion | bytes 2097152 | tf_op jit(solution)/shard_map/owner_share_exchange/slice | solution.py:109
  57.3 0.8 fusion.34
  58.0 0.8 fusion.35
  58.9 0.8 fusion.32
  59.6 1.3 %copy-done.1 = bf16[512,2,2048]{2,0,1:T(8,128)(2,1)S(1)} copy-done((bf16[512,2,2048]{2,0,1:T(8,128)(2,1)S(1)}, bf16[512,2,2048]{2,0,1:T(8,128)(2,1)}, u32[]{:S(2)}) %copy-start.1) | copy-done | bytes 4194328
  60.9 5.1 %fusion.11 = (bf16[512,2048]{1,0:T(8,128)(2,1)S(1)}, bf16[512,2048]{1,0:T(8,128)(2,1)S(1)}, bf16[512,2048]{1,0:T(8,128)(2,1)S(1)}, bf16[512,2048]{1,0:T(8,128)(2,1)S(1)}) fusion(bf16[512,2048]{1,0:T(8,128)(2,1)S(1)} %fusion.32, f32[2048]{0:T(1024)S(1)} %dynamic-slice-done, bf16[512,2,2048]{2,0,1:T(8,128)(2,1)S(1)} %copy-done.1, ...), kind=kOutput, calls=%fused_computation.19 | convolution fusion | flops 163610624 | bytes 23341056 | tf_op jit(solution)/shard_map/cross_spectra/dot_general | solution.py:50
  66.0 0.7 fusion.28
  66.8 0.7 fusion.29
  67.5 0.8 reduce-precision_convert_fusion
  68.4 0.9 reduce-precision_convert_fusion.1
  69.3 0.6 copy-done.4
  70.0 1.2 %fusion.18 = f32[512,512]{1,0:T(8,128)S(1)} fusion(bf16[2048,512]{1,0:T(8,128)(2,1)S(1)} %bitcast.118, bf16[256,2048]{1,0:T(8,128)(2,1)S(1)} %get-tuple-element.20, bf16[256,2048]{1,0:T(8,128)(2,1)S(1)} %get-tuple-element.19), kind=kOutput, calls=%fused_computation.38 | convolution fusion | flops 1077936128 | bytes 5242880 | tf_op jit(solution)/shard_map/lag_product/dot_general | solution.py:67
  71.5 1.3 %fusion.14 = f32[512,512]{1,0:T(8,128)S(1)} fusion(bf16[2048,512]{1,0:T(8,128)(2,1)S(1)} %bitcast.117, bf16[256,2048]{1,0:T(8,128)(2,1)S(1)} %get-tuple-element.23, bf16[256,2048]{1,0:T(8,128)(2,1)S(1)} %get-tuple-element.21), kind=kOutput, calls=%fused_computation.34 | convolution fusion | flops 1077936128 | bytes 5242880 | tf_op jit(solution)/shard_map/lag_product/dot_general | solution.py:67
  73.1 0.9 select_bitcast_fusion
  74.0 2.2 %collective-permute-done = f32[2,2,64,512]{3,2,0,1:T(8,128)} collective-permute-done((f32[2,2,64,512]{3,2,0,1:T(8,128)}, f32[2,2,64,512]{3,2,0,1:T(8,128)}, u32[]{:S(2)}, u32[]{:S(2)}) %collective-permute-start) | collective-permute-done | bytes 524320 | tf_op jit(solution)/shard_map/bin_exchange/ppermute | solution.py:81
  76.3 1.2 %fusion.27 = f32[2,1,2,64,512]{4,3,0,2,1:T(8,128)S(1)} fusion(f32[2,2,64,512]{3,2,0,1:T(8,128)} %collective-permute-done, f32[2,2,1,64,512]{4,3,2,1,0:T(8,128)S(1)} %get-tuple-element.25, f32[2,2,1,64,512]{4,3,2,1,0:T(8,128)S(1)} %get-tuple-element.24, pred[]{:T(512)S(6)} %eq.131), kind=kLoop, calls=%fused_computation.54 | loop fusion | flops 262144 | bytes 2097153 | tf_op jit(solution)/shard_map/bin_exchange/reshape | solution.py:76
  77.5 1.6 %collective-permute-start.1 = (f32[2,1,64,512]{3,2,0,1:T(8,128)S(1)}, f32[2,1,64,512]{3,2,0,1:T(8,128)S(1)}, u32[]{:S(2)}, u32[]{:S(2)}) collective-permute-start(f32[2,1,64,512]{3,2,0,1:T(8,128)S(1)} %select_bitcast_fusion.1), channel_id=1, source_target_pairs={{0,2},{1,3},{2,0},{3,1},{4,6},{5,7},{6,4},{7,5},{8,10},{9,11},{10,... | collective-permute-start | bytes 786440 | tf_op jit(solution)/shard_map/bin_exchange/ppermute | solution.py:81
  79.1 6.9 %collective-permute-done.1 = f32[2,1,64,512]{3,2,0,1:T(8,128)S(1)} collective-permute-done((f32[2,1,64,512]{3,2,0,1:T(8,128)S(1)}, f32[2,1,64,512]{3,2,0,1:T(8,128)S(1)}, u32[]{:S(2)}, u32[]{:S(2)}) %collective-permute-start.1) | collective-permute-done | bytes 262176 | tf_op jit(solution)/shard_map/bin_exchange/ppermute | solution.py:81
  86.0 11.7 %all_to_all.15 = f32[2,8,8,512]{3,2,0,1:T(8,128)S(1)} all-to-all(f32[2,8,8,512]{3,2,0,1:T(8,128)S(1)} %copy.79), channel_id=1, replica_groups=mesh['wide'=8,'narrow'=4] {'wide'}, dimensions={1} | all-to-all | bytes 524288 | tf_op jit(solution)/shard_map/bin_exchange/all_to_all | solution.py:151
  98.1 0.7 maximum_multiply_fusion
  (41 shorter events, 2.8 us)
Async XLA Ops:
  0.0 1.6 %copy-start = (bf16[64,2,8192]{2,1,0:T(2,128)(2,1)S(1)}, bf16[64,2,8192]{2,1,0:T(2,128)(2,1)}, u32[]{:S(2)}) copy-start(bf16[64,2,8192]{2,1,0:T(2,128)(2,1)} %param.6) | copy-start | bytes 6291460
  1.6 8.8 %copy-start.5 = (s32[2]{0:T(128)S(1)}, s32[2]{0:T(128)}, u32[]{:S(2)}) copy-start(s32[2]{0:T(128)} %param.8) | copy-start | bytes 28
  1.6 13.3 %copy-start.6 = (s32[1,2,128]{2,1,0:T(2,128)S(1)}, s32[1,2,128]{2,1,0:T(2,128)}, u32[]{:S(2)}) copy-start(s32[1,2,128]{2,1,0:T(2,128)} %param.11) | copy-start | bytes 3076
  1.6 13.4 %copy-start.7 = (s32[1,2,128]{2,1,0:T(2,128)S(1)}, s32[1,2,128]{2,1,0:T(2,128)}, u32[]{:S(2)}) copy-start(s32[1,2,128]{2,1,0:T(2,128)} %param.10) | copy-start | bytes 3076
  1.6 13.4 %copy-start.8 = (s32[1,2,128]{2,1,0:T(2,128)S(1)}, s32[1,2,128]{2,1,0:T(2,128)}, u32[]{:S(2)}) copy-start(s32[1,2,128]{2,1,0:T(2,128)} %param.9) | copy-start | bytes 3076
  3.1 21.8 %all-to-all-start = ((bf16[8,8,2,2048]{3,1,2,0:T(8,128)(2,1)}), bf16[8,8,2,2048]{3,1,2,0:T(8,128)(2,1)S(1)}, u32[]{:S(2)}, u32[]{:S(2)}) async-start(bf16[8,8,2,2048]{3,1,2,0:T(8,128)(2,1)} %copy.73), calls=%async_computation | async-start | bytes 1048576 | tf_op jit(solution)/shard_map/owner_share_exchange/all_to_all | solution.py:102
  26.0 29.9 %all-to-all-start.1 = ((bf16[8,2,8,2,2048]{4,2,3,1,0:T(8,128)(2,1)}), bf16[8,2,8,2,2048]{4,2,3,1,0:T(8,128)(2,1)}, u32[]{:S(2)}, u32[]{:S(2)}) async-start(bf16[8,2,8,2,2048]{4,2,3,1,0:T(8,128)(2,1)} %broadcast_in_dim.12), calls=%async_computation.1 | async-start | bytes 2097152 | tf_op jit(solution)/shard_map/owner_share_exchange/all_to_all | solution.py:107
  57.2 2.4 %copy-start.2 = (bf16[512,2,2048]{2,0,1:T(8,128)(2,1)S(1)}, bf16[512,2,2048]{2,0,1:T(8,128)(2,1)}, u32[]{:S(2)}) copy-start(bf16[512,2,2048]{2,0,1:T(8,128)(2,1)} %fusion.25) | copy-start | bytes 12582916
  58.0 2.9 %copy-start.1 = (bf16[512,2,2048]{2,0,1:T(8,128)(2,1)S(1)}, bf16[512,2,2048]{2,0,1:T(8,128)(2,1)}, u32[]{:S(2)}) copy-start(bf16[512,2,2048]{2,0,1:T(8,128)(2,1)} %fusion.23) | copy-start | bytes 12582916
  58.8 2.1 %dynamic-slice-start = ((f32[8192]{0:T(1024)}, s32[]{:T(128)}), f32[2048]{0:T(1024)S(1)}, s32[]{:S(2)}) async-start(f32[8192]{0:T(1024)} %param.7, s32[]{:T(128)} %select_n.120), calls=%async_computation.3 | async-start | bytes 16896 | tf_op jit(solution)/shard_map/dynamic_slice | solution.py:97
  68.4 1.6 %copy-start.4 = (bf16[32,64,512]{2,1,0:T(8,128)(2,1)S(1)}, bf16[32,64,512]{2,1,0:T(8,128)(2,1)}, u32[]{:S(2)}) copy-start(bf16[32,64,512]{2,1,0:T(8,128)(2,1)} %get-tuple-element.30) | copy-start | bytes 6291460
  70.0 1.6 %copy-start.3 = (bf16[32,64,512]{2,1,0:T(8,128)(2,1)S(1)}, bf16[32,64,512]{2,1,0:T(8,128)(2,1)}, u32[]{:S(2)}) copy-start(bf16[32,64,512]{2,1,0:T(8,128)(2,1)} %get-tuple-element.31) | copy-start | bytes 6291460
  74.0 2.3 %collective-permute-start = (f32[2,2,64,512]{3,2,0,1:T(8,128)}, f32[2,2,64,512]{3,2,0,1:T(8,128)}, u32[]{:S(2)}, u32[]{:S(2)}) collective-permute-start(f32[2,2,64,512]{3,2,0,1:T(8,128)} %select_bitcast_fusion), channel_id=1, source_target_pairs={{0,1},{1,0},{2,3},{3,2},{4,5},{5,4},{6,7},{7,6},{8,9},{9,8},{10,11... | collective-permute-start | bytes 1572872 | tf_op jit(solution)/shard_map/bin_exchange/ppermute | solution.py:81
  77.5 8.4 %collective-permute-start.1 = (f32[2,1,64,512]{3,2,0,1:T(8,128)S(1)}, f32[2,1,64,512]{3,2,0,1:T(8,128)S(1)}, u32[]{:S(2)}, u32[]{:S(2)}) collective-permute-start(f32[2,1,64,512]{3,2,0,1:T(8,128)S(1)} %select_bitcast_fusion.1), channel_id=1, source_target_pairs={{0,2},{1,3},{2,0},{3,1},{4,6},{5,7},{6,4},{7,5},{8,10},{9,11},{10,... | collective-permute-start | bytes 786440 | tf_op jit(solution)/shard_map/bin_exchange/ppermute | solution.py:81

commit v15 on v13

--- a/solution.py
+++ b/solution.py
@@ -69,16 +69,11 @@
 
 
 def halving_sum(parts, axis, count):
-    index = lax.axis_index(axis)
     bit = 1
     while bit < count:
-        mine = (index // bit) % 2
         paired = parts.reshape((parts.shape[0], parts.shape[1] // 2, 2) + parts.shape[2:])
-        first, second = paired[:, :, 0], paired[:, :, 1]
-        keep = jnp.where(mine == 0, first, second)
-        send = jnp.where(mine == 0, second, first)
         pairs = [(i, i ^ bit) for i in range(count)]
-        parts = keep + lax.ppermute(send, axis, pairs)
+        parts = paired[:, :, 0] + lax.ppermute(paired[:, :, 1], axis, pairs)
         bit *= 2
     return parts[:, 0]
 
@@ -114,7 +109,9 @@
     ids = jnp.stack([pair_near[0], pair_far[0], stack_bins[0]])
     ids = lax.all_gather(ids, "narrow", axis=2, tiled=True)
     near_ids, far_ids = ids[0], ids[1]
-    bin_ids = ids[2]
+    bins_each = wide_count * GW
+    owner_slot = lax.bitwise_xor(ids[2] // bins_each, narrow_index)
+    bin_ids = owner_slot * bins_each + ids[2] % bins_each
 
     with jax.named_scope("cross_spectra"):
         parts = []

time: 97.3 us -> 97.2 us (level)
    unnamed x14 -> x15, local copies, waits for them, and re-layouts: 1.92 us -> 1.96 us
where the time goes in v15:
time: 97.2 us; the launch traced here: 96.7 us
  waiting for transfers between devices  27.8 us (29%)
  matrix products  19.9 us (20%)
  blocking collectives  17.1 us (18%)
  starting transfers between devices  12.5 us (13%)
  local copies, waits for them, and re-layouts  10.2 us (10%)
  other arithmetic  4.93 us (5%)
  between operations  4.24 us (4%)
    all_to_all x1, waiting for transfers between devices, local(): lax.all_to_all(copies, 'wide', split_axis=0, concat_axis=4, tiled=True)  14.3 us
    all_to_all x1, blocking collectives, local(): lax.all_to_all(owned, 'wide', split_axis=1, concat_axis=1, tiled=True)  12 us
    ppermute x2, waiting for transfers between devices, halving_sum(): parts = paired[:, :, 0] + lax.ppermute(paired[:, :, 1], axis, pairs)  8.77 us
    dot_general x4, matrix products, pick_rows(): return jnp.dot(picker, block, preferred_element_type=jnp.bfloat16)  7.58 us
    all_to_all x1, starting transfers between devices, local(): lax.all_to_all(outgoing, 'wide', split_axis=0, concat_axis=0, tiled=True)  7.28 us
    dot_general x2, matrix products, select_rows(): chosen = jnp.dot(picker, flat_block, preferred_element_type=jnp.bfloat16)  6.57 us
    all_gather x1, blocking collectives, local(): ids = lax.all_gather(ids, 'narrow', axis=2, tiled=True)  5.1 us
    all_to_all x1, waiting for transfers between devices, local(): lax.all_to_all(outgoing, 'wide', split_axis=0, concat_axis=0, tiled=True)  4.68 us
  transfers between devices with their start and end apart: 4, of which 4 were waited for; matrix products, arithmetic and copies ran while one was open for 13% of the time, Pallas kernels for 0%

profile of v15, /device:TPU:0, one launch (start us, length us, event | category | flops | bytes accessed | tf_op | source)
XLA Modules:
  0.0 96.7 jit_solution(882625682532334154)
XLA Ops:
  0.0 3.1 %reshape.238 = bf16[64,2,4,8,256]{4,3,2,1,0:T(8,128)(2,1)S(1)} reshape(bf16[64,2,8192]{2,1,0:T(2,128)(2,1)} %param.6) | data formatting | bytes 4194304 | tf_op jit(solution)/shard_map/owner_share_exchange/reshape | solution.py:97
  3.3 1.2 %copy.37 = bf16[8,2,64,256]{3,1,2,0:T(2,128)(2,1)} copy(bf16[8,2,64,256]{3,0,1,2:T(8,128)(2,1)S(1)} %dynamic-slice_bitcast_fusion) | data formatting | bytes 1048576 | tf_op jit(solution)/shard_map/owner_share_exchange/transpose | solution.py:101
  4.5 7.3 %all-to-all-start = ((bf16[8,2,64,256]{3,1,2,0:T(2,128)(2,1)}), bf16[8,2,64,256]{3,1,2,0:T(2,128)(2,1)S(1)}, u32[]{:S(2)}, u32[]{:S(2)}) async-start(bf16[8,2,64,256]{3,1,2,0:T(2,128)(2,1)} %copy.37), calls=%async_computation | async-start | bytes 1048576 | tf_op jit(solution)/shard_map/owner_share_exchange/all_to_all | solution.py:102
  11.8 0.6 fusion.72
  16.4 5.1 %all_gather.3 = s32[3,2,512]{2,1,0:T(2,128)S(1)} all-gather(s32[3,2,128]{2,1,0:T(2,128)S(1)} %pad_add_fusion), channel_id=1, replica_groups=mesh['wide'=8,'narrow'=4] {'narrow'}, dimensions={2}, use_global_device_ids=true | all-gather | bytes 15360 | tf_op jit(solution)/shard_map/all_gather | solution.py:110
  21.6 4.7 %all-to-all-done = bf16[8,2,64,256]{3,1,2,0:T(2,128)(2,1)S(1)} async-done(((bf16[8,2,64,256]{3,1,2,0:T(2,128)(2,1)}), bf16[8,2,64,256]{3,1,2,0:T(2,128)(2,1)S(1)}, u32[]{:S(2)}, u32[]{:S(2)}) %all-to-all-start) | async-done | bytes 524320 | tf_op jit(solution)/shard_map/owner_share_exchange/all_to_all | solution.py:102
  26.6 1.1 %broadcast_in_dim.12 = bf16[8,2,2,64,256]{4,3,2,1,0:T(8,128)(2,1)} broadcast(bf16[2,2,64,256]{3,2,1,0:T(8,128)(2,1)S(1)} %copy.38), dimensions={1,2,3,4} | broadcast | bytes 1179648 | tf_op jit(solution)/shard_map/owner_share_exchange/broadcast_in_dim | solution.py:106
  27.7 3.6 %all-to-all-start.1 = ((bf16[8,2,2,64,256]{4,3,2,1,0:T(8,128)(2,1)}), bf16[8,2,2,64,256]{4,3,2,1,0:T(8,128)(2,1)S(1)}, u32[]{:S(2)}, u32[]{:S(2)}) async-start(bf16[8,2,2,64,256]{4,3,2,1,0:T(8,128)(2,1)} %broadcast_in_dim.12), calls=%async_computation.1 | async-start | bytes 2097152 | tf_op jit(solution)/shard_map/owner_share_exchange/all_to_all | solution.py:107
  31.3 0.3 fusion.66
  31.7 0.5 fusion.62
  32.2 1.4 %constant_dynamic-slice_fusion.2 = bf16[64,2,2048]{2,1,0:T(2,128)(2,1)S(1)} fusion(bf16[64,2,8192]{2,1,0:T(2,128)(2,1)} %param.6, s32[]{:T(128)} %select_n.65), kind=kLoop, calls=%fused_computation.132 | loop fusion | bytes 1048580 | tf_op jit(solution)/shard_map/dynamic_slice | solution.py:92
  33.6 2.7 %add_convert_fusion = (bf16[32,64,512]{2,1,0:T(8,128)(2,1)}, bf16[32,64,512]{2,1,0:T(8,128)(2,1)S(1)}) fusion(f32[64,512]{1,0:T(8,128)S(1)} %get-tuple-element.43, f32[32,512]{1,0:T(8,128)S(1)} %get-tuple-element.41, f32[64,512]{1,0:T(8,128)S(1)} %get-tuple-element.42, f32[32,512]{1,0:T(8,128)S(1)} %get-tuple-element.40), kind=kLoop, calls=%fused_computation.20 | loop fusion | flops 8388608 | bytes 4587520 | tf_op jit(solution)/shard_map/lag_product/convert_element_type | solution.py:32
  36.3 3.3 %fusion.23 = bf16[512,2,2048]{2,0,1:T(8,128)(2,1)} fusion(s32[512]{0:T(512)S(1)} %bitcast.145, bf16[8,8,2,2048]{3,2,1,0:T(2,128)(2,1)S(1)} %bitcast.125), kind=kOutput, calls=%fused_computation.45 | convolution fusion | flops 268468224 | bytes 4720640 | tf_op jit(solution)/shard_map/cross_spectra/dot_general | solution.py:42
  39.6 3.3 %fusion.25 = bf16[512,2,2048]{2,0,1:T(8,128)(2,1)} fusion(s32[512]{0:T(512)S(1)} %bitcast.144, bf16[8,8,2,2048]{3,2,1,0:T(2,128)(2,1)S(1)} %bitcast.126), kind=kOutput, calls=%fused_computation.47 | convolution fusion | flops 268468224 | bytes 4720640 | tf_op jit(solution)/shard_map/cross_spectra/dot_general | solution.py:42
  42.9 14.3 %all-to-all-done.1 = bf16[8,2,2,64,256]{4,3,2,1,0:T(8,128)(2,1)S(1)} async-done(((bf16[8,2,2,64,256]{4,3,2,1,0:T(8,128)(2,1)}), bf16[8,2,2,64,256]{4,3,2,1,0:T(8,128)(2,1)S(1)}, u32[]{:S(2)}, u32[]{:S(2)}) %all-to-all-start.1) | async-done | bytes 1048608 | tf_op jit(solution)/shard_map/owner_share_exchange/all_to_all | solution.py:107
  57.4 0.8 fusion.37
  58.2 0.8 fusion.38
  58.9 0.8 fusion.35
  59.7 1.3 %copy-done = bf16[512,2,2048]{2,0,1:T(8,128)(2,1)S(1)} copy-done((bf16[512,2,2048]{2,0,1:T(8,128)(2,1)S(1)}, bf16[512,2,2048]{2,0,1:T(8,128)(2,1)}, u32[]{:S(2)}) %copy-start) | copy-done | bytes 4194328
  61.0 5.3 %fusion.11 = (bf16[512,2048]{1,0:T(8,128)(2,1)S(1)}, bf16[512,2048]{1,0:T(8,128)(2,1)S(1)}, bf16[512,2048]{1,0:T(8,128)(2,1)S(1)}, bf16[512,2048]{1,0:T(8,128)(2,1)S(1)}) fusion(bf16[512,2048]{1,0:T(8,128)(2,1)S(1)} %fusion.35, f32[2048]{0:T(1024)S(1)} %dynamic-slice-done, bf16[512,2,2048]{2,0,1:T(8,128)(2,1)S(1)} %copy-done, ...), kind=kOutput, calls=%fused_computation.19 | convolution fusion | flops 163610624 | bytes 23341056 | tf_op jit(solution)/shard_map/cross_spectra/dot_general | solution.py:50
  66.3 0.7 fusion.29
  67.0 0.7 fusion.30
  67.8 0.8 reduce-precision_convert_fusion
  68.6 0.9 reduce-precision_convert_fusion.1
  69.6 0.6 copy-done.2
  70.2 1.3 %fusion.18 = f32[512,512]{1,0:T(8,128)S(1)} fusion(bf16[2048,512]{1,0:T(8,128)(2,1)S(1)} %bitcast.133, bf16[256,2048]{1,0:T(8,128)(2,1)S(1)} %get-tuple-element.20, bf16[256,2048]{1,0:T(8,128)(2,1)S(1)} %get-tuple-element.19), kind=kOutput, calls=%fused_computation.38 | convolution fusion | flops 1077936128 | bytes 5242880 | tf_op jit(solution)/shard_map/lag_product/dot_general | solution.py:67
  71.5 1.3 %fusion.14 = f32[512,512]{1,0:T(8,128)S(1)} fusion(bf16[2048,512]{1,0:T(8,128)(2,1)S(1)} %bitcast.132, bf16[256,2048]{1,0:T(8,128)(2,1)S(1)} %get-tuple-element.23, bf16[256,2048]{1,0:T(8,128)(2,1)S(1)} %get-tuple-element.21), kind=kOutput, calls=%fused_computation.34 | convolution fusion | flops 1077936128 | bytes 5242880 | tf_op jit(solution)/shard_map/lag_product/dot_general | solution.py:67
  73.1 1.9 %collective-permute-done = f32[2,2,64,512]{3,2,0,1:T(8,128)S(1)} collective-permute-done((f32[2,2,64,512]{3,2,0,1:T(8,128)S(1)}, f32[2,2,64,512]{3,2,0,1:T(8,128)S(1)}, u32[]{:S(2)}, u32[]{:S(2)}) %collective-permute-start) | collective-permute-done | bytes 524320 | tf_op jit(solution)/shard_map/bin_exchange/ppermute | solution.py:76
  75.2 1.5 %collective-permute-start.1 = (f32[2,1,64,512]{3,2,0,1:T(8,128)S(1)}, f32[2,1,64,512]{3,2,0,1:T(8,128)S(1)}, u32[]{:S(2)}, u32[]{:S(2)}) collective-permute-start(f32[2,1,64,512]{3,2,0,1:T(8,128)S(1)} %slice_bitcast_fusion.4), channel_id=1, source_target_pairs={{0,2},{1,3},{2,0},{3,1},{4,6},{5,7},{6,4},{7,5},{8,10},{9,11},{10,... | collective-permute-start | bytes 786440 | tf_op jit(solution)/shard_map/bin_exchange/ppermute | solution.py:76
  76.7 6.9 %collective-permute-done.1 = f32[2,1,64,512]{3,2,0,1:T(8,128)S(1)} collective-permute-done((f32[2,1,64,512]{3,2,0,1:T(8,128)S(1)}, f32[2,1,64,512]{3,2,0,1:T(8,128)S(1)}, u32[]{:S(2)}, u32[]{:S(2)}) %collective-permute-start.1) | collective-permute-done | bytes 262176 | tf_op jit(solution)/shard_map/bin_exchange/ppermute | solution.py:76
  83.6 12.0 %all_to_all.28 = f32[2,8,8,512]{3,2,0,1:T(8,128)S(1)} all-to-all(f32[2,8,8,512]{3,2,0,1:T(8,128)S(1)} %copy.43), channel_id=1, replica_groups=mesh['wide'=8,'narrow'=4] {'wide'}, dimensions={1} | all-to-all | bytes 524288 | tf_op jit(solution)/shard_map/bin_exchange/all_to_all | solution.py:150
  96.0 0.7 maximum_multiply_fusion
  (39 shorter events, 1.5 us)
Async XLA Ops:
  3.2 8.6 %copy-start.3 = (s32[2]{0:T(128)S(1)}, s32[2]{0:T(128)}, u32[]{:S(2)}) copy-start(s32[2]{0:T(128)} %param.8) | copy-start | bytes 28
  3.2 9.3 %copy-start.4 = (s32[1,2,128]{2,1,0:T(2,128)S(1)}, s32[1,2,128]{2,1,0:T(2,128)}, u32[]{:S(2)}) copy-start(s32[1,2,128]{2,1,0:T(2,128)} %param.11) | copy-start | bytes 3076
  3.2 9.3 %copy-start.5 = (s32[1,2,128]{2,1,0:T(2,128)S(1)}, s32[1,2,128]{2,1,0:T(2,128)}, u32[]{:S(2)}) copy-start(s32[1,2,128]{2,1,0:T(2,128)} %param.10) | copy-start | bytes 3076
  3.2 9.3 %copy-start.6 = (s32[1,2,128]{2,1,0:T(2,128)S(1)}, s32[1,2,128]{2,1,0:T(2,128)}, u32[]{:S(2)}) copy-start(s32[1,2,128]{2,1,0:T(2,128)} %param.9) | copy-start | bytes 3076
  4.5 21.8 %all-to-all-start = ((bf16[8,2,64,256]{3,1,2,0:T(2,128)(2,1)}), bf16[8,2,64,256]{3,1,2,0:T(2,128)(2,1)S(1)}, u32[]{:S(2)}, u32[]{:S(2)}) async-start(bf16[8,2,64,256]{3,1,2,0:T(2,128)(2,1)} %copy.37), calls=%async_computation | async-start | bytes 1048576 | tf_op jit(solution)/shard_map/owner_share_exchange/all_to_all | solution.py:102
  27.7 29.6 %all-to-all-start.1 = ((bf16[8,2,2,64,256]{4,3,2,1,0:T(8,128)(2,1)}), bf16[8,2,2,64,256]{4,3,2,1,0:T(8,128)(2,1)S(1)}, u32[]{:S(2)}, u32[]{:S(2)}) async-start(bf16[8,2,2,64,256]{4,3,2,1,0:T(8,128)(2,1)} %broadcast_in_dim.12), calls=%async_computation.1 | async-start | bytes 2097152 | tf_op jit(solution)/shard_map/owner_share_exchange/all_to_all | solution.py:107
  57.3 2.4 %copy-start.1 = (bf16[512,2,2048]{2,0,1:T(8,128)(2,1)S(1)}, bf16[512,2,2048]{2,0,1:T(8,128)(2,1)}, u32[]{:S(2)}) copy-start(bf16[512,2,2048]{2,0,1:T(8,128)(2,1)} %fusion.25) | copy-start | bytes 12582916
  58.2 2.8 %copy-start = (bf16[512,2,2048]{2,0,1:T(8,128)(2,1)S(1)}, bf16[512,2,2048]{2,0,1:T(8,128)(2,1)}, u32[]{:S(2)}) copy-start(bf16[512,2,2048]{2,0,1:T(8,128)(2,1)} %fusion.23) | copy-start | bytes 12582916
  58.2 2.8 %dynamic-slice-start = ((f32[8192]{0:T(1024)}, s32[]{:T(128)}), f32[2048]{0:T(1024)S(1)}, s32[]{:S(2)}) async-start(f32[8192]{0:T(1024)} %param.7, s32[]{:T(128)} %select_n.65), calls=%async_computation.3 | async-start | bytes 16896 | tf_op jit(solution)/shard_map/dynamic_slice | solution.py:93
  68.6 1.6 %copy-start.2 = (bf16[32,64,512]{2,1,0:T(8,128)(2,1)S(1)}, bf16[32,64,512]{2,1,0:T(8,128)(2,1)}, u32[]{:S(2)}) copy-start(bf16[32,64,512]{2,1,0:T(8,128)(2,1)} %get-tuple-element.28) | copy-start | bytes 6291460
  73.1 2.0 %collective-permute-start = (f32[2,2,64,512]{3,2,0,1:T(8,128)S(1)}, f32[2,2,64,512]{3,2,0,1:T(8,128)S(1)}, u32[]{:S(2)}, u32[]{:S(2)}) collective-permute-start(f32[2,2,64,512]{3,2,0,1:T(8,128)S(1)} %bitcast.136), channel_id=1, source_target_pairs={{0,1},{1,0},{2,3},{3,2},{4,5},{5,4},{6,7},{7,6},{8,9},{9,8},{10,11... | collective-permute-start | bytes 1572872 | tf_op jit(solution)/shard_map/bin_exchange/ppermute | solution.py:76
  75.2 8.4 %collective-permute-start.1 = (f32[2,1,64,512]{3,2,0,1:T(8,128)S(1)}, f32[2,1,64,512]{3,2,0,1:T(8,128)S(1)}, u32[]{:S(2)}, u32[]{:S(2)}) collective-permute-start(f32[2,1,64,512]{3,2,0,1:T(8,128)S(1)} %slice_bitcast_fusion.4), channel_id=1, source_target_pairs={{0,2},{1,3},{2,0},{3,1},{4,6},{5,7},{6,4},{7,5},{8,10},{9,11},{10,... | collective-permute-start | bytes 786440 | tf_op jit(solution)/shard_map/bin_exchange/ppermute | solution.py:76

commit v16 on v14

--- a/solution.py
+++ b/solution.py
@@ -69,16 +69,11 @@
 
 
 def halving_sum(parts, axis, count):
-    index = lax.axis_index(axis)
     bit = 1
     while bit < count:
-        mine = (index // bit) % 2
         paired = parts.reshape((parts.shape[0], parts.shape[1] // 2, 2) + parts.shape[2:])
-        first, second = paired[:, :, 0], paired[:, :, 1]
-        keep = jnp.where(mine == 0, first, second)
-        send = jnp.where(mine == 0, second, first)
         pairs = [(i, i ^ bit) for i in range(count)]
-        parts = keep + lax.ppermute(send, axis, pairs)
+        parts = paired[:, :, 0] + lax.ppermute(paired[:, :, 1], axis, pairs)
         bit *= 2
     return parts[:, 0]
 
@@ -112,7 +107,9 @@
     ids = jnp.stack([pair_near[0], pair_far[0], stack_bins[0]])
     ids = lax.all_gather(ids, "narrow", axis=2, tiled=True)
     near_ids, far_ids = ids[0], ids[1]
-    bin_ids = ids[2]
+    bins_each = wide_count * GW
+    owner_slot = lax.bitwise_xor(ids[2] // bins_each, narrow_index)
+    bin_ids = owner_slot * bins_each + ids[2] % bins_each
 
     with jax.named_scope("cross_spectra"):
         parts = []

time: 99.3 us -> 97.1 us (0.978)
  other arithmetic: 7.41 us -> 5.34 us
    all_to_all x1, waiting for transfers between devices: 9.72 us -> 14.8 us  [local(): lax.all_to_all(copies, 'wide', split_axis=0, concat_axis=0, tiled=True)]
    all_to_all x1, waiting for transfers between devices: 9.9 us -> 4.9 us  [local(): lax.all_to_all(outgoing, 'wide', split_axis=0, concat_axis=0, tiled=True)]
    reshape x1, other arithmetic: 1.19 us -> 0.08 us  [halving_sum(): parts.reshape((parts.shape[0], parts.shape[1] // 2, 2) + parts.shape[2:])]
    unnamed x19 -> x20, local copies, waits for them, and re-layouts: 4.02 us -> 4.05 us
where the time goes in v16:
time: 97.1 us; the launch traced here: 96.7 us
  waiting for transfers between devices  28.5 us (29%)
  matrix products  19.9 us (20%)
  blocking collectives  16.8 us (17%)
  starting transfers between devices  13.2 us (14%)
  local copies, waits for them, and re-layouts  8.92 us (9%)
  other arithmetic  5.34 us (5%)
  between operations  4.08 us (4%)
    all_to_all x1, waiting for transfers between devices, local(): lax.all_to_all(copies, 'wide', split_axis=0, concat_axis=0, tiled=True)  14.8 us
    all_to_all x1, blocking collectives, local(): lax.all_to_all(owned, 'wide', split_axis=1, concat_axis=1, tiled=True)  11.7 us
    ppermute x2, waiting for transfers between devices, halving_sum(): parts = paired[:, :, 0] + lax.ppermute(paired[:, :, 1], axis, pairs)  8.74 us
    dot_general x4, matrix products, pick_rows(): return jnp.dot(picker, block, preferred_element_type=jnp.bfloat16)  7.57 us
    all_to_all x1, starting transfers between devices, local(): lax.all_to_all(outgoing, 'wide', split_axis=0, concat_axis=0, tiled=True)  7.28 us
    dot_general x2, matrix products, select_rows(): chosen = jnp.dot(picker, flat_block, preferred_element_type=jnp.bfloat16)  6.56 us
    all_gather x1, blocking collectives, local(): ids = lax.all_gather(ids, 'narrow', axis=2, tiled=True)  5.1 us
    all_to_all x1, waiting for transfers between devices, local(): lax.all_to_all(outgoing, 'wide', split_axis=0, concat_axis=0, tiled=True)  4.9 us
  transfers between devices with their start and end apart: 4, of which 4 were waited for; matrix products, arithmetic and copies ran while one was open for 12% of the time, Pallas kernels for 0%

profile of v16, /device:TPU:0, one launch (start us, length us, event | category | flops | bytes accessed | tf_op | source)
XLA Modules:
  0.0 96.7 jit_solution(1296350197899818073)
XLA Ops:
  0.0 1.6 %copy-done = bf16[64,2,8192]{2,1,0:T(2,128)(2,1)S(1)} copy-done((bf16[64,2,8192]{2,1,0:T(2,128)(2,1)S(1)}, bf16[64,2,8192]{2,1,0:T(2,128)(2,1)}, u32[]{:S(2)}) %copy-start) | copy-done | bytes 2097176
  1.6 0.5 constant_dynamic-slice_fusion.2
  2.3 0.8 copy.43
  3.1 7.3 %all-to-all-start = ((bf16[8,8,2,2048]{3,1,2,0:T(8,128)(2,1)}), bf16[8,8,2,2048]{3,1,2,0:T(8,128)(2,1)S(1)}, u32[]{:S(2)}, u32[]{:S(2)}) async-start(bf16[8,8,2,2048]{3,1,2,0:T(8,128)(2,1)} %copy.43), calls=%async_computation | async-start | bytes 1048576 | tf_op jit(solution)/shard_map/owner_share_exchange/all_to_all | solution.py:97
  10.4 0.6 fusion.73
  14.8 5.1 %all_gather.3 = s32[3,2,512]{2,1,0:T(2,128)S(1)} all-gather(s32[3,2,128]{2,1,0:T(2,128)S(1)} %pad_add_fusion), channel_id=1, replica_groups=mesh['wide'=8,'narrow'=4] {'narrow'}, dimensions={2}, use_global_device_ids=true | all-gather | bytes 15360 | tf_op jit(solution)/shard_map/all_gather | solution.py:108
  20.0 4.9 %all-to-all-done = bf16[8,8,2,2048]{3,1,2,0:T(8,128)(2,1)S(1)} async-done(((bf16[8,8,2,2048]{3,1,2,0:T(8,128)(2,1)}), bf16[8,8,2,2048]{3,1,2,0:T(8,128)(2,1)S(1)}, u32[]{:S(2)}, u32[]{:S(2)}) %all-to-all-start) | async-done | bytes 524320 | tf_op jit(solution)/shard_map/owner_share_exchange/all_to_all | solution.py:97
  24.9 1.1 %broadcast_in_dim.12 = bf16[8,2,8,2,2048]{4,2,3,1,0:T(8,128)(2,1)} broadcast(bf16[2,8,2,2048]{3,1,2,0:T(8,128)(2,1)S(1)} %pad_maximum_fusion.1), dimensions={1,2,3,4} | broadcast | bytes 1179648 | tf_op jit(solution)/shard_map/owner_share_exchange/broadcast_in_dim | solution.py:101
  26.0 4.2 %all-to-all-start.1 = ((bf16[8,2,8,2,2048]{4,2,3,1,0:T(8,128)(2,1)}), bf16[8,2,8,2,2048]{4,2,3,1,0:T(8,128)(2,1)}, u32[]{:S(2)}, u32[]{:S(2)}) async-start(bf16[8,2,8,2,2048]{4,2,3,1,0:T(8,128)(2,1)} %broadcast_in_dim.12), calls=%async_computation.1 | async-start | bytes 2097152 | tf_op jit(solution)/shard_map/owner_share_exchange/all_to_all | solution.py:102
  30.7 0.5 fusion.62
  31.2 3.3 %add_convert_fusion = (bf16[32,64,512]{2,1,0:T(8,128)(2,1)}, bf16[32,64,512]{2,1,0:T(8,128)(2,1)}) fusion(f32[64,512]{1,0:T(8,128)S(1)} %get-tuple-element.45, f32[32,512]{1,0:T(8,128)S(1)} %get-tuple-element.43, f32[64,512]{1,0:T(8,128)S(1)} %get-tuple-element.44, f32[32,512]{1,0:T(8,128)S(1)} %get-tuple-element.42), kind=kLoop, calls=%fused_computation.20 | loop fusion | flops 8388608 | bytes 4587520 | tf_op jit(solution)/shard_map/lag_product/convert_element_type | solution.py:32
  34.5 3.2 %fusion.23 = bf16[512,2,2048]{2,0,1:T(8,128)(2,1)} fusion(s32[512]{0:T(512)S(1)} %bitcast.144, bf16[8,8,2,2048]{3,2,1,0:T(2,128)(2,1)S(1)} %bitcast.124), kind=kOutput, calls=%fused_computation.45 | convolution fusion | flops 268468224 | bytes 4720640 | tf_op jit(solution)/shard_map/cross_spectra/dot_general | solution.py:42
  37.8 3.3 %fusion.25 = bf16[512,2,2048]{2,0,1:T(8,128)(2,1)} fusion(s32[512]{0:T(512)S(1)} %bitcast.143, bf16[8,8,2,2048]{3,2,1,0:T(2,128)(2,1)S(1)} %bitcast.125), kind=kOutput, calls=%fused_computation.47 | convolution fusion | flops 268468224 | bytes 4720640 | tf_op jit(solution)/shard_map/cross_spectra/dot_general | solution.py:42
  41.1 14.8 %all-to-all-done.1 = bf16[8,2,8,2,2048]{4,2,3,1,0:T(8,128)(2,1)} async-done(((bf16[8,2,8,2,2048]{4,2,3,1,0:T(8,128)(2,1)}), bf16[8,2,8,2,2048]{4,2,3,1,0:T(8,128)(2,1)}, u32[]{:S(2)}, u32[]{:S(2)}) %all-to-all-start.1) | async-done | bytes 1048608 | tf_op jit(solution)/shard_map/owner_share_exchange/all_to_all | solution.py:102
  55.9 1.3 %fusion.70 = (bf16[8,1,8,2,2048]{4,2,3,1,0:T(8,128)(2,1)S(1)}, bf16[8,1,8,2,2048]{4,2,3,1,0:T(8,128)(2,1)S(1)}) fusion(bf16[8,2,8,2,2048]{4,2,3,1,0:T(8,128)(2,1)} %all-to-all-done.1), kind=kLoop, calls=%fused_computation.138 | loop fusion | bytes 2097152 | tf_op jit(solution)/shard_map/owner_share_exchange/slice | solution.py:104
  57.3 0.8 fusion.37
  58.0 0.8 fusion.38
  58.9 0.8 fusion.35
  59.6 1.3 %copy-done.1 = bf16[512,2,2048]{2,0,1:T(8,128)(2,1)S(1)} copy-done((bf16[512,2,2048]{2,0,1:T(8,128)(2,1)S(1)}, bf16[512,2,2048]{2,0,1:T(8,128)(2,1)}, u32[]{:S(2)}) %copy-start.1) | copy-done | bytes 4194328
  60.9 5.3 %fusion.11 = (bf16[512,2048]{1,0:T(8,128)(2,1)S(1)}, bf16[512,2048]{1,0:T(8,128)(2,1)S(1)}, bf16[512,2048]{1,0:T(8,128)(2,1)S(1)}, bf16[512,2048]{1,0:T(8,128)(2,1)S(1)}) fusion(bf16[512,2048]{1,0:T(8,128)(2,1)S(1)} %fusion.35, f32[2048]{0:T(1024)S(1)} %dynamic-slice-done, bf16[512,2,2048]{2,0,1:T(8,128)(2,1)S(1)} %copy-done.1, ...), kind=kOutput, calls=%fused_computation.19 | convolution fusion | flops 163610624 | bytes 23341056 | tf_op jit(solution)/shard_map/cross_spectra/dot_general | solution.py:50
  66.2 0.7 fusion.29
  67.0 0.7 fusion.30
  67.7 0.8 reduce-precision_convert_fusion
  68.5 0.9 reduce-precision_convert_fusion.1
  69.5 0.6 copy-done.4
  70.1 1.2 %fusion.18 = f32[512,512]{1,0:T(8,128)S(1)} fusion(bf16[2048,512]{1,0:T(8,128)(2,1)S(1)} %bitcast.127, bf16[256,2048]{1,0:T(8,128)(2,1)S(1)} %get-tuple-element.20, bf16[256,2048]{1,0:T(8,128)(2,1)S(1)} %get-tuple-element.19), kind=kOutput, calls=%fused_computation.38 | convolution fusion | flops 1077936128 | bytes 5242880 | tf_op jit(solution)/shard_map/lag_product/dot_general | solution.py:67
  71.7 1.3 %fusion.14 = f32[512,512]{1,0:T(8,128)S(1)} fusion(bf16[2048,512]{1,0:T(8,128)(2,1)S(1)} %bitcast.126, bf16[256,2048]{1,0:T(8,128)(2,1)S(1)} %get-tuple-element.23, bf16[256,2048]{1,0:T(8,128)(2,1)S(1)} %get-tuple-element.21), kind=kOutput, calls=%fused_computation.34 | convolution fusion | flops 1077936128 | bytes 5242880 | tf_op jit(solution)/shard_map/lag_product/dot_general | solution.py:67
  73.4 1.9 %collective-permute-done = f32[2,2,64,512]{3,2,0,1:T(8,128)S(1)} collective-permute-done((f32[2,2,64,512]{3,2,0,1:T(8,128)S(1)}, f32[2,2,64,512]{3,2,0,1:T(8,128)S(1)}, u32[]{:S(2)}, u32[]{:S(2)}) %collective-permute-start) | collective-permute-done | bytes 524320 | tf_op jit(solution)/shard_map/bin_exchange/ppermute | solution.py:76
  75.4 1.6 %collective-permute-start.1 = (f32[2,1,64,512]{3,2,0,1:T(8,128)S(1)}, f32[2,1,64,512]{3,2,0,1:T(8,128)S(1)}, u32[]{:S(2)}, u32[]{:S(2)}) collective-permute-start(f32[2,1,64,512]{3,2,0,1:T(8,128)S(1)} %slice_bitcast_fusion.4), channel_id=1, source_target_pairs={{0,2},{1,3},{2,0},{3,1},{4,6},{5,7},{6,4},{7,5},{8,10},{9,11},{10,... | collective-permute-start | bytes 786440 | tf_op jit(solution)/shard_map/bin_exchange/ppermute | solution.py:76
  76.9 6.8 %collective-permute-done.1 = f32[2,1,64,512]{3,2,0,1:T(8,128)S(1)} collective-permute-done((f32[2,1,64,512]{3,2,0,1:T(8,128)S(1)}, f32[2,1,64,512]{3,2,0,1:T(8,128)S(1)}, u32[]{:S(2)}, u32[]{:S(2)}) %collective-permute-start.1) | collective-permute-done | bytes 262176 | tf_op jit(solution)/shard_map/bin_exchange/ppermute | solution.py:76
  83.8 11.7 %all_to_all.15 = f32[2,8,8,512]{3,2,0,1:T(8,128)S(1)} all-to-all(f32[2,8,8,512]{3,2,0,1:T(8,128)S(1)} %copy.49), channel_id=1, replica_groups=mesh['wide'=8,'narrow'=4] {'wide'}, dimensions={1} | all-to-all | bytes 524288 | tf_op jit(solution)/shard_map/bin_exchange/all_to_all | solution.py:148
  96.0 0.7 maximum_multiply_fusion
  (43 shorter events, 1.9 us)
Async XLA Ops:
  0.0 1.6 %copy-start = (bf16[64,2,8192]{2,1,0:T(2,128)(2,1)S(1)}, bf16[64,2,8192]{2,1,0:T(2,128)(2,1)}, u32[]{:S(2)}) copy-start(bf16[64,2,8192]{2,1,0:T(2,128)(2,1)} %param.6) | copy-start | bytes 6291460
  1.6 8.8 %copy-start.5 = (s32[2]{0:T(128)S(1)}, s32[2]{0:T(128)}, u32[]{:S(2)}) copy-start(s32[2]{0:T(128)} %param.8) | copy-start | bytes 28
  1.6 13.2 %copy-start.6 = (s32[1,2,128]{2,1,0:T(2,128)S(1)}, s32[1,2,128]{2,1,0:T(2,128)}, u32[]{:S(2)}) copy-start(s32[1,2,128]{2,1,0:T(2,128)} %param.11) | copy-start | bytes 3076
  1.6 13.2 %copy-start.7 = (s32[1,2,128]{2,1,0:T(2,128)S(1)}, s32[1,2,128]{2,1,0:T(2,128)}, u32[]{:S(2)}) copy-start(s32[1,2,128]{2,1,0:T(2,128)} %param.10) | copy-start | bytes 3076
  1.6 13.2 %copy-start.8 = (s32[1,2,128]{2,1,0:T(2,128)S(1)}, s32[1,2,128]{2,1,0:T(2,128)}, u32[]{:S(2)}) copy-start(s32[1,2,128]{2,1,0:T(2,128)} %param.9) | copy-start | bytes 3076
  3.1 21.8 %all-to-all-start = ((bf16[8,8,2,2048]{3,1,2,0:T(8,128)(2,1)}), bf16[8,8,2,2048]{3,1,2,0:T(8,128)(2,1)S(1)}, u32[]{:S(2)}, u32[]{:S(2)}) async-start(bf16[8,8,2,2048]{3,1,2,0:T(8,128)(2,1)} %copy.43), calls=%async_computation | async-start | bytes 1048576 | tf_op jit(solution)/shard_map/owner_share_exchange/all_to_all | solution.py:97
  26.0 29.9 %all-to-all-start.1 = ((bf16[8,2,8,2,2048]{4,2,3,1,0:T(8,128)(2,1)}), bf16[8,2,8,2,2048]{4,2,3,1,0:T(8,128)(2,1)}, u32[]{:S(2)}, u32[]{:S(2)}) async-start(bf16[8,2,8,2,2048]{4,2,3,1,0:T(8,128)(2,1)} %broadcast_in_dim.12), calls=%async_computation.1 | async-start | bytes 2097152 | tf_op jit(solution)/shard_map/owner_share_exchange/all_to_all | solution.py:102
  57.2 2.4 %copy-start.2 = (bf16[512,2,2048]{2,0,1:T(8,128)(2,1)S(1)}, bf16[512,2,2048]{2,0,1:T(8,128)(2,1)}, u32[]{:S(2)}) copy-start(bf16[512,2,2048]{2,0,1:T(8,128)(2,1)} %fusion.25) | copy-start | bytes 12582916
  58.0 2.9 %copy-start.1 = (bf16[512,2,2048]{2,0,1:T(8,128)(2,1)S(1)}, bf16[512,2,2048]{2,0,1:T(8,128)(2,1)}, u32[]{:S(2)}) copy-start(bf16[512,2,2048]{2,0,1:T(8,128)(2,1)} %fusion.23) | copy-start | bytes 12582916
  58.8 2.1 %dynamic-slice-start = ((f32[8192]{0:T(1024)}, s32[]{:T(128)}), f32[2048]{0:T(1024)S(1)}, s32[]{:S(2)}) async-start(f32[8192]{0:T(1024)} %param.7, s32[]{:T(128)} %select_n.61), calls=%async_computation.3 | async-start | bytes 16896 | tf_op jit(solution)/shard_map/dynamic_slice | solution.py:92
  68.5 1.6 %copy-start.4 = (bf16[32,64,512]{2,1,0:T(8,128)(2,1)S(1)}, bf16[32,64,512]{2,1,0:T(8,128)(2,1)}, u32[]{:S(2)}) copy-start(bf16[32,64,512]{2,1,0:T(8,128)(2,1)} %get-tuple-element.30) | copy-start | bytes 6291460
  70.1 1.6 %copy-start.3 = (bf16[32,64,512]{2,1,0:T(8,128)(2,1)S(1)}, bf16[32,64,512]{2,1,0:T(8,128)(2,1)}, u32[]{:S(2)}) copy-start(bf16[32,64,512]{2,1,0:T(8,128)(2,1)} %get-tuple-element.31) | copy-start | bytes 6291460
  73.3 2.0 %collective-permute-start = (f32[2,2,64,512]{3,2,0,1:T(8,128)S(1)}, f32[2,2,64,512]{3,2,0,1:T(8,128)S(1)}, u32[]{:S(2)}, u32[]{:S(2)}) collective-permute-start(f32[2,2,64,512]{3,2,0,1:T(8,128)S(1)} %bitcast.135), channel_id=1, source_target_pairs={{0,1},{1,0},{2,3},{3,2},{4,5},{5,4},{6,7},{7,6},{8,9},{9,8},{10,11... | collective-permute-start | bytes 1572872 | tf_op jit(solution)/shard_map/bin_exchange/ppermute | solution.py:76
  75.4 8.4 %collective-permute-start.1 = (f32[2,1,64,512]{3,2,0,1:T(8,128)S(1)}, f32[2,1,64,512]{3,2,0,1:T(8,128)S(1)}, u32[]{:S(2)}, u32[]{:S(2)}) collective-permute-start(f32[2,1,64,512]{3,2,0,1:T(8,128)S(1)} %slice_bitcast_fusion.4), channel_id=1, source_target_pairs={{0,2},{1,3},{2,0},{3,1},{4,6},{5,7},{6,4},{7,5},{8,10},{9,11},{10,... | collective-permute-start | bytes 786440 | tf_op jit(solution)/shard_map/bin_exchange/ppermute | solution.py:76

commit v17 on v15

--- a/solution.py
+++ b/solution.py
@@ -71,11 +71,13 @@
 def halving_sum(parts, axis, count):
     bit = 1
     while bit < count:
-        paired = parts.reshape((parts.shape[0], parts.shape[1] // 2, 2) + parts.shape[2:])
         pairs = [(i, i ^ bit) for i in range(count)]
-        parts = paired[:, :, 0] + lax.ppermute(paired[:, :, 1], axis, pairs)
+        parts = [
+            parts[2 * j] + lax.ppermute(parts[2 * j + 1], axis, pairs)
+            for j in range(len(parts) // 2)
+        ]
         bit *= 2
-    return parts[:, 0]
+    return parts[0]
 
 
 def local(spectra, band_gain, owners, pair_near, pair_far, stack_bins):
@@ -137,15 +139,17 @@
 
     with jax.named_scope("lag_product"):
         cosine, sine = lag_halves(first_freq, share, freqs, LAGS)
-        even = split_product(real_sum, cosine)
-        odd = split_product(imag_sum, sine)
-        zero_lag = jnp.sum(real_sum, axis=1, keepdims=True)
         last = jnp.arange(LAGS // 2, dtype=jnp.int32)[None, :] == LAGS // 2 - 1
-        binned = jnp.stack([even + odd, jnp.where(last, zero_lag, even - odd)])
+        slots = []
+        for slot in range(narrow_count):
+            rows = slice(slot * bins_each, (slot + 1) * bins_each)
+            even = split_product(real_sum[rows], cosine)
+            odd = split_product(imag_sum[rows], sine)
+            zero_lag = jnp.sum(real_sum[rows], axis=1, keepdims=True)
+            slots.append(jnp.stack([even + odd, jnp.where(last, zero_lag, even - odd)]))
 
     with jax.named_scope("bin_exchange"):
-        binned = binned.reshape(2, narrow_count, wide_count * GW, LAGS // 2)
-        owned = halving_sum(binned, "narrow", narrow_count)
+        owned = halving_sum(slots, "narrow", narrow_count)
         owned = owned.reshape(2, wide_count, GW, LAGS // 2)
         owned = lax.all_to_all(owned, "wide", split_axis=1, concat_axis=1, tiled=True)
         plus, minus = jnp.sum(owned, axis=1)

time: 97.2 us -> 97.4 us (level)
  waiting for transfers between devices: 27.8 us -> 25.4 us
  matrix products: 19.9 us -> 20.9 us
    ppermute x2 -> x3, waiting for transfers between devices: 8.77 us -> 6.17 us  [halving_sum(): lax.ppermute(parts[2 * j + 1], axis, pairs)]
    dot_general x2 -> x8, matrix products: 2.52 us -> 3.77 us  [split_product(): both = jnp.dot(split, table, preferred_element_type=jnp.float32)]
    another operation x1 -> x7, other arithmetic: 0.07 us -> 1.06 us  [local(): binned = jnp.stack([even + odd, jnp.where(last, zero_lag, even - odd)])]
    ppermute x2 -> x3, starting transfers between devices: 1.61 us -> 2.19 us  [halving_sum(): lax.ppermute(parts[2 * j + 1], axis, pairs)]
    unnamed x15 -> x14, local copies, waits for them, and re-layouts: 1.96 us -> 2.49 us
  transfers between devices with their start and end apart: 4 -> 5, of which waited for: 4 -> 3; matrix products, arithmetic and copies ran while one was open for 13% -> 15% of each run, Pallas kernels for 0% -> 0%
where the time goes in v17:
time: 97.4 us; the launch traced here: 96.9 us
  waiting for transfers between devices  25.4 us (26%)
  matrix products  20.9 us (21%)
  blocking collectives  16.9 us (17%)
  starting transfers between devices  13.1 us (13%)
  local copies, waits for them, and re-layouts  10.7 us (11%)
  other arithmetic  5.66 us (6%)
  between operations  4.2 us (4%)
    all_to_all x1, waiting for transfers between devices, local(): lax.all_to_all(copies, 'wide', split_axis=0, concat_axis=4, tiled=True)  14.4 us
    all_to_all x1, blocking collectives, local(): lax.all_to_all(owned, 'wide', split_axis=1, concat_axis=1, tiled=True)  11.8 us
    dot_general x4, matrix products, pick_rows(): return jnp.dot(picker, block, preferred_element_type=jnp.bfloat16)  7.56 us
    all_to_all x1, starting transfers between devices, local(): lax.all_to_all(outgoing, 'wide', split_axis=0, concat_axis=0, tiled=True)  7.28 us
    dot_general x2, matrix products, select_rows(): chosen = jnp.dot(picker, flat_block, preferred_element_type=jnp.bfloat16)  6.55 us
    ppermute x3, waiting for transfers between devices, halving_sum(): lax.ppermute(parts[2 * j + 1], axis, pairs)  6.17 us
    all_gather x1, blocking collectives, local(): ids = lax.all_gather(ids, 'narrow', axis=2, tiled=True)  5.1 us
    all_to_all x1, waiting for transfers between devices, local(): lax.all_to_all(outgoing, 'wide', split_axis=0, concat_axis=0, tiled=True)  4.81 us
  transfers between devices with their start and end apart: 5, of which 3 were waited for; matrix products, arithmetic and copies ran while one was open for 15% of the time, Pallas kernels for 0%

profile of v17, /device:TPU:0, one launch (start us, length us, event | category | flops | bytes accessed | tf_op | source)
XLA Modules:
  0.0 96.9 jit_solution(9818161287729608164)
XLA Ops:
  0.0 3.1 %reshape.236 = bf16[64,2,4,8,256]{4,3,2,1,0:T(8,128)(2,1)S(1)} reshape(bf16[64,2,8192]{2,1,0:T(2,128)(2,1)} %param.6) | data formatting | bytes 4194304 | tf_op jit(solution)/shard_map/owner_share_exchange/reshape | solution.py:99
  3.3 1.2 %copy.21 = bf16[8,2,64,256]{3,1,2,0:T(2,128)(2,1)} copy(bf16[8,2,64,256]{3,0,1,2:T(8,128)(2,1)S(1)} %dynamic-slice_bitcast_fusion) | data formatting | bytes 1048576 | tf_op jit(solution)/shard_map/owner_share_exchange/transpose | solution.py:103
  4.5 7.3 %all-to-all-start = ((bf16[8,2,64,256]{3,1,2,0:T(2,128)(2,1)}), bf16[8,2,64,256]{3,1,2,0:T(2,128)(2,1)S(1)}, u32[]{:S(2)}, u32[]{:S(2)}) async-start(bf16[8,2,64,256]{3,1,2,0:T(2,128)(2,1)} %copy.21), calls=%async_computation | async-start | bytes 1048576 | tf_op jit(solution)/shard_map/owner_share_exchange/all_to_all | solution.py:104
  11.8 0.6 fusion.104
  16.3 5.1 %all_gather.3 = s32[3,2,512]{2,1,0:T(2,128)S(1)} all-gather(s32[3,2,128]{2,1,0:T(2,128)S(1)} %pad_add_fusion), channel_id=1, replica_groups=mesh['wide'=8,'narrow'=4] {'narrow'}, dimensions={2}, use_global_device_ids=true | all-gather | bytes 15360 | tf_op jit(solution)/shard_map/all_gather | solution.py:112
  21.4 4.8 %all-to-all-done = bf16[8,2,64,256]{3,1,2,0:T(2,128)(2,1)S(1)} async-done(((bf16[8,2,64,256]{3,1,2,0:T(2,128)(2,1)}), bf16[8,2,64,256]{3,1,2,0:T(2,128)(2,1)S(1)}, u32[]{:S(2)}, u32[]{:S(2)}) %all-to-all-start) | async-done | bytes 524320 | tf_op jit(solution)/shard_map/owner_share_exchange/all_to_all | solution.py:104
  26.6 1.1 %broadcast_in_dim.82 = bf16[8,2,2,64,256]{4,3,2,1,0:T(8,128)(2,1)} broadcast(bf16[2,2,64,256]{3,2,1,0:T(8,128)(2,1)S(1)} %copy.22), dimensions={1,2,3,4} | broadcast | bytes 1179648 | tf_op jit(solution)/shard_map/owner_share_exchange/broadcast_in_dim | solution.py:108
  27.7 3.6 %all-to-all-start.1 = ((bf16[8,2,2,64,256]{4,3,2,1,0:T(8,128)(2,1)}), bf16[8,2,2,64,256]{4,3,2,1,0:T(8,128)(2,1)S(1)}, u32[]{:S(2)}, u32[]{:S(2)}) async-start(bf16[8,2,2,64,256]{4,3,2,1,0:T(8,128)(2,1)} %broadcast_in_dim.82), calls=%async_computation.1 | async-start | bytes 2097152 | tf_op jit(solution)/shard_map/owner_share_exchange/all_to_all | solution.py:109
  31.7 0.5 fusion.88
  32.2 1.4 %constant_dynamic-slice_fusion.2 = bf16[64,2,2048]{2,1,0:T(2,128)(2,1)S(1)} fusion(bf16[64,2,8192]{2,1,0:T(2,128)(2,1)} %param.6, s32[]{:T(128)} %select_n.74), kind=kLoop, calls=%fused_computation.184 | loop fusion | bytes 1048580 | tf_op jit(solution)/shard_map/dynamic_slice | solution.py:94
  33.6 2.7 %add_convert_fusion = (bf16[32,64,512]{2,1,0:T(8,128)(2,1)}, bf16[32,64,512]{2,1,0:T(8,128)(2,1)S(1)}) fusion(f32[64,512]{1,0:T(8,128)S(1)} %get-tuple-element.66, f32[32,512]{1,0:T(8,128)S(1)} %get-tuple-element.64, f32[64,512]{1,0:T(8,128)S(1)} %get-tuple-element.65, f32[32,512]{1,0:T(8,128)S(1)} %get-tuple-element.63), kind=kLoop, calls=%fused_computation.20 | loop fusion | flops 8388608 | bytes 4587520 | tf_op jit(solution)/shard_map/lag_product/convert_element_type | solution.py:32
  36.3 3.3 %fusion.20 = bf16[512,2,2048]{2,0,1:T(8,128)(2,1)} fusion(s32[512]{0:T(512)S(1)} %bitcast.149, bf16[8,8,2,2048]{3,2,1,0:T(2,128)(2,1)S(1)} %bitcast.134), kind=kOutput, calls=%fused_computation.52 | convolution fusion | flops 268468224 | bytes 4720640 | tf_op jit(solution)/shard_map/cross_spectra/dot_general | solution.py:42
  39.6 3.3 %fusion.22 = bf16[512,2,2048]{2,0,1:T(8,128)(2,1)} fusion(s32[512]{0:T(512)S(1)} %bitcast.148, bf16[8,8,2,2048]{3,2,1,0:T(2,128)(2,1)S(1)} %bitcast.135), kind=kOutput, calls=%fused_computation.54 | convolution fusion | flops 268468224 | bytes 4720640 | tf_op jit(solution)/shard_map/cross_spectra/dot_general | solution.py:42
  42.9 14.4 %all-to-all-done.1 = bf16[8,2,2,64,256]{4,3,2,1,0:T(8,128)(2,1)S(1)} async-done(((bf16[8,2,2,64,256]{4,3,2,1,0:T(8,128)(2,1)}), bf16[8,2,2,64,256]{4,3,2,1,0:T(8,128)(2,1)S(1)}, u32[]{:S(2)}, u32[]{:S(2)}) %all-to-all-start.1) | async-done | bytes 1048608 | tf_op jit(solution)/shard_map/owner_share_exchange/all_to_all | solution.py:109
  57.4 0.8 fusion.62
  58.2 0.8 fusion.63
  58.9 0.8 fusion.60
  59.7 1.3 %copy-done.1 = bf16[512,2,2048]{2,0,1:T(8,128)(2,1)S(1)} copy-done((bf16[512,2,2048]{2,0,1:T(8,128)(2,1)S(1)}, bf16[512,2,2048]{2,0,1:T(8,128)(2,1)}, u32[]{:S(2)}) %copy-start.1) | copy-done | bytes 4194328
  60.9 5.3 %fusion.11 = (bf16[512,2048]{1,0:T(8,128)(2,1)S(1)}, bf16[512,2048]{1,0:T(8,128)(2,1)S(1)}, bf16[512,2048]{1,0:T(8,128)(2,1)S(1)}, bf16[512,2048]{1,0:T(8,128)(2,1)S(1)}) fusion(bf16[512,2048]{1,0:T(8,128)(2,1)S(1)} %fusion.60, f32[2048]{0:T(1024)S(1)} %dynamic-slice-done, bf16[512,2,2048]{2,0,1:T(8,128)(2,1)S(1)} %copy-done.1, ...), kind=kOutput, calls=%fused_computation.19 | convolution fusion | flops 163610624 | bytes 23341056 | tf_op jit(solution)/shard_map/cross_spectra/dot_general | solution.py:50
  66.3 0.7 fusion.56
  67.0 0.8 convolution_add_fusion
  68.2 0.7 fusion.57
  68.9 0.8 convolution_add_fusion.1
  70.1 1.2 %copy-done = bf16[32,64,512]{2,1,0:T(8,128)(2,1)S(1)} copy-done((bf16[32,64,512]{2,1,0:T(8,128)(2,1)S(1)}, bf16[32,64,512]{2,1,0:T(8,128)(2,1)}, u32[]{:S(2)}) %copy-start) | copy-done | bytes 2097176
  72.2 0.5 fusion.32
  72.7 0.5 fusion.48
  73.4 0.6 collective-permute-start.1
  74.0 0.5 fusion.44
  75.6 1.6 %collective-permute-start.2 = (f32[2,64,512]{2,1,0:T(8,128)S(1)}, f32[2,64,512]{2,1,0:T(8,128)S(1)}, u32[]{:S(2)}, u32[]{:S(2)}) collective-permute-start(f32[2,64,512]{2,1,0:T(8,128)S(1)} %maximum_add_fusion.1), channel_id=1, source_target_pairs={{0,2},{1,3},{2,0},{3,1},{4,6},{5,7},{6,4},{7,5},{8,10},{9,11},{10,... | collective-permute-start | bytes 786440 | tf_op jit(solution)/shard_map/bin_exchange/ppermute | solution.py:76
  77.7 6.2 %collective-permute-done.2 = f32[2,64,512]{2,1,0:T(8,128)S(1)} collective-permute-done((f32[2,64,512]{2,1,0:T(8,128)S(1)}, f32[2,64,512]{2,1,0:T(8,128)S(1)}, u32[]{:S(2)}, u32[]{:S(2)}) %collective-permute-start.2) | collective-permute-done | bytes 262176 | tf_op jit(solution)/shard_map/bin_exchange/ppermute | solution.py:76
  84.0 11.8 %all_to_all.28 = f32[2,8,8,512]{3,2,0,1:T(8,128)S(1)} all-to-all(f32[2,8,8,512]{3,2,0,1:T(8,128)S(1)} %copy.25), channel_id=1, replica_groups=mesh['wide'=8,'narrow'=4] {'wide'}, dimensions={1} | all-to-all | bytes 524288 | tf_op jit(solution)/shard_map/bin_exchange/all_to_all | solution.py:154
  96.2 0.7 maximum_multiply_fusion
  (50 shorter events, 4.9 us)
Async XLA Ops:
  3.2 8.6 %copy-start.3 = (s32[2]{0:T(128)S(1)}, s32[2]{0:T(128)}, u32[]{:S(2)}) copy-start(s32[2]{0:T(128)} %param.8) | copy-start | bytes 28
  3.2 9.3 %copy-start.4 = (s32[1,2,128]{2,1,0:T(2,128)S(1)}, s32[1,2,128]{2,1,0:T(2,128)}, u32[]{:S(2)}) copy-start(s32[1,2,128]{2,1,0:T(2,128)} %param.11) | copy-start | bytes 3076
  3.2 9.2 %copy-start.5 = (s32[1,2,128]{2,1,0:T(2,128)S(1)}, s32[1,2,128]{2,1,0:T(2,128)}, u32[]{:S(2)}) copy-start(s32[1,2,128]{2,1,0:T(2,128)} %param.10) | copy-start | bytes 3076
  3.2 9.2 %copy-start.6 = (s32[1,2,128]{2,1,0:T(2,128)S(1)}, s32[1,2,128]{2,1,0:T(2,128)}, u32[]{:S(2)}) copy-start(s32[1,2,128]{2,1,0:T(2,128)} %param.9) | copy-start | bytes 3076
  4.5 21.8 %all-to-all-start = ((bf16[8,2,64,256]{3,1,2,0:T(2,128)(2,1)}), bf16[8,2,64,256]{3,1,2,0:T(2,128)(2,1)S(1)}, u32[]{:S(2)}, u32[]{:S(2)}) async-start(bf16[8,2,64,256]{3,1,2,0:T(2,128)(2,1)} %copy.21), calls=%async_computation | async-start | bytes 1048576 | tf_op jit(solution)/shard_map/owner_share_exchange/all_to_all | solution.py:104
  27.7 29.6 %all-to-all-start.1 = ((bf16[8,2,2,64,256]{4,3,2,1,0:T(8,128)(2,1)}), bf16[8,2,2,64,256]{4,3,2,1,0:T(8,128)(2,1)S(1)}, u32[]{:S(2)}, u32[]{:S(2)}) async-start(bf16[8,2,2,64,256]{4,3,2,1,0:T(8,128)(2,1)} %broadcast_in_dim.82), calls=%async_computation.1 | async-start | bytes 2097152 | tf_op jit(solution)/shard_map/owner_share_exchange/all_to_all | solution.py:109
  57.3 2.4 %copy-start.2 = (bf16[512,2,2048]{2,0,1:T(8,128)(2,1)S(1)}, bf16[512,2,2048]{2,0,1:T(8,128)(2,1)}, u32[]{:S(2)}) copy-start(bf16[512,2,2048]{2,0,1:T(8,128)(2,1)} %fusion.22) | copy-start | bytes 12582916
  58.1 2.8 %copy-start.1 = (bf16[512,2,2048]{2,0,1:T(8,128)(2,1)S(1)}, bf16[512,2,2048]{2,0,1:T(8,128)(2,1)}, u32[]{:S(2)}) copy-start(bf16[512,2,2048]{2,0,1:T(8,128)(2,1)} %fusion.20) | copy-start | bytes 12582916
  58.1 2.8 %dynamic-slice-start = ((f32[8192]{0:T(1024)}, s32[]{:T(128)}), f32[2048]{0:T(1024)S(1)}, s32[]{:S(2)}) async-start(f32[8192]{0:T(1024)} %param.7, s32[]{:T(128)} %select_n.74), calls=%async_computation.3 | async-start | bytes 16896 | tf_op jit(solution)/shard_map/dynamic_slice | solution.py:95
  69.7 1.6 %copy-start = (bf16[32,64,512]{2,1,0:T(8,128)(2,1)S(1)}, bf16[32,64,512]{2,1,0:T(8,128)(2,1)}, u32[]{:S(2)}) copy-start(bf16[32,64,512]{2,1,0:T(8,128)(2,1)} %get-tuple-element.51) | copy-start | bytes 6291460
  73.3 4.4 %collective-permute-start = (f32[2,64,512]{2,1,0:T(8,128)S(1)}, f32[2,64,512]{2,1,0:T(8,128)S(1)}, u32[]{:S(2)}, u32[]{:S(2)}) collective-permute-start(f32[2,64,512]{2,1,0:T(8,128)S(1)} %pad_maximum_fusion), channel_id=1, source_target_pairs={{0,1},{1,0},{2,3},{3,2},{4,5},{5,4},{6,7},{7,6},{8,9},{9,8},{10,11... | collective-permute-start | bytes 786440 | tf_op jit(solution)/shard_map/bin_exchange/ppermute | solution.py:76
  73.4 2.1 %collective-permute-start.1 = (f32[2,64,512]{2,1,0:T(8,128)S(1)}, f32[2,64,512]{2,1,0:T(8,128)S(1)}, u32[]{:S(2)}, u32[]{:S(2)}) collective-permute-start(f32[2,64,512]{2,1,0:T(8,128)S(1)} %pad_maximum_fusion.1), channel_id=1, source_target_pairs={{0,1},{1,0},{2,3},{3,2},{4,5},{5,4},{6,7},{7,6},{8,9},{9,8},{10,11... | collective-permute-start | bytes 786440 | tf_op jit(solution)/shard_map/bin_exchange/ppermute | solution.py:76
  75.6 8.3 %collective-permute-start.2 = (f32[2,64,512]{2,1,0:T(8,128)S(1)}, f32[2,64,512]{2,1,0:T(8,128)S(1)}, u32[]{:S(2)}, u32[]{:S(2)}) collective-permute-start(f32[2,64,512]{2,1,0:T(8,128)S(1)} %maximum_add_fusion.1), channel_id=1, source_target_pairs={{0,2},{1,3},{2,0},{3,1},{4,6},{5,7},{6,4},{7,5},{8,10},{9,11},{10,... | collective-permute-start | bytes 786440 | tf_op jit(solution)/shard_map/bin_exchange/ppermute | solution.py:76

commit v18 on v15

--- a/solution.py
+++ b/solution.py
@@ -100,10 +100,7 @@
             keepdims=False,
         ).transpose(2, 1, 0, 3)
         arrived = lax.all_to_all(outgoing, "wide", split_axis=0, concat_axis=0, tiled=True)
-        chosen = jnp.stack(
-            [lax.dynamic_index_in_dim(arrived, owners[s], 0, keepdims=False) for s in range(steps)]
-        )
-        copies = jnp.broadcast_to(chosen[None], (wide_count,) + chosen.shape)
+        copies = arrived[jnp.broadcast_to(owners[None, :], (wide_count, steps))]
         gathered = lax.all_to_all(copies, "wide", split_axis=0, concat_axis=4, tiled=True)
 
     ids = jnp.stack([pair_near[0], pair_far[0], stack_bins[0]])

time: 97.2 us -> 97 us (level)
  waiting for transfers between devices: 27.8 us -> 32.3 us
  between operations: 4.24 us -> 0.32 us
    all_to_all x1, waiting for transfers between devices: 4.68 us -> 9.16 us  [local(): lax.all_to_all(outgoing, 'wide', split_axis=0, concat_axis=0, tiled=True)]
    gather x0 -> x1, local copies, waits for them, and re-layouts: none -> 1.59 us  [local(): copies = arrived[jnp.broadcast_to(owners[None, :], (wide_count, steps))]]
    transpose x2 -> x0, local copies, waits for them, and re-layouts: 1.29 us -> none  [local(): outgoing = lax.dynamic_index_in_dim(spectra.reshape(block_rows, 2, narrow...]
    broadcast_in_dim x1 -> x0, local copies, waits for them, and re-layouts: 1.1 us -> none  [local(): copies = jnp.broadcast_to(chosen[None], (wide_count,) + chosen.shape)]
    unnamed x15 -> x16, local copies, waits for them, and re-layouts: 1.96 us -> 2.91 us
  transfers between devices with their start and end apart: 4 -> 4, of which waited for: 4 -> 4; matrix products, arithmetic and copies ran while one was open for 13% -> 12% of each run, Pallas kernels for 0% -> 0%
where the time goes in v18:
time: 97 us; the launch traced here: 96.6 us
  waiting for transfers between devices  32.3 us (33%)
  matrix products  19.9 us (21%)
  blocking collectives  17.1 us (18%)
  starting transfers between devices  12.6 us (13%)
  local copies, waits for them, and re-layouts  9.76 us (10%)
  other arithmetic  4.76 us (5%)
    all_to_all x1, waiting for transfers between devices, local(): lax.all_to_all(copies, 'wide', split_axis=0, concat_axis=4, tiled=True)  14.4 us
    all_to_all x1, blocking collectives, local(): lax.all_to_all(owned, 'wide', split_axis=1, concat_axis=1, tiled=True)  12 us
    all_to_all x1, waiting for transfers between devices, local(): lax.all_to_all(outgoing, 'wide', split_axis=0, concat_axis=0, tiled=True)  9.16 us
    ppermute x2, waiting for transfers between devices, halving_sum(): parts = paired[:, :, 0] + lax.ppermute(paired[:, :, 1], axis, pairs)  8.74 us
    dot_general x4, matrix products, pick_rows(): return jnp.dot(picker, block, preferred_element_type=jnp.bfloat16)  7.58 us
    all_to_all x1, starting transfers between devices, local(): lax.all_to_all(outgoing, 'wide', split_axis=0, concat_axis=0, tiled=True)  7.28 us
    dot_general x2, matrix products, select_rows(): chosen = jnp.dot(picker, flat_block, preferred_element_type=jnp.bfloat16)  6.56 us
    all_gather x1, blocking collectives, local(): ids = lax.all_gather(ids, 'narrow', axis=2, tiled=True)  5.09 us
  transfers between devices with their start and end apart: 4, of which 4 were waited for; matrix products, arithmetic and copies ran while one was open for 12% of the time, Pallas kernels for 0%

profile of v18, /device:TPU:0, one launch (start us, length us, event | category | flops | bytes accessed | tf_op | source)
XLA Modules:
  0.0 96.6 jit_solution(16082553422810263505)
XLA Ops:
  0.0 3.1 %reshape.281 = bf16[64,2,4,8,256]{4,3,2,1,0:T(8,128)(2,1)S(1)} reshape(bf16[64,2,8192]{2,1,0:T(2,128)(2,1)} %param.6) | data formatting | bytes 4194304 | tf_op jit(solution)/shard_map/owner_share_exchange/reshape | solution.py:97
  3.3 1.0 copy.60
  4.2 7.3 %all-to-all-start = ((bf16[8,2,64,256]{3,2,1,0:T(8,128)(2,1)}), bf16[8,2,64,256]{3,2,1,0:T(8,128)(2,1)S(1)}, u32[]{:S(2)}, u32[]{:S(2)}) async-start(bf16[8,2,64,256]{3,2,1,0:T(8,128)(2,1)} %bitcast.125), calls=%async_computation | async-start | bytes 1048576 | tf_op jit(solution)/shard_map/owner_share_exchange/all_to_all | solution.py:102
  11.7 5.1 %all_gather.3 = s32[3,2,512]{2,1,0:T(2,128)S(1)} all-gather(s32[3,2,128]{2,1,0:T(2,128)S(1)} %pad_add_fusion), channel_id=1, replica_groups=mesh['wide'=8,'narrow'=4] {'narrow'}, dimensions={2}, use_global_device_ids=true | all-gather | bytes 15360 | tf_op jit(solution)/shard_map/all_gather | solution.py:107
  16.9 9.2 %all-to-all-done = bf16[8,2,64,256]{3,2,1,0:T(8,128)(2,1)S(1)} async-done(((bf16[8,2,64,256]{3,2,1,0:T(8,128)(2,1)}), bf16[8,2,64,256]{3,2,1,0:T(8,128)(2,1)S(1)}, u32[]{:S(2)}, u32[]{:S(2)}) %all-to-all-start) | async-done | bytes 524320 | tf_op jit(solution)/shard_map/owner_share_exchange/all_to_all | solution.py:102
  26.0 1.6 %gather_fusion = bf16[16,2,64,256]{3,2,1,0:T(8,128)(2,1)} fusion(bf16[8,2,64,256]{3,2,1,0:T(8,128)(2,1)S(1)} %all-to-all-done, s32[1024]{0:T(1024)S(1)} %pad_clamp_fusion), kind=kCustom, calls=%fused_computation | custom fusion | bytes 2097216 | tf_op jit(solution)/shard_map/owner_share_exchange/gather | solution.py:103
  27.6 3.6 %all-to-all-start.1 = ((bf16[8,2,2,64,256]{4,3,2,1,0:T(8,128)(2,1)}), bf16[8,2,2,64,256]{4,3,2,1,0:T(8,128)(2,1)S(1)}, u32[]{:S(2)}, u32[]{:S(2)}) async-start(bf16[8,2,2,64,256]{4,3,2,1,0:T(8,128)(2,1)} %bitcast.9), calls=%async_computation.1 | async-start | bytes 2097152 | tf_op jit(solution)/shard_map/owner_share_exchange/all_to_all | solution.py:104
  31.2 0.3 fusion.66
  31.6 0.5 fusion.62
  32.1 1.4 %constant_dynamic-slice_fusion.1 = bf16[64,2,2048]{2,1,0:T(2,128)(2,1)S(1)} fusion(bf16[64,2,8192]{2,1,0:T(2,128)(2,1)} %param.6, s32[]{:T(128)} %select_n.68), kind=kLoop, calls=%fused_computation.134 | loop fusion | bytes 1048580 | tf_op jit(solution)/shard_map/dynamic_slice | solution.py:92
  33.5 2.7 %add_convert_fusion = (bf16[32,64,512]{2,1,0:T(8,128)(2,1)}, bf16[32,64,512]{2,1,0:T(8,128)(2,1)S(1)}) fusion(f32[64,512]{1,0:T(8,128)S(1)} %get-tuple-element.41, f32[32,512]{1,0:T(8,128)S(1)} %get-tuple-element.39, f32[64,512]{1,0:T(8,128)S(1)} %get-tuple-element.40, f32[32,512]{1,0:T(8,128)S(1)} %get-tuple-element.38), kind=kLoop, calls=%fused_computation.21 | loop fusion | flops 8388608 | bytes 4587520 | tf_op jit(solution)/shard_map/lag_product/convert_element_type | solution.py:32
  36.3 3.3 %fusion.23 = bf16[512,2,2048]{2,0,1:T(8,128)(2,1)} fusion(s32[512]{0:T(512)S(1)} %bitcast.146, bf16[8,8,2,2048]{3,2,1,0:T(2,128)(2,1)S(1)} %bitcast.126), kind=kOutput, calls=%fused_computation.46 | convolution fusion | flops 268468224 | bytes 4720640 | tf_op jit(solution)/shard_map/cross_spectra/dot_general | solution.py:42
  39.5 3.3 %fusion.25 = bf16[512,2,2048]{2,0,1:T(8,128)(2,1)} fusion(s32[512]{0:T(512)S(1)} %bitcast.145, bf16[8,8,2,2048]{3,2,1,0:T(2,128)(2,1)S(1)} %bitcast.127), kind=kOutput, calls=%fused_computation.48 | convolution fusion | flops 268468224 | bytes 4720640 | tf_op jit(solution)/shard_map/cross_spectra/dot_general | solution.py:42
  42.8 14.4 %all-to-all-done.1 = bf16[8,2,2,64,256]{4,3,2,1,0:T(8,128)(2,1)S(1)} async-done(((bf16[8,2,2,64,256]{4,3,2,1,0:T(8,128)(2,1)}), bf16[8,2,2,64,256]{4,3,2,1,0:T(8,128)(2,1)S(1)}, u32[]{:S(2)}, u32[]{:S(2)}) %all-to-all-start.1) | async-done | bytes 1048608 | tf_op jit(solution)/shard_map/owner_share_exchange/all_to_all | solution.py:104
  57.3 0.8 fusion.37
  58.1 0.8 fusion.38
  58.9 0.8 fusion.35
  59.6 1.3 %copy-done = bf16[512,2,2048]{2,0,1:T(8,128)(2,1)S(1)} copy-done((bf16[512,2,2048]{2,0,1:T(8,128)(2,1)S(1)}, bf16[512,2,2048]{2,0,1:T(8,128)(2,1)}, u32[]{:S(2)}) %copy-start) | copy-done | bytes 4194328
  60.9 5.3 %fusion.11 = (bf16[512,2048]{1,0:T(8,128)(2,1)S(1)}, bf16[512,2048]{1,0:T(8,128)(2,1)S(1)}, bf16[512,2048]{1,0:T(8,128)(2,1)S(1)}, bf16[512,2048]{1,0:T(8,128)(2,1)S(1)}) fusion(bf16[512,2048]{1,0:T(8,128)(2,1)S(1)} %fusion.35, f32[2048]{0:T(1024)S(1)} %dynamic-slice-done, bf16[512,2,2048]{2,0,1:T(8,128)(2,1)S(1)} %copy-done, ...), kind=kOutput, calls=%fused_computation.20 | convolution fusion | flops 163610624 | bytes 23341056 | tf_op jit(solution)/shard_map/cross_spectra/dot_general | solution.py:50
  66.2 0.7 fusion.29
  67.0 0.7 fusion.30
  67.7 0.8 reduce-precision_convert_fusion
  68.5 0.9 reduce-precision_convert_fusion.1
  69.5 0.6 copy-done.2
  70.1 1.3 %fusion.18 = f32[512,512]{1,0:T(8,128)S(1)} fusion(bf16[2048,512]{1,0:T(8,128)(2,1)S(1)} %bitcast.134, bf16[256,2048]{1,0:T(8,128)(2,1)S(1)} %get-tuple-element.20, bf16[256,2048]{1,0:T(8,128)(2,1)S(1)} %get-tuple-element.19), kind=kOutput, calls=%fused_computation.39 | convolution fusion | flops 1077936128 | bytes 5242880 | tf_op jit(solution)/shard_map/lag_product/dot_general | solution.py:67
  71.4 1.3 %fusion.14 = f32[512,512]{1,0:T(8,128)S(1)} fusion(bf16[2048,512]{1,0:T(8,128)(2,1)S(1)} %bitcast.133, bf16[256,2048]{1,0:T(8,128)(2,1)S(1)} %get-tuple-element.23, bf16[256,2048]{1,0:T(8,128)(2,1)S(1)} %get-tuple-element.21), kind=kOutput, calls=%fused_computation.35 | convolution fusion | flops 1077936128 | bytes 5242880 | tf_op jit(solution)/shard_map/lag_product/dot_general | solution.py:67
  73.1 1.9 %collective-permute-done = f32[2,2,64,512]{3,2,0,1:T(8,128)S(1)} collective-permute-done((f32[2,2,64,512]{3,2,0,1:T(8,128)S(1)}, f32[2,2,64,512]{3,2,0,1:T(8,128)S(1)}, u32[]{:S(2)}, u32[]{:S(2)}) %collective-permute-start) | collective-permute-done | bytes 524320 | tf_op jit(solution)/shard_map/bin_exchange/ppermute | solution.py:76
  75.1 1.6 %collective-permute-start.1 = (f32[2,1,64,512]{3,2,0,1:T(8,128)S(1)}, f32[2,1,64,512]{3,2,0,1:T(8,128)S(1)}, u32[]{:S(2)}, u32[]{:S(2)}) collective-permute-start(f32[2,1,64,512]{3,2,0,1:T(8,128)S(1)} %slice_bitcast_fusion.4), channel_id=1, source_target_pairs={{0,2},{1,3},{2,0},{3,1},{4,6},{5,7},{6,4},{7,5},{8,10},{9,11},{10,... | collective-permute-start | bytes 786440 | tf_op jit(solution)/shard_map/bin_exchange/ppermute | solution.py:76
  76.6 6.8 %collective-permute-done.1 = f32[2,1,64,512]{3,2,0,1:T(8,128)S(1)} collective-permute-done((f32[2,1,64,512]{3,2,0,1:T(8,128)S(1)}, f32[2,1,64,512]{3,2,0,1:T(8,128)S(1)}, u32[]{:S(2)}, u32[]{:S(2)}) %collective-permute-start.1) | collective-permute-done | bytes 262176 | tf_op jit(solution)/shard_map/bin_exchange/ppermute | solution.py:76
  83.5 12.0 %all_to_all.28 = f32[2,8,8,512]{3,2,0,1:T(8,128)S(1)} all-to-all(f32[2,8,8,512]{3,2,0,1:T(8,128)S(1)} %copy.30), channel_id=1, replica_groups=mesh['wide'=8,'narrow'=4] {'wide'}, dimensions={1} | all-to-all | bytes 524288 | tf_op jit(solution)/shard_map/bin_exchange/all_to_all | solution.py:147
  95.6 0.3 rev.4
  95.9 0.7 maximum_multiply_fusion
  (40 shorter events, 1.0 us)
Async XLA Ops:
  3.2 8.4 %copy-start.6 = (s32[2]{0:T(128)S(1)}, s32[2]{0:T(128)}, u32[]{:S(2)}) copy-start(s32[2]{0:T(128)} %param.8) | copy-start | bytes 28
  3.2 8.4 %copy-start.3 = (s32[1,2,128]{2,1,0:T(2,128)S(1)}, s32[1,2,128]{2,1,0:T(2,128)}, u32[]{:S(2)}) copy-start(s32[1,2,128]{2,1,0:T(2,128)} %param.11) | copy-start | bytes 3076
  3.2 8.4 %copy-start.4 = (s32[1,2,128]{2,1,0:T(2,128)S(1)}, s32[1,2,128]{2,1,0:T(2,128)}, u32[]{:S(2)}) copy-start(s32[1,2,128]{2,1,0:T(2,128)} %param.10) | copy-start | bytes 3076
  3.2 8.4 %copy-start.5 = (s32[1,2,128]{2,1,0:T(2,128)S(1)}, s32[1,2,128]{2,1,0:T(2,128)}, u32[]{:S(2)}) copy-start(s32[1,2,128]{2,1,0:T(2,128)} %param.9) | copy-start | bytes 3076
  4.2 21.8 %all-to-all-start = ((bf16[8,2,64,256]{3,2,1,0:T(8,128)(2,1)}), bf16[8,2,64,256]{3,2,1,0:T(8,128)(2,1)S(1)}, u32[]{:S(2)}, u32[]{:S(2)}) async-start(bf16[8,2,64,256]{3,2,1,0:T(8,128)(2,1)} %bitcast.125), calls=%async_computation | async-start | bytes 1048576 | tf_op jit(solution)/shard_map/owner_share_exchange/all_to_all | solution.py:102
  27.6 29.6 %all-to-all-start.1 = ((bf16[8,2,2,64,256]{4,3,2,1,0:T(8,128)(2,1)}), bf16[8,2,2,64,256]{4,3,2,1,0:T(8,128)(2,1)S(1)}, u32[]{:S(2)}, u32[]{:S(2)}) async-start(bf16[8,2,2,64,256]{4,3,2,1,0:T(8,128)(2,1)} %bitcast.9), calls=%async_computation.1 | async-start | bytes 2097152 | tf_op jit(solution)/shard_map/owner_share_exchange/all_to_all | solution.py:104
  57.2 2.4 %copy-start.1 = (bf16[512,2,2048]{2,0,1:T(8,128)(2,1)S(1)}, bf16[512,2,2048]{2,0,1:T(8,128)(2,1)}, u32[]{:S(2)}) copy-start(bf16[512,2,2048]{2,0,1:T(8,128)(2,1)} %fusion.25) | copy-start | bytes 12582916
  58.1 2.8 %copy-start = (bf16[512,2,2048]{2,0,1:T(8,128)(2,1)S(1)}, bf16[512,2,2048]{2,0,1:T(8,128)(2,1)}, u32[]{:S(2)}) copy-start(bf16[512,2,2048]{2,0,1:T(8,128)(2,1)} %fusion.23) | copy-start | bytes 12582916
  58.1 2.8 %dynamic-slice-start = ((f32[8192]{0:T(1024)}, s32[]{:T(128)}), f32[2048]{0:T(1024)S(1)}, s32[]{:S(2)}) async-start(f32[8192]{0:T(1024)} %param.7, s32[]{:T(128)} %select_n.68), calls=%async_computation.3 | async-start | bytes 16896 | tf_op jit(solution)/shard_map/dynamic_slice | solution.py:93
  68.5 1.6 %copy-start.2 = (bf16[32,64,512]{2,1,0:T(8,128)(2,1)S(1)}, bf16[32,64,512]{2,1,0:T(8,128)(2,1)}, u32[]{:S(2)}) copy-start(bf16[32,64,512]{2,1,0:T(8,128)(2,1)} %get-tuple-element.26) | copy-start | bytes 6291460
  73.0 2.0 %collective-permute-start = (f32[2,2,64,512]{3,2,0,1:T(8,128)S(1)}, f32[2,2,64,512]{3,2,0,1:T(8,128)S(1)}, u32[]{:S(2)}, u32[]{:S(2)}) collective-permute-start(f32[2,2,64,512]{3,2,0,1:T(8,128)S(1)} %bitcast.137), channel_id=1, source_target_pairs={{0,1},{1,0},{2,3},{3,2},{4,5},{5,4},{6,7},{7,6},{8,9},{9,8},{10,11... | collective-permute-start | bytes 1572872 | tf_op jit(solution)/shard_map/bin_exchange/ppermute | solution.py:76
  75.1 8.4 %collective-permute-start.1 = (f32[2,1,64,512]{3,2,0,1:T(8,128)S(1)}, f32[2,1,64,512]{3,2,0,1:T(8,128)S(1)}, u32[]{:S(2)}, u32[]{:S(2)}) collective-permute-start(f32[2,1,64,512]{3,2,0,1:T(8,128)S(1)} %slice_bitcast_fusion.4), channel_id=1, source_target_pairs={{0,2},{1,3},{2,0},{3,1},{4,6},{5,7},{6,4},{7,5},{8,10},{9,11},{10,... | collective-permute-start | bytes 786440 | tf_op jit(solution)/shard_map/bin_exchange/ppermute | solution.py:76

commit v19 on v15

--- a/solution.py
+++ b/solution.py
@@ -117,8 +117,12 @@
         parts = []
         for s in range(steps):
             near_rows = select_rows(near, near_ids[s])
-            far_real = pick_rows(gathered[0, s, 0], far_ids[s])
-            far_imag = pick_rows(gathered[0, s, 1], far_ids[s])
+            picker = (
+                far_ids[s][:, None] == jnp.arange(block_rows, dtype=jnp.int32)[None, :]
+            ).astype(jnp.bfloat16)
+            far_real, far_imag = jnp.einsum(
+                "pc,rcf->rpf", picker, gathered[0, s], preferred_element_type=jnp.bfloat16
+            )
             parts.append(
                 lax.optimization_barrier(cross_rows(near_rows, far_real, far_imag, gain))
             )

time: 97.2 us -> 97.6 us (level)
  other arithmetic: 4.93 us -> 10.6 us
  matrix products: 19.9 us -> 14.9 us
    convert_element_type x0 -> x1, other arithmetic: none -> 5.61 us  [cross_rows(): return (real_part.astype(jnp.bfloat16), imag_part.astype(jnp.bfloat16))]
    dot_general x4 -> x2, matrix products: 7.58 us -> 2.6 us  [local(): jnp.einsum('pc,rcf->rpf', picker, gathered[0, s], preferred_element_type=...]
where the time goes in v19:
time: 97.6 us; the launch traced here: 97.2 us
  waiting for transfers between devices  27.8 us (28%)
  blocking collectives  17.1 us (18%)
  matrix products  14.9 us (15%)
  starting transfers between devices  12.6 us (13%)
  other arithmetic  10.6 us (11%)
  local copies, waits for them, and re-layouts  10 us (10%)
  between operations  4.25 us (4%)
    all_to_all x1, waiting for transfers between devices, local(): lax.all_to_all(copies, 'wide', split_axis=0, concat_axis=4, tiled=True)  14.3 us
    all_to_all x1, blocking collectives, local(): lax.all_to_all(owned, 'wide', split_axis=1, concat_axis=1, tiled=True)  12 us
    ppermute x2, waiting for transfers between devices, halving_sum(): parts = paired[:, :, 0] + lax.ppermute(paired[:, :, 1], axis, pairs)  8.75 us
    all_to_all x1, starting transfers between devices, local(): lax.all_to_all(outgoing, 'wide', split_axis=0, concat_axis=0, tiled=True)  7.28 us
    dot_general x2, matrix products, select_rows(): chosen = jnp.dot(picker, flat_block, preferred_element_type=jnp.bfloat16)  6.57 us
    convert_element_type x1, other arithmetic, cross_rows(): return (real_part.astype(jnp.bfloat16), imag_part.astype(jnp.bfloat16))  5.61 us
    all_gather x1, blocking collectives, local(): ids = lax.all_gather(ids, 'narrow', axis=2, tiled=True)  5.1 us
    all_to_all x1, waiting for transfers between devices, local(): lax.all_to_all(outgoing, 'wide', split_axis=0, concat_axis=0, tiled=True)  4.68 us
  transfers between devices with their start and end apart: 4, of which 4 were waited for; matrix products, arithmetic and copies ran while one was open for 13% of the time, Pallas kernels for 0%

profile of v19, /device:TPU:0, one launch (start us, length us, event | category | flops | bytes accessed | tf_op | source)
XLA Modules:
  0.0 97.2 jit_solution(17299693541282765661)
XLA Ops:
  0.0 3.1 %reshape.252 = bf16[64,2,4,8,256]{4,3,2,1,0:T(8,128)(2,1)S(1)} reshape(bf16[64,2,8192]{2,1,0:T(2,128)(2,1)} %param.6) | data formatting | bytes 4194304 | tf_op jit(solution)/shard_map/owner_share_exchange/reshape | solution.py:97
  3.3 1.2 %copy.45 = bf16[8,2,64,256]{3,1,2,0:T(2,128)(2,1)} copy(bf16[8,2,64,256]{3,0,1,2:T(8,128)(2,1)S(1)} %dynamic-slice_bitcast_fusion) | data formatting | bytes 1048576 | tf_op jit(solution)/shard_map/owner_share_exchange/transpose | solution.py:101
  4.5 7.3 %all-to-all-start = ((bf16[8,2,64,256]{3,1,2,0:T(2,128)(2,1)}), bf16[8,2,64,256]{3,1,2,0:T(2,128)(2,1)S(1)}, u32[]{:S(2)}, u32[]{:S(2)}) async-start(bf16[8,2,64,256]{3,1,2,0:T(2,128)(2,1)} %copy.45), calls=%async_computation | async-start | bytes 1048576 | tf_op jit(solution)/shard_map/owner_share_exchange/all_to_all | solution.py:102
  11.8 0.6 fusion.70
  16.4 5.1 %all_gather.3 = s32[3,2,512]{2,1,0:T(2,128)S(1)} all-gather(s32[3,2,128]{2,1,0:T(2,128)S(1)} %pad_add_fusion), channel_id=1, replica_groups=mesh['wide'=8,'narrow'=4] {'narrow'}, dimensions={2}, use_global_device_ids=true | all-gather | bytes 15360 | tf_op jit(solution)/shard_map/all_gather | solution.py:110
  21.6 4.7 %all-to-all-done = bf16[8,2,64,256]{3,1,2,0:T(2,128)(2,1)S(1)} async-done(((bf16[8,2,64,256]{3,1,2,0:T(2,128)(2,1)}), bf16[8,2,64,256]{3,1,2,0:T(2,128)(2,1)S(1)}, u32[]{:S(2)}, u32[]{:S(2)}) %all-to-all-start) | async-done | bytes 524320 | tf_op jit(solution)/shard_map/owner_share_exchange/all_to_all | solution.py:102
  26.6 1.1 %broadcast_in_dim.12 = bf16[8,2,2,64,256]{4,3,2,1,0:T(8,128)(2,1)} broadcast(bf16[2,2,64,256]{3,2,1,0:T(8,128)(2,1)S(1)} %copy.46), dimensions={1,2,3,4} | broadcast | bytes 1179648 | tf_op jit(solution)/shard_map/owner_share_exchange/broadcast_in_dim | solution.py:106
  27.7 3.6 %all-to-all-start.1 = ((bf16[8,2,2,64,256]{4,3,2,1,0:T(8,128)(2,1)}), bf16[8,2,2,64,256]{4,3,2,1,0:T(8,128)(2,1)S(1)}, u32[]{:S(2)}, u32[]{:S(2)}) async-start(bf16[8,2,2,64,256]{4,3,2,1,0:T(8,128)(2,1)} %broadcast_in_dim.12), calls=%async_computation.1 | async-start | bytes 2097152 | tf_op jit(solution)/shard_map/owner_share_exchange/all_to_all | solution.py:107
  31.3 0.3 fusion.64
  31.7 0.5 fusion.58
  32.2 1.4 %constant_dynamic-slice_fusion.2 = bf16[64,2,2048]{2,1,0:T(2,128)(2,1)S(1)} fusion(bf16[64,2,8192]{2,1,0:T(2,128)(2,1)} %param.6, s32[]{:T(128)} %select_n.65), kind=kLoop, calls=%fused_computation.132 | loop fusion | bytes 1048580 | tf_op jit(solution)/shard_map/dynamic_slice | solution.py:92
  33.6 2.7 %add_convert_fusion = (bf16[32,64,512]{2,1,0:T(8,128)(2,1)}, bf16[32,64,512]{2,1,0:T(8,128)(2,1)S(1)}) fusion(f32[64,512]{1,0:T(8,128)S(1)} %get-tuple-element.43, f32[32,512]{1,0:T(8,128)S(1)} %get-tuple-element.41, f32[64,512]{1,0:T(8,128)S(1)} %get-tuple-element.42, f32[32,512]{1,0:T(8,128)S(1)} %get-tuple-element.40), kind=kLoop, calls=%fused_computation.20 | loop fusion | flops 8388608 | bytes 4587520 | tf_op jit(solution)/shard_map/lag_product/convert_element_type | solution.py:32
  36.3 3.3 %fusion.23 = bf16[512,2,2048]{2,0,1:T(8,128)(2,1)} fusion(s32[512]{0:T(512)S(1)} %bitcast.173, bf16[8,8,2,2048]{3,2,1,0:T(2,128)(2,1)S(1)} %bitcast.155), kind=kOutput, calls=%fused_computation.51 | convolution fusion | flops 268468224 | bytes 4720640 | tf_op jit(solution)/shard_map/cross_spectra/dot_general | solution.py:42
  39.6 3.3 %fusion.25 = bf16[512,2,2048]{2,0,1:T(8,128)(2,1)} fusion(s32[512]{0:T(512)S(1)} %bitcast.172, bf16[8,8,2,2048]{3,2,1,0:T(2,128)(2,1)S(1)} %bitcast.156), kind=kOutput, calls=%fused_computation.53 | convolution fusion | flops 268468224 | bytes 4720640 | tf_op jit(solution)/shard_map/cross_spectra/dot_general | solution.py:42
  42.9 14.3 %all-to-all-done.1 = bf16[8,2,2,64,256]{4,3,2,1,0:T(8,128)(2,1)S(1)} async-done(((bf16[8,2,2,64,256]{4,3,2,1,0:T(8,128)(2,1)}), bf16[8,2,2,64,256]{4,3,2,1,0:T(8,128)(2,1)S(1)}, u32[]{:S(2)}, u32[]{:S(2)}) %all-to-all-start.1) | async-done | bytes 1048608 | tf_op jit(solution)/shard_map/owner_share_exchange/all_to_all | solution.py:107
  57.4 1.3 %convolution_bitcast_fusion = bf16[2,512,2048]{2,1,0:T(8,128)(2,1)S(1)} fusion(bf16[1,2,2,64,2048]{4,3,2,1,0:T(8,128)(2,1)S(1)} %bitcast.157, s32[512]{0:T(512)S(1)} %bitcast.171), kind=kOutput, calls=%fused_computation.22 | convolution fusion | flops 268468224 | bytes 4720640 | tf_op jit(solution)/shard_map/cross_spectra/pc,rcf->rpf/dot_general | solution.py:123
  58.7 1.3 %convolution_bitcast_fusion.1 = bf16[2,512,2048]{2,1,0:T(8,128)(2,1)S(1)} fusion(bf16[1,2,2,64,2048]{4,3,2,1,0:T(8,128)(2,1)S(1)} %bitcast.158, s32[512]{0:T(512)S(1)} %bitcast.170), kind=kOutput, calls=%fused_computation.23 | convolution fusion | flops 268468224 | bytes 4720640 | tf_op jit(solution)/shard_map/cross_spectra/pc,rcf->rpf/dot_general | solution.py:123
  60.1 1.1 %copy-done = bf16[512,2,2048]{2,0,1:T(8,128)(2,1)S(1)} copy-done((bf16[512,2,2048]{2,0,1:T(8,128)(2,1)S(1)}, bf16[512,2,2048]{2,0,1:T(8,128)(2,1)}, u32[]{:S(2)}) %copy-start) | copy-done | bytes 4194328
  61.1 5.6 %fusion.8 = (bf16[512,2048]{1,0:T(8,128)(2,1)S(1)}, bf16[512,2048]{1,0:T(8,128)(2,1)S(1)}, bf16[512,2048]{1,0:T(8,128)(2,1)S(1)}, bf16[512,2048]{1,0:T(8,128)(2,1)S(1)}) fusion(f32[2048]{0:T(1024)S(1)} %dynamic-slice-done, bf16[512,2,2048]{2,0,1:T(8,128)(2,1)S(1)} %copy-done, bf16[2,512,2048]{2,1,0:T(8,128)(2,1)S(1)} %convolution_bitcast_fusion, ...), kind=kLoop, calls=%fused_computation.16 | loop fusion | flops 29360128 | bytes 25174016 | tf_op jit(solution)/shard_map/cross_spectra/convert_element_type | solution.py:60
  66.7 0.7 fusion.29
  67.5 0.7 fusion.30
  68.2 0.8 reduce-precision_convert_fusion
  69.0 0.9 reduce-precision_convert_fusion.1
  70.0 0.7 copy-done.2
  70.6 1.3 %fusion.18 = f32[512,512]{1,0:T(8,128)S(1)} fusion(bf16[2048,512]{1,0:T(8,128)(2,1)S(1)} %bitcast.161, bf16[256,2048]{1,0:T(8,128)(2,1)S(1)} %get-tuple-element.20, bf16[256,2048]{1,0:T(8,128)(2,1)S(1)} %get-tuple-element.19), kind=kOutput, calls=%fused_computation.44 | convolution fusion | flops 1077936128 | bytes 5242880 | tf_op jit(solution)/shard_map/lag_product/dot_general | solution.py:67
  71.9 1.3 %fusion.14 = f32[512,512]{1,0:T(8,128)S(1)} fusion(bf16[2048,512]{1,0:T(8,128)(2,1)S(1)} %bitcast.160, bf16[256,2048]{1,0:T(8,128)(2,1)S(1)} %get-tuple-element.23, bf16[256,2048]{1,0:T(8,128)(2,1)S(1)} %get-tuple-element.21), kind=kOutput, calls=%fused_computation.40 | convolution fusion | flops 1077936128 | bytes 5242880 | tf_op jit(solution)/shard_map/lag_product/dot_general | solution.py:67
  73.6 1.9 %collective-permute-done = f32[2,2,64,512]{3,2,0,1:T(8,128)S(1)} collective-permute-done((f32[2,2,64,512]{3,2,0,1:T(8,128)S(1)}, f32[2,2,64,512]{3,2,0,1:T(8,128)S(1)}, u32[]{:S(2)}, u32[]{:S(2)}) %collective-permute-start) | collective-permute-done | bytes 524320 | tf_op jit(solution)/shard_map/bin_exchange/ppermute | solution.py:76
  75.6 1.6 %collective-permute-start.1 = (f32[2,1,64,512]{3,2,0,1:T(8,128)S(1)}, f32[2,1,64,512]{3,2,0,1:T(8,128)S(1)}, u32[]{:S(2)}, u32[]{:S(2)}) collective-permute-start(f32[2,1,64,512]{3,2,0,1:T(8,128)S(1)} %slice_bitcast_fusion.12), channel_id=1, source_target_pairs={{0,2},{1,3},{2,0},{3,1},{4,6},{5,7},{6,4},{7,5},{8,10},{9,11},{10,... | collective-permute-start | bytes 786440 | tf_op jit(solution)/shard_map/bin_exchange/ppermute | solution.py:76
  77.2 6.8 %collective-permute-done.1 = f32[2,1,64,512]{3,2,0,1:T(8,128)S(1)} collective-permute-done((f32[2,1,64,512]{3,2,0,1:T(8,128)S(1)}, f32[2,1,64,512]{3,2,0,1:T(8,128)S(1)}, u32[]{:S(2)}, u32[]{:S(2)}) %collective-permute-start.1) | collective-permute-done | bytes 262176 | tf_op jit(solution)/shard_map/bin_exchange/ppermute | solution.py:76
  84.1 12.0 %all_to_all.28 = f32[2,8,8,512]{3,2,0,1:T(8,128)S(1)} all-to-all(f32[2,8,8,512]{3,2,0,1:T(8,128)S(1)} %copy.53), channel_id=1, replica_groups=mesh['wide'=8,'narrow'=4] {'wide'}, dimensions={1} | all-to-all | bytes 524288 | tf_op jit(solution)/shard_map/bin_exchange/all_to_all | solution.py:154
  96.2 0.3 rev.4
  96.5 0.7 maximum_multiply_fusion
  (38 shorter events, 1.3 us)
Async XLA Ops:
  3.2 8.6 %copy-start.3 = (s32[2]{0:T(128)S(1)}, s32[2]{0:T(128)}, u32[]{:S(2)}) copy-start(s32[2]{0:T(128)} %param.8) | copy-start | bytes 28
  3.2 9.3 %copy-start.4 = (s32[1,2,128]{2,1,0:T(2,128)S(1)}, s32[1,2,128]{2,1,0:T(2,128)}, u32[]{:S(2)}) copy-start(s32[1,2,128]{2,1,0:T(2,128)} %param.11) | copy-start | bytes 3076
  3.2 9.3 %copy-start.5 = (s32[1,2,128]{2,1,0:T(2,128)S(1)}, s32[1,2,128]{2,1,0:T(2,128)}, u32[]{:S(2)}) copy-start(s32[1,2,128]{2,1,0:T(2,128)} %param.10) | copy-start | bytes 3076
  3.2 9.3 %copy-start.6 = (s32[1,2,128]{2,1,0:T(2,128)S(1)}, s32[1,2,128]{2,1,0:T(2,128)}, u32[]{:S(2)}) copy-start(s32[1,2,128]{2,1,0:T(2,128)} %param.9) | copy-start | bytes 3076
  4.5 21.8 %all-to-all-start = ((bf16[8,2,64,256]{3,1,2,0:T(2,128)(2,1)}), bf16[8,2,64,256]{3,1,2,0:T(2,128)(2,1)S(1)}, u32[]{:S(2)}, u32[]{:S(2)}) async-start(bf16[8,2,64,256]{3,1,2,0:T(2,128)(2,1)} %copy.45), calls=%async_computation | async-start | bytes 1048576 | tf_op jit(solution)/shard_map/owner_share_exchange/all_to_all | solution.py:102
  27.7 29.6 %all-to-all-start.1 = ((bf16[8,2,2,64,256]{4,3,2,1,0:T(8,128)(2,1)}), bf16[8,2,2,64,256]{4,3,2,1,0:T(8,128)(2,1)S(1)}, u32[]{:S(2)}, u32[]{:S(2)}) async-start(bf16[8,2,2,64,256]{4,3,2,1,0:T(8,128)(2,1)} %broadcast_in_dim.12), calls=%async_computation.1 | async-start | bytes 2097152 | tf_op jit(solution)/shard_map/owner_share_exchange/all_to_all | solution.py:107
  57.4 2.7 %copy-start.1 = (bf16[512,2,2048]{2,0,1:T(8,128)(2,1)S(1)}, bf16[512,2,2048]{2,0,1:T(8,128)(2,1)}, u32[]{:S(2)}) copy-start(bf16[512,2,2048]{2,0,1:T(8,128)(2,1)} %fusion.25) | copy-start | bytes 12582916
  58.7 2.4 %copy-start = (bf16[512,2,2048]{2,0,1:T(8,128)(2,1)S(1)}, bf16[512,2,2048]{2,0,1:T(8,128)(2,1)}, u32[]{:S(2)}) copy-start(bf16[512,2,2048]{2,0,1:T(8,128)(2,1)} %fusion.23) | copy-start | bytes 12582916
  58.7 2.4 %dynamic-slice-start = ((f32[8192]{0:T(1024)}, s32[]{:T(128)}), f32[2048]{0:T(1024)S(1)}, s32[]{:S(2)}) async-start(f32[8192]{0:T(1024)} %param.7, s32[]{:T(128)} %select_n.65), calls=%async_computation.3 | async-start | bytes 16896 | tf_op jit(solution)/shard_map/dynamic_slice | solution.py:93
  69.0 1.6 %copy-start.2 = (bf16[32,64,512]{2,1,0:T(8,128)(2,1)S(1)}, bf16[32,64,512]{2,1,0:T(8,128)(2,1)}, u32[]{:S(2)}) copy-start(bf16[32,64,512]{2,1,0:T(8,128)(2,1)} %get-tuple-element.28) | copy-start | bytes 6291460
  73.5 2.0 %collective-permute-start = (f32[2,2,64,512]{3,2,0,1:T(8,128)S(1)}, f32[2,2,64,512]{3,2,0,1:T(8,128)S(1)}, u32[]{:S(2)}, u32[]{:S(2)}) collective-permute-start(f32[2,2,64,512]{3,2,0,1:T(8,128)S(1)} %bitcast.164), channel_id=1, source_target_pairs={{0,1},{1,0},{2,3},{3,2},{4,5},{5,4},{6,7},{7,6},{8,9},{9,8},{10,11... | collective-permute-start | bytes 1572872 | tf_op jit(solution)/shard_map/bin_exchange/ppermute | solution.py:76
  75.6 8.4 %collective-permute-start.1 = (f32[2,1,64,512]{3,2,0,1:T(8,128)S(1)}, f32[2,1,64,512]{3,2,0,1:T(8,128)S(1)}, u32[]{:S(2)}, u32[]{:S(2)}) collective-permute-start(f32[2,1,64,512]{3,2,0,1:T(8,128)S(1)} %slice_bitcast_fusion.12), channel_id=1, source_target_pairs={{0,2},{1,3},{2,0},{3,1},{4,6},{5,7},{6,4},{7,5},{8,10},{9,11},{10,... | collective-permute-start | bytes 786440 | tf_op jit(solution)/shard_map/bin_exchange/ppermute | solution.py:76

commit v20 on v15

--- a/solution.py
+++ b/solution.py
@@ -119,9 +119,7 @@
             near_rows = select_rows(near, near_ids[s])
             far_real = pick_rows(gathered[0, s, 0], far_ids[s])
             far_imag = pick_rows(gathered[0, s, 1], far_ids[s])
-            parts.append(
-                lax.optimization_barrier(cross_rows(near_rows, far_real, far_imag, gain))
-            )
+            parts.append(cross_rows(near_rows, far_real, far_imag, gain))
 
     with jax.named_scope("bin_sums"):
         real_sum = None

time: 97.2 us -> 95.6 us (0.984)
    dot_general x4, matrix products: 7.58 us -> 3.01 us  [pick_rows(): return jnp.dot(picker, block, preferred_element_type=jnp.bfloat16)]
    dot_general x2, matrix products: 1.68 us -> 3.65 us  [local(): jnp.dot(bin_hits, parts[s][0], preferred_element_type=jnp.float32)]
    dot_general x2, matrix products: 1.56 us -> 3.34 us  [local(): jnp.dot(bin_hits, parts[s][1], preferred_element_type=jnp.float32)]
  transfers between devices with their start and end apart: 4 -> 4, of which waited for: 4 -> 4; matrix products, arithmetic and copies ran while one was open for 13% -> 14% of each run, Pallas kernels for 0% -> 0%
where the time goes in v20:
time: 95.6 us; the launch traced here: 95.1 us
  waiting for transfers between devices  27.3 us (29%)
  matrix products  19.1 us (20%)
  blocking collectives  17 us (18%)
  starting transfers between devices  12.5 us (13%)
  local copies, waits for them, and re-layouts  10.1 us (11%)
  other arithmetic  4.9 us (5%)
  between operations  4.12 us (4%)
    all_to_all x1, waiting for transfers between devices, local(): lax.all_to_all(copies, 'wide', split_axis=0, concat_axis=4, tiled=True)  14.4 us
    all_to_all x1, blocking collectives, local(): lax.all_to_all(owned, 'wide', split_axis=1, concat_axis=1, tiled=True)  12 us
    ppermute x2, waiting for transfers between devices, halving_sum(): parts = paired[:, :, 0] + lax.ppermute(paired[:, :, 1], axis, pairs)  8.76 us
    all_to_all x1, starting transfers between devices, local(): lax.all_to_all(outgoing, 'wide', split_axis=0, concat_axis=0, tiled=True)  7.28 us
    dot_general x2, matrix products, select_rows(): chosen = jnp.dot(picker, flat_block, preferred_element_type=jnp.bfloat16)  6.57 us
    all_gather x1, blocking collectives, local(): ids = lax.all_gather(ids, 'narrow', axis=2, tiled=True)  5.09 us
    all_to_all x1, waiting for transfers between devices, local(): lax.all_to_all(outgoing, 'wide', split_axis=0, concat_axis=0, tiled=True)  4.15 us
    dot_general x2, matrix products, local(): jnp.dot(bin_hits, parts[s][0], preferred_element_type=jnp.float32)  3.65 us
  transfers between devices with their start and end apart: 4, of which 4 were waited for; matrix products, arithmetic and copies ran while one was open for 14% of the time, Pallas kernels for 0%

profile of v20, /device:TPU:0, one launch (start us, length us, event | category | flops | bytes accessed | tf_op | source)
XLA Modules:
  0.0 95.1 jit_solution(14038053761603323632)
XLA Ops:
  0.0 3.1 %reshape.238 = bf16[64,2,4,8,256]{4,3,2,1,0:T(8,128)(2,1)S(1)} reshape(bf16[64,2,8192]{2,1,0:T(2,128)(2,1)} %param.6) | data formatting | bytes 4194304 | tf_op jit(solution)/shard_map/owner_share_exchange/reshape | solution.py:97
  3.3 1.2 %copy.37 = bf16[8,2,64,256]{3,1,2,0:T(2,128)(2,1)} copy(bf16[8,2,64,256]{3,0,1,2:T(8,128)(2,1)S(1)} %dynamic-slice_bitcast_fusion) | data formatting | bytes 1048576 | tf_op jit(solution)/shard_map/owner_share_exchange/transpose | solution.py:101
  4.5 7.3 %all-to-all-start = ((bf16[8,2,64,256]{3,1,2,0:T(2,128)(2,1)}), bf16[8,2,64,256]{3,1,2,0:T(2,128)(2,1)S(1)}, u32[]{:S(2)}, u32[]{:S(2)}) async-start(bf16[8,2,64,256]{3,1,2,0:T(2,128)(2,1)} %copy.37), calls=%async_computation | async-start | bytes 1048576 | tf_op jit(solution)/shard_map/owner_share_exchange/all_to_all | solution.py:102
  11.8 0.6 fusion.80
  16.3 0.7 dynamic_slice.21
  17.0 5.1 %all_gather.3 = s32[3,2,512]{2,1,0:T(2,128)S(1)} all-gather(s32[3,2,128]{2,1,0:T(2,128)S(1)} %pad_add_fusion), channel_id=1, replica_groups=mesh['wide'=8,'narrow'=4] {'narrow'}, dimensions={2}, use_global_device_ids=true | all-gather | bytes 15360 | tf_op jit(solution)/shard_map/all_gather | solution.py:110
  22.1 4.2 %all-to-all-done = bf16[8,2,64,256]{3,1,2,0:T(2,128)(2,1)S(1)} async-done(((bf16[8,2,64,256]{3,1,2,0:T(2,128)(2,1)}), bf16[8,2,64,256]{3,1,2,0:T(2,128)(2,1)S(1)}, u32[]{:S(2)}, u32[]{:S(2)}) %all-to-all-start) | async-done | bytes 524320 | tf_op jit(solution)/shard_map/owner_share_exchange/all_to_all | solution.py:102
  26.6 1.1 %broadcast_in_dim.12 = bf16[8,2,2,64,256]{4,3,2,1,0:T(8,128)(2,1)} broadcast(bf16[2,2,64,256]{3,2,1,0:T(8,128)(2,1)S(1)} %copy.38), dimensions={1,2,3,4} | broadcast | bytes 1179648 | tf_op jit(solution)/shard_map/owner_share_exchange/broadcast_in_dim | solution.py:106
  27.7 3.6 %all-to-all-start.1 = ((bf16[8,2,2,64,256]{4,3,2,1,0:T(8,128)(2,1)}), bf16[8,2,2,64,256]{4,3,2,1,0:T(8,128)(2,1)S(1)}, u32[]{:S(2)}, u32[]{:S(2)}) async-start(bf16[8,2,2,64,256]{4,3,2,1,0:T(8,128)(2,1)} %broadcast_in_dim.12), calls=%async_computation.1 | async-start | bytes 2097152 | tf_op jit(solution)/shard_map/owner_share_exchange/all_to_all | solution.py:107
  31.6 0.5 fusion.70
  32.2 1.4 %constant_dynamic-slice_fusion.2 = bf16[64,2,2048]{2,1,0:T(2,128)(2,1)S(1)} fusion(bf16[64,2,8192]{2,1,0:T(2,128)(2,1)} %param.6, s32[]{:T(128)S(6)} %select_n.65), kind=kLoop, calls=%fused_computation.136 | loop fusion | bytes 1048580 | tf_op jit(solution)/shard_map/dynamic_slice | solution.py:92
  33.6 2.7 %add_convert_fusion = (bf16[32,64,512]{2,1,0:T(8,128)(2,1)}, bf16[32,64,512]{2,1,0:T(8,128)(2,1)S(1)}) fusion(f32[64,512]{1,0:T(8,128)S(1)} %get-tuple-element.29, f32[32,512]{1,0:T(8,128)S(1)} %get-tuple-element.27, f32[64,512]{1,0:T(8,128)S(1)} %get-tuple-element.28, f32[32,512]{1,0:T(8,128)S(1)} %get-tuple-element.26), kind=kLoop, calls=%fused_computation.20 | loop fusion | flops 8388608 | bytes 4587520 | tf_op jit(solution)/shard_map/lag_product/convert_element_type | solution.py:32
  36.3 3.3 %fusion.35 = bf16[512,2,2048]{2,0,1:T(8,128)(2,1)} fusion(s32[512]{0:T(512)S(1)} %bitcast.153, bf16[8,8,2,2048]{3,2,1,0:T(2,128)(2,1)S(1)} %bitcast.135), kind=kOutput, calls=%fused_computation.53 | convolution fusion | flops 268468224 | bytes 4720640 | tf_op jit(solution)/shard_map/cross_spectra/dot_general | solution.py:42
  39.6 3.3 %fusion.33 = bf16[512,2,2048]{2,0,1:T(8,128)(2,1)} fusion(s32[512]{0:T(512)S(1)} %bitcast.152, bf16[8,8,2,2048]{3,2,1,0:T(2,128)(2,1)S(1)} %bitcast.136), kind=kOutput, calls=%fused_computation.51 | convolution fusion | flops 268468224 | bytes 4720640 | tf_op jit(solution)/shard_map/cross_spectra/dot_general | solution.py:42
  42.9 14.4 %all-to-all-done.1 = bf16[8,2,2,64,256]{4,3,2,1,0:T(8,128)(2,1)S(1)} async-done(((bf16[8,2,2,64,256]{4,3,2,1,0:T(8,128)(2,1)}), bf16[8,2,2,64,256]{4,3,2,1,0:T(8,128)(2,1)S(1)}, u32[]{:S(2)}, u32[]{:S(2)}) %all-to-all-start.1) | async-done | bytes 1048608 | tf_op jit(solution)/shard_map/owner_share_exchange/all_to_all | solution.py:107
  57.4 0.8 fusion.45
  58.1 0.8 fusion.46
  58.9 0.8 fusion.43
  59.7 0.8 fusion.44
  60.4 0.7 copy-done.1
  61.1 1.7 %fusion.16 = f32[256,2048]{1,0:T(8,128)S(1)} fusion(bf16[512,2048]{1,0:T(8,128)(2,1)S(1)} %fusion.46, bf16[512,2048]{1,0:T(8,128)(2,1)S(1)} %fusion.45, f32[2048]{0:T(1024)S(1)} %dynamic_slice.21, bf16[512,2,2048]{2,0,1:T(8,128)(2,1)S(1)} %copy-done.1, s32[512]{0:T(512)S(1)} %bitcast.156), kind=kOutput, calls=%fused_computation.30 | convolution fusion | flops 546439168 | bytes 10496000 | tf_op jit(solution)/shard_map/bin_sums/dot_general | solution.py:132
  62.8 1.7 %fusion.18 = f32[256,2048]{1,0:T(8,128)S(1)} fusion(bf16[512,2048]{1,0:T(8,128)(2,1)S(1)} %fusion.45, bf16[512,2048]{1,0:T(8,128)(2,1)S(1)} %fusion.46, f32[2048]{0:T(1024)S(1)} %dynamic_slice.21, bf16[512,2,2048]{2,0,1:T(8,128)(2,1)S(1)} %copy-done.1, s32[512]{0:T(512)S(1)} %bitcast.157), kind=kOutput, calls=%fused_computation.31 | convolution fusion | flops 546439168 | bytes 10496000 | tf_op jit(solution)/shard_map/bin_sums/dot_general | solution.py:131
  64.4 0.5 copy-done
  64.9 1.7 %reduce-precision_convert_fusion = (bf16[256,2048]{1,0:T(8,128)(2,1)S(1)}, bf16[256,2048]{1,0:T(8,128)(2,1)S(1)}) fusion(f32[256,2048]{1,0:T(8,128)S(1)} %fusion.16, bf16[512,2048]{1,0:T(8,128)(2,1)S(1)} %fusion.44, bf16[512,2048]{1,0:T(8,128)(2,1)S(1)} %fusion.43, f32[2048]{0:T(1024)S(1)} %dynamic_slice.21, bf16[512,2,2048]{2,0,1:T(8,128)(2,1)S(1)} %copy-done, ...), kind=kOutput, calls=%fused_computation.23 | convolution fusion | flops 549060608 | bytes 12593152 | tf_op jit(solution)/shard_map/bin_sums/dot_general | solution.py:132
  66.6 2.0 %reduce-precision_convert_fusion.1 = (bf16[256,2048]{1,0:T(8,128)(2,1)S(1)}, f32[256]{0:T(256)S(1)}, bf16[256,2048]{1,0:T(8,128)(2,1)S(1)}) fusion(f32[256,2048]{1,0:T(8,128)S(1)} %fusion.18, bf16[512,2048]{1,0:T(8,128)(2,1)S(1)} %fusion.43, bf16[512,2048]{1,0:T(8,128)(2,1)S(1)} %fusion.44, f32[2048]{0:T(1024)S(1)} %dynamic_slice.21, ...), kind=kOutput, calls=%fused_computation.25 | convolution fusion | flops 549584640 | bytes 12594176 | tf_op jit(solution)/shard_map/bin_sums/dot_general | solution.py:131
  68.6 1.2 %fusion.24 = f32[512,512]{1,0:T(8,128)S(1)} fusion(bf16[2048,512]{1,0:T(8,128)(2,1)S(1)} %bitcast.143, bf16[256,2048]{1,0:T(8,128)(2,1)S(1)} %get-tuple-element.8, bf16[256,2048]{1,0:T(8,128)(2,1)S(1)} %get-tuple-element.7), kind=kOutput, calls=%fused_computation.40 | convolution fusion | flops 1077936128 | bytes 5242880 | tf_op jit(solution)/shard_map/lag_product/dot_general | solution.py:67
  69.9 1.2 %fusion.20 = f32[512,512]{1,0:T(8,128)S(1)} fusion(bf16[2048,512]{1,0:T(8,128)(2,1)S(1)} %bitcast.142, bf16[256,2048]{1,0:T(8,128)(2,1)S(1)} %get-tuple-element.11, bf16[256,2048]{1,0:T(8,128)(2,1)S(1)} %get-tuple-element.9), kind=kOutput, calls=%fused_computation.36 | convolution fusion | flops 1077936128 | bytes 5242880 | tf_op jit(solution)/shard_map/lag_product/dot_general | solution.py:67
  71.5 1.9 %collective-permute-done = f32[2,2,64,512]{3,2,0,1:T(8,128)S(1)} collective-permute-done((f32[2,2,64,512]{3,2,0,1:T(8,128)S(1)}, f32[2,2,64,512]{3,2,0,1:T(8,128)S(1)}, u32[]{:S(2)}, u32[]{:S(2)}) %collective-permute-start) | collective-permute-done | bytes 524320 | tf_op jit(solution)/shard_map/bin_exchange/ppermute | solution.py:76
  73.5 1.5 %collective-permute-start.1 = (f32[2,1,64,512]{3,2,0,1:T(8,128)S(1)}, f32[2,1,64,512]{3,2,0,1:T(8,128)S(1)}, u32[]{:S(2)}, u32[]{:S(2)}) collective-permute-start(f32[2,1,64,512]{3,2,0,1:T(8,128)S(1)} %slice_bitcast_fusion.12), channel_id=1, source_target_pairs={{0,2},{1,3},{2,0},{3,1},{4,6},{5,7},{6,4},{7,5},{8,10},{9,11},{10,... | collective-permute-start | bytes 786440 | tf_op jit(solution)/shard_map/bin_exchange/ppermute | solution.py:76
  75.1 6.9 %collective-permute-done.1 = f32[2,1,64,512]{3,2,0,1:T(8,128)S(1)} collective-permute-done((f32[2,1,64,512]{3,2,0,1:T(8,128)S(1)}, f32[2,1,64,512]{3,2,0,1:T(8,128)S(1)}, u32[]{:S(2)}, u32[]{:S(2)}) %collective-permute-start.1) | collective-permute-done | bytes 262176 | tf_op jit(solution)/shard_map/bin_exchange/ppermute | solution.py:76
  82.0 12.0 %all_to_all.28 = f32[2,8,8,512]{3,2,0,1:T(8,128)S(1)} all-to-all(f32[2,8,8,512]{3,2,0,1:T(8,128)S(1)} %copy.43), channel_id=1, replica_groups=mesh['wide'=8,'narrow'=4] {'wide'}, dimensions={1} | all-to-all | bytes 524288 | tf_op jit(solution)/shard_map/bin_exchange/all_to_all | solution.py:148
  94.4 0.7 maximum_multiply_fusion
  (38 shorter events, 1.8 us)
Async XLA Ops:
  3.2 8.6 %copy-start.3 = (s32[2]{0:T(128)S(1)}, s32[2]{0:T(128)}, u32[]{:S(2)}) copy-start(s32[2]{0:T(128)} %param.8) | copy-start | bytes 28
  3.2 9.2 %copy-start.4 = (s32[1,2,128]{2,1,0:T(2,128)S(1)}, s32[1,2,128]{2,1,0:T(2,128)}, u32[]{:S(2)}) copy-start(s32[1,2,128]{2,1,0:T(2,128)} %param.11) | copy-start | bytes 3076
  3.2 9.2 %copy-start.5 = (s32[1,2,128]{2,1,0:T(2,128)S(1)}, s32[1,2,128]{2,1,0:T(2,128)}, u32[]{:S(2)}) copy-start(s32[1,2,128]{2,1,0:T(2,128)} %param.10) | copy-start | bytes 3076
  3.2 9.2 %copy-start.6 = (s32[1,2,128]{2,1,0:T(2,128)S(1)}, s32[1,2,128]{2,1,0:T(2,128)}, u32[]{:S(2)}) copy-start(s32[1,2,128]{2,1,0:T(2,128)} %param.9) | copy-start | bytes 3076
  4.5 21.8 %all-to-all-start = ((bf16[8,2,64,256]{3,1,2,0:T(2,128)(2,1)}), bf16[8,2,64,256]{3,1,2,0:T(2,128)(2,1)S(1)}, u32[]{:S(2)}, u32[]{:S(2)}) async-start(bf16[8,2,64,256]{3,1,2,0:T(2,128)(2,1)} %copy.37), calls=%async_computation | async-start | bytes 1048576 | tf_op jit(solution)/shard_map/owner_share_exchange/all_to_all | solution.py:102
  27.7 29.6 %all-to-all-start.1 = ((bf16[8,2,2,64,256]{4,3,2,1,0:T(8,128)(2,1)}), bf16[8,2,2,64,256]{4,3,2,1,0:T(8,128)(2,1)S(1)}, u32[]{:S(2)}, u32[]{:S(2)}) async-start(bf16[8,2,2,64,256]{4,3,2,1,0:T(8,128)(2,1)} %broadcast_in_dim.12), calls=%async_computation.1 | async-start | bytes 2097152 | tf_op jit(solution)/shard_map/owner_share_exchange/all_to_all | solution.py:107
  58.9 2.2 %copy-start.1 = (bf16[512,2,2048]{2,0,1:T(8,128)(2,1)S(1)}, bf16[512,2,2048]{2,0,1:T(8,128)(2,1)}, u32[]{:S(2)}) copy-start(bf16[512,2,2048]{2,0,1:T(8,128)(2,1)} %fusion.35) | copy-start | bytes 12582916
  62.7 2.2 %copy-start = (bf16[512,2,2048]{2,0,1:T(8,128)(2,1)S(1)}, bf16[512,2,2048]{2,0,1:T(8,128)(2,1)}, u32[]{:S(2)}) copy-start(bf16[512,2,2048]{2,0,1:T(8,128)(2,1)} %fusion.33) | copy-start | bytes 12582916
  66.6 2.0 %copy-start.2 = (bf16[32,64,512]{2,1,0:T(8,128)(2,1)S(1)}, bf16[32,64,512]{2,1,0:T(8,128)(2,1)}, u32[]{:S(2)}) copy-start(bf16[32,64,512]{2,1,0:T(8,128)(2,1)} %get-tuple-element.16) | copy-start | bytes 6291460
  71.5 2.0 %collective-permute-start = (f32[2,2,64,512]{3,2,0,1:T(8,128)S(1)}, f32[2,2,64,512]{3,2,0,1:T(8,128)S(1)}, u32[]{:S(2)}, u32[]{:S(2)}) collective-permute-start(f32[2,2,64,512]{3,2,0,1:T(8,128)S(1)} %bitcast.146), channel_id=1, source_target_pairs={{0,1},{1,0},{2,3},{3,2},{4,5},{5,4},{6,7},{7,6},{8,9},{9,8},{10,11... | collective-permute-start | bytes 1572872 | tf_op jit(solution)/shard_map/bin_exchange/ppermute | solution.py:76
  73.5 8.4 %collective-permute-start.1 = (f32[2,1,64,512]{3,2,0,1:T(8,128)S(1)}, f32[2,1,64,512]{3,2,0,1:T(8,128)S(1)}, u32[]{:S(2)}, u32[]{:S(2)}) collective-permute-start(f32[2,1,64,512]{3,2,0,1:T(8,128)S(1)} %slice_bitcast_fusion.12), channel_id=1, source_target_pairs={{0,2},{1,3},{2,0},{3,1},{4,6},{5,7},{6,4},{7,5},{8,10},{9,11},{10,... | collective-permute-start | bytes 786440 | tf_op jit(solution)/shard_map/bin_exchange/ppermute | solution.py:76

commit v21 on v19

--- a/solution.py
+++ b/solution.py
@@ -123,9 +123,7 @@
             far_real, far_imag = jnp.einsum(
                 "pc,rcf->rpf", picker, gathered[0, s], preferred_element_type=jnp.bfloat16
             )
-            parts.append(
-                lax.optimization_barrier(cross_rows(near_rows, far_real, far_imag, gain))
-            )
+            parts.append(cross_rows(near_rows, far_real, far_imag, gain))
 
     with jax.named_scope("bin_sums"):
         real_sum = None

time: 97.6 us -> 95.8 us (0.982)
  other arithmetic: 10.6 us -> 4.9 us
  matrix products: 14.9 us -> 18.7 us
    convert_element_type x1 -> x0, other arithmetic: 5.61 us -> none  [cross_rows(): return (real_part.astype(jnp.bfloat16), imag_part.astype(jnp.bfloat16))]
    dot_general x2, matrix products: 1.66 us -> 3.72 us  [local(): jnp.dot(bin_hits, parts[s][0], preferred_element_type=jnp.float32)]
    dot_general x2, matrix products: 1.54 us -> 3.36 us  [local(): jnp.dot(bin_hits, parts[s][1], preferred_element_type=jnp.float32)]
  transfers between devices with their start and end apart: 4 -> 4, of which waited for: 4 -> 4; matrix products, arithmetic and copies ran while one was open for 13% -> 14% of each run, Pallas kernels for 0% -> 0%
where the time goes in v21:
time: 95.8 us; the launch traced here: 95.2 us
  waiting for transfers between devices  27.3 us (28%)
  matrix products  18.7 us (20%)
  blocking collectives  17 us (18%)
  starting transfers between devices  12.5 us (13%)
  local copies, waits for them, and re-layouts  10.6 us (11%)
  other arithmetic  4.9 us (5%)
  between operations  4.1 us (4%)
    all_to_all x1, waiting for transfers between devices, local(): lax.all_to_all(copies, 'wide', split_axis=0, concat_axis=4, tiled=True)  14.4 us
    all_to_all x1, blocking collectives, local(): lax.all_to_all(owned, 'wide', split_axis=1, concat_axis=1, tiled=True)  12 us
    ppermute x2, waiting for transfers between devices, halving_sum(): parts = paired[:, :, 0] + lax.ppermute(paired[:, :, 1], axis, pairs)  8.76 us
    all_to_all x1, starting transfers between devices, local(): lax.all_to_all(outgoing, 'wide', split_axis=0, concat_axis=0, tiled=True)  7.28 us
    dot_general x2, matrix products, select_rows(): chosen = jnp.dot(picker, flat_block, preferred_element_type=jnp.bfloat16)  6.57 us
    all_gather x1, blocking collectives, local(): ids = lax.all_gather(ids, 'narrow', axis=2, tiled=True)  5.09 us
    all_to_all x1, waiting for transfers between devices, local(): lax.all_to_all(outgoing, 'wide', split_axis=0, concat_axis=0, tiled=True)  4.15 us
    dot_general x2, matrix products, local(): jnp.dot(bin_hits, parts[s][0], preferred_element_type=jnp.float32)  3.72 us
  transfers between devices with their start and end apart: 4, of which 4 were waited for; matrix products, arithmetic and copies ran while one was open for 14% of the time, Pallas kernels for 0%

profile of v21, /device:TPU:0, one launch (start us, length us, event | category | flops | bytes accessed | tf_op | source)
XLA Modules:
  0.0 95.2 jit_solution(15639636271878122765)
XLA Ops:
  0.0 3.2 %reshape.252 = bf16[64,2,4,8,256]{4,3,2,1,0:T(8,128)(2,1)S(1)} reshape(bf16[64,2,8192]{2,1,0:T(2,128)(2,1)} %param.6) | data formatting | bytes 4194304 | tf_op jit(solution)/shard_map/owner_share_exchange/reshape | solution.py:97
  3.3 1.2 %copy.45 = bf16[8,2,64,256]{3,1,2,0:T(2,128)(2,1)} copy(bf16[8,2,64,256]{3,0,1,2:T(8,128)(2,1)S(1)} %dynamic-slice_bitcast_fusion) | data formatting | bytes 1048576 | tf_op jit(solution)/shard_map/owner_share_exchange/transpose | solution.py:101
  4.5 7.3 %all-to-all-start = ((bf16[8,2,64,256]{3,1,2,0:T(2,128)(2,1)}), bf16[8,2,64,256]{3,1,2,0:T(2,128)(2,1)S(1)}, u32[]{:S(2)}, u32[]{:S(2)}) async-start(bf16[8,2,64,256]{3,1,2,0:T(2,128)(2,1)} %copy.45), calls=%async_computation | async-start | bytes 1048576 | tf_op jit(solution)/shard_map/owner_share_exchange/all_to_all | solution.py:102
  11.8 0.6 fusion.78
  16.3 0.7 dynamic_slice.21
  17.0 5.1 %all_gather.3 = s32[3,2,512]{2,1,0:T(2,128)S(1)} all-gather(s32[3,2,128]{2,1,0:T(2,128)S(1)} %pad_add_fusion), channel_id=1, replica_groups=mesh['wide'=8,'narrow'=4] {'narrow'}, dimensions={2}, use_global_device_ids=true | all-gather | bytes 15360 | tf_op jit(solution)/shard_map/all_gather | solution.py:110
  22.1 4.2 %all-to-all-done = bf16[8,2,64,256]{3,1,2,0:T(2,128)(2,1)S(1)} async-done(((bf16[8,2,64,256]{3,1,2,0:T(2,128)(2,1)}), bf16[8,2,64,256]{3,1,2,0:T(2,128)(2,1)S(1)}, u32[]{:S(2)}, u32[]{:S(2)}) %all-to-all-start) | async-done | bytes 524320 | tf_op jit(solution)/shard_map/owner_share_exchange/all_to_all | solution.py:102
  26.6 1.1 %broadcast_in_dim.12 = bf16[8,2,2,64,256]{4,3,2,1,0:T(8,128)(2,1)} broadcast(bf16[2,2,64,256]{3,2,1,0:T(8,128)(2,1)S(1)} %copy.46), dimensions={1,2,3,4} | broadcast | bytes 1179648 | tf_op jit(solution)/shard_map/owner_share_exchange/broadcast_in_dim | solution.py:106
  27.7 3.6 %all-to-all-start.1 = ((bf16[8,2,2,64,256]{4,3,2,1,0:T(8,128)(2,1)}), bf16[8,2,2,64,256]{4,3,2,1,0:T(8,128)(2,1)S(1)}, u32[]{:S(2)}, u32[]{:S(2)}) async-start(bf16[8,2,2,64,256]{4,3,2,1,0:T(8,128)(2,1)} %broadcast_in_dim.12), calls=%async_computation.1 | async-start | bytes 2097152 | tf_op jit(solution)/shard_map/owner_share_exchange/all_to_all | solution.py:107
  31.3 0.3 fusion.72
  31.7 0.5 fusion.66
  32.2 1.4 %constant_dynamic-slice_fusion.2 = bf16[64,2,2048]{2,1,0:T(2,128)(2,1)S(1)} fusion(bf16[64,2,8192]{2,1,0:T(2,128)(2,1)} %param.6, s32[]{:T(128)S(6)} %select_n.65), kind=kLoop, calls=%fused_computation.136 | loop fusion | bytes 1048580 | tf_op jit(solution)/shard_map/dynamic_slice | solution.py:92
  33.6 2.7 %add_convert_fusion = (bf16[32,64,512]{2,1,0:T(8,128)(2,1)}, bf16[32,64,512]{2,1,0:T(8,128)(2,1)S(1)}) fusion(f32[64,512]{1,0:T(8,128)S(1)} %get-tuple-element.29, f32[32,512]{1,0:T(8,128)S(1)} %get-tuple-element.27, f32[64,512]{1,0:T(8,128)S(1)} %get-tuple-element.28, f32[32,512]{1,0:T(8,128)S(1)} %get-tuple-element.26), kind=kLoop, calls=%fused_computation.20 | loop fusion | flops 8388608 | bytes 4587520 | tf_op jit(solution)/shard_map/lag_product/convert_element_type | solution.py:32
  36.3 3.3 %fusion.35 = bf16[512,2,2048]{2,0,1:T(8,128)(2,1)} fusion(s32[512]{0:T(512)S(1)} %bitcast.197, bf16[8,8,2,2048]{3,2,1,0:T(2,128)(2,1)S(1)} %bitcast.183), kind=kOutput, calls=%fused_computation.59 | convolution fusion | flops 268468224 | bytes 4720640 | tf_op jit(solution)/shard_map/cross_spectra/dot_general | solution.py:42
  39.6 3.3 %fusion.33 = bf16[512,2,2048]{2,0,1:T(8,128)(2,1)} fusion(s32[512]{0:T(512)S(1)} %bitcast.196, bf16[8,8,2,2048]{3,2,1,0:T(2,128)(2,1)S(1)} %bitcast.184), kind=kOutput, calls=%fused_computation.57 | convolution fusion | flops 268468224 | bytes 4720640 | tf_op jit(solution)/shard_map/cross_spectra/dot_general | solution.py:42
  42.9 14.4 %all-to-all-done.1 = bf16[8,2,2,64,256]{4,3,2,1,0:T(8,128)(2,1)S(1)} async-done(((bf16[8,2,2,64,256]{4,3,2,1,0:T(8,128)(2,1)}), bf16[8,2,2,64,256]{4,3,2,1,0:T(8,128)(2,1)S(1)}, u32[]{:S(2)}, u32[]{:S(2)}) %all-to-all-start.1) | async-done | bytes 1048608 | tf_op jit(solution)/shard_map/owner_share_exchange/all_to_all | solution.py:107
  57.4 1.3 %convolution_bitcast_fusion.1 = bf16[2,512,2048]{2,1,0:T(8,128)(2,1)S(1)} fusion(bf16[1,2,2,64,2048]{4,3,2,1,0:T(8,128)(2,1)S(1)} %bitcast.185, s32[512]{0:T(512)S(1)} %bitcast.195), kind=kOutput, calls=%fused_computation.23 | convolution fusion | flops 268468224 | bytes 4720640 | tf_op jit(solution)/shard_map/cross_spectra/pc,rcf->rpf/dot_general | solution.py:123
  58.7 0.8 copy-done.1
  59.5 1.5 %fusion.18 = f32[256,2048]{1,0:T(8,128)S(1)} fusion(f32[2048]{0:T(1024)S(1)} %dynamic_slice.21, bf16[512,2,2048]{2,0,1:T(8,128)(2,1)S(1)} %copy-done.1, bf16[2,512,2048]{2,1,0:T(8,128)(2,1)S(1)} %convolution_bitcast_fusion.1, s32[512]{0:T(512)S(1)} %bitcast.200), kind=kOutput, calls=%fused_computation.33 | convolution fusion | flops 546439168 | bytes 10496000 | tf_op jit(solution)/shard_map/bin_sums/dot_general | solution.py:136
  61.0 1.5 %fusion.16 = f32[256,2048]{1,0:T(8,128)S(1)} fusion(f32[2048]{0:T(1024)S(1)} %dynamic_slice.21, bf16[512,2,2048]{2,0,1:T(8,128)(2,1)S(1)} %copy-done.1, bf16[2,512,2048]{2,1,0:T(8,128)(2,1)S(1)} %convolution_bitcast_fusion.1, s32[512]{0:T(512)S(1)} %bitcast.201), kind=kOutput, calls=%fused_computation.32 | convolution fusion | flops 546439168 | bytes 10496000 | tf_op jit(solution)/shard_map/bin_sums/dot_general | solution.py:135
  62.5 1.3 %convolution_bitcast_fusion = bf16[2,512,2048]{2,1,0:T(8,128)(2,1)S(1)} fusion(bf16[1,2,2,64,2048]{4,3,2,1,0:T(8,128)(2,1)S(1)} %bitcast.186, s32[512]{0:T(512)S(1)} %bitcast.194), kind=kOutput, calls=%fused_computation.22 | convolution fusion | flops 268468224 | bytes 4720640 | tf_op jit(solution)/shard_map/cross_spectra/pc,rcf->rpf/dot_general | solution.py:123
  63.8 0.9 copy-done
  64.7 1.8 %reduce-precision_convert_fusion = (bf16[256,2048]{1,0:T(8,128)(2,1)S(1)}, bf16[256,2048]{1,0:T(8,128)(2,1)S(1)}) fusion(f32[256,2048]{1,0:T(8,128)S(1)} %fusion.18, f32[2048]{0:T(1024)S(1)} %dynamic_slice.21, bf16[512,2,2048]{2,0,1:T(8,128)(2,1)S(1)} %copy-done, bf16[2,512,2048]{2,1,0:T(8,128)(2,1)S(1)} %convolution_bitcast_fusion, s32[512]{0:T(512)S(1)} %bitcast.198), kind=kOutput, calls=%fused_computation.25 | convolution fusion | flops 549060608 | bytes 12593152 | tf_op jit(solution)/shard_map/bin_sums/dot_general | solution.py:136
  66.6 2.2 %reduce-precision_convert_fusion.1 = (bf16[256,2048]{1,0:T(8,128)(2,1)S(1)}, f32[256]{0:T(256)S(1)}, bf16[256,2048]{1,0:T(8,128)(2,1)S(1)}) fusion(f32[256,2048]{1,0:T(8,128)S(1)} %fusion.16, f32[2048]{0:T(1024)S(1)} %dynamic_slice.21, bf16[512,2,2048]{2,0,1:T(8,128)(2,1)S(1)} %copy-done, bf16[2,512,2048]{2,1,0:T(8,128)(2,1)S(1)} %convolution_bitcast_fusion, ...), kind=kOutput, calls=%fused_computation.27 | convolution fusion | flops 549584640 | bytes 12594176 | tf_op jit(solution)/shard_map/bin_sums/dot_general | solution.py:135
  68.8 1.2 %fusion.24 = f32[512,512]{1,0:T(8,128)S(1)} fusion(bf16[2048,512]{1,0:T(8,128)(2,1)S(1)} %bitcast.189, bf16[256,2048]{1,0:T(8,128)(2,1)S(1)} %get-tuple-element.8, bf16[256,2048]{1,0:T(8,128)(2,1)S(1)} %get-tuple-element.7), kind=kOutput, calls=%fused_computation.46 | convolution fusion | flops 1077936128 | bytes 5242880 | tf_op jit(solution)/shard_map/lag_product/dot_general | solution.py:67
  70.0 1.2 %fusion.20 = f32[512,512]{1,0:T(8,128)S(1)} fusion(bf16[2048,512]{1,0:T(8,128)(2,1)S(1)} %bitcast.188, bf16[256,2048]{1,0:T(8,128)(2,1)S(1)} %get-tuple-element.11, bf16[256,2048]{1,0:T(8,128)(2,1)S(1)} %get-tuple-element.9), kind=kOutput, calls=%fused_computation.42 | convolution fusion | flops 1077936128 | bytes 5242880 | tf_op jit(solution)/shard_map/lag_product/dot_general | solution.py:67
  71.7 1.9 %collective-permute-done = f32[2,2,64,512]{3,2,0,1:T(8,128)S(1)} collective-permute-done((f32[2,2,64,512]{3,2,0,1:T(8,128)S(1)}, f32[2,2,64,512]{3,2,0,1:T(8,128)S(1)}, u32[]{:S(2)}, u32[]{:S(2)}) %collective-permute-start) | collective-permute-done | bytes 524320 | tf_op jit(solution)/shard_map/bin_exchange/ppermute | solution.py:76
  73.7 1.5 %collective-permute-start.1 = (f32[2,1,64,512]{3,2,0,1:T(8,128)S(1)}, f32[2,1,64,512]{3,2,0,1:T(8,128)S(1)}, u32[]{:S(2)}, u32[]{:S(2)}) collective-permute-start(f32[2,1,64,512]{3,2,0,1:T(8,128)S(1)} %slice_bitcast_fusion.28), channel_id=1, source_target_pairs={{0,2},{1,3},{2,0},{3,1},{4,6},{5,7},{6,4},{7,5},{8,10},{9,11},{10,... | collective-permute-start | bytes 786440 | tf_op jit(solution)/shard_map/bin_exchange/ppermute | solution.py:76
  75.2 6.9 %collective-permute-done.1 = f32[2,1,64,512]{3,2,0,1:T(8,128)S(1)} collective-permute-done((f32[2,1,64,512]{3,2,0,1:T(8,128)S(1)}, f32[2,1,64,512]{3,2,0,1:T(8,128)S(1)}, u32[]{:S(2)}, u32[]{:S(2)}) %collective-permute-start.1) | collective-permute-done | bytes 262176 | tf_op jit(solution)/shard_map/bin_exchange/ppermute | solution.py:76
  82.2 12.0 %all_to_all.28 = f32[2,8,8,512]{3,2,0,1:T(8,128)S(1)} all-to-all(f32[2,8,8,512]{3,2,0,1:T(8,128)S(1)} %copy.53), channel_id=1, replica_groups=mesh['wide'=8,'narrow'=4] {'wide'}, dimensions={1} | all-to-all | bytes 524288 | tf_op jit(solution)/shard_map/bin_exchange/all_to_all | solution.py:152
  94.2 0.3 rev.4
  94.5 0.7 maximum_multiply_fusion
  (36 shorter events, 1.2 us)
Async XLA Ops:
  0.0 11.8 %copy-start.3 = (s32[2]{0:T(128)S(1)}, s32[2]{0:T(128)}, u32[]{:S(2)}) copy-start(s32[2]{0:T(128)} %param.8) | copy-start | bytes 28
  0.0 12.4 %copy-start.5 = (s32[1,2,128]{2,1,0:T(2,128)S(1)}, s32[1,2,128]{2,1,0:T(2,128)}, u32[]{:S(2)}) copy-start(s32[1,2,128]{2,1,0:T(2,128)} %param.10) | copy-start | bytes 3076
  0.0 12.4 %copy-start.4 = (s32[1,2,128]{2,1,0:T(2,128)S(1)}, s32[1,2,128]{2,1,0:T(2,128)}, u32[]{:S(2)}) copy-start(s32[1,2,128]{2,1,0:T(2,128)} %param.11) | copy-start | bytes 3076
  0.0 12.4 %copy-start.6 = (s32[1,2,128]{2,1,0:T(2,128)S(1)}, s32[1,2,128]{2,1,0:T(2,128)}, u32[]{:S(2)}) copy-start(s32[1,2,128]{2,1,0:T(2,128)} %param.9) | copy-start | bytes 3076
  4.5 21.8 %all-to-all-start = ((bf16[8,2,64,256]{3,1,2,0:T(2,128)(2,1)}), bf16[8,2,64,256]{3,1,2,0:T(2,128)(2,1)S(1)}, u32[]{:S(2)}, u32[]{:S(2)}) async-start(bf16[8,2,64,256]{3,1,2,0:T(2,128)(2,1)} %copy.45), calls=%async_computation | async-start | bytes 1048576 | tf_op jit(solution)/shard_map/owner_share_exchange/all_to_all | solution.py:102
  27.7 29.6 %all-to-all-start.1 = ((bf16[8,2,2,64,256]{4,3,2,1,0:T(8,128)(2,1)}), bf16[8,2,2,64,256]{4,3,2,1,0:T(8,128)(2,1)S(1)}, u32[]{:S(2)}, u32[]{:S(2)}) async-start(bf16[8,2,2,64,256]{4,3,2,1,0:T(8,128)(2,1)} %broadcast_in_dim.12), calls=%async_computation.1 | async-start | bytes 2097152 | tf_op jit(solution)/shard_map/owner_share_exchange/all_to_all | solution.py:107
  57.3 2.2 %copy-start.1 = (bf16[512,2,2048]{2,0,1:T(8,128)(2,1)S(1)}, bf16[512,2,2048]{2,0,1:T(8,128)(2,1)}, u32[]{:S(2)}) copy-start(bf16[512,2,2048]{2,0,1:T(8,128)(2,1)} %fusion.35) | copy-start | bytes 12582916
  62.5 2.2 %copy-start = (bf16[512,2,2048]{2,0,1:T(8,128)(2,1)S(1)}, bf16[512,2,2048]{2,0,1:T(8,128)(2,1)}, u32[]{:S(2)}) copy-start(bf16[512,2,2048]{2,0,1:T(8,128)(2,1)} %fusion.33) | copy-start | bytes 12582916
  66.6 2.2 %copy-start.2 = (bf16[32,64,512]{2,1,0:T(8,128)(2,1)S(1)}, bf16[32,64,512]{2,1,0:T(8,128)(2,1)}, u32[]{:S(2)}) copy-start(bf16[32,64,512]{2,1,0:T(8,128)(2,1)} %get-tuple-element.16) | copy-start | bytes 6291460
  71.6 2.0 %collective-permute-start = (f32[2,2,64,512]{3,2,0,1:T(8,128)S(1)}, f32[2,2,64,512]{3,2,0,1:T(8,128)S(1)}, u32[]{:S(2)}, u32[]{:S(2)}) collective-permute-start(f32[2,2,64,512]{3,2,0,1:T(8,128)S(1)} %bitcast.192), channel_id=1, source_target_pairs={{0,1},{1,0},{2,3},{3,2},{4,5},{5,4},{6,7},{7,6},{8,9},{9,8},{10,11... | collective-permute-start | bytes 1572872 | tf_op jit(solution)/shard_map/bin_exchange/ppermute | solution.py:76
  73.7 8.4 %collective-permute-start.1 = (f32[2,1,64,512]{3,2,0,1:T(8,128)S(1)}, f32[2,1,64,512]{3,2,0,1:T(8,128)S(1)}, u32[]{:S(2)}, u32[]{:S(2)}) collective-permute-start(f32[2,1,64,512]{3,2,0,1:T(8,128)S(1)} %slice_bitcast_fusion.28), channel_id=1, source_target_pairs={{0,2},{1,3},{2,0},{3,1},{4,6},{5,7},{6,4},{7,5},{8,10},{9,11},{10,... | collective-permute-start | bytes 786440 | tf_op jit(solution)/shard_map/bin_exchange/ppermute | solution.py:76
